TPU v7x, 128 devices: a whole 4x4x4 slice. The times are simulated.
128 devices in a mesh: sub: 8 (over x_hi, z), grp: 16 (over x_lo, y, core).
Axes of the slice: x: 4 (x_hi: 2, x_lo: 2; x = x_hi * 2 + x_lo), y: 4, z: 4, core: 2. Of those that a mesh axis runs over, the one named last changes fastest.
Arguments:
- potential_init: float32 [64, 128, 128, 128], P('grp', 'sub'), may hold values from -6 to 6
- conductivity: float32 [128, 128, 128], P('sub')
- inverse_rows: float32 [128, 24, 128, 128], P('sub', None, 'grp')
- electrodes: int32 [64, 2], replicated, may hold values from 0 to 2097151
- intersection_width: int32 [8], P('sub'), may hold values from 1 to 4, as said below
Outputs:
- potential: float32 [64, 128, 128, 128], P('grp', 'sub')
- residual_norms: float32 [64], P('grp')
Inputs may be any that keep to these rules, and one draw needn't show every extreme that they name: `intersection_width`: some subdomain has intersection 4.
All inputs are finite; a program needn't handle non-finite values.
Results may differ from a plain program's by a relative error of at most 0.0003.
Values sent between devices are 32-bit elements; how exact they have to be, the bound alone decides.
No kernel may reach another device: no remote copies, remote signals or barrier semaphores. Data moves between devices by JAX's collectives and lax.ppermute only.
A program may use at most 448 MiB of HBM per device.

v0:
```python
import jax
import jax.numpy as jnp
from jax import lax
from jax.sharding import PartitionSpec as P

ITERS = 2


CURRENT = 16.0
MASS = 1.0


def extended_2(cells, sides, width):
    for axis, dim in sides:
        count = lax.axis_size(axis)
        ends = count - 1
        head = lax.slice_in_dim(cells, 0, width, axis=dim)
        tail = lax.slice_in_dim(cells, cells.shape[dim] - width, cells.shape[dim], axis=dim)
        cells = jnp.concatenate(
            [
                lax.ppermute(tail, axis, [(i, (i + 1) % count) for i in range(ends)]),
                cells,
                lax.ppermute(head, axis, [((i + 1) % count, i) for i in range(ends)]),
            ],
            axis=dim,
        )
    return cells


def neighbours(padded):
    return [
        padded[..., 2:, 1:-1, 1:-1],
        padded[..., :-2, 1:-1, 1:-1],
        padded[..., 1:-1, 2:, 1:-1],
        padded[..., 1:-1, :-2, 1:-1],
        padded[..., 1:-1, 1:-1, 2:],
        padded[..., 1:-1, 1:-1, :-2],
    ]


def face_terms(conduct_pad):
    center_cells = conduct_pad[1:-1, 1:-1, 1:-1]
    face_coefs = [0.5 * (center_cells + beside_cell) for beside_cell in neighbours(conduct_pad)]
    center_coef = MASS * center_cells
    for face_coef in face_coefs:
        center_coef = center_coef + face_coef
    return (center_coef, face_coefs)


def apply_operator(values_in, padded, center_coef, face_coefs):
    image = center_coef * values_in
    for face_coef, beside_cell in zip(face_coefs, neighbours(padded)):
        image = image - face_coef * beside_cell
    return image


def source_block(pairs, x_start, width_x, rows_y, full_y, depth):
    x_ids = x_start + lax.broadcasted_iota(jnp.int32, (width_x, rows_y, depth), 0)
    y_ids = lax.broadcasted_iota(jnp.int32, (width_x, rows_y, depth), 1)
    z_ids = lax.broadcasted_iota(jnp.int32, (width_x, rows_y, depth), 2)
    flat_ids = (x_ids * full_y + y_ids) * depth + z_ids
    first = (flat_ids[None] == pairs[:, 0][:, None, None, None]).astype(jnp.float32)
    second = (flat_ids[None] == pairs[:, 1][:, None, None, None]).astype(jnp.float32)
    return CURRENT * first - CURRENT * second


def on_device(potential_init, conductivity, inverse_rows, electrodes, intersection_width):
    local_src, width_x, full_y, depth = potential_init.shape
    grp_index = lax.axis_index("grp")
    sub_index = lax.axis_index("sub")
    extended = inverse_rows.shape[1]
    margin = (extended - width_x) // 2
    cell_count = float(width_x * lax.axis_size("sub") * full_y * depth)
    column_ids = jnp.arange(extended, dtype=jnp.int32)
    reach = intersection_width[0]
    intersection_mask = (
        (column_ids >= margin - reach) & (column_ids < width_x + margin + reach)
    ).astype(jnp.float32)[:, None, None]
    conduct_rim = extended_2(conductivity, (("sub", 0),), 1)
    conduct_pad = jnp.pad(conduct_rim, ((0, 0), (1, 1), (1, 1)))
    x_start = sub_index * width_x
    center_coef, face_coefs = face_terms(conduct_pad)
    own_pairs = lax.dynamic_slice_in_dim(electrodes, grp_index * local_src, local_src, 0)
    source_term = source_block(own_pairs, x_start, width_x, full_y, full_y, depth)

    def residual_of(potential):
        padded = extended_2(potential, (("sub", 1),), 1)
        padded = jnp.pad(padded, ((0, 0), (0, 0), (1, 1), (1, 1)))
        return source_term - apply_operator(potential, padded, center_coef, face_coefs)

    potential = potential_init
    for sweep in range(ITERS):
        residual = residual_of(potential)
        residual_cells = lax.all_to_all(residual, "grp", split_axis=2, concat_axis=0, tiled=True)
        extended_resid = extended_2(residual_cells, (("sub", 1),), margin) * intersection_mask
        correction = jnp.einsum(
            "ijyz,sjyz->siyz", inverse_rows, extended_resid, precision=lax.Precision.HIGHEST
        )
        potential = potential + lax.all_to_all(
            correction, "grp", split_axis=0, concat_axis=2, tiled=True
        )
    residual = residual_of(potential)
    totals = lax.psum(jnp.sum(residual * residual, axis=(1, 2, 3)), "sub")
    residual_norms = jnp.sqrt(totals / cell_count)
    return (potential, residual_norms)


def solution(mesh):
    in_specs = (
        P("grp", "sub", None, None),
        P("sub", None, None),
        P("sub", None, "grp", None),
        P(),
        P("sub"),
    )
    out_specs = (P("grp", "sub", None, None), P("grp"))
    return jax.shard_map(
        on_device, mesh=mesh, in_specs=in_specs, out_specs=out_specs, check_vma=False
    )
```

profile of v0, /device:TPU:6, one launch (start us, length us, event | category | flops | bytes accessed | tf_op | source)
XLA Modules:
  0.0 553.2 jit_solution(2252300085221742015)
XLA Ops:
  1.5 3.8 collective-permute-start.1
  5.4 5.6 %collective-permute-start = (f32[1,128,128]{2,1,0:T(8,128)S(1)}, f32[1,128,128]{2,1,0:T(8,128)S(1)}, u32[]{:S(2)}, u32[]{:S(2)}) collective-permute-start(f32[1,128,128]{2,1,0:T(8,128)S(1)} %get-tuple-element.20), channel_id=1, source_target_pairs={{16,0},{32,16},{48,32},{64,48},{80,64},{96,80},{112,96},{17,1},{33... | collective-permute-start | bytes 196616 | tf_op jit(solution)/shard_map/ppermute | solution.py:23
  11.0 1.9 fusion.47
  12.9 1.9 collective-permute-start.3
  14.8 7.5 %collective-permute-start.2 = (f32[4,1,128,128]{3,2,1,0:T(8,128)}, f32[4,1,128,128]{3,2,1,0:T(8,128)}, u32[]{:S(2)}, u32[]{:S(2)}) collective-permute-start(f32[4,1,128,128]{3,2,1,0:T(8,128)} %get-tuple-element.11), channel_id=1, source_target_pairs={{16,0},{32,16},{48,32},{64,48},{80,64},{96,80},{112,96},{17,1},{33... | collective-permute-start | bytes 786440 | tf_op jit(solution)/shard_map/ppermute | solution.py:23
  22.3 1.2 iota_add_fusion
  23.6 2.0 select_maximum_fusion.6
  25.7 3.2 add_add_fusion
  28.9 8.6 %select_maximum_fusion.4 = f32[4,18,130,130]{3,2,1,0:T(8,128)} fusion(f32[4,1,128,128]{3,2,1,0:T(8,128)} %collective-permute-done.2, f32[4,16,128,128]{3,2,1,0:T(8,128)S(1)} %copy-done.4, f32[4,1,128,128]{3,2,1,0:T(8,128)S(1)} %collective-permute-done.3), kind=kLoop, calls=%fused_computation.8 | loop fusion | flops 18252000 | bytes 9585792 | tf_op jit(solution)/shard_map/concatenate | solution.py:19
  37.5 20.5 %fusion.24 = f32[4,16,128,128]{3,2,1,0:T(8,128)} fusion(f32[4,18,130,130]{3,2,1,0:T(8,128)} %select_maximum_fusion.4, f32[4,16,128,128]{3,2,1,0:T(8,128)} %param.5, f32[4,1,128,128]{3,2,1,0:T(8,128)S(1)} %collective-permute-done.3, f32[4,1,128,128]{3,2,1,0:T(8,128)} %collective-permute-done.2, f32[16,128,128]{2,1,0:T(8,128)} %get-tuple-element.15, ...), kind=kLoop, calls=%fused_computation.49 | loop fusion | flops 22020096 | bytes 34078752 | tf_op jit(solution)/shard_map/sub | solution.py:89
  57.9 4.6 copy.29
  62.5 54.8 %all_to_all.72 = f32[4,16,128,128]{3,1,0,2:T(8,128)S(1)} all-to-all(f32[4,16,128,128]{3,1,0,2:T(8,128)S(1)} %copy.29), channel_id=1, replica_groups=mesh['sub'=8,'grp'=16] {'grp'}, dimensions={2} | all-to-all | bytes 8388608 | tf_op jit(solution)/shard_map/all_to_all | solution.py:94
  117.3 3.3 copy.31
  120.6 2.0 copy-done.7
  122.6 1.6 fusion.46
  124.2 1.9 collective-permute-start.4
  126.1 7.5 %collective-permute-start.5 = (f32[64,4,8,128]{3,2,1,0:T(8,128)}, f32[64,4,8,128]{3,2,1,0:T(8,128)}, u32[]{:S(2)}, u32[]{:S(2)}) collective-permute-start(f32[64,4,8,128]{3,2,1,0:T(8,128)} %get-tuple-element.9), channel_id=1, source_target_pairs={{16,0},{32,16},{48,32},{64,48},{80,64},{96,80},{112,96},{17,1},{33... | collective-permute-start | bytes 3145736 | tf_op jit(solution)/shard_map/ppermute | solution.py:23
  134.3 5.6 %copy.33 = f32[16,24,8,128]{1,0,3,2:T(8,128)} copy(f32[16,24,8,128]{3,2,1,0:T(8,128)} %param.7) | data formatting | bytes 3145728 | tf_op args[2]
  139.9 15.3 %collective-permute-done.4 = f32[64,4,8,128]{3,2,1,0:T(8,128)} collective-permute-done((f32[64,4,8,128]{3,2,1,0:T(8,128)}, f32[64,4,8,128]{3,2,1,0:T(8,128)}, u32[]{:S(2)}, u32[]{:S(2)}) %collective-permute-start.4) | collective-permute-done | bytes 1048608 | tf_op jit(solution)/shard_map/ppermute | solution.py:21
  155.2 1.2 collective-permute-done.5
  156.4 5.0 maximum_multiply_fusion
  161.3 10.3 %copy.32 = f32[64,24,8,128]{0,1,3,2:T(8,128)} copy(f32[64,24,8,128]{3,2,1,0:T(8,128)} %maximum_multiply_fusion) | data formatting | bytes 12582912 | tf_op jit(solution)/shard_map/mul | solution.py:95
  171.6 17.7 %convolution_bitcast_fusion.1 = f32[64,16,8,128]{0,1,3,2:T(8,128)} fusion(f32[64,24,8,128]{0,1,3,2:T(8,128)} %copy.32, f32[16,24,8,128]{1,0,3,2:T(8,128)} %copy.33), kind=kOutput, calls=%fused_computation.70 | convolution fusion | flops 301989888 | bytes 12058624 | tf_op jit(solution)/shard_map/ijyz,sjyz->siyz/dot_general | solution.py:96
  189.3 7.1 %copy.34 = f32[64,16,8,128]{3,2,1,0:T(8,128)} copy(f32[64,16,8,128]{0,1,3,2:T(8,128)} %convolution_bitcast_fusion.1) | data formatting | bytes 8388608 | tf_op jit(solution)/shard_map/ijyz,sjyz->siyz/transpose | solution.py:96
  196.4 53.2 %all_to_all.73 = f32[64,16,8,128]{3,2,1,0:T(8,128)S(1)} all-to-all(f32[64,16,8,128]{3,2,1,0:T(8,128)} %copy.34), channel_id=1, replica_groups=mesh['sub'=8,'grp'=16] {'grp'}, dimensions={0} | all-to-all | bytes 8388608 | tf_op jit(solution)/shard_map/all_to_all | solution.py:99
  250.5 1.9 collective-permute-start.7
  252.4 17.2 %collective-permute-start.6 = (f32[4,1,128,128]{3,2,1,0:T(8,128)S(1)}, f32[4,1,128,128]{3,2,1,0:T(8,128)S(1)}, u32[]{:S(2)}, u32[]{:S(2)}) collective-permute-start(f32[4,1,128,128]{3,2,1,0:T(8,128)S(1)} %get-tuple-element.7), channel_id=1, source_target_pairs={{16,0},{32,16},{48,32},{64,48},{80,64},{96,80},{112,96},{17,1},{33... | collective-permute-start | bytes 786440 | tf_op jit(solution)/shard_map/ppermute | solution.py:23
  270.4 7.6 %select_maximum_fusion.2 = f32[4,18,130,130]{3,2,1,0:T(8,128)} fusion(f32[4,1,128,128]{3,2,1,0:T(8,128)S(1)} %collective-permute-done.6, f32[4,16,128,128]{3,2,1,0:T(8,128)S(1)} %bitcast_add_fusion.1, f32[4,1,128,128]{3,2,1,0:T(8,128)S(1)} %collective-permute-done.7), kind=kLoop, calls=%fused_computation.6 | loop fusion | flops 18252000 | bytes 9585792 | tf_op jit(solution)/shard_map/concatenate | solution.py:19
  278.0 20.6 %fusion.15 = f32[4,16,128,128]{3,2,1,0:T(8,128)} fusion(f32[4,18,130,130]{3,2,1,0:T(8,128)} %select_maximum_fusion.2, f32[4,16,128,128]{3,2,1,0:T(8,128)} %copy-done.2, f32[4,1,128,128]{3,2,1,0:T(8,128)S(1)} %collective-permute-done.7, f32[4,1,128,128]{3,2,1,0:T(8,128)} %copy-done.10, f32[16,128,128]{2,1,0:T(8,128)} %get-tuple-element.15, ...), kind=kLoop, calls=%fused_computation.34 | loop fusion | flops 22020096 | bytes 34078752 | tf_op jit(solution)/shard_map/sub | solution.py:89
  298.6 4.6 copy.36
  303.2 52.7 %all_to_all.74 = f32[4,16,128,128]{3,1,0,2:T(8,128)S(1)} all-to-all(f32[4,16,128,128]{3,1,0,2:T(8,128)S(1)} %copy.36), channel_id=1, replica_groups=mesh['sub'=8,'grp'=16] {'grp'}, dimensions={2} | all-to-all | bytes 8388608 | tf_op jit(solution)/shard_map/all_to_all | solution.py:94
  356.0 3.3 copy.38
  359.5 1.9 collective-permute-start.8
  361.4 7.7 %collective-permute-start.9 = (f32[64,4,8,128]{3,2,1,0:T(8,128)S(1)}, f32[64,4,8,128]{3,2,1,0:T(8,128)S(1)}, u32[]{:S(2)}, u32[]{:S(2)}) collective-permute-start(f32[64,4,8,128]{3,2,1,0:T(8,128)S(1)} %get-tuple-element.5), channel_id=1, source_target_pairs={{16,0},{32,16},{48,32},{64,48},{80,64},{96,80},{112,96},{17,1},{33... | collective-permute-start | bytes 3145736 | tf_op jit(solution)/shard_map/ppermute | solution.py:23
  369.1 21.0 %collective-permute-done.8 = f32[64,4,8,128]{3,2,1,0:T(8,128)S(1)} collective-permute-done((f32[64,4,8,128]{3,2,1,0:T(8,128)S(1)}, f32[64,4,8,128]{3,2,1,0:T(8,128)S(1)}, u32[]{:S(2)}, u32[]{:S(2)}) %collective-permute-start.8) | collective-permute-done | bytes 1048608 | tf_op jit(solution)/shard_map/ppermute | solution.py:21
  390.1 1.2 collective-permute-done.9
  391.3 3.1 maximum_multiply_fusion.1
  394.5 10.3 %copy.39 = f32[64,24,8,128]{0,1,3,2:T(8,128)} copy(f32[64,24,8,128]{3,2,1,0:T(8,128)} %maximum_multiply_fusion.1) | data formatting | bytes 12582912 | tf_op jit(solution)/shard_map/mul | solution.py:95
  404.7 17.7 %convolution_bitcast_fusion = f32[64,16,8,128]{0,1,3,2:T(8,128)} fusion(f32[64,24,8,128]{0,1,3,2:T(8,128)} %copy.39, f32[16,24,8,128]{1,0,3,2:T(8,128)} %copy.33), kind=kOutput, calls=%fused_computation.69 | convolution fusion | flops 301989888 | bytes 12058624 | tf_op jit(solution)/shard_map/ijyz,sjyz->siyz/dot_general | solution.py:96
  422.5 7.1 %copy.41 = f32[64,16,8,128]{3,2,1,0:T(8,128)} copy(f32[64,16,8,128]{0,1,3,2:T(8,128)} %convolution_bitcast_fusion) | data formatting | bytes 8388608 | tf_op jit(solution)/shard_map/ijyz,sjyz->siyz/transpose | solution.py:96
  429.6 53.2 %all_to_all.75 = f32[64,16,8,128]{3,2,1,0:T(8,128)S(1)} all-to-all(f32[64,16,8,128]{3,2,1,0:T(8,128)} %copy.41), channel_id=1, replica_groups=mesh['sub'=8,'grp'=16] {'grp'}, dimensions={0} | all-to-all | bytes 8388608 | tf_op jit(solution)/shard_map/all_to_all | solution.py:99
  483.7 1.9 collective-permute-start.11
  485.6 8.9 %collective-permute-start.10 = (f32[4,1,128,128]{3,2,1,0:T(8,128)S(1)}, f32[4,1,128,128]{3,2,1,0:T(8,128)S(1)}, u32[]{:S(2)}, u32[]{:S(2)}) collective-permute-start(f32[4,1,128,128]{3,2,1,0:T(8,128)S(1)} %get-tuple-element.3), channel_id=1, source_target_pairs={{16,0},{32,16},{48,32},{64,48},{80,64},{96,80},{112,96},{17,1},{33... | collective-permute-start | bytes 786440 | tf_op jit(solution)/shard_map/ppermute | solution.py:23
  494.5 4.4 collective-permute-done.11
  498.9 1.2 collective-permute-done.10
  500.8 7.6 %select_maximum_fusion = f32[4,18,130,130]{3,2,1,0:T(8,128)} fusion(f32[4,1,128,128]{3,2,1,0:T(8,128)S(1)} %collective-permute-done.10, f32[4,16,128,128]{3,2,1,0:T(8,128)S(1)} %bitcast_add_fusion, f32[4,1,128,128]{3,2,1,0:T(8,128)S(1)} %collective-permute-done.11), kind=kLoop, calls=%fused_computation.4 | loop fusion | flops 18252000 | bytes 9585792 | tf_op jit(solution)/shard_map/concatenate | solution.py:19
  508.3 18.8 %fusion.6 = f32[4]{0:T(128)S(1)} fusion(f32[4,18,130,130]{3,2,1,0:T(8,128)} %select_maximum_fusion, f32[4,16,128,128]{3,2,1,0:T(8,128)} %copy-done.6, f32[4,1,128,128]{3,2,1,0:T(8,128)S(1)} %collective-permute-done.11, f32[4,1,128,128]{3,2,1,0:T(8,128)} %copy-done.9, f32[16,128,128]{2,1,0:T(8,128)} %get-tuple-element.15, ...), kind=kLoop, calls=%fused_computation.19 | loop fusion | flops 24117244 | bytes 29884464 | tf_op jit(solution)/shard_map/reduce_sum | solution.py:103
  527.1 25.1 %psum.7 = f32[4]{0:T(128)S(1)} all-reduce(f32[4]{0:T(128)S(1)} %fusion.6), channel_id=1, replica_groups=mesh['sub'=8,'grp'=16] {'sub'}, use_global_device_ids=true, to_apply=%region_1.2 | all-reduce | flops 4 | bytes 32 | tf_op jit(solution)/shard_map/psum | solution.py:103
  (38 shorter events, 4.9 us)
Async XLA Ops:
  0.6 22.9 %copy-start = (s32[64,2]{0,1:T(2,128)S(1)}, s32[64,2]{0,1:T(2,128)}, u32[]{:S(2)}) copy-start(s32[64,2]{0,1:T(2,128)} %param.8) | copy-start | bytes 1540
  1.5 22.1 %collective-permute-start.1 = (f32[1,128,128]{2,1,0:T(8,128)S(1)}, f32[1,128,128]{2,1,0:T(8,128)S(1)}, u32[]{:S(2)}, u32[]{:S(2)}) collective-permute-start(f32[1,128,128]{2,1,0:T(8,128)S(1)} %get-tuple-element.19), channel_id=1, source_target_pairs={{0,16},{16,32},{32,48},{48,64},{64,80},{80,96},{96,112},{1,17},{17... | collective-permute-start | bytes 196616 | tf_op jit(solution)/shard_map/ppermute | solution.py:21
  5.4 18.2 %collective-permute-start = (f32[1,128,128]{2,1,0:T(8,128)S(1)}, f32[1,128,128]{2,1,0:T(8,128)S(1)}, u32[]{:S(2)}, u32[]{:S(2)}) collective-permute-start(f32[1,128,128]{2,1,0:T(8,128)S(1)} %get-tuple-element.20), channel_id=1, source_target_pairs={{16,0},{32,16},{48,32},{64,48},{80,64},{96,80},{112,96},{17,1},{33... | collective-permute-start | bytes 196616 | tf_op jit(solution)/shard_map/ppermute | solution.py:23
  12.9 16.0 %collective-permute-start.3 = (f32[4,1,128,128]{3,2,1,0:T(8,128)}, f32[4,1,128,128]{3,2,1,0:T(8,128)S(1)}, u32[]{:S(2)}, u32[]{:S(2)}) collective-permute-start(f32[4,1,128,128]{3,2,1,0:T(8,128)} %get-tuple-element.10), channel_id=1, source_target_pairs={{0,16},{16,32},{32,48},{48,64},{64,80},{80,96},{96,112},{1,17},{17... | collective-permute-start | bytes 786440 | tf_op jit(solution)/shard_map/ppermute | solution.py:21
  14.8 14.1 %collective-permute-start.2 = (f32[4,1,128,128]{3,2,1,0:T(8,128)}, f32[4,1,128,128]{3,2,1,0:T(8,128)}, u32[]{:S(2)}, u32[]{:S(2)}) collective-permute-start(f32[4,1,128,128]{3,2,1,0:T(8,128)} %get-tuple-element.11), channel_id=1, source_target_pairs={{16,0},{32,16},{48,32},{64,48},{80,64},{96,80},{112,96},{17,1},{33... | collective-permute-start | bytes 786440 | tf_op jit(solution)/shard_map/ppermute | solution.py:23
  23.5 2.1 copy-start.8
  25.6 3.2 copy-start.4
  120.6 2.0 copy-start.7
  124.2 31.0 %collective-permute-start.4 = (f32[64,4,8,128]{3,2,1,0:T(8,128)}, f32[64,4,8,128]{3,2,1,0:T(8,128)}, u32[]{:S(2)}, u32[]{:S(2)}) collective-permute-start(f32[64,4,8,128]{3,2,1,0:T(8,128)} %get-tuple-element.8), channel_id=1, source_target_pairs={{0,16},{16,32},{32,48},{48,64},{64,80},{80,96},{96,112},{1,17},{17... | collective-permute-start | bytes 3145736 | tf_op jit(solution)/shard_map/ppermute | solution.py:21
  126.1 30.3 %collective-permute-start.5 = (f32[64,4,8,128]{3,2,1,0:T(8,128)}, f32[64,4,8,128]{3,2,1,0:T(8,128)}, u32[]{:S(2)}, u32[]{:S(2)}) collective-permute-start(f32[64,4,8,128]{3,2,1,0:T(8,128)} %get-tuple-element.9), channel_id=1, source_target_pairs={{16,0},{32,16},{48,32},{64,48},{80,64},{96,80},{112,96},{17,1},{33... | collective-permute-start | bytes 3145736 | tf_op jit(solution)/shard_map/ppermute | solution.py:23
  196.4 53.2 %copy-start.5 = (f32[4,16,128,128]{3,2,1,0:T(8,128)S(1)}, f32[4,16,128,128]{3,2,1,0:T(8,128)}, u32[]{:S(2)}) copy-start(f32[4,16,128,128]{3,2,1,0:T(8,128)} %param.5) | copy-start | bytes 12582916
  250.4 19.2 %copy-start.2 = (f32[4,16,128,128]{3,2,1,0:T(8,128)}, f32[4,16,128,128]{3,2,1,0:T(8,128)S(1)}, u32[]{:S(2)}) copy-start(f32[4,16,128,128]{3,2,1,0:T(8,128)S(1)} %bitcast_add_fusion.1) | copy-start | bytes 12582916
  250.5 19.2 %collective-permute-start.7 = (f32[4,1,128,128]{3,2,1,0:T(8,128)S(1)}, f32[4,1,128,128]{3,2,1,0:T(8,128)S(1)}, u32[]{:S(2)}, u32[]{:S(2)}) collective-permute-start(f32[4,1,128,128]{3,2,1,0:T(8,128)S(1)} %get-tuple-element.6), channel_id=1, source_target_pairs={{0,16},{16,32},{32,48},{48,64},{64,80},{80,96},{96,112},{1,17},{17... | collective-permute-start | bytes 786440 | tf_op jit(solution)/shard_map/ppermute | solution.py:21
  252.4 17.3 %collective-permute-start.6 = (f32[4,1,128,128]{3,2,1,0:T(8,128)S(1)}, f32[4,1,128,128]{3,2,1,0:T(8,128)S(1)}, u32[]{:S(2)}, u32[]{:S(2)}) collective-permute-start(f32[4,1,128,128]{3,2,1,0:T(8,128)S(1)} %get-tuple-element.7), channel_id=1, source_target_pairs={{16,0},{32,16},{48,32},{64,48},{80,64},{96,80},{112,96},{17,1},{33... | collective-permute-start | bytes 786440 | tf_op jit(solution)/shard_map/ppermute | solution.py:23
  269.7 0.7 copy-start.10
  359.5 30.7 %collective-permute-start.8 = (f32[64,4,8,128]{3,2,1,0:T(8,128)S(1)}, f32[64,4,8,128]{3,2,1,0:T(8,128)S(1)}, u32[]{:S(2)}, u32[]{:S(2)}) collective-permute-start(f32[64,4,8,128]{3,2,1,0:T(8,128)S(1)} %get-tuple-element.4), channel_id=1, source_target_pairs={{0,16},{16,32},{32,48},{48,64},{64,80},{80,96},{96,112},{1,17},{17... | collective-permute-start | bytes 3145736 | tf_op jit(solution)/shard_map/ppermute | solution.py:21
  361.4 29.9 %collective-permute-start.9 = (f32[64,4,8,128]{3,2,1,0:T(8,128)S(1)}, f32[64,4,8,128]{3,2,1,0:T(8,128)S(1)}, u32[]{:S(2)}, u32[]{:S(2)}) collective-permute-start(f32[64,4,8,128]{3,2,1,0:T(8,128)S(1)} %get-tuple-element.5), channel_id=1, source_target_pairs={{16,0},{32,16},{48,32},{64,48},{80,64},{96,80},{112,96},{17,1},{33... | collective-permute-start | bytes 3145736 | tf_op jit(solution)/shard_map/ppermute | solution.py:23
  429.6 53.2 %copy-start.3 = (f32[4,16,128,128]{3,2,1,0:T(8,128)S(1)}, f32[4,16,128,128]{3,2,1,0:T(8,128)}, u32[]{:S(2)}) copy-start(f32[4,16,128,128]{3,2,1,0:T(8,128)} %copy-done.2) | copy-start | bytes 12582916
  483.6 16.4 %copy-start.6 = (f32[4,16,128,128]{3,2,1,0:T(8,128)}, f32[4,16,128,128]{3,2,1,0:T(8,128)S(1)}, u32[]{:S(2)}) copy-start(f32[4,16,128,128]{3,2,1,0:T(8,128)S(1)} %bitcast_add_fusion) | copy-start | bytes 12582916
  483.7 15.2 %collective-permute-start.11 = (f32[4,1,128,128]{3,2,1,0:T(8,128)S(1)}, f32[4,1,128,128]{3,2,1,0:T(8,128)S(1)}, u32[]{:S(2)}, u32[]{:S(2)}) collective-permute-start(f32[4,1,128,128]{3,2,1,0:T(8,128)S(1)} %get-tuple-element.2), channel_id=1, source_target_pairs={{0,16},{16,32},{32,48},{48,64},{64,80},{80,96},{96,112},{1,17},{17... | collective-permute-start | bytes 786440 | tf_op jit(solution)/shard_map/ppermute | solution.py:21
  485.6 14.4 %collective-permute-start.10 = (f32[4,1,128,128]{3,2,1,0:T(8,128)S(1)}, f32[4,1,128,128]{3,2,1,0:T(8,128)S(1)}, u32[]{:S(2)}, u32[]{:S(2)}) collective-permute-start(f32[4,1,128,128]{3,2,1,0:T(8,128)S(1)} %get-tuple-element.3), channel_id=1, source_target_pairs={{16,0},{32,16},{48,32},{64,48},{80,64},{96,80},{112,96},{17,1},{33... | collective-permute-start | bytes 786440 | tf_op jit(solution)/shard_map/ppermute | solution.py:23
  500.0 0.7 copy-start.9
  508.3 44.4 %copy-start.1 = (s32[64,2]{0,1:T(2,128)S(1)}, s32[64,2]{0,1:T(2,128)}, u32[]{:S(2)}) copy-start(s32[64,2]{0,1:T(2,128)} %param.8) | copy-start | bytes 1540
where the time goes:
time: 561 us; the launch traced here: 553 us
  blocking collectives  239 us (43%)
  other arithmetic  100 us (18%)
  starting transfers between devices  67.9 us (12%)
  local copies, waits for them, and re-layouts  64.2 us (11%)
  waiting for transfers between devices  44.3 us (8%)
  matrix products  35.5 us (6%)
    all_to_all x2, blocking collectives, on_device(): lax.all_to_all(residual, 'grp', split_axis=2, concat_axis=0, tiled=True)  108 us
    all_to_all x2, blocking collectives, on_device(): lax.all_to_all(correction, 'grp', split_axis=0, concat_axis=2, tiled=True)  106 us
    ppermute x6, starting transfers between devices, extended_2(): lax.ppermute(head, axis, [((i + 1) % count, i) for i in range(ends)])  54.5 us
    sub x2, other arithmetic, residual_of(): source_term - apply_operator(potential, padded, center_coef, face_coefs)  41.1 us
    ppermute x6, waiting for transfers between devices, extended_2(): lax.ppermute(tail, axis, [(i, (i + 1) % count) for i in range(ends)])  40.7 us
    dot_general x2, matrix products, on_device(): jnp.einsum('ijyz,sjyz->siyz', inverse_rows, extended_resid, precision=lax...  35.5 us
    concatenate x4, other arithmetic, extended_2(): jnp.concatenate([lax.ppermute(tail, axis, [(i, (i + 1) % count) for i in...  25.8 us
    psum x1, blocking collectives, on_device(): totals = lax.psum(jnp.sum(residual * residual, axis=(1, 2, 3)), 'sub')  25.1 us
  transfers between devices with their start and end apart: 12, of which 6 were waited for; matrix products, arithmetic and copies ran while one was open for 3% of the time, Pallas kernels for 0%

commit v1 on v0

--- a/solution.py
+++ b/solution.py
@@ -1,13 +1,17 @@
 import jax
 import jax.numpy as jnp
 from jax import lax
-from jax.sharding import PartitionSpec as P
+from jax.sharding import Mesh, PartitionSpec as P
 
 ITERS = 2
 
 
 CURRENT = 16.0
 MASS = 1.0
+
+CHIP_AXES = ("xl", "y")
+CORE = "core"
+GRP = ("xl", "y", "core")
 
 
 def extended_2(cells, sides, width):
@@ -66,9 +70,13 @@
 
 def on_device(potential_init, conductivity, inverse_rows, electrodes, intersection_width):
     local_src, width_x, full_y, depth = potential_init.shape
-    grp_index = lax.axis_index("grp")
+    n_core = lax.axis_size(CORE)
+    core = lax.axis_index(CORE)
+    grp_index = (lax.axis_index("xl") * lax.axis_size("y") + lax.axis_index("y")) * n_core + core
     sub_index = lax.axis_index("sub")
     extended = inverse_rows.shape[1]
+    rows = inverse_rows.shape[2]
+    blocks = full_y // (rows * n_core)
     margin = (extended - width_x) // 2
     cell_count = float(width_x * lax.axis_size("sub") * full_y * depth)
     column_ids = jnp.arange(extended, dtype=jnp.int32)
@@ -76,12 +84,14 @@
     intersection_mask = (
         (column_ids >= margin - reach) & (column_ids < width_x + margin + reach)
     ).astype(jnp.float32)[:, None, None]
+    inverse_mine = lax.all_gather(inverse_rows, CHIP_AXES, axis=2, tiled=True)
     conduct_rim = extended_2(conductivity, (("sub", 0),), 1)
     conduct_pad = jnp.pad(conduct_rim, ((0, 0), (1, 1), (1, 1)))
     x_start = sub_index * width_x
     center_coef, face_coefs = face_terms(conduct_pad)
     own_pairs = lax.dynamic_slice_in_dim(electrodes, grp_index * local_src, local_src, 0)
     source_term = source_block(own_pairs, x_start, width_x, full_y, full_y, depth)
+    swap = [(0, 1), (1, 0)]
 
     def residual_of(potential):
         padded = extended_2(potential, (("sub", 1),), 1)
@@ -91,14 +101,21 @@
     potential = potential_init
     for sweep in range(ITERS):
         residual = residual_of(potential)
-        residual_cells = lax.all_to_all(residual, "grp", split_axis=2, concat_axis=0, tiled=True)
-        extended_resid = extended_2(residual_cells, (("sub", 1),), margin) * intersection_mask
+        split = residual.reshape(local_src, width_x, blocks, n_core, rows, depth)
+        own = lax.dynamic_index_in_dim(split, core, axis=3, keepdims=False)
+        other = lax.dynamic_index_in_dim(split, 1 - core, axis=3, keepdims=False)
+        got = lax.ppermute(other, CORE, swap)
+        cells = jnp.concatenate([own, got], axis=0).reshape(2 * local_src, width_x, blocks * rows, depth)
+        extended_resid = extended_2(cells, (("sub", 1),), margin) * intersection_mask
         correction = jnp.einsum(
-            "ijyz,sjyz->siyz", inverse_rows, extended_resid, precision=lax.Precision.HIGHEST
-        )
-        potential = potential + lax.all_to_all(
-            correction, "grp", split_axis=0, concat_axis=2, tiled=True
-        )
+            "ijyz,sjyz->siyz", inverse_mine, extended_resid, precision=lax.Precision.HIGHEST
+        ).reshape(2 * local_src, width_x, blocks, rows, depth)
+        mine = correction[:local_src]
+        back = lax.ppermute(correction[local_src:], CORE, swap)
+        first = jnp.where(core == 0, mine, back)
+        second = jnp.where(core == 0, back, mine)
+        update = jnp.stack([first, second], axis=3).reshape(potential.shape)
+        potential = potential + update
     residual = residual_of(potential)
     totals = lax.psum(jnp.sum(residual * residual, axis=(1, 2, 3)), "sub")
     residual_norms = jnp.sqrt(totals / cell_count)
@@ -106,14 +123,21 @@
 
 
 def solution(mesh):
+    n_sub, n_grp = mesh.devices.shape
+    n_core = 2
+    n_y = 4
+    view = Mesh(
+        mesh.devices.reshape(n_sub, n_grp // (n_y * n_core), n_y, n_core),
+        ("sub", "xl", "y", "core"),
+    )
     in_specs = (
-        P("grp", "sub", None, None),
+        P(GRP, "sub", None, None),
         P("sub", None, None),
-        P("sub", None, "grp", None),
+        P("sub", None, GRP, None),
         P(),
         P("sub"),
     )
-    out_specs = (P("grp", "sub", None, None), P("grp"))
+    out_specs = (P(GRP, "sub", None, None), P(GRP))
     return jax.shard_map(
-        on_device, mesh=mesh, in_specs=in_specs, out_specs=out_specs, check_vma=False
+        on_device, mesh=view, in_specs=in_specs, out_specs=out_specs, check_vma=False
     )

time: 561 us -> 745 us (1.33)
  blocking collectives: 239 us -> 25.1 us
  matrix products: 35.5 us -> 226 us
  local copies, waits for them, and re-layouts: 64.2 us -> 193 us
  waiting for transfers between devices: 44.3 us -> 111 us
  between operations: 2.01 us -> 15.3 us
  starting transfers between devices: 67.9 us -> 58.4 us
    all_to_all x4 -> x0, blocking collectives: 214 us -> none  [the longest x2 108 us: on_device(): lax.all_to_all(residual, 'grp', split_axis=2, concat_axis=0, tiled=True)]
    dot_general x2, matrix products: 35.5 us -> 226 us  [on_device(): jnp.einsum('ijyz,sjyz->siyz', inverse_mine, extended_resid, precision=lax...]
    slice x0 -> x6, local copies, waits for them, and re-layouts: none -> 113 us  [the longest x4 91.7 us: on_device(): mine = correction[:local_src]]
    ppermute x6, waiting for transfers between devices: 40.7 us -> 78.1 us  [extended_2(): lax.ppermute(tail, axis, [(i, (i + 1) % count) for i in range(ends)])]
    all_gather x0 -> x1, local copies, waits for them, and re-layouts: none -> 33.5 us  [on_device(): inverse_mine = lax.all_gather(inverse_rows, CHIP_AXES, axis=2, tiled=True)]
    all_gather x0 -> x1, waiting for transfers between devices: none -> 18.3 us  [on_device(): inverse_mine = lax.all_gather(inverse_rows, CHIP_AXES, axis=2, tiled=True)]
    transpose x2 -> x0, local copies, waits for them, and re-layouts: 14.2 us -> none  [on_device(): jnp.einsum('ijyz,sjyz->siyz', inverse_rows, extended_resid, precision=lax...]
    mul x2, local copies, waits for them, and re-layouts: 20.5 us -> 30.9 us  [on_device(): extended_2(cells, (('sub', 1),), margin) * intersection_mask]
  transfers between devices with their start and end apart: 12 -> 17, of which waited for: 6 -> 13; matrix products, arithmetic and copies ran while one was open for 3% -> 11% of each run, Pallas kernels for 0% -> 0%
where the time goes in v1:
time: 745 us; the launch traced here: 735 us
  matrix products  226 us (30%)
  local copies, waits for them, and re-layouts  193 us (26%)
  waiting for transfers between devices  111 us (15%)
  other arithmetic  106 us (14%)
  starting transfers between devices  58.4 us (8%)
  blocking collectives  25.1 us (3%)
  between operations  15.3 us (2%)
    dot_general x2, matrix products, on_device(): jnp.einsum('ijyz,sjyz->siyz', inverse_mine, extended_resid, precision=lax...  226 us
    slice x4, local copies, waits for them, and re-layouts, on_device(): mine = correction[:local_src]  91.7 us
    ppermute x6, waiting for transfers between devices, extended_2(): lax.ppermute(tail, axis, [(i, (i + 1) % count) for i in range(ends)])  78.1 us
    ppermute x6, starting transfers between devices, extended_2(): lax.ppermute(head, axis, [((i + 1) % count, i) for i in range(ends)])  44.8 us
    sub x2, other arithmetic, residual_of(): source_term - apply_operator(potential, padded, center_coef, face_coefs)  40.7 us
    all_gather x1, local copies, waits for them, and re-layouts, on_device(): inverse_mine = lax.all_gather(inverse_rows, CHIP_AXES, axis=2, tiled=True)  33.5 us
    mul x2, local copies, waits for them, and re-layouts, on_device(): extended_2(cells, (('sub', 1),), margin) * intersection_mask  30.9 us
    psum x1, blocking collectives, on_device(): totals = lax.psum(jnp.sum(residual * residual, axis=(1, 2, 3)), 'sub')  25.1 us
  transfers between devices with their start and end apart: 17, of which 13 were waited for; matrix products, arithmetic and copies ran while one was open for 11% of the time, Pallas kernels for 0%

profile of v1, /device:TPU:6, one launch (start us, length us, event | category | flops | bytes accessed | tf_op | source)
XLA Modules:
  0.0 734.8 jit_solution(12421549910816491784)
XLA Ops:
  7.2 2.9 copy.22
  10.2 3.8 collective-permute-start.1
  14.1 5.6 collective-permute-start
  19.7 1.9 fusion.47
  21.6 1.9 collective-permute-start.3
  23.5 7.5 %collective-permute-start.2 = (f32[4,1,128,128]{3,2,1,0:T(8,128)}, f32[4,1,128,128]{3,2,1,0:T(8,128)}, u32[]{:S(2)}, u32[]{:S(2)}) collective-permute-start(f32[4,1,128,128]{3,2,1,0:T(8,128)} %get-tuple-element.23), channel_id=1, source_target_pairs={{16,0},{32,16},{48,32},{64,48},{80,64},{96,80},{112,96},{17,1},{33... | collective-permute-start | bytes 786440 | tf_op jit(solution)/shard_map/ppermute | solution.py:27
  33.1 5.3 add_add_fusion
  38.4 3.1 collective-permute-done.3
  43.0 8.7 %select_maximum_fusion.4 = f32[4,18,130,130]{3,2,1,0:T(8,128)} fusion(f32[4,1,128,128]{3,2,1,0:T(8,128)} %collective-permute-done.2, f32[4,16,128,128]{3,2,1,0:T(8,128)S(1)} %copy-done.4, f32[4,1,128,128]{3,2,1,0:T(8,128)S(1)} %collective-permute-done.3), kind=kLoop, calls=%fused_computation.10 | loop fusion | flops 18252000 | bytes 9585792 | tf_op jit(solution)/shard_map/concatenate | solution.py:23
  51.7 20.4 %fusion.24 = f32[4,16,128,128]{3,2,1,0:T(8,128)} fusion(f32[4,18,130,130]{3,2,1,0:T(8,128)} %select_maximum_fusion.4, f32[4,16,128,128]{3,2,1,0:T(8,128)} %param.5, f32[4,1,128,128]{3,2,1,0:T(8,128)S(1)} %collective-permute-done.3, f32[4,1,128,128]{3,2,1,0:T(8,128)} %collective-permute-done.2, f32[16,128,128]{2,1,0:T(8,128)} %get-tuple-element.27, ...), kind=kLoop, calls=%fused_computation.51 | loop fusion | flops 22020096 | bytes 34078752 | tf_op jit(solution)/shard_map/sub | solution.py:99
  72.1 2.6 dynamic-slice_bitcast_fusion.3
  74.8 4.1 collective-permute-done.4
  79.2 1.9 collective-permute-start.5
  81.1 8.0 %collective-permute-start.6 = (f32[8,4,64,128]{3,2,1,0:T(8,128)S(1)}, f32[8,4,64,128]{3,2,1,0:T(8,128)S(1)}, u32[]{:S(2)}, u32[]{:S(2)}) collective-permute-start(f32[8,4,64,128]{3,2,1,0:T(8,128)S(1)} %get-tuple-element.19), channel_id=1, source_target_pairs={{16,0},{32,16},{48,32},{64,48},{80,64},{96,80},{112,96},{17,1},{33... | collective-permute-start | bytes 3145736 | tf_op jit(solution)/shard_map/ppermute | solution.py:27
  89.8 43.7 %collective-permute-done.5 = f32[8,4,64,128]{3,2,1,0:T(8,128)S(1)} collective-permute-done((f32[8,4,64,128]{3,2,1,0:T(8,128)S(1)}, f32[8,4,64,128]{3,2,1,0:T(8,128)S(1)}, u32[]{:S(2)}, u32[]{:S(2)}) %collective-permute-start.5) | collective-permute-done | bytes 1048608 | tf_op jit(solution)/shard_map/ppermute | solution.py:25
  134.9 3.1 maximum_multiply_fusion
  138.1 15.5 %copy.23 = f32[8,24,64,128]{1,0,3,2:T(8,128)} copy(f32[8,24,64,128]{3,2,1,0:T(8,128)} %maximum_multiply_fusion) | data formatting | bytes 12582912 | tf_op jit(solution)/shard_map/mul | solution.py:109
  153.6 18.3 %all-gather.2.cloned.1.call-done = f32[16,24,64,128]{3,1,0,2:T(8,128)} async-done(((f32[16,24,8,128]{3,1,0,2:T(8,128)}), f32[16,24,64,128]{3,1,0,2:T(8,128)}) %all-gather.2.cloned.1.call-update) | async-done | bytes 12582928 | tf_op jit(solution)/shard_map/all_gather | solution.py:87
  171.9 33.5 %copy.24 = f32[16,24,64,128]{1,0,3,2:T(8,128)} copy(f32[16,24,64,128]{3,1,0,2:T(8,128)} %all-gather.2.cloned.1.call-done) | data formatting | bytes 25165824 | tf_op jit(solution)/shard_map/all_gather | solution.py:87
  205.4 112.9 %convolution_bitcast_fusion.1 = f32[8,16,64,128]{1,0,3,2:T(8,128)} fusion(f32[8,24,64,128]{1,0,3,2:T(8,128)} %copy.23, f32[16,24,64,128]{1,0,3,2:T(8,128)} %copy.24), kind=kOutput, calls=%fused_computation.5 | convolution fusion | flops 301989888 | bytes 23068672 | tf_op jit(solution)/shard_map/ijyz,sjyz->siyz/dot_general | solution.py:110
  318.3 34.9 %fusion.44 = (f32[4,16,64,128]{1,0,3,2:T(4,128)}, f32[4,16,64,128]{1,0,3,2:T(4,128)}) fusion(f32[8,16,64,128]{1,0,3,2:T(8,128)} %convolution_bitcast_fusion.1), kind=kLoop, calls=%fused_computation.113 | loop fusion | bytes 8388608 | tf_op jit(solution)/shard_map/slice | solution.py:113
  353.2 10.9 %copy.25 = f32[4,16,8,8,128]{4,3,2,1,0:T(8,128)} copy(f32[4,16,8,8,128]{1,0,4,3,2:T(4,128)} %bitcast.52) | data formatting | bytes 4194304 | tf_op jit(solution)/shard_map/slice | solution.py:114
  364.1 10.8 %copy.26 = f32[4,16,8,8,128]{4,3,2,1,0:T(8,128)} copy(f32[4,16,8,8,128]{1,0,4,3,2:T(4,128)} %bitcast.50) | data formatting | bytes 4194304 | tf_op jit(solution)/shard_map/slice | solution.py:113
  374.9 2.7 select_bitcast_fusion.3
  377.9 1.8 copy-done.5
  381.0 1.9 collective-permute-start.9
  382.9 7.5 %collective-permute-start.8 = (f32[4,1,128,128]{3,2,1,0:T(8,128)S(1)}, f32[4,1,128,128]{3,2,1,0:T(8,128)S(1)}, u32[]{:S(2)}, u32[]{:S(2)}) collective-permute-start(f32[4,1,128,128]{3,2,1,0:T(8,128)S(1)} %get-tuple-element.15), channel_id=1, source_target_pairs={{16,0},{32,16},{48,32},{64,48},{80,64},{96,80},{112,96},{17,1},{33... | collective-permute-start | bytes 786440 | tf_op jit(solution)/shard_map/ppermute | solution.py:27
  390.5 4.8 collective-permute-done.9
  397.1 7.6 %select_maximum_fusion.2 = f32[4,18,130,130]{3,2,1,0:T(8,128)} fusion(f32[4,1,128,128]{3,2,1,0:T(8,128)S(1)} %collective-permute-done.8, f32[4,16,128,128]{3,2,1,0:T(8,128)S(1)} %bitcast_add_fusion.1, f32[4,1,128,128]{3,2,1,0:T(8,128)S(1)} %collective-permute-done.9), kind=kLoop, calls=%fused_computation.8 | loop fusion | flops 18252000 | bytes 9585792 | tf_op jit(solution)/shard_map/concatenate | solution.py:23
  404.8 20.3 %fusion.15 = f32[4,16,128,128]{3,2,1,0:T(8,128)} fusion(f32[4,18,130,130]{3,2,1,0:T(8,128)} %select_maximum_fusion.2, f32[4,16,128,128]{3,2,1,0:T(8,128)} %copy-done.2, f32[4,1,128,128]{3,2,1,0:T(8,128)S(1)} %collective-permute-done.9, f32[4,1,128,128]{3,2,1,0:T(8,128)} %copy-done.9, f32[16,128,128]{2,1,0:T(8,128)} %get-tuple-element.27, ...), kind=kLoop, calls=%fused_computation.36 | loop fusion | flops 22020096 | bytes 34078752 | tf_op jit(solution)/shard_map/sub | solution.py:99
  425.0 2.6 dynamic-slice_bitcast_fusion.1
  427.7 4.1 collective-permute-done.10
  432.1 1.9 collective-permute-start.11
  434.1 8.0 %collective-permute-start.12 = (f32[8,4,64,128]{3,2,1,0:T(8,128)S(1)}, f32[8,4,64,128]{3,2,1,0:T(8,128)S(1)}, u32[]{:S(2)}, u32[]{:S(2)}) collective-permute-start(f32[8,4,64,128]{3,2,1,0:T(8,128)S(1)} %get-tuple-element.11), channel_id=1, source_target_pairs={{16,0},{32,16},{48,32},{64,48},{80,64},{96,80},{112,96},{17,1},{33... | collective-permute-start | bytes 3145736 | tf_op jit(solution)/shard_map/ppermute | solution.py:27
  442.1 21.5 %collective-permute-done.11 = f32[8,4,64,128]{3,2,1,0:T(8,128)S(1)} collective-permute-done((f32[8,4,64,128]{3,2,1,0:T(8,128)S(1)}, f32[8,4,64,128]{3,2,1,0:T(8,128)S(1)}, u32[]{:S(2)}, u32[]{:S(2)}) %collective-permute-start.11) | collective-permute-done | bytes 1048608 | tf_op jit(solution)/shard_map/ppermute | solution.py:25
  464.8 3.1 maximum_multiply_fusion.1
  467.9 15.4 %copy.30 = f32[8,24,64,128]{1,0,3,2:T(8,128)} copy(f32[8,24,64,128]{3,2,1,0:T(8,128)} %maximum_multiply_fusion.1) | data formatting | bytes 12582912 | tf_op jit(solution)/shard_map/mul | solution.py:109
  483.3 112.7 %convolution_bitcast_fusion = f32[8,16,64,128]{1,0,3,2:T(8,128)} fusion(f32[8,24,64,128]{1,0,3,2:T(8,128)} %copy.30, f32[16,24,64,128]{1,0,3,2:T(8,128)} %copy.24), kind=kOutput, calls=%fused_computation.4 | convolution fusion | flops 301989888 | bytes 23068672 | tf_op jit(solution)/shard_map/ijyz,sjyz->siyz/dot_general | solution.py:110
  596.0 35.1 %fusion.43 = (f32[4,16,64,128]{1,0,3,2:T(4,128)}, f32[4,16,64,128]{1,0,3,2:T(4,128)}) fusion(f32[8,16,64,128]{1,0,3,2:T(8,128)} %convolution_bitcast_fusion), kind=kLoop, calls=%fused_computation.112 | loop fusion | bytes 8388608 | tf_op jit(solution)/shard_map/slice | solution.py:113
  631.1 10.9 %copy.32 = f32[4,16,8,8,128]{4,3,2,1,0:T(8,128)} copy(f32[4,16,8,8,128]{1,0,4,3,2:T(4,128)} %bitcast.53) | data formatting | bytes 4194304 | tf_op jit(solution)/shard_map/slice | solution.py:114
  641.9 10.9 %copy.33 = f32[4,16,8,8,128]{4,3,2,1,0:T(8,128)} copy(f32[4,16,8,8,128]{1,0,4,3,2:T(4,128)} %bitcast.51) | data formatting | bytes 4194304 | tf_op jit(solution)/shard_map/slice | solution.py:113
  652.8 2.7 select_bitcast_fusion.1
  658.9 1.9 collective-permute-start.15
  660.9 8.0 %collective-permute-start.14 = (f32[4,1,128,128]{3,2,1,0:T(8,128)S(1)}, f32[4,1,128,128]{3,2,1,0:T(8,128)S(1)}, u32[]{:S(2)}, u32[]{:S(2)}) collective-permute-start(f32[4,1,128,128]{3,2,1,0:T(8,128)S(1)} %get-tuple-element.7), channel_id=1, source_target_pairs={{16,0},{32,16},{48,32},{64,48},{80,64},{96,80},{112,96},{17,1},{33... | collective-permute-start | bytes 786440 | tf_op jit(solution)/shard_map/ppermute | solution.py:27
  668.9 5.0 collective-permute-done.15
  675.8 7.6 %select_maximum_fusion = f32[4,18,130,130]{3,2,1,0:T(8,128)} fusion(f32[4,1,128,128]{3,2,1,0:T(8,128)S(1)} %collective-permute-done.14, f32[4,16,128,128]{3,2,1,0:T(8,128)S(1)} %bitcast_add_fusion, f32[4,1,128,128]{3,2,1,0:T(8,128)S(1)} %collective-permute-done.15), kind=kLoop, calls=%fused_computation.6 | loop fusion | flops 18252000 | bytes 9585792 | tf_op jit(solution)/shard_map/concatenate | solution.py:23
  683.4 18.7 %fusion.6 = f32[4]{0:T(128)S(1)} fusion(f32[4,18,130,130]{3,2,1,0:T(8,128)} %select_maximum_fusion, f32[4,16,128,128]{3,2,1,0:T(8,128)} %copy-done.6, f32[4,1,128,128]{3,2,1,0:T(8,128)S(1)} %collective-permute-done.15, f32[4,1,128,128]{3,2,1,0:T(8,128)} %copy-done.8, f32[16,128,128]{2,1,0:T(8,128)} %get-tuple-element.27, ...), kind=kLoop, calls=%fused_computation.21 | loop fusion | flops 24117244 | bytes 29884464 | tf_op jit(solution)/shard_map/reduce_sum | solution.py:120
  702.1 25.1 %psum.7 = f32[4]{0:T(128)S(1)} all-reduce(f32[4]{0:T(128)S(1)} %fusion.6), channel_id=1, replica_groups=mesh['sub'=8,'xl'=2,'y'=4,'core'=2] {'sub'}, use_global_device_ids=true, to_apply=%region_1.2 | all-reduce | flops 4 | bytes 32 | tf_op jit(solution)/shard_map/psum | solution.py:120
  (50 shorter events, 16.1 us)
Async XLA Ops:
  7.2 23.9 %copy-start = (s32[64,2]{0,1:T(2,128)S(1)}, s32[64,2]{0,1:T(2,128)}, u32[]{:S(2)}) copy-start(s32[64,2]{0,1:T(2,128)} %param.8) | copy-start | bytes 1540
  7.2 3.0 copy-start.7
  7.2 164.7 %all-gather.2.cloned.1.call-start = ((), (), s32[]{:S(2)}) async-start(), calls=%async_computation | async-start | bytes 14155776 | tf_op jit(solution)/shard_map/all_gather | solution.py:87
  10.2 22.1 %collective-permute-start.1 = (f32[1,128,128]{2,1,0:T(8,128)S(1)}, f32[1,128,128]{2,1,0:T(8,128)S(1)}, u32[]{:S(2)}, u32[]{:S(2)}) collective-permute-start(f32[1,128,128]{2,1,0:T(8,128)S(1)} %get-tuple-element.31), channel_id=1, source_target_pairs={{0,16},{16,32},{32,48},{48,64},{64,80},{80,96},{96,112},{1,17},{17... | collective-permute-start | bytes 196616 | tf_op jit(solution)/shard_map/ppermute | solution.py:25
  14.1 18.3 %collective-permute-start = (f32[1,128,128]{2,1,0:T(8,128)S(1)}, f32[1,128,128]{2,1,0:T(8,128)S(1)}, u32[]{:S(2)}, u32[]{:S(2)}) collective-permute-start(f32[1,128,128]{2,1,0:T(8,128)S(1)} %get-tuple-element.32), channel_id=1, source_target_pairs={{16,0},{32,16},{48,32},{64,48},{80,64},{96,80},{112,96},{17,1},{33... | collective-permute-start | bytes 196616 | tf_op jit(solution)/shard_map/ppermute | solution.py:27
  21.6 20.0 %collective-permute-start.3 = (f32[4,1,128,128]{3,2,1,0:T(8,128)}, f32[4,1,128,128]{3,2,1,0:T(8,128)S(1)}, u32[]{:S(2)}, u32[]{:S(2)}) collective-permute-start(f32[4,1,128,128]{3,2,1,0:T(8,128)} %get-tuple-element.22), channel_id=1, source_target_pairs={{0,16},{16,32},{32,48},{48,64},{64,80},{80,96},{96,112},{1,17},{17... | collective-permute-start | bytes 786440 | tf_op jit(solution)/shard_map/ppermute | solution.py:25
  23.5 19.5 %collective-permute-start.2 = (f32[4,1,128,128]{3,2,1,0:T(8,128)}, f32[4,1,128,128]{3,2,1,0:T(8,128)}, u32[]{:S(2)}, u32[]{:S(2)}) collective-permute-start(f32[4,1,128,128]{3,2,1,0:T(8,128)} %get-tuple-element.23), channel_id=1, source_target_pairs={{16,0},{32,16},{48,32},{64,48},{80,64},{96,80},{112,96},{17,1},{33... | collective-permute-start | bytes 786440 | tf_op jit(solution)/shard_map/ppermute | solution.py:27
  33.1 9.9 %copy-start.4 = (f32[4,16,128,128]{3,2,1,0:T(8,128)S(1)}, f32[4,16,128,128]{3,2,1,0:T(8,128)}, u32[]{:S(2)}) copy-start(f32[4,16,128,128]{3,2,1,0:T(8,128)} %param.5) | copy-start | bytes 12582916
  74.7 4.2 collective-permute-start.4
  79.2 54.4 %collective-permute-start.5 = (f32[8,4,64,128]{3,2,1,0:T(8,128)S(1)}, f32[8,4,64,128]{3,2,1,0:T(8,128)S(1)}, u32[]{:S(2)}, u32[]{:S(2)}) collective-permute-start(f32[8,4,64,128]{3,2,1,0:T(8,128)S(1)} %get-tuple-element.18), channel_id=1, source_target_pairs={{0,16},{16,32},{32,48},{48,64},{64,80},{80,96},{96,112},{1,17},{17... | collective-permute-start | bytes 3145736 | tf_op jit(solution)/shard_map/ppermute | solution.py:25
  81.1 53.8 %collective-permute-start.6 = (f32[8,4,64,128]{3,2,1,0:T(8,128)S(1)}, f32[8,4,64,128]{3,2,1,0:T(8,128)S(1)}, u32[]{:S(2)}, u32[]{:S(2)}) collective-permute-start(f32[8,4,64,128]{3,2,1,0:T(8,128)S(1)} %get-tuple-element.19), channel_id=1, source_target_pairs={{16,0},{32,16},{48,32},{64,48},{80,64},{96,80},{112,96},{17,1},{33... | collective-permute-start | bytes 3145736 | tf_op jit(solution)/shard_map/ppermute | solution.py:27
  364.1 10.8 %collective-permute-start.7 = (f32[4,16,8,8,128]{4,3,2,1,0:T(8,128)}, f32[4,16,8,8,128]{4,3,2,1,0:T(8,128)}, u32[]{:S(2)}, u32[]{:S(2)}) collective-permute-start(f32[4,16,8,8,128]{4,3,2,1,0:T(8,128)} %copy.25), channel_id=1, source_target_pairs={{0,1},{1,0},{2,3},{3,2},{4,5},{5,4},{6,7},{7,6},{8,9},{9,8},{10,11... | collective-permute-start | bytes 6291464 | tf_op jit(solution)/shard_map/ppermute | solution.py:114
  377.6 2.2 copy-start.5
  380.9 15.5 %copy-start.2 = (f32[4,16,128,128]{3,2,1,0:T(8,128)}, f32[4,16,128,128]{3,2,1,0:T(8,128)S(1)}, u32[]{:S(2)}) copy-start(f32[4,16,128,128]{3,2,1,0:T(8,128)S(1)} %bitcast_add_fusion.1) | copy-start | bytes 12582916
  381.0 14.2 %collective-permute-start.9 = (f32[4,1,128,128]{3,2,1,0:T(8,128)S(1)}, f32[4,1,128,128]{3,2,1,0:T(8,128)S(1)}, u32[]{:S(2)}, u32[]{:S(2)}) collective-permute-start(f32[4,1,128,128]{3,2,1,0:T(8,128)S(1)} %get-tuple-element.14), channel_id=1, source_target_pairs={{0,16},{16,32},{32,48},{48,64},{64,80},{80,96},{96,112},{1,17},{17... | collective-permute-start | bytes 786440 | tf_op jit(solution)/shard_map/ppermute | solution.py:25
  382.9 13.5 %collective-permute-start.8 = (f32[4,1,128,128]{3,2,1,0:T(8,128)S(1)}, f32[4,1,128,128]{3,2,1,0:T(8,128)S(1)}, u32[]{:S(2)}, u32[]{:S(2)}) collective-permute-start(f32[4,1,128,128]{3,2,1,0:T(8,128)S(1)} %get-tuple-element.15), channel_id=1, source_target_pairs={{16,0},{32,16},{48,32},{64,48},{80,64},{96,80},{112,96},{17,1},{33... | collective-permute-start | bytes 786440 | tf_op jit(solution)/shard_map/ppermute | solution.py:27
  396.4 0.7 copy-start.9
  427.6 4.2 collective-permute-start.10
  432.1 31.5 %collective-permute-start.11 = (f32[8,4,64,128]{3,2,1,0:T(8,128)S(1)}, f32[8,4,64,128]{3,2,1,0:T(8,128)S(1)}, u32[]{:S(2)}, u32[]{:S(2)}) collective-permute-start(f32[8,4,64,128]{3,2,1,0:T(8,128)S(1)} %get-tuple-element.10), channel_id=1, source_target_pairs={{0,16},{16,32},{32,48},{48,64},{64,80},{80,96},{96,112},{1,17},{17... | collective-permute-start | bytes 3145736 | tf_op jit(solution)/shard_map/ppermute | solution.py:25
  434.1 30.7 %collective-permute-start.12 = (f32[8,4,64,128]{3,2,1,0:T(8,128)S(1)}, f32[8,4,64,128]{3,2,1,0:T(8,128)S(1)}, u32[]{:S(2)}, u32[]{:S(2)}) collective-permute-start(f32[8,4,64,128]{3,2,1,0:T(8,128)S(1)} %get-tuple-element.11), channel_id=1, source_target_pairs={{16,0},{32,16},{48,32},{64,48},{80,64},{96,80},{112,96},{17,1},{33... | collective-permute-start | bytes 3145736 | tf_op jit(solution)/shard_map/ppermute | solution.py:27
  641.9 10.9 %collective-permute-start.13 = (f32[4,16,8,8,128]{4,3,2,1,0:T(8,128)}, f32[4,16,8,8,128]{4,3,2,1,0:T(8,128)}, u32[]{:S(2)}, u32[]{:S(2)}) collective-permute-start(f32[4,16,8,8,128]{4,3,2,1,0:T(8,128)} %copy.32), channel_id=1, source_target_pairs={{0,1},{1,0},{2,3},{3,2},{4,5},{5,4},{6,7},{7,6},{8,9},{9,8},{10,11... | collective-permute-start | bytes 6291464 | tf_op jit(solution)/shard_map/ppermute | solution.py:114
  655.5 2.2 copy-start.3
  658.9 16.2 %copy-start.6 = (f32[4,16,128,128]{3,2,1,0:T(8,128)}, f32[4,16,128,128]{3,2,1,0:T(8,128)S(1)}, u32[]{:S(2)}) copy-start(f32[4,16,128,128]{3,2,1,0:T(8,128)S(1)} %bitcast_add_fusion) | copy-start | bytes 12582916
  658.9 15.0 %collective-permute-start.15 = (f32[4,1,128,128]{3,2,1,0:T(8,128)S(1)}, f32[4,1,128,128]{3,2,1,0:T(8,128)S(1)}, u32[]{:S(2)}, u32[]{:S(2)}) collective-permute-start(f32[4,1,128,128]{3,2,1,0:T(8,128)S(1)} %get-tuple-element.6), channel_id=1, source_target_pairs={{0,16},{16,32},{32,48},{48,64},{64,80},{80,96},{96,112},{1,17},{17... | collective-permute-start | bytes 786440 | tf_op jit(solution)/shard_map/ppermute | solution.py:25
  660.9 14.2 %collective-permute-start.14 = (f32[4,1,128,128]{3,2,1,0:T(8,128)S(1)}, f32[4,1,128,128]{3,2,1,0:T(8,128)S(1)}, u32[]{:S(2)}, u32[]{:S(2)}) collective-permute-start(f32[4,1,128,128]{3,2,1,0:T(8,128)S(1)} %get-tuple-element.7), channel_id=1, source_target_pairs={{16,0},{32,16},{48,32},{64,48},{80,64},{96,80},{112,96},{17,1},{33... | collective-permute-start | bytes 786440 | tf_op jit(solution)/shard_map/ppermute | solution.py:27
  675.1 0.7 copy-start.8
  683.4 44.2 %copy-start.1 = (s32[64,2]{0,1:T(2,128)S(1)}, s32[64,2]{0,1:T(2,128)}, u32[]{:S(2)}) copy-start(s32[64,2]{0,1:T(2,128)} %param.8) | copy-start | bytes 1540
Sparse Core Ops, SparseCore 0:
  10.3 161.4 all-gather.1

commit v2 on v1

--- a/solution.py
+++ b/solution.py
@@ -2,6 +2,37 @@
 import jax.numpy as jnp
 from jax import lax
 from jax.sharding import Mesh, PartitionSpec as P
+from jax.experimental import pallas as pl
+
+def correction_kernel(inv_ref, ext_ref, out_ref):
+    n_out, n_col = inv_ref.shape[0], inv_ref.shape[1]
+    n_src = ext_ref.shape[0]
+
+    def row(i, carry):
+        accs = [None] * n_src
+        for j in range(n_col):
+            w = inv_ref[i, j]
+            for s in range(n_src):
+                term = w * ext_ref[s, j]
+                accs[s] = term if accs[s] is None else accs[s] + term
+        for s in range(n_src):
+            out_ref[s, i] = accs[s]
+        return carry
+
+    lax.fori_loop(0, n_out, row, 0)
+
+def correction_of(inv, ext, rows=8):
+    n_out, n_col, ny, nz = inv.shape
+    n_src = ext.shape[0]
+    return pl.pallas_call(
+        correction_kernel,
+        grid=(ny // rows,),
+        in_specs=[pl.BlockSpec((n_out, n_col, rows, nz), lambda b: (0, 0, b, 0)),
+                  pl.BlockSpec((n_src, n_col, rows, nz), lambda b: (0, 0, b, 0))],
+        out_specs=pl.BlockSpec((n_src, n_out, rows, nz), lambda b: (0, 0, b, 0)),
+        out_shape=jax.ShapeDtypeStruct((n_src, n_out, ny, nz), jnp.float32),
+    )(inv, ext)
+
 
 ITERS = 2
 
@@ -107,9 +138,9 @@
         got = lax.ppermute(other, CORE, swap)
         cells = jnp.concatenate([own, got], axis=0).reshape(2 * local_src, width_x, blocks * rows, depth)
         extended_resid = extended_2(cells, (("sub", 1),), margin) * intersection_mask
-        correction = jnp.einsum(
-            "ijyz,sjyz->siyz", inverse_mine, extended_resid, precision=lax.Precision.HIGHEST
-        ).reshape(2 * local_src, width_x, blocks, rows, depth)
+        correction = correction_of(inverse_mine, extended_resid).reshape(
+            2 * local_src, width_x, blocks, rows, depth
+        )
         mine = correction[:local_src]
         back = lax.ppermute(correction[local_src:], CORE, swap)
         first = jnp.where(core == 0, mine, back)

time: 745 us -> 389 us (0.52); the launches traced: 735 us -> 387 us
  matrix products: 226 us -> 0 us
  local copies, waits for them, and re-layouts: 193 us -> 19.5 us
  Pallas kernels: 0 us -> 28.2 us
  waiting for transfers between devices: 111 us -> 139 us
    dot_general x2 -> x0, matrix products: 226 us -> none  [on_device(): jnp.einsum('ijyz,sjyz->siyz', inverse_mine, extended_resid, precision=lax...]
    slice x4 -> x0, local copies, waits for them, and re-layouts: 91.7 us -> none  [on_device(): mine = correction[:local_src]]
    all_gather x1 -> x0, local copies, waits for them, and re-layouts: 33.5 us -> none  [on_device(): inverse_mine = lax.all_gather(inverse_rows, CHIP_AXES, axis=2, tiled=True)]
    mul x2 -> x0, local copies, waits for them, and re-layouts: 30.9 us -> none  [on_device(): extended_2(cells, (('sub', 1),), margin) * intersection_mask]
    pallas_call x0 -> x2, Pallas kernels: none -> 28.2 us  [correction_of(): pl.pallas_call(correction_kernel, grid=(ny // rows,), in_specs=[pl.BlockS...]
    all_gather x1, waiting for transfers between devices: 18.3 us -> 35.7 us  [on_device(): inverse_mine = lax.all_gather(inverse_rows, CHIP_AXES, axis=2, tiled=True)]
    slice x2, local copies, waits for them, and re-layouts: 21.7 us -> 5.03 us  [on_device(): back = lax.ppermute(correction[local_src:], CORE, swap)]
    ppermute x2, waiting for transfers between devices: 0.01 us -> 8.65 us  [on_device(): back = lax.ppermute(correction[local_src:], CORE, swap)]
  transfers between devices with their start and end apart: 17 -> 17, of which waited for: 13 -> 15; matrix products, arithmetic and copies ran while one was open for 11% -> 11% of each run, Pallas kernels for 0% -> 0%
where the time goes in v2:
time: 389 us; the launch traced here: 387 us
  waiting for transfers between devices  139 us (36%)
  other arithmetic  101 us (26%)
  starting transfers between devices  58.7 us (15%)
  Pallas kernels  28.2 us (7%)
  blocking collectives  25.1 us (6%)
  local copies, waits for them, and re-layouts  19.5 us (5%)
  between operations  15 us (4%)
    ppermute x6, waiting for transfers between devices, extended_2(): lax.ppermute(tail, axis, [(i, (i + 1) % count) for i in range(ends)])  78.1 us
    ppermute x6, starting transfers between devices, extended_2(): lax.ppermute(head, axis, [((i + 1) % count, i) for i in range(ends)])  45 us
    sub x2, other arithmetic, residual_of(): source_term - apply_operator(potential, padded, center_coef, face_coefs)  40 us
    all_gather x1, waiting for transfers between devices, on_device(): inverse_mine = lax.all_gather(inverse_rows, CHIP_AXES, axis=2, tiled=True)  35.7 us
    pallas_call x2, Pallas kernels, correction_of(): pl.pallas_call(correction_kernel, grid=(ny // rows,), in_specs=[pl.BlockS...  28.2 us
    psum x1, blocking collectives, on_device(): totals = lax.psum(jnp.sum(residual * residual, axis=(1, 2, 3)), 'sub')  25.1 us
    concatenate x4, other arithmetic, extended_2(): jnp.concatenate([lax.ppermute(tail, axis, [(i, (i + 1) % count) for i in...  24.7 us
    reduce_sum x1, other arithmetic, on_device(): totals = lax.psum(jnp.sum(residual * residual, axis=(1, 2, 3)), 'sub')  18.5 us
  transfers between devices with their start and end apart: 17, of which 15 were waited for; matrix products, arithmetic and copies ran while one was open for 11% of the time, Pallas kernels for 0%

profile of v2, /device:TPU:6, one launch (start us, length us, event | category | flops | bytes accessed | tf_op | source)
XLA Modules:
  0.0 386.6 jit_solution(16080256921422832064)
XLA Ops:
  8.8 3.8 collective-permute-start.1
  12.6 5.6 %collective-permute-start = (f32[1,128,128]{2,1,0:T(8,128)S(1)}, f32[1,128,128]{2,1,0:T(8,128)S(1)}, u32[]{:S(2)}, u32[]{:S(2)}) collective-permute-start(f32[1,128,128]{2,1,0:T(8,128)S(1)} %get-tuple-element.28), channel_id=1, source_target_pairs={{16,0},{32,16},{48,32},{64,48},{80,64},{96,80},{112,96},{17,1},{33... | collective-permute-start | bytes 196616 | tf_op jit(solution)/shard_map/ppermute | solution.py:58
  18.3 1.9 fusion.45
  20.2 1.9 collective-permute-start.3
  22.1 7.5 %collective-permute-start.2 = (f32[4,1,128,128]{3,2,1,0:T(8,128)}, f32[4,1,128,128]{3,2,1,0:T(8,128)}, u32[]{:S(2)}, u32[]{:S(2)}) collective-permute-start(f32[4,1,128,128]{3,2,1,0:T(8,128)} %get-tuple-element.19), channel_id=1, source_target_pairs={{16,0},{32,16},{48,32},{64,48},{80,64},{96,80},{112,96},{17,1},{33... | collective-permute-start | bytes 786440 | tf_op jit(solution)/shard_map/ppermute | solution.py:58
  32.1 3.2 add_add_fusion
  35.3 4.8 %collective-permute-done.3 = f32[4,1,128,128]{3,2,1,0:T(8,128)S(1)} collective-permute-done((f32[4,1,128,128]{3,2,1,0:T(8,128)}, f32[4,1,128,128]{3,2,1,0:T(8,128)S(1)}, u32[]{:S(2)}, u32[]{:S(2)}) %collective-permute-start.3) | collective-permute-done | bytes 262176 | tf_op jit(solution)/shard_map/ppermute | solution.py:56
  40.1 1.5 collective-permute-done.2
  41.6 8.7 %select_maximum_fusion.4 = f32[4,18,130,130]{3,2,1,0:T(8,128)} fusion(f32[4,1,128,128]{3,2,1,0:T(8,128)} %collective-permute-done.2, f32[4,16,128,128]{3,2,1,0:T(8,128)S(1)} %copy-done.4, f32[4,1,128,128]{3,2,1,0:T(8,128)S(1)} %collective-permute-done.3), kind=kLoop, calls=%fused_computation.8 | loop fusion | flops 18252000 | bytes 9585792 | tf_op jit(solution)/shard_map/concatenate | solution.py:54
  50.3 20.1 %fusion.24 = f32[4,16,128,128]{3,2,1,0:T(8,128)} fusion(f32[4,18,130,130]{3,2,1,0:T(8,128)} %select_maximum_fusion.4, f32[4,16,128,128]{3,2,1,0:T(8,128)} %param.5, f32[4,1,128,128]{3,2,1,0:T(8,128)S(1)} %collective-permute-done.3, f32[4,1,128,128]{3,2,1,0:T(8,128)} %collective-permute-done.2, f32[16,128,128]{2,1,0:T(8,128)} %get-tuple-element.23, ...), kind=kLoop, calls=%fused_computation.49 | loop fusion | flops 22020096 | bytes 34078752 | tf_op jit(solution)/shard_map/sub | solution.py:130
  70.4 2.7 dynamic-slice_bitcast_fusion.3
  73.2 4.1 %collective-permute-done.4 = f32[4,16,8,8,128]{4,3,2,1,0:T(8,128)S(1)} collective-permute-done((f32[4,16,8,8,128]{4,3,2,1,0:T(8,128)S(1)}, f32[4,16,8,8,128]{4,3,2,1,0:T(8,128)S(1)}, u32[]{:S(2)}, u32[]{:S(2)}) %collective-permute-start.4) | collective-permute-done | bytes 2097184 | tf_op jit(solution)/shard_map/ppermute | solution.py:138
  77.6 1.9 collective-permute-start.5
  79.5 7.9 %collective-permute-start.6 = (f32[8,4,64,128]{3,2,1,0:T(8,128)S(1)}, f32[8,4,64,128]{3,2,1,0:T(8,128)S(1)}, u32[]{:S(2)}, u32[]{:S(2)}) collective-permute-start(f32[8,4,64,128]{3,2,1,0:T(8,128)S(1)} %get-tuple-element.15), channel_id=1, source_target_pairs={{16,0},{32,16},{48,32},{64,48},{80,64},{96,80},{112,96},{17,1},{33... | collective-permute-start | bytes 3145736 | tf_op jit(solution)/shard_map/ppermute | solution.py:58
  88.0 43.1 %collective-permute-done.5 = f32[8,4,64,128]{3,2,1,0:T(8,128)S(1)} collective-permute-done((f32[8,4,64,128]{3,2,1,0:T(8,128)S(1)}, f32[8,4,64,128]{3,2,1,0:T(8,128)S(1)}, u32[]{:S(2)}, u32[]{:S(2)}) %collective-permute-start.5) | collective-permute-done | bytes 1048608 | tf_op jit(solution)/shard_map/ppermute | solution.py:56
  131.1 2.0 collective-permute-done.6
  133.1 3.1 maximum_multiply_fusion.ext_ref
  136.2 35.7 %all-gather.2.cloned.1.call-done.inv_ref = f32[16,24,64,128]{3,2,1,0:T(8,128)} async-done(((f32[16,24,8,128]{3,2,1,0:T(8,128)}), f32[16,24,64,128]{3,2,1,0:T(8,128)}) %all-gather.2.cloned.1.call-update) | async-done | bytes 12582928 | tf_op jit(solution)/shard_map/all_gather | solution.py:118
  171.9 14.0 %shard_map.68 = f32[8,16,64,128]{3,2,1,0:T(8,128)} custom-call(f32[16,24,64,128]{3,2,1,0:T(8,128)} %all-gather.2.cloned.1.call-done.inv_ref, f32[8,24,64,128]{3,2,1,0:T(8,128)} %maximum_multiply_fusion.ext_ref), custom_call_target="tpu_custom_call" | custom-call | tf_op jit(solution)/shard_map/pallas_call | solution.py:27
  186.0 3.2 slice_bitcast_fusion.2
  189.1 4.5 %collective-permute-done.7 = f32[4,16,8,8,128]{4,3,2,1,0:T(8,128)} collective-permute-done((f32[4,16,8,8,128]{4,3,2,1,0:T(8,128)}, f32[4,16,8,8,128]{4,3,2,1,0:T(8,128)}, u32[]{:S(2)}, u32[]{:S(2)}) %collective-permute-start.7) | collective-permute-done | bytes 2097184 | tf_op jit(solution)/shard_map/ppermute | solution.py:145
  193.6 2.7 select_bitcast_fusion.3
  197.3 1.8 copy-done.5
  199.1 1.2 bitcast_add_fusion.1
  200.3 1.9 collective-permute-start.9
  202.3 7.7 %collective-permute-start.8 = (f32[4,1,128,128]{3,2,1,0:T(8,128)S(1)}, f32[4,1,128,128]{3,2,1,0:T(8,128)S(1)}, u32[]{:S(2)}, u32[]{:S(2)}) collective-permute-start(f32[4,1,128,128]{3,2,1,0:T(8,128)S(1)} %get-tuple-element.13), channel_id=1, source_target_pairs={{16,0},{32,16},{48,32},{64,48},{80,64},{96,80},{112,96},{17,1},{33... | collective-permute-start | bytes 786440 | tf_op jit(solution)/shard_map/ppermute | solution.py:58
  210.0 4.2 %collective-permute-done.9 = f32[4,1,128,128]{3,2,1,0:T(8,128)S(1)} collective-permute-done((f32[4,1,128,128]{3,2,1,0:T(8,128)S(1)}, f32[4,1,128,128]{3,2,1,0:T(8,128)S(1)}, u32[]{:S(2)}, u32[]{:S(2)}) %collective-permute-start.9) | collective-permute-done | bytes 262176 | tf_op jit(solution)/shard_map/ppermute | solution.py:56
  214.2 1.4 collective-permute-done.8
  216.3 7.7 %select_maximum_fusion.2 = f32[4,18,130,130]{3,2,1,0:T(8,128)} fusion(f32[4,1,128,128]{3,2,1,0:T(8,128)S(1)} %collective-permute-done.8, f32[4,16,128,128]{3,2,1,0:T(8,128)S(1)} %bitcast_add_fusion.1, f32[4,1,128,128]{3,2,1,0:T(8,128)S(1)} %collective-permute-done.9), kind=kLoop, calls=%fused_computation.6 | loop fusion | flops 18252000 | bytes 9585792 | tf_op jit(solution)/shard_map/concatenate | solution.py:54
  223.9 19.9 %fusion.15 = f32[4,16,128,128]{3,2,1,0:T(8,128)} fusion(f32[4,18,130,130]{3,2,1,0:T(8,128)} %select_maximum_fusion.2, f32[4,16,128,128]{3,2,1,0:T(8,128)} %copy-done.2, f32[4,1,128,128]{3,2,1,0:T(8,128)S(1)} %collective-permute-done.9, f32[4,1,128,128]{3,2,1,0:T(8,128)} %copy-done.11, f32[16,128,128]{2,1,0:T(8,128)} %get-tuple-element.23, ...), kind=kLoop, calls=%fused_computation.34 | loop fusion | flops 22020096 | bytes 34078752 | tf_op jit(solution)/shard_map/sub | solution.py:130
  243.9 2.6 dynamic-slice_bitcast_fusion.1
  246.6 4.1 %collective-permute-done.10 = f32[4,16,8,8,128]{4,3,2,1,0:T(8,128)S(1)} collective-permute-done((f32[4,16,8,8,128]{4,3,2,1,0:T(8,128)S(1)}, f32[4,16,8,8,128]{4,3,2,1,0:T(8,128)S(1)}, u32[]{:S(2)}, u32[]{:S(2)}) %collective-permute-start.10) | collective-permute-done | bytes 2097184 | tf_op jit(solution)/shard_map/ppermute | solution.py:138
  251.0 1.9 collective-permute-start.11
  252.9 8.0 %collective-permute-start.12 = (f32[8,4,64,128]{3,2,1,0:T(8,128)S(1)}, f32[8,4,64,128]{3,2,1,0:T(8,128)S(1)}, u32[]{:S(2)}, u32[]{:S(2)}) collective-permute-start(f32[8,4,64,128]{3,2,1,0:T(8,128)S(1)} %get-tuple-element.9), channel_id=1, source_target_pairs={{16,0},{32,16},{48,32},{64,48},{80,64},{96,80},{112,96},{17,1},{33... | collective-permute-start | bytes 3145736 | tf_op jit(solution)/shard_map/ppermute | solution.py:58
  260.9 21.5 %collective-permute-done.11 = f32[8,4,64,128]{3,2,1,0:T(8,128)S(1)} collective-permute-done((f32[8,4,64,128]{3,2,1,0:T(8,128)S(1)}, f32[8,4,64,128]{3,2,1,0:T(8,128)S(1)}, u32[]{:S(2)}, u32[]{:S(2)}) %collective-permute-start.11) | collective-permute-done | bytes 1048608 | tf_op jit(solution)/shard_map/ppermute | solution.py:56
  282.4 1.2 collective-permute-done.12
  283.6 3.1 maximum_multiply_fusion.1.ext_ref
  286.7 14.1 %shard_map.69 = f32[8,16,64,128]{3,2,1,0:T(8,128)} custom-call(f32[16,24,64,128]{3,2,1,0:T(8,128)} %all-gather.2.cloned.1.call-done.inv_ref, f32[8,24,64,128]{3,2,1,0:T(8,128)} %maximum_multiply_fusion.1.ext_ref), custom_call_target="tpu_custom_call" | custom-call | tf_op jit(solution)/shard_map/pallas_call | solution.py:27
  300.8 1.9 slice_bitcast_fusion
  302.8 4.1 %collective-permute-done.13 = f32[4,16,8,8,128]{4,3,2,1,0:T(8,128)S(1)} collective-permute-done((f32[4,16,8,8,128]{4,3,2,1,0:T(8,128)S(1)}, f32[4,16,8,8,128]{4,3,2,1,0:T(8,128)S(1)}, u32[]{:S(2)}, u32[]{:S(2)}) %collective-permute-start.13) | collective-permute-done | bytes 2097184 | tf_op jit(solution)/shard_map/ppermute | solution.py:145
  308.5 1.8 copy-done.3
  310.3 1.2 bitcast_add_fusion
  311.5 1.9 collective-permute-start.15
  313.5 8.2 %collective-permute-start.14 = (f32[4,1,128,128]{3,2,1,0:T(8,128)S(1)}, f32[4,1,128,128]{3,2,1,0:T(8,128)S(1)}, u32[]{:S(2)}, u32[]{:S(2)}) collective-permute-start(f32[4,1,128,128]{3,2,1,0:T(8,128)S(1)} %get-tuple-element.7), channel_id=1, source_target_pairs={{16,0},{32,16},{48,32},{64,48},{80,64},{96,80},{112,96},{17,1},{33... | collective-permute-start | bytes 786440 | tf_op jit(solution)/shard_map/ppermute | solution.py:58
  321.7 4.4 %collective-permute-done.15 = f32[4,1,128,128]{3,2,1,0:T(8,128)S(1)} collective-permute-done((f32[4,1,128,128]{3,2,1,0:T(8,128)S(1)}, f32[4,1,128,128]{3,2,1,0:T(8,128)S(1)}, u32[]{:S(2)}, u32[]{:S(2)}) %collective-permute-start.15) | collective-permute-done | bytes 262176 | tf_op jit(solution)/shard_map/ppermute | solution.py:56
  328.0 7.6 %select_maximum_fusion = f32[4,18,130,130]{3,2,1,0:T(8,128)} fusion(f32[4,1,128,128]{3,2,1,0:T(8,128)S(1)} %collective-permute-done.14, f32[4,16,128,128]{3,2,1,0:T(8,128)S(1)} %bitcast_add_fusion, f32[4,1,128,128]{3,2,1,0:T(8,128)S(1)} %collective-permute-done.15), kind=kLoop, calls=%fused_computation.4 | loop fusion | flops 18252000 | bytes 9585792 | tf_op jit(solution)/shard_map/concatenate | solution.py:54
  335.7 18.5 %fusion.6 = f32[4]{0:T(128)S(1)} fusion(f32[4,18,130,130]{3,2,1,0:T(8,128)} %select_maximum_fusion, f32[4,16,128,128]{3,2,1,0:T(8,128)} %copy-done.6, f32[4,1,128,128]{3,2,1,0:T(8,128)S(1)} %collective-permute-done.15, f32[4,1,128,128]{3,2,1,0:T(8,128)} %copy-done.10, f32[16,128,128]{2,1,0:T(8,128)} %get-tuple-element.23, ...), kind=kLoop, calls=%fused_computation.19 | loop fusion | flops 24117244 | bytes 29884464 | tf_op jit(solution)/shard_map/reduce_sum | solution.py:151
  354.2 25.1 %psum.7 = f32[4]{0:T(128)S(1)} all-reduce(f32[4]{0:T(128)S(1)} %fusion.6), channel_id=1, replica_groups=mesh['sub'=8,'xl'=2,'y'=4,'core'=2] {'sub'}, use_global_device_ids=true, to_apply=%region_1.2 | all-reduce | flops 4 | bytes 32 | tf_op jit(solution)/shard_map/psum | solution.py:151
  (48 shorter events, 10.5 us)
Async XLA Ops:
  7.2 22.5 %copy-start = (s32[64,2]{0,1:T(2,128)S(1)}, s32[64,2]{0,1:T(2,128)}, u32[]{:S(2)}) copy-start(s32[64,2]{0,1:T(2,128)} %param.8) | copy-start | bytes 1540
  7.2 23.7 %copy-start.8 = (f32[16,128,128]{2,1,0:T(8,128)S(1)}, f32[16,128,128]{2,1,0:T(8,128)}, u32[]{:S(2)}) copy-start(f32[16,128,128]{2,1,0:T(8,128)} %param.6) | copy-start | bytes 3145732
  7.2 164.7 %all-gather.2.cloned.1.call-start = ((), (), s32[]{:S(2)}) async-start(), calls=%async_computation | async-start | bytes 14155776 | tf_op jit(solution)/shard_map/all_gather | solution.py:118
  8.8 22.1 %collective-permute-start.1 = (f32[1,128,128]{2,1,0:T(8,128)S(1)}, f32[1,128,128]{2,1,0:T(8,128)S(1)}, u32[]{:S(2)}, u32[]{:S(2)}) collective-permute-start(f32[1,128,128]{2,1,0:T(8,128)S(1)} %get-tuple-element.27), channel_id=1, source_target_pairs={{0,16},{16,32},{32,48},{48,64},{64,80},{80,96},{96,112},{1,17},{17... | collective-permute-start | bytes 196616 | tf_op jit(solution)/shard_map/ppermute | solution.py:56
  12.6 18.2 %collective-permute-start = (f32[1,128,128]{2,1,0:T(8,128)S(1)}, f32[1,128,128]{2,1,0:T(8,128)S(1)}, u32[]{:S(2)}, u32[]{:S(2)}) collective-permute-start(f32[1,128,128]{2,1,0:T(8,128)S(1)} %get-tuple-element.28), channel_id=1, source_target_pairs={{16,0},{32,16},{48,32},{64,48},{80,64},{96,80},{112,96},{17,1},{33... | collective-permute-start | bytes 196616 | tf_op jit(solution)/shard_map/ppermute | solution.py:58
  20.2 20.0 %collective-permute-start.3 = (f32[4,1,128,128]{3,2,1,0:T(8,128)}, f32[4,1,128,128]{3,2,1,0:T(8,128)S(1)}, u32[]{:S(2)}, u32[]{:S(2)}) collective-permute-start(f32[4,1,128,128]{3,2,1,0:T(8,128)} %get-tuple-element.18), channel_id=1, source_target_pairs={{0,16},{16,32},{32,48},{48,64},{64,80},{80,96},{96,112},{1,17},{17... | collective-permute-start | bytes 786440 | tf_op jit(solution)/shard_map/ppermute | solution.py:56
  22.1 19.5 %collective-permute-start.2 = (f32[4,1,128,128]{3,2,1,0:T(8,128)}, f32[4,1,128,128]{3,2,1,0:T(8,128)}, u32[]{:S(2)}, u32[]{:S(2)}) collective-permute-start(f32[4,1,128,128]{3,2,1,0:T(8,128)} %get-tuple-element.19), channel_id=1, source_target_pairs={{16,0},{32,16},{48,32},{64,48},{80,64},{96,80},{112,96},{17,1},{33... | collective-permute-start | bytes 786440 | tf_op jit(solution)/shard_map/ppermute | solution.py:58
  30.9 1.2 copy-start.9
  32.1 9.5 %copy-start.4 = (f32[4,16,128,128]{3,2,1,0:T(8,128)S(1)}, f32[4,16,128,128]{3,2,1,0:T(8,128)}, u32[]{:S(2)}) copy-start(f32[4,16,128,128]{3,2,1,0:T(8,128)} %param.5) | copy-start | bytes 12582916
  73.1 4.2 %collective-permute-start.4 = (f32[4,16,8,8,128]{4,3,2,1,0:T(8,128)S(1)}, f32[4,16,8,8,128]{4,3,2,1,0:T(8,128)S(1)}, u32[]{:S(2)}, u32[]{:S(2)}) collective-permute-start(f32[4,16,8,8,128]{4,3,2,1,0:T(8,128)S(1)} %get-tuple-element.17), channel_id=1, source_target_pairs={{0,1},{1,0},{2,3},{3,2},{4,5},{5,4},{6,7},{7,6},{8,9},{9,8},{10,11... | collective-permute-start | bytes 6291464 | tf_op jit(solution)/shard_map/ppermute | solution.py:138
  77.6 53.5 %collective-permute-start.5 = (f32[8,4,64,128]{3,2,1,0:T(8,128)S(1)}, f32[8,4,64,128]{3,2,1,0:T(8,128)S(1)}, u32[]{:S(2)}, u32[]{:S(2)}) collective-permute-start(f32[8,4,64,128]{3,2,1,0:T(8,128)S(1)} %get-tuple-element.14), channel_id=1, source_target_pairs={{0,16},{16,32},{32,48},{48,64},{64,80},{80,96},{96,112},{1,17},{17... | collective-permute-start | bytes 3145736 | tf_op jit(solution)/shard_map/ppermute | solution.py:56
  79.5 53.6 %collective-permute-start.6 = (f32[8,4,64,128]{3,2,1,0:T(8,128)S(1)}, f32[8,4,64,128]{3,2,1,0:T(8,128)S(1)}, u32[]{:S(2)}, u32[]{:S(2)}) collective-permute-start(f32[8,4,64,128]{3,2,1,0:T(8,128)S(1)} %get-tuple-element.15), channel_id=1, source_target_pairs={{16,0},{32,16},{48,32},{64,48},{80,64},{96,80},{112,96},{17,1},{33... | collective-permute-start | bytes 3145736 | tf_op jit(solution)/shard_map/ppermute | solution.py:58
  189.1 4.5 %collective-permute-start.7 = (f32[4,16,8,8,128]{4,3,2,1,0:T(8,128)}, f32[4,16,8,8,128]{4,3,2,1,0:T(8,128)}, u32[]{:S(2)}, u32[]{:S(2)}) collective-permute-start(f32[4,16,8,8,128]{4,3,2,1,0:T(8,128)} %slice_bitcast_fusion.2), channel_id=1, source_target_pairs={{0,1},{1,0},{2,3},{3,2},{4,5},{5,4},{6,7},{7,6},{8,9},{9,8},{10,11... | collective-permute-start | bytes 6291464 | tf_op jit(solution)/shard_map/ppermute | solution.py:145
  196.9 2.2 copy-start.5
  200.3 15.3 %copy-start.2 = (f32[4,16,128,128]{3,2,1,0:T(8,128)}, f32[4,16,128,128]{3,2,1,0:T(8,128)S(1)}, u32[]{:S(2)}) copy-start(f32[4,16,128,128]{3,2,1,0:T(8,128)S(1)} %bitcast_add_fusion.1) | copy-start | bytes 12582916
  200.3 13.9 %collective-permute-start.9 = (f32[4,1,128,128]{3,2,1,0:T(8,128)S(1)}, f32[4,1,128,128]{3,2,1,0:T(8,128)S(1)}, u32[]{:S(2)}, u32[]{:S(2)}) collective-permute-start(f32[4,1,128,128]{3,2,1,0:T(8,128)S(1)} %get-tuple-element.12), channel_id=1, source_target_pairs={{0,16},{16,32},{32,48},{48,64},{64,80},{80,96},{96,112},{1,17},{17... | collective-permute-start | bytes 786440 | tf_op jit(solution)/shard_map/ppermute | solution.py:56
  202.3 13.3 %collective-permute-start.8 = (f32[4,1,128,128]{3,2,1,0:T(8,128)S(1)}, f32[4,1,128,128]{3,2,1,0:T(8,128)S(1)}, u32[]{:S(2)}, u32[]{:S(2)}) collective-permute-start(f32[4,1,128,128]{3,2,1,0:T(8,128)S(1)} %get-tuple-element.13), channel_id=1, source_target_pairs={{16,0},{32,16},{48,32},{64,48},{80,64},{96,80},{112,96},{17,1},{33... | collective-permute-start | bytes 786440 | tf_op jit(solution)/shard_map/ppermute | solution.py:58
  215.5 0.7 copy-start.11
  246.5 4.2 %collective-permute-start.10 = (f32[4,16,8,8,128]{4,3,2,1,0:T(8,128)S(1)}, f32[4,16,8,8,128]{4,3,2,1,0:T(8,128)S(1)}, u32[]{:S(2)}, u32[]{:S(2)}) collective-permute-start(f32[4,16,8,8,128]{4,3,2,1,0:T(8,128)S(1)} %get-tuple-element.11), channel_id=1, source_target_pairs={{0,1},{1,0},{2,3},{3,2},{4,5},{5,4},{6,7},{7,6},{8,9},{9,8},{10,11... | collective-permute-start | bytes 6291464 | tf_op jit(solution)/shard_map/ppermute | solution.py:138
  251.0 31.5 %collective-permute-start.11 = (f32[8,4,64,128]{3,2,1,0:T(8,128)S(1)}, f32[8,4,64,128]{3,2,1,0:T(8,128)S(1)}, u32[]{:S(2)}, u32[]{:S(2)}) collective-permute-start(f32[8,4,64,128]{3,2,1,0:T(8,128)S(1)} %get-tuple-element.8), channel_id=1, source_target_pairs={{0,16},{16,32},{32,48},{48,64},{64,80},{80,96},{96,112},{1,17},{17... | collective-permute-start | bytes 3145736 | tf_op jit(solution)/shard_map/ppermute | solution.py:56
  252.9 30.7 %collective-permute-start.12 = (f32[8,4,64,128]{3,2,1,0:T(8,128)S(1)}, f32[8,4,64,128]{3,2,1,0:T(8,128)S(1)}, u32[]{:S(2)}, u32[]{:S(2)}) collective-permute-start(f32[8,4,64,128]{3,2,1,0:T(8,128)S(1)} %get-tuple-element.9), channel_id=1, source_target_pairs={{16,0},{32,16},{48,32},{64,48},{80,64},{96,80},{112,96},{17,1},{33... | collective-permute-start | bytes 3145736 | tf_op jit(solution)/shard_map/ppermute | solution.py:58
  300.8 6.1 %copy-start.7 = (f32[8,16,64,128]{3,2,1,0:T(8,128)S(1)}, f32[8,16,64,128]{3,2,1,0:T(8,128)}, u32[]{:S(2)}) copy-start(f32[8,16,64,128]{3,2,1,0:T(8,128)} %shard_map.69) | copy-start | bytes 12582916
  302.7 4.2 %collective-permute-start.13 = (f32[4,16,8,8,128]{4,3,2,1,0:T(8,128)S(1)}, f32[4,16,8,8,128]{4,3,2,1,0:T(8,128)S(1)}, u32[]{:S(2)}, u32[]{:S(2)}) collective-permute-start(f32[4,16,8,8,128]{4,3,2,1,0:T(8,128)S(1)} %slice_bitcast_fusion), channel_id=1, source_target_pairs={{0,1},{1,0},{2,3},{3,2},{4,5},{5,4},{6,7},{7,6},{8,9},{9,8},{10,11... | collective-permute-start | bytes 6291464 | tf_op jit(solution)/shard_map/ppermute | solution.py:145
  308.1 2.2 copy-start.3
  311.5 15.8 %copy-start.6 = (f32[4,16,128,128]{3,2,1,0:T(8,128)}, f32[4,16,128,128]{3,2,1,0:T(8,128)S(1)}, u32[]{:S(2)}) copy-start(f32[4,16,128,128]{3,2,1,0:T(8,128)S(1)} %bitcast_add_fusion) | copy-start | bytes 12582916
  311.5 14.6 %collective-permute-start.15 = (f32[4,1,128,128]{3,2,1,0:T(8,128)S(1)}, f32[4,1,128,128]{3,2,1,0:T(8,128)S(1)}, u32[]{:S(2)}, u32[]{:S(2)}) collective-permute-start(f32[4,1,128,128]{3,2,1,0:T(8,128)S(1)} %get-tuple-element.6), channel_id=1, source_target_pairs={{0,16},{16,32},{32,48},{48,64},{64,80},{80,96},{96,112},{1,17},{17... | collective-permute-start | bytes 786440 | tf_op jit(solution)/shard_map/ppermute | solution.py:56
  313.5 13.9 %collective-permute-start.14 = (f32[4,1,128,128]{3,2,1,0:T(8,128)S(1)}, f32[4,1,128,128]{3,2,1,0:T(8,128)S(1)}, u32[]{:S(2)}, u32[]{:S(2)}) collective-permute-start(f32[4,1,128,128]{3,2,1,0:T(8,128)S(1)} %get-tuple-element.7), channel_id=1, source_target_pairs={{16,0},{32,16},{48,32},{64,48},{80,64},{96,80},{112,96},{17,1},{33... | collective-permute-start | bytes 786440 | tf_op jit(solution)/shard_map/ppermute | solution.py:58
  327.3 0.7 copy-start.10
  335.7 44.1 %copy-start.1 = (s32[64,2]{0,1:T(2,128)S(1)}, s32[64,2]{0,1:T(2,128)}, u32[]{:S(2)}) copy-start(s32[64,2]{0,1:T(2,128)} %param.8) | copy-start | bytes 1540
Sparse Core Ops, SparseCore 0:
  9.6 162.3 all-gather.1

commit v3 on v2

--- a/solution.py
+++ b/solution.py
@@ -3,6 +3,45 @@
 from jax import lax
 from jax.sharding import Mesh, PartitionSpec as P
 from jax.experimental import pallas as pl
+from jax.experimental.pallas import tpu as pltpu
+
+
+def stencil_kernel(v_ref, lo_ref, hi_ref, st_ref, cc_ref, fxp_ref, fxm_ref, fyp_ref, fym_ref, fzp_ref, fzm_ref, out_ref):
+    width = v_ref.shape[1]
+    ny, nz = v_ref.shape[2], v_ref.shape[3]
+
+    def plane(x, carry):
+        v = v_ref[0, x]
+        up = v_ref[0, jnp.minimum(x + 1, width - 1)]
+        down = v_ref[0, jnp.maximum(x - 1, 0)]
+        up = jnp.where(x == width - 1, hi_ref[0, 0], up)
+        down = jnp.where(x == 0, lo_ref[0, 0], down)
+        image = cc_ref[x] * v
+        image = image - fxp_ref[x] * up
+        image = image - fxm_ref[x] * down
+        image = image - fyp_ref[x] * pltpu.roll(v, ny - 1, 0)
+        image = image - fym_ref[x] * pltpu.roll(v, 1, 0)
+        image = image - fzp_ref[x] * pltpu.roll(v, nz - 1, 1)
+        image = image - fzm_ref[x] * pltpu.roll(v, 1, 1)
+        out_ref[0, x] = st_ref[0, x] - image
+        return carry
+
+    lax.fori_loop(0, width, plane, 0)
+
+
+def residual_kernel_call(v, lo, hi, st, coefs):
+    n_src, width, ny, nz = v.shape
+    src_block = pl.BlockSpec((1, width, ny, nz), lambda s: (s, 0, 0, 0))
+    rim_block = pl.BlockSpec((1, 1, ny, nz), lambda s: (s, 0, 0, 0))
+    coef_block = pl.BlockSpec((width, ny, nz), lambda s: (0, 0, 0))
+    return pl.pallas_call(
+        stencil_kernel,
+        grid=(n_src,),
+        in_specs=[src_block, rim_block, rim_block, src_block] + [coef_block] * 7,
+        out_specs=src_block,
+        out_shape=jax.ShapeDtypeStruct(v.shape, jnp.float32),
+    )(v, lo, hi, st, *coefs)
+
 
 def correction_kernel(inv_ref, ext_ref, out_ref):
     n_out, n_col = inv_ref.shape[0], inv_ref.shape[1]
@@ -124,10 +163,23 @@
     source_term = source_block(own_pairs, x_start, width_x, full_y, full_y, depth)
     swap = [(0, 1), (1, 0)]
 
+    y_ids = lax.broadcasted_iota(jnp.int32, center_coef.shape, 1)
+    z_ids = lax.broadcasted_iota(jnp.int32, center_coef.shape, 2)
+    coefs = [
+        center_coef,
+        face_coefs[0],
+        face_coefs[1],
+        jnp.where(y_ids == full_y - 1, 0.0, face_coefs[2]),
+        jnp.where(y_ids == 0, 0.0, face_coefs[3]),
+        jnp.where(z_ids == depth - 1, 0.0, face_coefs[4]),
+        jnp.where(z_ids == 0, 0.0, face_coefs[5]),
+    ]
+    n_sub = lax.axis_size("sub")
+
     def residual_of(potential):
-        padded = extended_2(potential, (("sub", 1),), 1)
-        padded = jnp.pad(padded, ((0, 0), (0, 0), (1, 1), (1, 1)))
-        return source_term - apply_operator(potential, padded, center_coef, face_coefs)
+        lo = lax.ppermute(potential[:, width_x - 1 :], "sub", [(i, i + 1) for i in range(n_sub - 1)])
+        hi = lax.ppermute(potential[:, :1], "sub", [(i + 1, i) for i in range(n_sub - 1)])
+        return residual_kernel_call(potential, lo, hi, source_term, coefs)
 
     potential = potential_init
     for sweep in range(ITERS):

time: 389 us -> 369 us (0.949)
  other arithmetic: 101 us -> 24.3 us
  Pallas kernels: 28.2 us -> 65.2 us
  waiting for transfers between devices: 139 us -> 170 us
  blocking collectives: 25.1 us -> 19 us
  starting transfers between devices: 58.7 us -> 53.6 us
    sub x2 -> x1, other arithmetic: 40 us -> 2.76 us  [source_block(): return CURRENT * first - CURRENT * second]
    pallas_call x0 -> x3, Pallas kernels: none -> 37 us  [residual_kernel_call(): pl.pallas_call(stencil_kernel, grid=(n_src,), in_specs=[src_block, rim_bl...]
    ppermute x0 -> x6, waiting for transfers between devices: none -> 32.3 us  [the longest x3 23.4 us: residual_of(): lax.ppermute(potential[:, width_x - 1:], 'sub', [(i, i + 1) for i in rang...]
    ppermute x0 -> x6, starting transfers between devices: none -> 24.7 us  [the longest x3 18.2 us: residual_of(): lax.ppermute(potential[:, :1], 'sub', [(i + 1, i) for i in range(n_sub -...]
    ppermute x6 -> x3, starting transfers between devices: 45 us -> 20.7 us  [extended_2(): lax.ppermute(head, axis, [((i + 1) % count, i) for i in range(ends)])]
    concatenate x4 -> x1, other arithmetic: 24.7 us -> 0.71 us  [extended_2(): jnp.concatenate([lax.ppermute(tail, axis, [(i, (i + 1) % count) for i in...]
    all_gather x1, waiting for transfers between devices: 35.7 us -> 52.4 us  [on_device(): inverse_mine = lax.all_gather(inverse_rows, CHIP_AXES, axis=2, tiled=True)]
    reduce_sum x1, other arithmetic: 18.5 us -> 2.61 us  [on_device(): totals = lax.psum(jnp.sum(residual * residual, axis=(1, 2, 3)), 'sub')]
  transfers between devices with their start and end apart: 17 -> 17, of which waited for: 15 -> 15; matrix products, arithmetic and copies ran while one was open for 11% -> 4% of each run, Pallas kernels for 0% -> 3%
where the time goes in v3:
time: 369 us; the launch traced here: 368 us
  waiting for transfers between devices  170 us (46%)
  Pallas kernels  65.2 us (18%)
  starting transfers between devices  53.6 us (15%)
  other arithmetic  24.3 us (7%)
  local copies, waits for them, and re-layouts  21.2 us (6%)
  blocking collectives  19 us (5%)
  between operations  15 us (4%)
    ppermute x3, waiting for transfers between devices, extended_2(): lax.ppermute(tail, axis, [(i, (i + 1) % count) for i in range(ends)])  64.9 us
    all_gather x1, waiting for transfers between devices, on_device(): inverse_mine = lax.all_gather(inverse_rows, CHIP_AXES, axis=2, tiled=True)  52.4 us
    pallas_call x3, Pallas kernels, residual_kernel_call(): pl.pallas_call(stencil_kernel, grid=(n_src,), in_specs=[src_block, rim_bl...  37 us
    pallas_call x2, Pallas kernels, correction_of(): pl.pallas_call(correction_kernel, grid=(ny // rows,), in_specs=[pl.BlockS...  28.1 us
    ppermute x3, waiting for transfers between devices, residual_of(): lax.ppermute(potential[:, width_x - 1:], 'sub', [(i, i + 1) for i in rang...  23.4 us
    ppermute x3, starting transfers between devices, extended_2(): lax.ppermute(head, axis, [((i + 1) % count, i) for i in range(ends)])  20.7 us
    psum x1, blocking collectives, on_device(): totals = lax.psum(jnp.sum(residual * residual, axis=(1, 2, 3)), 'sub')  19 us
    ppermute x3, starting transfers between devices, residual_of(): lax.ppermute(potential[:, :1], 'sub', [(i + 1, i) for i in range(n_sub -...  18.2 us
  transfers between devices with their start and end apart: 17, of which 15 were waited for; matrix products, arithmetic and copies ran while one was open for 4% of the time, Pallas kernels for 3%

profile of v3, /device:TPU:6, one launch (start us, length us, event | category | flops | bytes accessed | tf_op | source)
XLA Modules:
  0.0 367.8 jit_solution(17165546218873309556)
XLA Ops:
  8.9 3.8 %collective-permute-start.3 = (f32[1,128,128]{2,1,0:T(8,128)S(1)}, f32[1,128,128]{2,1,0:T(8,128)S(1)}, u32[]{:S(2)}, u32[]{:S(2)}) collective-permute-start(f32[1,128,128]{2,1,0:T(8,128)S(1)} %get-tuple-element.29), channel_id=1, source_target_pairs={{0,16},{16,32},{32,48},{48,64},{64,80},{80,96},{96,112},{1,17},{17... | collective-permute-start | bytes 196616 | tf_op jit(solution)/shard_map/ppermute | solution.py:95
  12.7 5.6 %collective-permute-start.2 = (f32[1,128,128]{2,1,0:T(8,128)S(1)}, f32[1,128,128]{2,1,0:T(8,128)S(1)}, u32[]{:S(2)}, u32[]{:S(2)}) collective-permute-start(f32[1,128,128]{2,1,0:T(8,128)S(1)} %get-tuple-element.30), channel_id=1, source_target_pairs={{16,0},{32,16},{48,32},{64,48},{80,64},{96,80},{112,96},{17,1},{33... | collective-permute-start | bytes 196616 | tf_op jit(solution)/shard_map/ppermute | solution.py:97
  19.4 3.2 collective-permute-start.1
  22.6 2.7 collective-permute-start
  25.6 2.8 select_subtract_fusion.st_ref
  29.1 4.2 %broadcast_select_fusion = (f32[16,128,128]{2,1,0:T(8,128)}, f32[16,128,128]{2,1,0:T(8,128)}, f32[16,128,128]{2,1,0:T(8,128)}, f32[16,128,128]{2,1,0:T(8,128)}, ...) fusion(f32[16,128,128]{2,1,0:T(8,128)S(1)} %copy-done.7, ...), kind=kLoop, calls=%fused_computation.49 | loop fusion | flops 6291456 | bytes 12716032 | tf_op jit(solution)/shard_map/jit(_where)/select_n | solution.py:175
  34.4 7.9 %collective-permute-done.lo_ref = f32[4,1,128,128]{3,2,1,0:T(8,128)S(1)} collective-permute-done((f32[4,1,128,128]{3,2,1,0:T(8,128)S(1)}, f32[4,1,128,128]{3,2,1,0:T(8,128)S(1)}, u32[]{:S(2)}, u32[]{:S(2)}) %collective-permute-start) | collective-permute-done | bytes 262176 | tf_op jit(solution)/shard_map/ppermute | solution.py:180
  43.0 12.4 %shard_map.68 = f32[4,16,128,128]{3,2,1,0:T(8,128)} custom-call(f32[4,16,128,128]{3,2,1,0:T(8,128)} %v_ref.1, f32[4,1,128,128]{3,2,1,0:T(8,128)} %copy-done.9, f32[4,1,128,128]{3,2,1,0:T(8,128)} %copy-done.8, f32[4,16,128,128]{3,2,1,0:T(8,128)} %select_subtract_fusion.st_ref, f32[16,128,128]{2,1,0:T(8,128)} %get-tuple-element.24.cc_ref, ...), custom_call_target="tpu_custom_call" | custom-call | tf_op jit(solution)/shard_map/pallas_call | solution.py:37
  55.4 2.6 dynamic-slice_bitcast_fusion.3
  58.1 4.1 %collective-permute-done.4 = f32[4,16,8,8,128]{4,3,2,1,0:T(8,128)S(1)} collective-permute-done((f32[4,16,8,8,128]{4,3,2,1,0:T(8,128)S(1)}, f32[4,16,8,8,128]{4,3,2,1,0:T(8,128)S(1)}, u32[]{:S(2)}, u32[]{:S(2)}) %collective-permute-start.4) | collective-permute-done | bytes 2097184 | tf_op jit(solution)/shard_map/ppermute | solution.py:190
  62.5 1.9 collective-permute-start.5
  64.4 7.5 %collective-permute-start.6 = (f32[8,4,64,128]{3,2,1,0:T(8,128)S(1)}, f32[8,4,64,128]{3,2,1,0:T(8,128)S(1)}, u32[]{:S(2)}, u32[]{:S(2)}) collective-permute-start(f32[8,4,64,128]{3,2,1,0:T(8,128)S(1)} %get-tuple-element.15), channel_id=1, source_target_pairs={{16,0},{32,16},{48,32},{64,48},{80,64},{96,80},{112,96},{17,1},{33... | collective-permute-start | bytes 3145736 | tf_op jit(solution)/shard_map/ppermute | solution.py:97
  72.6 43.6 %collective-permute-done.5 = f32[8,4,64,128]{3,2,1,0:T(8,128)S(1)} collective-permute-done((f32[8,4,64,128]{3,2,1,0:T(8,128)S(1)}, f32[8,4,64,128]{3,2,1,0:T(8,128)S(1)}, u32[]{:S(2)}, u32[]{:S(2)}) %collective-permute-start.5) | collective-permute-done | bytes 1048608 | tf_op jit(solution)/shard_map/ppermute | solution.py:95
  116.3 1.4 collective-permute-done.6
  117.6 3.2 maximum_multiply_fusion.ext_ref
  120.8 52.4 %all-gather.2.cloned.1.call-done.inv_ref = f32[16,24,64,128]{3,2,1,0:T(8,128)} async-done(((f32[16,24,8,128]{3,2,1,0:T(8,128)}), f32[16,24,64,128]{3,2,1,0:T(8,128)}) %all-gather.2.cloned.1.call-update) | async-done | bytes 12582928 | tf_op jit(solution)/shard_map/all_gather | solution.py:157
  173.2 14.0 %shard_map.69 = f32[8,16,64,128]{3,2,1,0:T(8,128)} custom-call(f32[16,24,64,128]{3,2,1,0:T(8,128)} %all-gather.2.cloned.1.call-done.inv_ref, f32[8,24,64,128]{3,2,1,0:T(8,128)} %maximum_multiply_fusion.ext_ref), custom_call_target="tpu_custom_call" | custom-call | tf_op jit(solution)/shard_map/pallas_call | solution.py:66
  187.3 1.7 slice_bitcast_fusion.2
  189.1 4.3 %collective-permute-done.7 = f32[4,16,8,8,128]{4,3,2,1,0:T(8,128)} collective-permute-done((f32[4,16,8,8,128]{4,3,2,1,0:T(8,128)S(1)}, f32[4,16,8,8,128]{4,3,2,1,0:T(8,128)}, u32[]{:S(2)}, u32[]{:S(2)}) %collective-permute-start.7) | collective-permute-done | bytes 2097184 | tf_op jit(solution)/shard_map/ppermute | solution.py:197
  193.4 2.7 select_bitcast_fusion.3
  197.0 1.8 copy-done.4
  198.8 1.2 bitcast_add_fusion.1.v_ref
  200.0 2.0 copy-done.2
  202.0 7.0 %collective-permute-start.9 = (f32[4,1,128,128]{3,2,1,0:T(8,128)S(1)}, f32[4,1,128,128]{3,2,1,0:T(8,128)S(1)}, u32[]{:S(2)}, u32[]{:S(2)}) collective-permute-start(f32[4,1,128,128]{3,2,1,0:T(8,128)S(1)} %get-tuple-element.12), channel_id=1, source_target_pairs={{16,0},{32,16},{48,32},{64,48},{80,64},{96,80},{112,96},{17,1},{33... | collective-permute-start | bytes 786440 | tf_op jit(solution)/shard_map/ppermute | solution.py:181
  209.1 1.9 collective-permute-start.8
  211.0 3.9 %collective-permute-done.9.hi_ref = f32[4,1,128,128]{3,2,1,0:T(8,128)S(1)} collective-permute-done((f32[4,1,128,128]{3,2,1,0:T(8,128)S(1)}, f32[4,1,128,128]{3,2,1,0:T(8,128)S(1)}, u32[]{:S(2)}, u32[]{:S(2)}) %collective-permute-start.9) | collective-permute-done | bytes 262176 | tf_op jit(solution)/shard_map/ppermute | solution.py:181
  214.9 7.7 %collective-permute-done.8.lo_ref = f32[4,1,128,128]{3,2,1,0:T(8,128)S(1)} collective-permute-done((f32[4,1,128,128]{3,2,1,0:T(8,128)S(1)}, f32[4,1,128,128]{3,2,1,0:T(8,128)S(1)}, u32[]{:S(2)}, u32[]{:S(2)}) %collective-permute-start.8) | collective-permute-done | bytes 262176 | tf_op jit(solution)/shard_map/ppermute | solution.py:180
  223.4 12.3 %shard_map.70 = f32[4,16,128,128]{3,2,1,0:T(8,128)} custom-call(f32[4,16,128,128]{3,2,1,0:T(8,128)} %copy-done.2, f32[4,1,128,128]{3,2,1,0:T(8,128)} %copy-done.13, f32[4,1,128,128]{3,2,1,0:T(8,128)} %copy-done.12, f32[4,16,128,128]{3,2,1,0:T(8,128)} %select_subtract_fusion.st_ref, f32[16,128,128]{2,1,0:T(8,128)} %get-tuple-element.24.cc_ref, ...), custom_call_target="tpu_custom_call" | custom-call | tf_op jit(solution)/shard_map/pallas_call | solution.py:37
  235.7 2.6 dynamic-slice_bitcast_fusion.1
  238.4 4.1 %collective-permute-done.10 = f32[4,16,8,8,128]{4,3,2,1,0:T(8,128)S(1)} collective-permute-done((f32[4,16,8,8,128]{4,3,2,1,0:T(8,128)S(1)}, f32[4,16,8,8,128]{4,3,2,1,0:T(8,128)S(1)}, u32[]{:S(2)}, u32[]{:S(2)}) %collective-permute-start.10) | collective-permute-done | bytes 2097184 | tf_op jit(solution)/shard_map/ppermute | solution.py:190
  242.8 1.9 collective-permute-start.11
  244.7 7.5 %collective-permute-start.12 = (f32[8,4,64,128]{3,2,1,0:T(8,128)S(1)}, f32[8,4,64,128]{3,2,1,0:T(8,128)S(1)}, u32[]{:S(2)}, u32[]{:S(2)}) collective-permute-start(f32[8,4,64,128]{3,2,1,0:T(8,128)S(1)} %get-tuple-element.9), channel_id=1, source_target_pairs={{16,0},{32,16},{48,32},{64,48},{80,64},{96,80},{112,96},{17,1},{33... | collective-permute-start | bytes 3145736 | tf_op jit(solution)/shard_map/ppermute | solution.py:97
  252.2 21.2 %collective-permute-done.11 = f32[8,4,64,128]{3,2,1,0:T(8,128)S(1)} collective-permute-done((f32[8,4,64,128]{3,2,1,0:T(8,128)S(1)}, f32[8,4,64,128]{3,2,1,0:T(8,128)S(1)}, u32[]{:S(2)}, u32[]{:S(2)}) %collective-permute-start.11) | collective-permute-done | bytes 1048608 | tf_op jit(solution)/shard_map/ppermute | solution.py:95
  273.5 1.2 collective-permute-done.12
  274.7 3.1 maximum_multiply_fusion.1.ext_ref
  277.8 14.1 %shard_map.71 = f32[8,16,64,128]{3,2,1,0:T(8,128)} custom-call(f32[16,24,64,128]{3,2,1,0:T(8,128)} %all-gather.2.cloned.1.call-done.inv_ref, f32[8,24,64,128]{3,2,1,0:T(8,128)} %maximum_multiply_fusion.1.ext_ref), custom_call_target="tpu_custom_call" | custom-call | tf_op jit(solution)/shard_map/pallas_call | solution.py:66
  291.9 1.9 slice_bitcast_fusion
  294.0 4.1 %collective-permute-done.13 = f32[4,16,8,8,128]{4,3,2,1,0:T(8,128)S(1)} collective-permute-done((f32[4,16,8,8,128]{4,3,2,1,0:T(8,128)S(1)}, f32[4,16,8,8,128]{4,3,2,1,0:T(8,128)S(1)}, u32[]{:S(2)}, u32[]{:S(2)}) %collective-permute-start.13) | collective-permute-done | bytes 2097184 | tf_op jit(solution)/shard_map/ppermute | solution.py:197
  299.1 1.9 copy-done.3
  301.0 1.2 bitcast_add_fusion.v_ref
  302.2 2.0 copy-done.5
  304.3 8.0 %collective-permute-start.15 = (f32[4,1,128,128]{3,2,1,0:T(8,128)S(1)}, f32[4,1,128,128]{3,2,1,0:T(8,128)S(1)}, u32[]{:S(2)}, u32[]{:S(2)}) collective-permute-start(f32[4,1,128,128]{3,2,1,0:T(8,128)S(1)} %get-tuple-element.6), channel_id=1, source_target_pairs={{16,0},{32,16},{48,32},{64,48},{80,64},{96,80},{112,96},{17,1},{33... | collective-permute-start | bytes 786440 | tf_op jit(solution)/shard_map/ppermute | solution.py:181
  312.3 1.9 collective-permute-start.14
  314.2 3.9 %collective-permute-done.15.hi_ref = f32[4,1,128,128]{3,2,1,0:T(8,128)S(1)} collective-permute-done((f32[4,1,128,128]{3,2,1,0:T(8,128)S(1)}, f32[4,1,128,128]{3,2,1,0:T(8,128)S(1)}, u32[]{:S(2)}, u32[]{:S(2)}) %collective-permute-start.15) | collective-permute-done | bytes 262176 | tf_op jit(solution)/shard_map/ppermute | solution.py:181
  318.1 7.7 %collective-permute-done.14.lo_ref = f32[4,1,128,128]{3,2,1,0:T(8,128)S(1)} collective-permute-done((f32[4,1,128,128]{3,2,1,0:T(8,128)S(1)}, f32[4,1,128,128]{3,2,1,0:T(8,128)S(1)}, u32[]{:S(2)}, u32[]{:S(2)}) %collective-permute-start.14) | collective-permute-done | bytes 262176 | tf_op jit(solution)/shard_map/ppermute | solution.py:180
  326.6 12.4 %shard_map.72 = f32[4,16,128,128]{3,2,1,0:T(8,128)} custom-call(f32[4,16,128,128]{3,2,1,0:T(8,128)} %copy-done.5, f32[4,1,128,128]{3,2,1,0:T(8,128)} %copy-done.11, f32[4,1,128,128]{3,2,1,0:T(8,128)} %copy-done.10, f32[4,16,128,128]{3,2,1,0:T(8,128)} %select_subtract_fusion.st_ref, f32[16,128,128]{2,1,0:T(8,128)} %get-tuple-element.24.cc_ref, ...), custom_call_target="tpu_custom_call" | custom-call | tf_op jit(solution)/shard_map/pallas_call | solution.py:37
  338.9 2.6 multiply_reduce_fusion
  341.5 19.0 %psum.7 = f32[4]{0:T(128)S(1)} all-reduce(f32[4]{0:T(128)S(1)} %multiply_reduce_fusion), channel_id=1, replica_groups=mesh['sub'=8,'xl'=2,'y'=4,'core'=2] {'sub'}, use_global_device_ids=true, to_apply=%region_1.2 | all-reduce | flops 4 | bytes 32 | tf_op jit(solution)/shard_map/psum | solution.py:203
  (51 shorter events, 10.4 us)
Async XLA Ops:
  7.2 18.2 %copy-start = (s32[64,2]{0,1:T(2,128)S(1)}, s32[64,2]{0,1:T(2,128)}, u32[]{:S(2)}) copy-start(s32[64,2]{0,1:T(2,128)} %param.8) | copy-start | bytes 1540
  7.2 166.0 %all-gather.2.cloned.1.call-start = ((), (), s32[]{:S(2)}) async-start(), calls=%async_computation | async-start | bytes 14155776 | tf_op jit(solution)/shard_map/all_gather | solution.py:157
  7.9 20.5 %copy-start.7 = (f32[16,128,128]{2,1,0:T(8,128)S(1)}, f32[16,128,128]{2,1,0:T(8,128)}, u32[]{:S(2)}) copy-start(f32[16,128,128]{2,1,0:T(8,128)} %param.6) | copy-start | bytes 3145732
  8.9 19.5 %collective-permute-start.3 = (f32[1,128,128]{2,1,0:T(8,128)S(1)}, f32[1,128,128]{2,1,0:T(8,128)S(1)}, u32[]{:S(2)}, u32[]{:S(2)}) collective-permute-start(f32[1,128,128]{2,1,0:T(8,128)S(1)} %get-tuple-element.29), channel_id=1, source_target_pairs={{0,16},{16,32},{32,48},{48,64},{64,80},{80,96},{96,112},{1,17},{17... | collective-permute-start | bytes 196616 | tf_op jit(solution)/shard_map/ppermute | solution.py:95
  12.7 15.6 %collective-permute-start.2 = (f32[1,128,128]{2,1,0:T(8,128)S(1)}, f32[1,128,128]{2,1,0:T(8,128)S(1)}, u32[]{:S(2)}, u32[]{:S(2)}) collective-permute-start(f32[1,128,128]{2,1,0:T(8,128)S(1)} %get-tuple-element.30), channel_id=1, source_target_pairs={{16,0},{32,16},{48,32},{64,48},{80,64},{96,80},{112,96},{17,1},{33... | collective-permute-start | bytes 196616 | tf_op jit(solution)/shard_map/ppermute | solution.py:97
  19.4 14.9 %collective-permute-start.1 = (f32[4,1,128,128]{3,2,1,0:T(8,128)S(1)}, f32[4,1,128,128]{3,2,1,0:T(8,128)S(1)}, u32[]{:S(2)}, u32[]{:S(2)}) collective-permute-start(f32[4,1,128,128]{3,2,1,0:T(8,128)S(1)} %get-tuple-element.18), channel_id=1, source_target_pairs={{16,0},{32,16},{48,32},{64,48},{80,64},{96,80},{112,96},{17,1},{33... | collective-permute-start | bytes 786440 | tf_op jit(solution)/shard_map/ppermute | solution.py:181
  22.6 19.7 %collective-permute-start = (f32[4,1,128,128]{3,2,1,0:T(8,128)S(1)}, f32[4,1,128,128]{3,2,1,0:T(8,128)S(1)}, u32[]{:S(2)}, u32[]{:S(2)}) collective-permute-start(f32[4,1,128,128]{3,2,1,0:T(8,128)S(1)} %get-tuple-element.19), channel_id=1, source_target_pairs={{0,16},{16,32},{32,48},{48,64},{64,80},{80,96},{96,112},{1,17},{17... | collective-permute-start | bytes 786440 | tf_op jit(solution)/shard_map/ppermute | solution.py:180
  34.4 8.0 %copy-start.8 = (f32[4,1,128,128]{3,2,1,0:T(8,128)}, f32[4,1,128,128]{3,2,1,0:T(8,128)S(1)}, u32[]{:S(2)}) copy-start(f32[4,1,128,128]{3,2,1,0:T(8,128)S(1)} %collective-permute-done.1.hi_ref) | copy-start | bytes 786436
  42.3 0.7 copy-start.9
  58.0 4.2 %collective-permute-start.4 = (f32[4,16,8,8,128]{4,3,2,1,0:T(8,128)S(1)}, f32[4,16,8,8,128]{4,3,2,1,0:T(8,128)S(1)}, u32[]{:S(2)}, u32[]{:S(2)}) collective-permute-start(f32[4,16,8,8,128]{4,3,2,1,0:T(8,128)S(1)} %get-tuple-element.17), channel_id=1, source_target_pairs={{0,1},{1,0},{2,3},{3,2},{4,5},{5,4},{6,7},{7,6},{8,9},{9,8},{10,11... | collective-permute-start | bytes 6291464 | tf_op jit(solution)/shard_map/ppermute | solution.py:190
  62.5 53.8 %collective-permute-start.5 = (f32[8,4,64,128]{3,2,1,0:T(8,128)S(1)}, f32[8,4,64,128]{3,2,1,0:T(8,128)S(1)}, u32[]{:S(2)}, u32[]{:S(2)}) collective-permute-start(f32[8,4,64,128]{3,2,1,0:T(8,128)S(1)} %get-tuple-element.14), channel_id=1, source_target_pairs={{0,16},{16,32},{32,48},{48,64},{64,80},{80,96},{96,112},{1,17},{17... | collective-permute-start | bytes 3145736 | tf_op jit(solution)/shard_map/ppermute | solution.py:95
  64.4 53.2 %collective-permute-start.6 = (f32[8,4,64,128]{3,2,1,0:T(8,128)S(1)}, f32[8,4,64,128]{3,2,1,0:T(8,128)S(1)}, u32[]{:S(2)}, u32[]{:S(2)}) collective-permute-start(f32[8,4,64,128]{3,2,1,0:T(8,128)S(1)} %get-tuple-element.15), channel_id=1, source_target_pairs={{16,0},{32,16},{48,32},{64,48},{80,64},{96,80},{112,96},{17,1},{33... | collective-permute-start | bytes 3145736 | tf_op jit(solution)/shard_map/ppermute | solution.py:97
  189.0 4.4 %collective-permute-start.7 = (f32[4,16,8,8,128]{4,3,2,1,0:T(8,128)S(1)}, f32[4,16,8,8,128]{4,3,2,1,0:T(8,128)}, u32[]{:S(2)}, u32[]{:S(2)}) collective-permute-start(f32[4,16,8,8,128]{4,3,2,1,0:T(8,128)S(1)} %slice_bitcast_fusion.2), channel_id=1, source_target_pairs={{0,1},{1,0},{2,3},{3,2},{4,5},{5,4},{6,7},{7,6},{8,9},{9,8},{10,11... | collective-permute-start | bytes 6291464 | tf_op jit(solution)/shard_map/ppermute | solution.py:197
  196.6 2.2 copy-start.4
  200.0 2.0 copy-start.2
  202.0 12.9 %collective-permute-start.9 = (f32[4,1,128,128]{3,2,1,0:T(8,128)S(1)}, f32[4,1,128,128]{3,2,1,0:T(8,128)S(1)}, u32[]{:S(2)}, u32[]{:S(2)}) collective-permute-start(f32[4,1,128,128]{3,2,1,0:T(8,128)S(1)} %get-tuple-element.12), channel_id=1, source_target_pairs={{16,0},{32,16},{48,32},{64,48},{80,64},{96,80},{112,96},{17,1},{33... | collective-permute-start | bytes 786440 | tf_op jit(solution)/shard_map/ppermute | solution.py:181
  209.1 13.6 %collective-permute-start.8 = (f32[4,1,128,128]{3,2,1,0:T(8,128)S(1)}, f32[4,1,128,128]{3,2,1,0:T(8,128)S(1)}, u32[]{:S(2)}, u32[]{:S(2)}) collective-permute-start(f32[4,1,128,128]{3,2,1,0:T(8,128)S(1)} %get-tuple-element.13), channel_id=1, source_target_pairs={{0,16},{16,32},{32,48},{48,64},{64,80},{80,96},{96,112},{1,17},{17... | collective-permute-start | bytes 786440 | tf_op jit(solution)/shard_map/ppermute | solution.py:180
  214.9 7.7 %copy-start.12 = (f32[4,1,128,128]{3,2,1,0:T(8,128)}, f32[4,1,128,128]{3,2,1,0:T(8,128)S(1)}, u32[]{:S(2)}) copy-start(f32[4,1,128,128]{3,2,1,0:T(8,128)S(1)} %collective-permute-done.9.hi_ref) | copy-start | bytes 786436
  222.6 0.7 copy-start.13
  238.3 4.2 %collective-permute-start.10 = (f32[4,16,8,8,128]{4,3,2,1,0:T(8,128)S(1)}, f32[4,16,8,8,128]{4,3,2,1,0:T(8,128)S(1)}, u32[]{:S(2)}, u32[]{:S(2)}) collective-permute-start(f32[4,16,8,8,128]{4,3,2,1,0:T(8,128)S(1)} %get-tuple-element.11), channel_id=1, source_target_pairs={{0,1},{1,0},{2,3},{3,2},{4,5},{5,4},{6,7},{7,6},{8,9},{9,8},{10,11... | collective-permute-start | bytes 6291464 | tf_op jit(solution)/shard_map/ppermute | solution.py:190
  242.8 30.7 %collective-permute-start.11 = (f32[8,4,64,128]{3,2,1,0:T(8,128)S(1)}, f32[8,4,64,128]{3,2,1,0:T(8,128)S(1)}, u32[]{:S(2)}, u32[]{:S(2)}) collective-permute-start(f32[8,4,64,128]{3,2,1,0:T(8,128)S(1)} %get-tuple-element.8), channel_id=1, source_target_pairs={{0,16},{16,32},{32,48},{48,64},{64,80},{80,96},{96,112},{1,17},{17... | collective-permute-start | bytes 3145736 | tf_op jit(solution)/shard_map/ppermute | solution.py:95
  244.7 30.0 %collective-permute-start.12 = (f32[8,4,64,128]{3,2,1,0:T(8,128)S(1)}, f32[8,4,64,128]{3,2,1,0:T(8,128)S(1)}, u32[]{:S(2)}, u32[]{:S(2)}) collective-permute-start(f32[8,4,64,128]{3,2,1,0:T(8,128)S(1)} %get-tuple-element.9), channel_id=1, source_target_pairs={{16,0},{32,16},{48,32},{64,48},{80,64},{96,80},{112,96},{17,1},{33... | collective-permute-start | bytes 3145736 | tf_op jit(solution)/shard_map/ppermute | solution.py:97
  291.9 6.3 %copy-start.6 = (f32[8,16,64,128]{3,2,1,0:T(8,128)S(1)}, f32[8,16,64,128]{3,2,1,0:T(8,128)}, u32[]{:S(2)}) copy-start(f32[8,16,64,128]{3,2,1,0:T(8,128)} %shard_map.71) | copy-start | bytes 12582916
  293.8 4.4 %collective-permute-start.13 = (f32[4,16,8,8,128]{4,3,2,1,0:T(8,128)S(1)}, f32[4,16,8,8,128]{4,3,2,1,0:T(8,128)S(1)}, u32[]{:S(2)}, u32[]{:S(2)}) collective-permute-start(f32[4,16,8,8,128]{4,3,2,1,0:T(8,128)S(1)} %slice_bitcast_fusion), channel_id=1, source_target_pairs={{0,1},{1,0},{2,3},{3,2},{4,5},{5,4},{6,7},{7,6},{8,9},{9,8},{10,11... | collective-permute-start | bytes 6291464 | tf_op jit(solution)/shard_map/ppermute | solution.py:197
  298.8 2.2 copy-start.3
  302.2 2.0 copy-start.5
  304.3 13.9 %collective-permute-start.15 = (f32[4,1,128,128]{3,2,1,0:T(8,128)S(1)}, f32[4,1,128,128]{3,2,1,0:T(8,128)S(1)}, u32[]{:S(2)}, u32[]{:S(2)}) collective-permute-start(f32[4,1,128,128]{3,2,1,0:T(8,128)S(1)} %get-tuple-element.6), channel_id=1, source_target_pairs={{16,0},{32,16},{48,32},{64,48},{80,64},{96,80},{112,96},{17,1},{33... | collective-permute-start | bytes 786440 | tf_op jit(solution)/shard_map/ppermute | solution.py:181
  312.3 13.6 %collective-permute-start.14 = (f32[4,1,128,128]{3,2,1,0:T(8,128)S(1)}, f32[4,1,128,128]{3,2,1,0:T(8,128)S(1)}, u32[]{:S(2)}, u32[]{:S(2)}) collective-permute-start(f32[4,1,128,128]{3,2,1,0:T(8,128)S(1)} %get-tuple-element.7), channel_id=1, source_target_pairs={{0,16},{16,32},{32,48},{48,64},{64,80},{80,96},{96,112},{1,17},{17... | collective-permute-start | bytes 786440 | tf_op jit(solution)/shard_map/ppermute | solution.py:180
  318.1 7.7 %copy-start.10 = (f32[4,1,128,128]{3,2,1,0:T(8,128)}, f32[4,1,128,128]{3,2,1,0:T(8,128)S(1)}, u32[]{:S(2)}) copy-start(f32[4,1,128,128]{3,2,1,0:T(8,128)S(1)} %collective-permute-done.15.hi_ref) | copy-start | bytes 786436
  325.8 0.7 copy-start.11
  326.5 34.5 %copy-start.1 = (s32[64,2]{0,1:T(2,128)S(1)}, s32[64,2]{0,1:T(2,128)}, u32[]{:S(2)}) copy-start(s32[64,2]{0,1:T(2,128)} %param.8) | copy-start | bytes 1540
Sparse Core Ops, SparseCore 0:
  9.6 163.6 all-gather.1

commit v4 on v1

v4 whole, which is shorter than its diff:
```python
import jax
import jax.numpy as jnp
from jax import lax
from jax.sharding import Mesh, PartitionSpec as P
from jax.experimental import pallas as pl
from jax.experimental.pallas import tpu as pltpu

ITERS = 2
INTERPRET = False

CURRENT = 16.0
MASS = 1.0

CHIP_AXES = ("xl", "y")
CORE = "core"
GRP = ("xl", "y", "core")


def make_stencil_kernel(planes, has_rim):
    def kernel(*refs):
        if has_rim:
            v_ref, lo_ref, hi_ref = refs[:3]
            rest = refs[3:]
        else:
            v_ref, lo_ref, hi_ref = refs[0], None, None
            rest = refs[1:]
        st_ref, cc_ref, fxp_ref, fxm_ref, fyp_ref, fym_ref, fzp_ref, fzm_ref, out_ref = rest
        width = v_ref.shape[1]
        ny, nz = v_ref.shape[2], v_ref.shape[3]

        def load(q):
            if q < 0:
                return lo_ref[0, lo_ref.shape[1] + q]
            if q >= width:
                return hi_ref[0, q - width]
            return v_ref[0, q]

        for o, p in enumerate(planes):
            v = load(p)
            image = cc_ref[o] * v
            image = image - fxp_ref[o] * load(p + 1)
            image = image - fxm_ref[o] * load(p - 1)
            image = image - fyp_ref[o] * pltpu.roll(v, ny - 1, 0)
            image = image - fym_ref[o] * pltpu.roll(v, 1, 0)
            image = image - fzp_ref[o] * pltpu.roll(v, nz - 1, 1)
            image = image - fzm_ref[o] * pltpu.roll(v, 1, 1)
            out_ref[0, o] = st_ref[0, o] - image

    return kernel


def stencil_call(planes, v, rims, st, coefs):
    n_src, width, ny, nz = v.shape
    n_out = len(planes)
    own_block = pl.BlockSpec((1, width, ny, nz), lambda s: (s, 0, 0, 0))
    out_block = pl.BlockSpec((1, n_out, ny, nz), lambda s: (s, 0, 0, 0))
    coef_block = pl.BlockSpec((n_out, ny, nz), lambda s: (0, 0, 0))
    rim_specs = [pl.BlockSpec((1, r.shape[1], ny, nz), lambda s: (s, 0, 0, 0)) for r in rims]
    return pl.pallas_call(
        make_stencil_kernel(tuple(planes), len(rims) > 0),
        grid=(n_src,),
        in_specs=[own_block] + rim_specs + [out_block] + [coef_block] * 7,
        out_specs=out_block,
        out_shape=jax.ShapeDtypeStruct((n_src, n_out, ny, nz), jnp.float32),
        interpret=INTERPRET,
    )(v, *rims, st, *coefs)


def make_correction_kernel(columns):
    def kernel(mask_ref, inv_ref, *refs):
        out_ref = refs[-1]
        pieces = refs[:-1]
        n_out = inv_ref.shape[0]
        halves = len(pieces) // 2

        def row(i, carry):
            accs = None
            for j, (piece, plane) in enumerate(columns):
                w = inv_ref[i, j] * mask_ref[j]
                terms = []
                for half in range(2):
                    src_ref = pieces[half * halves + piece]
                    for s in range(src_ref.shape[0]):
                        terms.append(w * src_ref[s, plane])
                accs = terms if accs is None else [a + t for a, t in zip(accs, terms)]
            for s, acc in enumerate(accs):
                out_ref[s, i] = acc
            return carry

        lax.fori_loop(0, n_out, row, 0)

    return kernel


def correction_call(mask, inv, own_pieces, got_pieces, columns, rows=8):
    n_out, n_col, ny, nz = inv.shape
    n_src = sum(p.shape[0] for p in own_pieces[:1]) * 2
    specs = [pl.BlockSpec((p.shape[0], p.shape[1], rows, nz), lambda b: (0, 0, b, 0)) for p in own_pieces + got_pieces]
    return pl.pallas_call(
        make_correction_kernel(tuple(columns)),
        grid=(ny // rows,),
        in_specs=[pl.BlockSpec(memory_space=pltpu.SMEM),
                  pl.BlockSpec((n_out, n_col, rows, nz), lambda b: (0, 0, b, 0))] + specs,
        out_specs=pl.BlockSpec((n_src, n_out, rows, nz), lambda b: (0, 0, b, 0)),
        out_shape=jax.ShapeDtypeStruct((n_src, n_out, ny, nz), jnp.float32),
        interpret=INTERPRET,
    )(mask, inv, *own_pieces, *got_pieces)


def rims_of(cells, depth_x, dim):
    count = lax.axis_size("sub")
    head = lax.slice_in_dim(cells, 0, depth_x, axis=dim)
    tail = lax.slice_in_dim(cells, cells.shape[dim] - depth_x, cells.shape[dim], axis=dim)
    lo = lax.ppermute(tail, "sub", [(i, i + 1) for i in range(count - 1)])
    hi = lax.ppermute(head, "sub", [(i + 1, i) for i in range(count - 1)])
    return lo, hi


def neighbours(padded):
    return [
        padded[..., 2:, 1:-1, 1:-1],
        padded[..., :-2, 1:-1, 1:-1],
        padded[..., 1:-1, 2:, 1:-1],
        padded[..., 1:-1, :-2, 1:-1],
        padded[..., 1:-1, 1:-1, 2:],
        padded[..., 1:-1, 1:-1, :-2],
    ]


def face_terms(conduct_pad):
    center_cells = conduct_pad[1:-1, 1:-1, 1:-1]
    face_coefs = [0.5 * (center_cells + beside_cell) for beside_cell in neighbours(conduct_pad)]
    center_coef = MASS * center_cells
    for face_coef in face_coefs:
        center_coef = center_coef + face_coef
    return (center_coef, face_coefs)


def source_block(pairs, x_start, width_x, rows_y, full_y, depth):
    x_ids = x_start + lax.broadcasted_iota(jnp.int32, (width_x, rows_y, depth), 0)
    y_ids = lax.broadcasted_iota(jnp.int32, (width_x, rows_y, depth), 1)
    z_ids = lax.broadcasted_iota(jnp.int32, (width_x, rows_y, depth), 2)
    flat_ids = (x_ids * full_y + y_ids) * depth + z_ids
    first = (flat_ids[None] == pairs[:, 0][:, None, None, None]).astype(jnp.float32)
    second = (flat_ids[None] == pairs[:, 1][:, None, None, None]).astype(jnp.float32)
    return CURRENT * first - CURRENT * second


def on_device(potential_init, conductivity, inverse_rows, electrodes, intersection_width):
    local_src, width_x, full_y, depth = potential_init.shape
    n_core = lax.axis_size(CORE)
    n_sub = lax.axis_size("sub")
    core = lax.axis_index(CORE)
    grp_index = (lax.axis_index("xl") * lax.axis_size("y") + lax.axis_index("y")) * n_core + core
    sub_index = lax.axis_index("sub")
    extended = inverse_rows.shape[1]
    rows = inverse_rows.shape[2]
    blocks = full_y // (rows * n_core)
    margin = (extended - width_x) // 2
    rim = margin + 1
    cell_count = float(width_x * n_sub * full_y * depth)
    x_start = sub_index * width_x
    column_ids = jnp.arange(extended, dtype=jnp.int32)
    reach = intersection_width[0]
    column_x = x_start - margin + column_ids
    column_mask = (
        (column_ids >= margin - reach)
        & (column_ids < width_x + margin + reach)
        & (column_x >= 0)
        & (column_x < width_x * n_sub)
    ).astype(jnp.float32)
    inverse_mine = lax.all_gather(inverse_rows, CHIP_AXES, axis=2, tiled=True)

    c_lo, c_hi = rims_of(conductivity, rim, 0)
    conduct_pad = jnp.pad(jnp.concatenate([c_lo, conductivity, c_hi], axis=0), ((0, 0), (1, 1), (1, 1)))
    center_coef, face_coefs = face_terms(conduct_pad)
    y_ids = lax.broadcasted_iota(jnp.int32, center_coef.shape, 1)
    z_ids = lax.broadcasted_iota(jnp.int32, center_coef.shape, 2)
    coefs = [
        center_coef,
        face_coefs[0],
        face_coefs[1],
        jnp.where(y_ids == full_y - 1, 0.0, face_coefs[2]),
        jnp.where(y_ids == 0, 0.0, face_coefs[3]),
        jnp.where(z_ids == depth - 1, 0.0, face_coefs[4]),
        jnp.where(z_ids == 0, 0.0, face_coefs[5]),
    ]
    own_pairs = lax.dynamic_slice_in_dim(electrodes, grp_index * local_src, local_src, 0)
    source_term = source_block(own_pairs, x_start - margin, extended, full_y, full_y, depth)

    mid_planes = list(range(1, width_x - 1))
    bnd_planes = list(range(-margin, 1)) + list(range(width_x - 1, width_x + margin))
    own_planes = list(range(width_x))

    def pick(arr, planes, axis):
        return jnp.concatenate([lax.slice_in_dim(arr, p + margin, p + margin + 1, axis=axis) for p in planes], axis=axis)

    def runs(planes):
        return [(p + margin) for p in planes]

    mid_coefs = [c[1 + margin : width_x - 1 + margin] for c in coefs]
    bnd_coefs = [jnp.concatenate([c[: margin + 1], c[width_x - 1 + margin :]], axis=0) for c in coefs]
    own_coefs = [c[margin : margin + width_x] for c in coefs]
    mid_st = source_term[:, 1 + margin : width_x - 1 + margin]
    bnd_st = jnp.concatenate([source_term[:, : margin + 1], source_term[:, width_x - 1 + margin :]], axis=1)
    own_st = source_term[:, margin : margin + width_x]

    columns = []
    for j in range(extended):
        p = j - margin
        if p in mid_planes:
            columns.append((0, mid_planes.index(p)))
        else:
            columns.append((1, bnd_planes.index(p)))

    swap = [(0, 1), (1, 0)]

    def swap_rows(piece):
        split = piece.reshape(local_src, piece.shape[1], blocks, n_core, rows, depth)
        own = lax.dynamic_index_in_dim(split, core, axis=3, keepdims=False).reshape(
            local_src, piece.shape[1], blocks * rows, depth)
        other = lax.dynamic_index_in_dim(split, 1 - core, axis=3, keepdims=False).reshape(
            local_src, piece.shape[1], blocks * rows, depth)
        return own, lax.ppermute(other, CORE, swap)

    potential = potential_init
    for sweep in range(ITERS):
        lo, hi = rims_of(potential, rim, 1)
        mid = stencil_call(mid_planes, potential, [], mid_st, mid_coefs)
        mid_own, mid_got = swap_rows(mid)
        bnd = stencil_call(bnd_planes, potential, [lo, hi], bnd_st, bnd_coefs)
        bnd_own, bnd_got = swap_rows(bnd)
        correction = correction_call(
            column_mask, inverse_mine, [mid_own, bnd_own], [mid_got, bnd_got], columns
        ).reshape(2 * local_src, width_x, blocks, rows, depth)
        mine = correction[:local_src]
        back = lax.ppermute(correction[local_src:], CORE, swap)
        first = jnp.where(core == 0, mine, back)
        second = jnp.where(core == 0, back, mine)
        update = jnp.stack([first, second], axis=3).reshape(potential.shape)
        potential = potential + update
    lo, hi = rims_of(potential, 1, 1)
    residual = stencil_call(own_planes, potential, [lo, hi], own_st, own_coefs)
    totals = lax.psum(jnp.sum(residual * residual, axis=(1, 2, 3)), "sub")
    residual_norms = jnp.sqrt(totals / cell_count)
    return (potential, residual_norms)


def solution(mesh):
    n_sub, n_grp = mesh.devices.shape
    n_core = 2
    n_y = 4
    view = Mesh(
        mesh.devices.reshape(n_sub, n_grp // (n_y * n_core), n_y, n_core),
        ("sub", "xl", "y", "core"),
    )
    in_specs = (
        P(GRP, "sub", None, None),
        P("sub", None, None),
        P("sub", None, GRP, None),
        P(),
        P("sub"),
    )
    out_specs = (P(GRP, "sub", None, None), P(GRP))
    return jax.shard_map(
        on_device, mesh=view, in_specs=in_specs, out_specs=out_specs, check_vma=False
    )
```

time: 745 us -> 354 us (0.48); the launches traced: 735 us -> 353 us
  matrix products: 226 us -> 0 us
  local copies, waits for them, and re-layouts: 193 us -> 62.3 us
  other arithmetic: 106 us -> 21.9 us
  Pallas kernels: 0 us -> 71.1 us
  starting transfers between devices: 58.4 us -> 35.5 us
  waiting for transfers between devices: 111 us -> 124 us
    dot_general x2 -> x0, matrix products: 226 us -> none  [on_device(): jnp.einsum('ijyz,sjyz->siyz', inverse_mine, extended_resid, precision=lax...]
    pallas_call x0 -> x7, Pallas kernels: none -> 71.1 us  [the longest x5 42.4 us: stencil_call(): pl.pallas_call(make_stencil_kernel(tuple(planes), len(rims) > 0), grid=(n...]
    slice x8 -> x25, local copies, waits for them, and re-layouts: 93.6 us -> 31.7 us  [the longest x7 8 us: on_device(): mid_coefs = [c[1 + margin:width_x - 1 + margin] for c in coefs]]
    all_gather x1, waiting for transfers between devices: 18.3 us -> 75.7 us  [on_device(): inverse_mine = lax.all_gather(inverse_rows, CHIP_AXES, axis=2, tiled=True)]
    ppermute x14 -> x12, waiting for transfers between devices: 92.8 us -> 39.5 us  [the longest x4 18.9 us: rims_of(): hi = lax.ppermute(head, 'sub', [(i + 1, i) for i in range(count - 1)])]
    sub x2 -> x1, other arithmetic: 40.7 us -> 1.08 us  [source_block(): return CURRENT * first - CURRENT * second]
    all_gather x1 -> x0, local copies, waits for them, and re-layouts: 33.5 us -> none  [on_device(): inverse_mine = lax.all_gather(inverse_rows, CHIP_AXES, axis=2, tiled=True)]
    mul x2 -> x0, local copies, waits for them, and re-layouts: 30.9 us -> none  [on_device(): extended_2(cells, (('sub', 1),), margin) * intersection_mask]
  transfers between devices with their start and end apart: 17 -> 15, of which waited for: 13 -> 10; matrix products, arithmetic and copies ran while one was open for 11% -> 17% of each run, Pallas kernels for 0% -> 9%
where the time goes in v4:
time: 354 us; the launch traced here: 353 us
  waiting for transfers between devices  124 us (35%)
  Pallas kernels  71.1 us (20%)
  local copies, waits for them, and re-layouts  62.3 us (18%)
  starting transfers between devices  35.5 us (10%)
  blocking collectives  22.6 us (6%)
  other arithmetic  21.9 us (6%)
  between operations  15.1 us (4%)
    all_gather x1, waiting for transfers between devices, on_device(): inverse_mine = lax.all_gather(inverse_rows, CHIP_AXES, axis=2, tiled=True)  75.7 us
    pallas_call x5, Pallas kernels, stencil_call(): pl.pallas_call(make_stencil_kernel(tuple(planes), len(rims) > 0), grid=(n...  42.4 us
    pallas_call x2, Pallas kernels, correction_call(): pl.pallas_call(make_correction_kernel(tuple(columns)), grid=(ny // rows,)...  28.7 us
    ppermute x4, starting transfers between devices, rims_of(): hi = lax.ppermute(head, 'sub', [(i + 1, i) for i in range(count - 1)])  25.4 us
    psum x1, blocking collectives, on_device(): totals = lax.psum(jnp.sum(residual * residual, axis=(1, 2, 3)), 'sub')  22.6 us
    ppermute x4, waiting for transfers between devices, rims_of(): hi = lax.ppermute(head, 'sub', [(i + 1, i) for i in range(count - 1)])  18.9 us
    ppermute x4, waiting for transfers between devices, rims_of(): lo = lax.ppermute(tail, 'sub', [(i, i + 1) for i in range(count - 1)])  15.4 us
    reshape x4, local copies, waits for them, and re-layouts, swap_rows(): lax.dynamic_index_in_dim(split, 1 - core, axis=3, keepdims=False)  14.7 us
  transfers between devices with their start and end apart: 15, of which 10 were waited for; matrix products, arithmetic and copies ran while one was open for 17% of the time, Pallas kernels for 9%

profile of v4, /device:TPU:6, one launch (start us, length us, event | category | flops | bytes accessed | tf_op | source)
XLA Modules:
  0.0 352.9 jit_solution(14308055955864954967)
XLA Ops:
  8.5 6.8 %collective-permute-start.1 = (f32[5,128,128]{2,1,0:T(8,128)S(1)}, f32[5,128,128]{2,1,0:T(8,128)}, u32[]{:S(2)}, u32[]{:S(2)}) collective-permute-start(f32[5,128,128]{2,1,0:T(8,128)S(1)} %get-tuple-element.48), channel_id=1, source_target_pairs={{16,0},{32,16},{48,32},{64,48},{80,64},{96,80},{112,96},{17,1},{33... | collective-permute-start | bytes 983048 | tf_op jit(solution)/shard_map/ppermute | solution.py:115
  15.3 1.9 collective-permute-start
  17.2 3.6 %fusion.16 = (f32[4,5,128,128]{3,2,1,0:T(8,128)}, f32[4,5,128,128]{3,2,1,0:T(8,128)}) fusion(f32[4,16,128,128]{3,2,1,0:T(8,128)} %refs_0_.3), kind=kLoop, calls=%fused_computation.67 | loop fusion | bytes 5242880 | tf_op jit(solution)/shard_map/slice | solution.py:112
  20.8 7.5 %collective-permute-start.3 = (f32[4,5,128,128]{3,2,1,0:T(8,128)}, f32[4,5,128,128]{3,2,1,0:T(8,128)}, u32[]{:S(2)}, u32[]{:S(2)}) collective-permute-start(f32[4,5,128,128]{3,2,1,0:T(8,128)} %get-tuple-element.15), channel_id=1, source_target_pairs={{16,0},{32,16},{48,32},{64,48},{80,64},{96,80},{112,96},{17,1},{33... | collective-permute-start | bytes 3932168 | tf_op jit(solution)/shard_map/ppermute | solution.py:115
  28.3 1.9 collective-permute-start.2
  31.7 2.6 copy-done.5
  34.7 4.3 %slice.231.refs_1_ = f32[4,14,128,128]{3,2,1,0:T(8,128)} slice(f32[4,24,128,128]{3,2,1,0:T(8,128)} %copy-done.5), slice={[0:4], [5:19], [0:128], [0:128]} | slice | bytes 7340032 | tf_op jit(solution)/shard_map/slice | solution.py:204
  38.9 1.8 pad_maximum_fusion.2.refs_3_
  42.8 2.4 broadcast_select_fusion
  46.4 1.5 slice.239.refs_6_
  47.9 1.2 slice.238.refs_5_
  53.3 8.7 %shard_map.68 = f32[4,14,128,128]{3,2,1,0:T(8,128)} custom-call(f32[4,16,128,128]{3,2,1,0:T(8,128)} %refs_0_.3, f32[4,14,128,128]{3,2,1,0:T(8,128)} %slice.231.refs_1_, f32[14,128,128]{2,1,0:T(8,128)} %slice.235.refs_2_, f32[14,128,128]{2,1,0:T(8,128)} %slice.236.refs_3_, f32[14,128,128]{2,1,0:T(8,128)} %slice.237.refs_4_, f32[14,128,128]{2,1,0:T(8,128)} %slice.238.refs_5_, ...), custom_call_target="tpu_custom_call" | custom-call | tf_op jit(solution)/shard_map/pallas_call | solution.py:59
  62.0 4.3 %dynamic-slice_bitcast_fusion.2 = (f32[4,14,64,128]{3,2,1,0:T(8,128)}, f32[4,14,64,128]{3,2,1,0:T(8,128)}) fusion(f32[4,14,8,2,8,128]{5,4,3,2,1,0:T(8,128)} %bitcast.75, s32[]{:T(128)S(6)} %select_n.57, s32[]{:T(128)S(6)} %select_n.56), kind=kLoop, calls=%fused_computation.21 | loop fusion | bytes 7340040 | tf_op jit(solution)/shard_map/reshape | solution.py:222
  68.3 1.4 fusion.17
  72.5 1.4 fusion.21
  76.5 5.1 %collective-permute-done.3.refs_2_ = f32[4,5,128,128]{3,2,1,0:T(8,128)} collective-permute-done((f32[4,5,128,128]{3,2,1,0:T(8,128)}, f32[4,5,128,128]{3,2,1,0:T(8,128)}, u32[]{:S(2)}, u32[]{:S(2)}) %collective-permute-start.3) | collective-permute-done | bytes 1310752 | tf_op jit(solution)/shard_map/ppermute | solution.py:115
  81.6 7.4 %collective-permute-done.2.refs_1_ = f32[4,5,128,128]{3,2,1,0:T(8,128)} collective-permute-done((f32[4,5,128,128]{3,2,1,0:T(8,128)}, f32[4,5,128,128]{3,2,1,0:T(8,128)}, u32[]{:S(2)}, u32[]{:S(2)}) %collective-permute-start.2) | collective-permute-done | bytes 1310752 | tf_op jit(solution)/shard_map/ppermute | solution.py:114
  89.0 8.0 %shard_map.69 = f32[4,10,128,128]{3,2,1,0:T(8,128)} custom-call(f32[4,16,128,128]{3,2,1,0:T(8,128)} %refs_0_.3, f32[4,5,128,128]{3,2,1,0:T(8,128)} %collective-permute-done.2.refs_1_, f32[4,5,128,128]{3,2,1,0:T(8,128)} %collective-permute-done.3.refs_2_, f32[4,10,128,128]{3,2,1,0:T(8,128)} %pad_maximum_fusion.2.refs_3_, ...), custom_call_target="tpu_custom_call" | custom-call | tf_op jit(solution)/shard_map/pallas_call | solution.py:59
  97.0 3.0 dynamic-slice_bitcast_fusion.6
  101.2 2.0 collective-permute-done.5.refs_3_
  103.2 75.7 %all-gather.2.cloned.1.call-done.inv_ref = f32[16,24,64,128]{3,2,1,0:T(8,128)} async-done(((f32[16,24,8,128]{3,2,1,0:T(8,128)}), f32[16,24,64,128]{3,2,1,0:T(8,128)}) %all-gather.2.cloned.1.call-update) | async-done | bytes 12582928 | tf_op jit(solution)/shard_map/all_gather | solution.py:172
  178.9 14.3 %shard_map.70 = f32[8,16,64,128]{3,2,1,0:T(8,128)} custom-call(f32[24]{0:T(128)} %and_convert_fusion.mask_ref, f32[16,24,64,128]{3,2,1,0:T(8,128)} %all-gather.2.cloned.1.call-done.inv_ref, f32[4,14,64,128]{3,2,1,0:T(8,128)} %get-tuple-element.20.refs_0_, f32[4,10,64,128]{3,2,1,0:T(8,128)} %get-tuple-element.24.refs_1_, ...), custom_call_target="tpu_custom_call" | custom-call | tf_op jit(solution)/shard_map/pallas_call | solution.py:99
  193.2 3.2 slice_bitcast_fusion.2
  196.4 4.5 %collective-permute-done.6 = f32[4,16,8,8,128]{4,3,2,1,0:T(8,128)} collective-permute-done((f32[4,16,8,8,128]{4,3,2,1,0:T(8,128)}, f32[4,16,8,8,128]{4,3,2,1,0:T(8,128)}, u32[]{:S(2)}, u32[]{:S(2)}) %collective-permute-start.6) | collective-permute-done | bytes 2097184 | tf_op jit(solution)/shard_map/ppermute | solution.py:237
  200.9 2.7 select_bitcast_fusion.3
  204.6 1.8 copy-done.4
  206.4 1.2 bitcast_add_fusion.1.refs_0_
  207.6 1.8 fusion.15
  210.4 9.2 %collective-permute-start.8 = (f32[4,5,128,128]{3,2,1,0:T(8,128)}, f32[4,5,128,128]{3,2,1,0:T(8,128)}, u32[]{:S(2)}, u32[]{:S(2)}) collective-permute-start(f32[4,5,128,128]{3,2,1,0:T(8,128)} %get-tuple-element.13), channel_id=1, source_target_pairs={{16,0},{32,16},{48,32},{64,48},{80,64},{96,80},{112,96},{17,1},{33... | collective-permute-start | bytes 3932168 | tf_op jit(solution)/shard_map/ppermute | solution.py:115
  219.5 1.9 collective-permute-start.7
  221.5 8.5 %shard_map.71 = f32[4,14,128,128]{3,2,1,0:T(8,128)} custom-call(f32[4,16,128,128]{3,2,1,0:T(8,128)} %copy-done.2, f32[4,14,128,128]{3,2,1,0:T(8,128)} %slice.231.refs_1_, f32[14,128,128]{2,1,0:T(8,128)} %slice.235.refs_2_, f32[14,128,128]{2,1,0:T(8,128)} %slice.236.refs_3_, f32[14,128,128]{2,1,0:T(8,128)} %slice.237.refs_4_, ...), custom_call_target="tpu_custom_call" | custom-call | tf_op jit(solution)/shard_map/pallas_call | solution.py:59
  230.0 4.3 %dynamic-slice_bitcast_fusion = (f32[4,14,64,128]{3,2,1,0:T(8,128)}, f32[4,14,64,128]{3,2,1,0:T(8,128)}) fusion(f32[4,14,8,2,8,128]{5,4,3,2,1,0:T(8,128)} %bitcast.74, s32[]{:T(128)S(6)} %select_n.57, s32[]{:T(128)S(6)} %select_n.56), kind=kLoop, calls=%fused_computation.19 | loop fusion | bytes 7340040 | tf_op jit(solution)/shard_map/reshape | solution.py:222
  234.3 13.9 %collective-permute-done.8.refs_2_ = f32[4,5,128,128]{3,2,1,0:T(8,128)} collective-permute-done((f32[4,5,128,128]{3,2,1,0:T(8,128)}, f32[4,5,128,128]{3,2,1,0:T(8,128)}, u32[]{:S(2)}, u32[]{:S(2)}) %collective-permute-start.8) | collective-permute-done | bytes 1310752 | tf_op jit(solution)/shard_map/ppermute | solution.py:115
  248.2 7.7 %collective-permute-done.7.refs_1_ = f32[4,5,128,128]{3,2,1,0:T(8,128)} collective-permute-done((f32[4,5,128,128]{3,2,1,0:T(8,128)}, f32[4,5,128,128]{3,2,1,0:T(8,128)}, u32[]{:S(2)}, u32[]{:S(2)}) %collective-permute-start.7) | collective-permute-done | bytes 1310752 | tf_op jit(solution)/shard_map/ppermute | solution.py:114
  255.9 7.7 %shard_map.72 = f32[4,10,128,128]{3,2,1,0:T(8,128)} custom-call(f32[4,16,128,128]{3,2,1,0:T(8,128)} %copy-done.2, f32[4,5,128,128]{3,2,1,0:T(8,128)} %collective-permute-done.7.refs_1_, f32[4,5,128,128]{3,2,1,0:T(8,128)} %collective-permute-done.8.refs_2_, f32[4,10,128,128]{3,2,1,0:T(8,128)} %pad_maximum_fusion.2.refs_3_, ...), custom_call_target="tpu_custom_call" | custom-call | tf_op jit(solution)/shard_map/pallas_call | solution.py:59
  263.6 3.0 dynamic-slice_bitcast_fusion.4
  266.7 3.2 collective-permute-done.10.refs_3_
  269.8 14.4 %shard_map.73 = f32[8,16,64,128]{3,2,1,0:T(8,128)} custom-call(f32[24]{0:T(128)} %and_convert_fusion.mask_ref, f32[16,24,64,128]{3,2,1,0:T(8,128)} %all-gather.2.cloned.1.call-done.inv_ref, f32[4,14,64,128]{3,2,1,0:T(8,128)} %get-tuple-element.18.refs_0_, f32[4,10,64,128]{3,2,1,0:T(8,128)} %get-tuple-element.22.refs_1_, ...), custom_call_target="tpu_custom_call" | custom-call | tf_op jit(solution)/shard_map/pallas_call | solution.py:99
  284.2 1.9 slice_bitcast_fusion
  286.3 4.0 %collective-permute-done.11 = f32[4,16,8,8,128]{4,3,2,1,0:T(8,128)S(1)} collective-permute-done((f32[4,16,8,8,128]{4,3,2,1,0:T(8,128)S(1)}, f32[4,16,8,8,128]{4,3,2,1,0:T(8,128)S(1)}, u32[]{:S(2)}, u32[]{:S(2)}) %collective-permute-start.11) | collective-permute-done | bytes 2097184 | tf_op jit(solution)/shard_map/ppermute | solution.py:237
  291.3 1.9 copy-done.3
  293.2 1.2 bitcast_add_fusion.refs_0_
  294.4 1.9 collective-permute-start.13
  296.3 4.1 %collective-permute-start.12 = (f32[4,1,128,128]{3,2,1,0:T(8,128)S(1)}, f32[4,1,128,128]{3,2,1,0:T(8,128)}, u32[]{:S(2)}, u32[]{:S(2)}) collective-permute-start(f32[4,1,128,128]{3,2,1,0:T(8,128)S(1)} %get-tuple-element.12), channel_id=1, source_target_pairs={{0,16},{16,32},{32,48},{48,64},{64,80},{80,96},{96,112},{1,17},{17... | collective-permute-start | bytes 786440 | tf_op jit(solution)/shard_map/ppermute | solution.py:114
  300.4 2.2 slice.266.refs_3_
  310.9 9.5 %shard_map.74 = f32[4,16,128,128]{3,2,1,0:T(8,128)} custom-call(f32[4,16,128,128]{3,2,1,0:T(8,128)} %copy-done.6, f32[4,1,128,128]{3,2,1,0:T(8,128)} %collective-permute-done.12.refs_1_, f32[4,1,128,128]{3,2,1,0:T(8,128)} %copy-done.20, f32[4,16,128,128]{3,2,1,0:T(8,128)} %slice.266.refs_3_, f32[16,128,128]{2,1,0:T(8,128)} %slice.267.refs_4_, ...), custom_call_target="tpu_custom_call" | custom-call | tf_op jit(solution)/shard_map/pallas_call | solution.py:59
  320.4 2.6 multiply_reduce_fusion
  323.0 22.6 %psum.7 = f32[4]{0:T(128)S(1)} all-reduce(f32[4]{0:T(128)S(1)} %multiply_reduce_fusion), channel_id=1, replica_groups=mesh['sub'=8,'xl'=2,'y'=4,'core'=2] {'sub'}, use_global_device_ids=true, to_apply=%region_1.2 | all-reduce | flops 4 | bytes 32 | tf_op jit(solution)/shard_map/psum | solution.py:244
  (98 shorter events, 30.2 us)
Async XLA Ops:
  7.2 23.1 %copy-start = (s32[64,2]{0,1:T(2,128)S(1)}, s32[64,2]{0,1:T(2,128)}, u32[]{:S(2)}) copy-start(s32[64,2]{0,1:T(2,128)} %param.8) | copy-start | bytes 1540
  7.2 1.2 copy-start.18
  7.2 171.7 %all-gather.2.cloned.1.call-start = ((), (), s32[]{:S(2)}) async-start(), calls=%async_computation | async-start | bytes 14155776 | tf_op jit(solution)/shard_map/all_gather | solution.py:172
  8.5 33.3 %collective-permute-start.1 = (f32[5,128,128]{2,1,0:T(8,128)S(1)}, f32[5,128,128]{2,1,0:T(8,128)}, u32[]{:S(2)}, u32[]{:S(2)}) collective-permute-start(f32[5,128,128]{2,1,0:T(8,128)S(1)} %get-tuple-element.48), channel_id=1, source_target_pairs={{16,0},{32,16},{48,32},{64,48},{80,64},{96,80},{112,96},{17,1},{33... | collective-permute-start | bytes 983048 | tf_op jit(solution)/shard_map/ppermute | solution.py:115
  15.3 25.4 %collective-permute-start = (f32[5,128,128]{2,1,0:T(8,128)S(1)}, f32[5,128,128]{2,1,0:T(8,128)}, u32[]{:S(2)}, u32[]{:S(2)}) collective-permute-start(f32[5,128,128]{2,1,0:T(8,128)S(1)} %get-tuple-element.49), channel_id=1, source_target_pairs={{0,16},{16,32},{32,48},{48,64},{64,80},{80,96},{96,112},{1,17},{17... | collective-permute-start | bytes 983048 | tf_op jit(solution)/shard_map/ppermute | solution.py:114
  20.8 60.8 %collective-permute-start.3 = (f32[4,5,128,128]{3,2,1,0:T(8,128)}, f32[4,5,128,128]{3,2,1,0:T(8,128)}, u32[]{:S(2)}, u32[]{:S(2)}) collective-permute-start(f32[4,5,128,128]{3,2,1,0:T(8,128)} %get-tuple-element.15), channel_id=1, source_target_pairs={{16,0},{32,16},{48,32},{64,48},{80,64},{96,80},{112,96},{17,1},{33... | collective-permute-start | bytes 3932168 | tf_op jit(solution)/shard_map/ppermute | solution.py:115
  28.3 60.7 %collective-permute-start.2 = (f32[4,5,128,128]{3,2,1,0:T(8,128)}, f32[4,5,128,128]{3,2,1,0:T(8,128)}, u32[]{:S(2)}, u32[]{:S(2)}) collective-permute-start(f32[4,5,128,128]{3,2,1,0:T(8,128)} %get-tuple-element.16), channel_id=1, source_target_pairs={{0,16},{16,32},{32,48},{48,64},{64,80},{80,96},{96,112},{1,17},{17... | collective-permute-start | bytes 3932168 | tf_op jit(solution)/shard_map/ppermute | solution.py:114
  31.7 2.6 copy-start.5
  38.9 2.8 copy-start.19
  45.2 2.7 copy-start.10
  45.2 3.9 %copy-start.8 = (f32[24,128,128]{2,1,0:T(8,128)}, f32[24,128,128]{2,1,0:T(8,128)S(1)}, u32[]{:S(2)}) copy-start(f32[24,128,128]{2,1,0:T(8,128)S(1)} %get-tuple-element.30) | copy-start | bytes 4718596
  45.2 6.0 %copy-start.14 = (f32[24,128,128]{2,1,0:T(8,128)}, f32[24,128,128]{2,1,0:T(8,128)S(1)}, u32[]{:S(2)}) copy-start(f32[24,128,128]{2,1,0:T(8,128)S(1)} %get-tuple-element.32) | copy-start | bytes 4718596
  45.2 7.0 %copy-start.16 = (f32[24,128,128]{2,1,0:T(8,128)}, f32[24,128,128]{2,1,0:T(8,128)S(1)}, u32[]{:S(2)}) copy-start(f32[24,128,128]{2,1,0:T(8,128)S(1)} %get-tuple-element.31) | copy-start | bytes 4718596
  45.3 7.0 %copy-start.12 = (f32[24,128,128]{2,1,0:T(8,128)}, f32[24,128,128]{2,1,0:T(8,128)S(1)}, u32[]{:S(2)}) copy-start(f32[24,128,128]{2,1,0:T(8,128)S(1)} %get-tuple-element.33) | copy-start | bytes 4718596
  66.3 34.9 %collective-permute-start.4 = (f32[4,14,64,128]{3,2,1,0:T(8,128)}, f32[4,14,64,128]{3,2,1,0:T(8,128)}, u32[]{:S(2)}, u32[]{:S(2)}) collective-permute-start(f32[4,14,64,128]{3,2,1,0:T(8,128)} %get-tuple-element.19), channel_id=1, source_target_pairs={{0,1},{1,0},{2,3},{3,2},{4,5},{5,4},{6,7},{7,6},{8,9},{9,8},{10,11... | collective-permute-start | bytes 5505032 | tf_op jit(solution)/shard_map/ppermute | solution.py:224
  100.0 3.2 collective-permute-start.5
  196.4 4.5 %collective-permute-start.6 = (f32[4,16,8,8,128]{4,3,2,1,0:T(8,128)}, f32[4,16,8,8,128]{4,3,2,1,0:T(8,128)}, u32[]{:S(2)}, u32[]{:S(2)}) collective-permute-start(f32[4,16,8,8,128]{4,3,2,1,0:T(8,128)} %slice_bitcast_fusion.2), channel_id=1, source_target_pairs={{0,1},{1,0},{2,3},{3,2},{4,5},{5,4},{6,7},{7,6},{8,9},{9,8},{10,11... | collective-permute-start | bytes 6291464 | tf_op jit(solution)/shard_map/ppermute | solution.py:237
  204.2 2.2 copy-start.4
  207.6 2.8 copy-start.2
  210.4 37.8 %collective-permute-start.8 = (f32[4,5,128,128]{3,2,1,0:T(8,128)}, f32[4,5,128,128]{3,2,1,0:T(8,128)}, u32[]{:S(2)}, u32[]{:S(2)}) collective-permute-start(f32[4,5,128,128]{3,2,1,0:T(8,128)} %get-tuple-element.13), channel_id=1, source_target_pairs={{16,0},{32,16},{48,32},{64,48},{80,64},{96,80},{112,96},{17,1},{33... | collective-permute-start | bytes 3932168 | tf_op jit(solution)/shard_map/ppermute | solution.py:115
  219.5 36.4 %collective-permute-start.7 = (f32[4,5,128,128]{3,2,1,0:T(8,128)}, f32[4,5,128,128]{3,2,1,0:T(8,128)}, u32[]{:S(2)}, u32[]{:S(2)}) collective-permute-start(f32[4,5,128,128]{3,2,1,0:T(8,128)} %get-tuple-element.14), channel_id=1, source_target_pairs={{0,16},{16,32},{32,48},{48,64},{64,80},{80,96},{96,112},{1,17},{17... | collective-permute-start | bytes 3932168 | tf_op jit(solution)/shard_map/ppermute | solution.py:114
  234.3 32.4 %collective-permute-start.9 = (f32[4,14,64,128]{3,2,1,0:T(8,128)}, f32[4,14,64,128]{3,2,1,0:T(8,128)}, u32[]{:S(2)}, u32[]{:S(2)}) collective-permute-start(f32[4,14,64,128]{3,2,1,0:T(8,128)} %get-tuple-element.17), channel_id=1, source_target_pairs={{0,1},{1,0},{2,3},{3,2},{4,5},{5,4},{6,7},{7,6},{8,9},{9,8},{10,11... | collective-permute-start | bytes 5505032 | tf_op jit(solution)/shard_map/ppermute | solution.py:224
  266.7 3.2 collective-permute-start.10
  284.2 6.1 %copy-start.7 = (f32[8,16,64,128]{3,2,1,0:T(8,128)S(1)}, f32[8,16,64,128]{3,2,1,0:T(8,128)}, u32[]{:S(2)}) copy-start(f32[8,16,64,128]{3,2,1,0:T(8,128)} %shard_map.73) | copy-start | bytes 12582916
  286.1 4.2 %collective-permute-start.11 = (f32[4,16,8,8,128]{4,3,2,1,0:T(8,128)S(1)}, f32[4,16,8,8,128]{4,3,2,1,0:T(8,128)S(1)}, u32[]{:S(2)}, u32[]{:S(2)}) collective-permute-start(f32[4,16,8,8,128]{4,3,2,1,0:T(8,128)S(1)} %slice_bitcast_fusion), channel_id=1, source_target_pairs={{0,1},{1,0},{2,3},{3,2},{4,5},{5,4},{6,7},{7,6},{8,9},{9,8},{10,11... | collective-permute-start | bytes 6291464 | tf_op jit(solution)/shard_map/ppermute | solution.py:237
  291.0 2.2 copy-start.3
  291.0 9.4 %slice-start = ((s8[6291456]{0:T(1024)(128)(4,1)}), s8[4194304]{0:T(1024)(128)(4,1)S(1)}, s32[]{:S(2)}) async-start(s8[6291456]{0:T(1024)(128)(4,1)} %bitcast.72), calls=%async_computation.1 | async-start | bytes 8388608
  293.2 7.3 %slice-start.1 = ((s8[6291456]{0:T(1024)(128)(4,1)}), s8[2097152]{0:T(1024)(128)(4,1)S(1)}, s32[]{:S(2)}) async-start(s8[6291456]{0:T(1024)(128)(4,1)} %bitcast.72), calls=%async_computation.2 | async-start | bytes 4194304
  294.4 8.3 %copy-start.6 = (f32[4,16,128,128]{3,2,1,0:T(8,128)}, f32[4,16,128,128]{3,2,1,0:T(8,128)S(1)}, u32[]{:S(2)}) copy-start(f32[4,16,128,128]{3,2,1,0:T(8,128)S(1)} %bitcast_add_fusion.refs_0_) | copy-start | bytes 12582916
  294.4 15.8 %collective-permute-start.13 = (f32[4,1,128,128]{3,2,1,0:T(8,128)S(1)}, f32[4,1,128,128]{3,2,1,0:T(8,128)S(1)}, u32[]{:S(2)}, u32[]{:S(2)}) collective-permute-start(f32[4,1,128,128]{3,2,1,0:T(8,128)S(1)} %get-tuple-element.11), channel_id=1, source_target_pairs={{16,0},{32,16},{48,32},{64,48},{80,64},{96,80},{112,96},{17,1},{33... | collective-permute-start | bytes 786440 | tf_op jit(solution)/shard_map/ppermute | solution.py:115
  296.3 6.3 %copy-start.17 = (f32[24,128,128]{2,1,0:T(8,128)S(1)}, f32[24,128,128]{2,1,0:T(8,128)}, u32[]{:S(2)}) copy-start(f32[24,128,128]{2,1,0:T(8,128)} %copy-done.16) | copy-start | bytes 4718596
  296.3 14.1 %collective-permute-start.12 = (f32[4,1,128,128]{3,2,1,0:T(8,128)S(1)}, f32[4,1,128,128]{3,2,1,0:T(8,128)}, u32[]{:S(2)}, u32[]{:S(2)}) collective-permute-start(f32[4,1,128,128]{3,2,1,0:T(8,128)S(1)} %get-tuple-element.12), channel_id=1, source_target_pairs={{0,16},{16,32},{32,48},{48,64},{64,80},{80,96},{96,112},{1,17},{17... | collective-permute-start | bytes 786440 | tf_op jit(solution)/shard_map/ppermute | solution.py:114
  300.4 3.3 copy-start.11
  302.7 2.1 copy-start.9
  305.9 2.1 copy-start.15
  307.0 2.1 copy-start.13
  310.2 0.7 copy-start.20
  310.9 35.2 %copy-start.1 = (s32[64,2]{0,1:T(2,128)S(1)}, s32[64,2]{0,1:T(2,128)}, u32[]{:S(2)}) copy-start(s32[64,2]{0,1:T(2,128)} %param.8) | copy-start | bytes 1540
Sparse Core Ops, SparseCore 0:
  9.6 169.2 all-gather.1

commit v5 on v4

--- a/solution.py
+++ b/solution.py
@@ -16,17 +16,16 @@
 GRP = ("xl", "y", "core")
 
 
-def make_stencil_kernel(planes, has_rim):
-    def kernel(*refs):
-        if has_rim:
-            v_ref, lo_ref, hi_ref = refs[:3]
-            rest = refs[3:]
-        else:
-            v_ref, lo_ref, hi_ref = refs[0], None, None
-            rest = refs[1:]
-        st_ref, cc_ref, fxp_ref, fxm_ref, fyp_ref, fym_ref, fzp_ref, fzm_ref, out_ref = rest
+def make_stencil_kernel(planes, has_rim, mode):
+    def kernel(core_ref, *refs):
+        n_in = 3 if has_rim else 1
+        v_ref = refs[0]
+        lo_ref, hi_ref = (refs[1], refs[2]) if has_rim else (None, None)
+        st_ref, cc_ref, fxp_ref, fxm_ref, fyp_ref, fym_ref, fzp_ref, fzm_ref = refs[n_in : n_in + 8]
+        outs = refs[n_in + 8 :]
         width = v_ref.shape[1]
         ny, nz = v_ref.shape[2], v_ref.shape[3]
+        core = core_ref[0]
 
         def load(q):
             if q < 0:
@@ -35,6 +34,7 @@
                 return hi_ref[0, q - width]
             return v_ref[0, q]
 
+        total = None
         for o, p in enumerate(planes):
             v = load(p)
             image = cc_ref[o] * v
@@ -44,26 +44,46 @@
             image = image - fym_ref[o] * pltpu.roll(v, 1, 0)
             image = image - fzp_ref[o] * pltpu.roll(v, nz - 1, 1)
             image = image - fzm_ref[o] * pltpu.roll(v, 1, 1)
-            out_ref[0, o] = st_ref[0, o] - image
+            resid = st_ref[0, o] - image
+            if mode == "norm":
+                square = resid * resid
+                total = square if total is None else total + square
+                continue
+            own_ref, other_ref = outs
+            tile = 8
+            for g in range(ny // (2 * tile)):
+                first = resid[2 * g * tile : (2 * g + 1) * tile]
+                second = resid[(2 * g + 1) * tile : (2 * g + 2) * tile]
+                own_ref[0, o, g * tile : (g + 1) * tile] = jnp.where(core == 0, first, second)
+                other_ref[0, o, g * tile : (g + 1) * tile] = jnp.where(core == 0, second, first)
+        if mode == "norm":
+            outs[0][0] = total.reshape(ny // 8, 8, nz).sum(axis=0)
 
     return kernel
 
 
-def stencil_call(planes, v, rims, st, coefs):
+def stencil_call(planes, core, v, rims, st, coefs, mode):
     n_src, width, ny, nz = v.shape
     n_out = len(planes)
     own_block = pl.BlockSpec((1, width, ny, nz), lambda s: (s, 0, 0, 0))
-    out_block = pl.BlockSpec((1, n_out, ny, nz), lambda s: (s, 0, 0, 0))
+    st_block = pl.BlockSpec((1, n_out, ny, nz), lambda s: (s, 0, 0, 0))
     coef_block = pl.BlockSpec((n_out, ny, nz), lambda s: (0, 0, 0))
     rim_specs = [pl.BlockSpec((1, r.shape[1], ny, nz), lambda s: (s, 0, 0, 0)) for r in rims]
+    if mode == "norm":
+        out_specs = pl.BlockSpec((1, 8, nz), lambda s: (s, 0, 0))
+        out_shape = jax.ShapeDtypeStruct((n_src, 8, nz), jnp.float32)
+    else:
+        half = pl.BlockSpec((1, n_out, ny // 2, nz), lambda s: (s, 0, 0, 0))
+        out_specs = [half, half]
+        out_shape = [jax.ShapeDtypeStruct((n_src, n_out, ny // 2, nz), jnp.float32)] * 2
     return pl.pallas_call(
-        make_stencil_kernel(tuple(planes), len(rims) > 0),
+        make_stencil_kernel(tuple(planes), len(rims) > 0, mode),
         grid=(n_src,),
-        in_specs=[own_block] + rim_specs + [out_block] + [coef_block] * 7,
-        out_specs=out_block,
-        out_shape=jax.ShapeDtypeStruct((n_src, n_out, ny, nz), jnp.float32),
+        in_specs=[pl.BlockSpec(memory_space=pltpu.SMEM), own_block] + rim_specs + [st_block] + [coef_block] * 7,
+        out_specs=out_specs,
+        out_shape=out_shape,
         interpret=INTERPRET,
-    )(v, *rims, st, *coefs)
+    )(core, v, *rims, st, *coefs)
 
 
 def make_correction_kernel(columns):
@@ -192,18 +212,16 @@
     bnd_planes = list(range(-margin, 1)) + list(range(width_x - 1, width_x + margin))
     own_planes = list(range(width_x))
 
-    def pick(arr, planes, axis):
-        return jnp.concatenate([lax.slice_in_dim(arr, p + margin, p + margin + 1, axis=axis) for p in planes], axis=axis)
-
-    def runs(planes):
-        return [(p + margin) for p in planes]
-
     mid_coefs = [c[1 + margin : width_x - 1 + margin] for c in coefs]
     bnd_coefs = [jnp.concatenate([c[: margin + 1], c[width_x - 1 + margin :]], axis=0) for c in coefs]
     own_coefs = [c[margin : margin + width_x] for c in coefs]
     mid_st = source_term[:, 1 + margin : width_x - 1 + margin]
     bnd_st = jnp.concatenate([source_term[:, : margin + 1], source_term[:, width_x - 1 + margin :]], axis=1)
     own_st = source_term[:, margin : margin + width_x]
+    mid_coefs, bnd_coefs, own_coefs, mid_st, bnd_st, own_st = lax.optimization_barrier(
+        (mid_coefs, bnd_coefs, own_coefs, mid_st, bnd_st, own_st)
+    )
+    core_vec = jnp.reshape(core, (1,)).astype(jnp.int32)
 
     columns = []
     for j in range(extended):
@@ -215,21 +233,13 @@
 
     swap = [(0, 1), (1, 0)]
 
-    def swap_rows(piece):
-        split = piece.reshape(local_src, piece.shape[1], blocks, n_core, rows, depth)
-        own = lax.dynamic_index_in_dim(split, core, axis=3, keepdims=False).reshape(
-            local_src, piece.shape[1], blocks * rows, depth)
-        other = lax.dynamic_index_in_dim(split, 1 - core, axis=3, keepdims=False).reshape(
-            local_src, piece.shape[1], blocks * rows, depth)
-        return own, lax.ppermute(other, CORE, swap)
-
     potential = potential_init
     for sweep in range(ITERS):
         lo, hi = rims_of(potential, rim, 1)
-        mid = stencil_call(mid_planes, potential, [], mid_st, mid_coefs)
-        mid_own, mid_got = swap_rows(mid)
-        bnd = stencil_call(bnd_planes, potential, [lo, hi], bnd_st, bnd_coefs)
-        bnd_own, bnd_got = swap_rows(bnd)
+        mid_own, mid_other = stencil_call(mid_planes, core_vec, potential, [], mid_st, mid_coefs, "split")
+        mid_got = lax.ppermute(mid_other, CORE, swap)
+        bnd_own, bnd_other = stencil_call(bnd_planes, core_vec, potential, [lo, hi], bnd_st, bnd_coefs, "split")
+        bnd_got = lax.ppermute(bnd_other, CORE, swap)
         correction = correction_call(
             column_mask, inverse_mine, [mid_own, bnd_own], [mid_got, bnd_got], columns
         ).reshape(2 * local_src, width_x, blocks, rows, depth)
@@ -240,8 +250,8 @@
         update = jnp.stack([first, second], axis=3).reshape(potential.shape)
         potential = potential + update
     lo, hi = rims_of(potential, 1, 1)
-    residual = stencil_call(own_planes, potential, [lo, hi], own_st, own_coefs)
-    totals = lax.psum(jnp.sum(residual * residual, axis=(1, 2, 3)), "sub")
+    squares = stencil_call(own_planes, core_vec, potential, [lo, hi], own_st, own_coefs, "norm")
+    totals = lax.psum(jnp.sum(squares, axis=(1, 2)), "sub")
     residual_norms = jnp.sqrt(totals / cell_count)
     return (potential, residual_norms)
 

time: 354 us -> 346 us (0.977)
  local copies, waits for them, and re-layouts: 62.3 us -> 38.2 us
  waiting for transfers between devices: 124 us -> 146 us
  blocking collectives: 22.6 us -> 19 us
    reshape x4 -> x0, local copies, waits for them, and re-layouts: 14.7 us -> none  [swap_rows(): lax.dynamic_index_in_dim(split, 1 - core, axis=3, keepdims=False)]
    ppermute x4, waiting for transfers between devices: 18.9 us -> 32.7 us  [rims_of(): hi = lax.ppermute(head, 'sub', [(i + 1, i) for i in range(count - 1)])]
    ppermute x4, waiting for transfers between devices: 15.4 us -> 20.6 us  [rims_of(): lo = lax.ppermute(tail, 'sub', [(i, i + 1) for i in range(count - 1)])]
    slice x4, local copies, waits for them, and re-layouts: 3.94 us -> 0.3 us  [on_device(): c[:margin + 1]]
    psum x1, blocking collectives: 22.6 us -> 19 us  [on_device(): totals = lax.psum(jnp.sum(squares, axis=(1, 2)), 'sub')]
    unnamed x48 -> x30, local copies, waits for them, and re-layouts: 9.39 us -> 9.9 us
  transfers between devices with their start and end apart: 15 -> 15, of which waited for: 10 -> 11; matrix products, arithmetic and copies ran while one was open for 17% -> 10% of each run, Pallas kernels for 9% -> 10%
where the time goes in v5:
time: 346 us; the launch traced here: 345 us
  waiting for transfers between devices  146 us (42%)
  Pallas kernels  70.4 us (20%)
  local copies, waits for them, and re-layouts  38.2 us (11%)
  starting transfers between devices  35.5 us (10%)
  other arithmetic  20.2 us (6%)
  blocking collectives  19 us (5%)
  between operations  15.1 us (4%)
    all_gather x1, waiting for transfers between devices, on_device(): inverse_mine = lax.all_gather(inverse_rows, CHIP_AXES, axis=2, tiled=True)  79 us
    pallas_call x5, Pallas kernels, stencil_call(): pl.pallas_call(make_stencil_kernel(tuple(planes), len(rims) > 0, mode), g...  41.7 us
    ppermute x4, waiting for transfers between devices, rims_of(): hi = lax.ppermute(head, 'sub', [(i + 1, i) for i in range(count - 1)])  32.7 us
    pallas_call x2, Pallas kernels, correction_call(): pl.pallas_call(make_correction_kernel(tuple(columns)), grid=(ny // rows,)...  28.7 us
    ppermute x4, starting transfers between devices, rims_of(): hi = lax.ppermute(head, 'sub', [(i + 1, i) for i in range(count - 1)])  25.4 us
    ppermute x4, waiting for transfers between devices, rims_of(): lo = lax.ppermute(tail, 'sub', [(i, i + 1) for i in range(count - 1)])  20.6 us
    psum x1, blocking collectives, on_device(): totals = lax.psum(jnp.sum(squares, axis=(1, 2)), 'sub')  19 us
    unnamed x30, local copies, waits for them, and re-layouts  9.9 us
  transfers between devices with their start and end apart: 15, of which 11 were waited for; matrix products, arithmetic and copies ran while one was open for 10% of the time, Pallas kernels for 10%

profile of v5, /device:TPU:6, one launch (start us, length us, event | category | flops | bytes accessed | tf_op | source)
XLA Modules:
  0.0 344.8 jit_solution(6368426267494141949)
XLA Ops:
  8.5 6.8 %collective-permute-start.1 = (f32[5,128,128]{2,1,0:T(8,128)S(1)}, f32[5,128,128]{2,1,0:T(8,128)S(1)}, u32[]{:S(2)}, u32[]{:S(2)}) collective-permute-start(f32[5,128,128]{2,1,0:T(8,128)S(1)} %get-tuple-element.104), channel_id=1, source_target_pairs={{16,0},{32,16},{48,32},{64,48},{80,64},{96,80},{112,96},{17,1},{33... | collective-permute-start | bytes 983048 | tf_op jit(solution)/shard_map/ppermute | solution.py:135
  15.3 1.9 collective-permute-start
  17.2 3.1 fusion.16
  20.3 7.5 %collective-permute-start.3 = (f32[4,5,128,128]{3,2,1,0:T(8,128)}, f32[4,5,128,128]{3,2,1,0:T(8,128)}, u32[]{:S(2)}, u32[]{:S(2)}) collective-permute-start(f32[4,5,128,128]{3,2,1,0:T(8,128)} %get-tuple-element.79), channel_id=1, source_target_pairs={{16,0},{32,16},{48,32},{64,48},{80,64},{96,80},{112,96},{17,1},{33... | collective-permute-start | bytes 3932168 | tf_op jit(solution)/shard_map/ppermute | solution.py:135
  27.8 1.9 collective-permute-start.2
  30.1 1.1 select_subtract_fusion
  31.5 2.0 slice.262.refs_1_
  33.5 2.2 slice.265.refs_3_
  35.7 1.7 pad_maximum_fusion.2.refs_3_
  38.6 2.3 broadcast_select_fusion
  43.9 1.1 slice.261.refs_10_
  48.2 1.1 slice.259.refs_8_
  50.2 1.1 slice.258.refs_7_
  52.4 1.1 slice.257.refs_6_
  54.5 1.1 slice.256.refs_5_
  62.1 8.6 %shard_map.68 = (f32[4,14,64,128]{3,2,1,0:T(8,128)}, f32[4,14,64,128]{3,2,1,0:T(8,128)}) custom-call(s32[1]{0:T(128)} %bitcast.2.core_ref, f32[4,16,128,128]{3,2,1,0:T(8,128)} %refs_0_.3, f32[4,14,128,128]{3,2,1,0:T(8,128)} %slice.262.refs_1_, f32[14,128,128]{2,1,0:T(8,128)} %slice.234.refs_2_, f32[14,128,128]{2,1,0:T(8,128)} %slice.235.refs_3_, ...), custom_call_target="tpu_custom_call" | custom-call | tf_op jit(solution)/shard_map/pallas_call | solution.py:79
  70.8 10.3 %collective-permute-done.3.refs_2_ = f32[4,5,128,128]{3,2,1,0:T(8,128)} collective-permute-done((f32[4,5,128,128]{3,2,1,0:T(8,128)}, f32[4,5,128,128]{3,2,1,0:T(8,128)}, u32[]{:S(2)}, u32[]{:S(2)}) %collective-permute-start.3) | collective-permute-done | bytes 1310752 | tf_op jit(solution)/shard_map/ppermute | solution.py:135
  81.1 7.5 %collective-permute-done.2.refs_1_ = f32[4,5,128,128]{3,2,1,0:T(8,128)} collective-permute-done((f32[4,5,128,128]{3,2,1,0:T(8,128)S(1)}, f32[4,5,128,128]{3,2,1,0:T(8,128)}, u32[]{:S(2)}, u32[]{:S(2)}) %collective-permute-start.2) | collective-permute-done | bytes 1310752 | tf_op jit(solution)/shard_map/ppermute | solution.py:134
  88.6 8.1 %shard_map.69 = (f32[4,10,64,128]{3,2,1,0:T(8,128)}, f32[4,10,64,128]{3,2,1,0:T(8,128)}) custom-call(s32[1]{0:T(128)} %bitcast.2.core_ref, f32[4,16,128,128]{3,2,1,0:T(8,128)} %refs_0_.3, f32[4,5,128,128]{3,2,1,0:T(8,128)} %collective-permute-done.2.refs_1_, f32[4,5,128,128]{3,2,1,0:T(8,128)} %collective-permute-done.3.refs_2_, ...), custom_call_target="tpu_custom_call" | custom-call | tf_op jit(solution)/shard_map/pallas_call | solution.py:79
  97.9 2.1 collective-permute-done.5.refs_3_
  99.9 79.0 %all-gather.2.cloned.1.call-done.inv_ref = f32[16,24,64,128]{3,2,1,0:T(8,128)} async-done(((f32[16,24,8,128]{3,2,1,0:T(8,128)}), f32[16,24,64,128]{3,2,1,0:T(8,128)}) %all-gather.2.cloned.1.call-update) | async-done | bytes 12582928 | tf_op jit(solution)/shard_map/all_gather | solution.py:192
  178.9 14.3 %shard_map.70 = f32[8,16,64,128]{3,2,1,0:T(8,128)} custom-call(f32[24]{0:T(128)} %and_convert_fusion.mask_ref, f32[16,24,64,128]{3,2,1,0:T(8,128)} %all-gather.2.cloned.1.call-done.inv_ref, f32[4,14,64,128]{3,2,1,0:T(8,128)} %get-tuple-element.42.refs_0_, f32[4,10,64,128]{3,2,1,0:T(8,128)} %get-tuple-element.51.refs_1_, f32[4,14,64,128]{3,2,1,0:T(8,128)} %copy-done.8, ...), custom_call_target="tpu_custom_call" | custom-call | tf_op jit(solution)/shard_map/pallas_call | solution.py:119
  193.2 1.7 slice_bitcast_fusion.2
  195.0 4.3 %collective-permute-done.6 = f32[4,16,8,8,128]{4,3,2,1,0:T(8,128)} collective-permute-done((f32[4,16,8,8,128]{4,3,2,1,0:T(8,128)S(1)}, f32[4,16,8,8,128]{4,3,2,1,0:T(8,128)}, u32[]{:S(2)}, u32[]{:S(2)}) %collective-permute-start.6) | collective-permute-done | bytes 2097184 | tf_op jit(solution)/shard_map/ppermute | solution.py:247
  199.3 2.7 select_bitcast_fusion.3
  203.0 1.8 copy-done.4
  204.8 1.2 bitcast_add_fusion.1.refs_0_
  206.0 1.5 fusion.15
  208.4 9.2 %collective-permute-start.8 = (f32[4,5,128,128]{3,2,1,0:T(8,128)}, f32[4,5,128,128]{3,2,1,0:T(8,128)}, u32[]{:S(2)}, u32[]{:S(2)}) collective-permute-start(f32[4,5,128,128]{3,2,1,0:T(8,128)} %get-tuple-element.77), channel_id=1, source_target_pairs={{16,0},{32,16},{48,32},{64,48},{80,64},{96,80},{112,96},{17,1},{33... | collective-permute-start | bytes 3932168 | tf_op jit(solution)/shard_map/ppermute | solution.py:135
  217.6 1.9 collective-permute-start.7
  219.5 8.7 %shard_map.71 = (f32[4,14,64,128]{3,2,1,0:T(8,128)}, f32[4,14,64,128]{3,2,1,0:T(8,128)}) custom-call(s32[1]{0:T(128)} %bitcast.2.core_ref, f32[4,16,128,128]{3,2,1,0:T(8,128)} %copy-done.2, f32[4,14,128,128]{3,2,1,0:T(8,128)} %slice.262.refs_1_, f32[14,128,128]{2,1,0:T(8,128)} %slice.234.refs_2_, f32[14,128,128]{2,1,0:T(8,128)} %slice.235.refs_3_, ...), custom_call_target="tpu_custom_call" | custom-call | tf_op jit(solution)/shard_map/pallas_call | solution.py:79
  228.2 18.0 %collective-permute-done.8.refs_2_ = f32[4,5,128,128]{3,2,1,0:T(8,128)} collective-permute-done((f32[4,5,128,128]{3,2,1,0:T(8,128)}, f32[4,5,128,128]{3,2,1,0:T(8,128)}, u32[]{:S(2)}, u32[]{:S(2)}) %collective-permute-start.8) | collective-permute-done | bytes 1310752 | tf_op jit(solution)/shard_map/ppermute | solution.py:135
  246.2 7.5 %collective-permute-done.7.refs_1_ = f32[4,5,128,128]{3,2,1,0:T(8,128)} collective-permute-done((f32[4,5,128,128]{3,2,1,0:T(8,128)S(1)}, f32[4,5,128,128]{3,2,1,0:T(8,128)}, u32[]{:S(2)}, u32[]{:S(2)}) %collective-permute-start.7) | collective-permute-done | bytes 1310752 | tf_op jit(solution)/shard_map/ppermute | solution.py:134
  253.7 7.8 %shard_map.72 = (f32[4,10,64,128]{3,2,1,0:T(8,128)}, f32[4,10,64,128]{3,2,1,0:T(8,128)}) custom-call(s32[1]{0:T(128)} %bitcast.2.core_ref, f32[4,16,128,128]{3,2,1,0:T(8,128)} %copy-done.2, f32[4,5,128,128]{3,2,1,0:T(8,128)} %collective-permute-done.7.refs_1_, f32[4,5,128,128]{3,2,1,0:T(8,128)} %collective-permute-done.8.refs_2_, ...), custom_call_target="tpu_custom_call" | custom-call | tf_op jit(solution)/shard_map/pallas_call | solution.py:79
  261.6 3.2 collective-permute-done.10.refs_3_
  264.8 1.1 copy-done.11
  265.9 14.4 %shard_map.73 = f32[8,16,64,128]{3,2,1,0:T(8,128)} custom-call(f32[24]{0:T(128)} %and_convert_fusion.mask_ref, f32[16,24,64,128]{3,2,1,0:T(8,128)} %all-gather.2.cloned.1.call-done.inv_ref, f32[4,14,64,128]{3,2,1,0:T(8,128)} %get-tuple-element.54.refs_0_, f32[4,10,64,128]{3,2,1,0:T(8,128)} %get-tuple-element.55.refs_1_, f32[4,14,64,128]{3,2,1,0:T(8,128)} %copy-done.9, ...), custom_call_target="tpu_custom_call" | custom-call | tf_op jit(solution)/shard_map/pallas_call | solution.py:119
  280.3 1.9 slice_bitcast_fusion
  282.4 4.0 %collective-permute-done.11 = f32[4,16,8,8,128]{4,3,2,1,0:T(8,128)S(1)} collective-permute-done((f32[4,16,8,8,128]{4,3,2,1,0:T(8,128)S(1)}, f32[4,16,8,8,128]{4,3,2,1,0:T(8,128)S(1)}, u32[]{:S(2)}, u32[]{:S(2)}) %collective-permute-start.11) | collective-permute-done | bytes 2097184 | tf_op jit(solution)/shard_map/ppermute | solution.py:247
  287.6 1.8 copy-done.3
  289.4 1.2 bitcast_add_fusion.refs_0_
  290.6 2.0 copy-done.5
  292.7 1.9 collective-permute-start.13
  294.6 3.9 %collective-permute-start.12 = (f32[4,1,128,128]{3,2,1,0:T(8,128)S(1)}, f32[4,1,128,128]{3,2,1,0:T(8,128)S(1)}, u32[]{:S(2)}, u32[]{:S(2)}) collective-permute-start(f32[4,1,128,128]{3,2,1,0:T(8,128)S(1)} %get-tuple-element.76), channel_id=1, source_target_pairs={{0,16},{16,32},{32,48},{48,64},{64,80},{80,96},{96,112},{1,17},{17... | collective-permute-start | bytes 786440 | tf_op jit(solution)/shard_map/ppermute | solution.py:134
  298.5 4.4 %collective-permute-done.13.refs_2_ = f32[4,1,128,128]{3,2,1,0:T(8,128)S(1)} collective-permute-done((f32[4,1,128,128]{3,2,1,0:T(8,128)S(1)}, f32[4,1,128,128]{3,2,1,0:T(8,128)S(1)}, u32[]{:S(2)}, u32[]{:S(2)}) %collective-permute-start.13) | collective-permute-done | bytes 262176 | tf_op jit(solution)/shard_map/ppermute | solution.py:135
  302.9 5.5 %collective-permute-done.12.refs_1_ = f32[4,1,128,128]{3,2,1,0:T(8,128)S(1)} collective-permute-done((f32[4,1,128,128]{3,2,1,0:T(8,128)S(1)}, f32[4,1,128,128]{3,2,1,0:T(8,128)S(1)}, u32[]{:S(2)}, u32[]{:S(2)}) %collective-permute-start.12) | collective-permute-done | bytes 262176 | tf_op jit(solution)/shard_map/ppermute | solution.py:134
  309.2 8.5 %shard_map.74 = f32[4,8,128]{2,1,0:T(8,128)} custom-call(s32[1]{0:T(128)} %bitcast.2.core_ref, f32[4,16,128,128]{3,2,1,0:T(8,128)} %copy-done.5, f32[4,1,128,128]{3,2,1,0:T(8,128)} %copy-done.13, f32[4,1,128,128]{3,2,1,0:T(8,128)} %copy-done.12, f32[4,16,128,128]{3,2,1,0:T(8,128)} %slice.265.refs_3_, f32[16,128,128]{2,1,0:T(8,128)} %slice.255.refs_4_, ...), custom_call_target="tpu_custom_call" | custom-call | tf_op jit(solution)/shard_map/pallas_call | solution.py:79
  318.4 19.0 %psum.7 = f32[4]{0:T(128)S(1)} all-reduce(f32[4]{0:T(128)S(1)} %reduce_sum.9), channel_id=1, replica_groups=mesh['sub'=8,'xl'=2,'y'=4,'core'=2] {'sub'}, use_global_device_ids=true, to_apply=%region_1.2 | all-reduce | flops 4 | bytes 32 | tf_op jit(solution)/shard_map/psum | solution.py:254
  (75 shorter events, 24.8 us)
Async XLA Ops:
  7.2 22.6 %copy-start = (s32[64,2]{0,1:T(2,128)S(1)}, s32[64,2]{0,1:T(2,128)}, u32[]{:S(2)}) copy-start(s32[64,2]{0,1:T(2,128)} %param.8) | copy-start | bytes 1540
  7.2 1.2 copy-start.7
  7.2 171.7 %all-gather.2.cloned.1.call-start = ((), (), s32[]{:S(2)}) async-start(), calls=%async_computation | async-start | bytes 14155776 | tf_op jit(solution)/shard_map/all_gather | solution.py:192
  8.5 30.1 %collective-permute-start.1 = (f32[5,128,128]{2,1,0:T(8,128)S(1)}, f32[5,128,128]{2,1,0:T(8,128)S(1)}, u32[]{:S(2)}, u32[]{:S(2)}) collective-permute-start(f32[5,128,128]{2,1,0:T(8,128)S(1)} %get-tuple-element.104), channel_id=1, source_target_pairs={{16,0},{32,16},{48,32},{64,48},{80,64},{96,80},{112,96},{17,1},{33... | collective-permute-start | bytes 983048 | tf_op jit(solution)/shard_map/ppermute | solution.py:135
  15.3 22.2 %collective-permute-start = (f32[5,128,128]{2,1,0:T(8,128)S(1)}, f32[5,128,128]{2,1,0:T(8,128)}, u32[]{:S(2)}, u32[]{:S(2)}) collective-permute-start(f32[5,128,128]{2,1,0:T(8,128)S(1)} %get-tuple-element.105), channel_id=1, source_target_pairs={{0,16},{16,32},{32,48},{48,64},{64,80},{80,96},{96,112},{1,17},{17... | collective-permute-start | bytes 983048 | tf_op jit(solution)/shard_map/ppermute | solution.py:134
  20.3 60.8 %collective-permute-start.3 = (f32[4,5,128,128]{3,2,1,0:T(8,128)}, f32[4,5,128,128]{3,2,1,0:T(8,128)}, u32[]{:S(2)}, u32[]{:S(2)}) collective-permute-start(f32[4,5,128,128]{3,2,1,0:T(8,128)} %get-tuple-element.79), channel_id=1, source_target_pairs={{16,0},{32,16},{48,32},{64,48},{80,64},{96,80},{112,96},{17,1},{33... | collective-permute-start | bytes 3932168 | tf_op jit(solution)/shard_map/ppermute | solution.py:135
  27.8 60.8 %collective-permute-start.2 = (f32[4,5,128,128]{3,2,1,0:T(8,128)S(1)}, f32[4,5,128,128]{3,2,1,0:T(8,128)}, u32[]{:S(2)}, u32[]{:S(2)}) collective-permute-start(f32[4,5,128,128]{3,2,1,0:T(8,128)S(1)} %get-tuple-element.80), channel_id=1, source_target_pairs={{0,16},{16,32},{32,48},{48,64},{64,80},{80,96},{96,112},{1,17},{17... | collective-permute-start | bytes 3932168 | tf_op jit(solution)/shard_map/ppermute | solution.py:134
  70.8 27.1 %collective-permute-start.4 = (f32[4,14,64,128]{3,2,1,0:T(8,128)}, f32[4,14,64,128]{3,2,1,0:T(8,128)S(1)}, u32[]{:S(2)}, u32[]{:S(2)}) collective-permute-start(f32[4,14,64,128]{3,2,1,0:T(8,128)} %get-tuple-element.52), channel_id=1, source_target_pairs={{0,1},{1,0},{2,3},{3,2},{4,5},{5,4},{6,7},{7,6},{8,9},{9,8},{10,11... | collective-permute-start | bytes 5505032 | tf_op jit(solution)/shard_map/ppermute | solution.py:240
  96.7 3.2 collective-permute-start.5
  97.9 81.0 %copy-start.8 = (f32[4,14,64,128]{3,2,1,0:T(8,128)}, f32[4,14,64,128]{3,2,1,0:T(8,128)S(1)}, u32[]{:S(2)}) copy-start(f32[4,14,64,128]{3,2,1,0:T(8,128)S(1)} %collective-permute-done.4.refs_2_) | copy-start | bytes 5505028
  99.9 79.0 %copy-start.10 = (f32[4,10,64,128]{3,2,1,0:T(8,128)}, f32[4,10,64,128]{3,2,1,0:T(8,128)S(1)}, u32[]{:S(2)}) copy-start(f32[4,10,64,128]{3,2,1,0:T(8,128)S(1)} %collective-permute-done.5.refs_3_) | copy-start | bytes 3932164
  194.9 4.4 %collective-permute-start.6 = (f32[4,16,8,8,128]{4,3,2,1,0:T(8,128)S(1)}, f32[4,16,8,8,128]{4,3,2,1,0:T(8,128)}, u32[]{:S(2)}, u32[]{:S(2)}) collective-permute-start(f32[4,16,8,8,128]{4,3,2,1,0:T(8,128)S(1)} %slice_bitcast_fusion.2), channel_id=1, source_target_pairs={{0,1},{1,0},{2,3},{3,2},{4,5},{5,4},{6,7},{7,6},{8,9},{9,8},{10,11... | collective-permute-start | bytes 6291464 | tf_op jit(solution)/shard_map/ppermute | solution.py:247
  202.6 2.2 copy-start.4
  206.0 2.4 copy-start.2
  208.4 37.8 %collective-permute-start.8 = (f32[4,5,128,128]{3,2,1,0:T(8,128)}, f32[4,5,128,128]{3,2,1,0:T(8,128)}, u32[]{:S(2)}, u32[]{:S(2)}) collective-permute-start(f32[4,5,128,128]{3,2,1,0:T(8,128)} %get-tuple-element.77), channel_id=1, source_target_pairs={{16,0},{32,16},{48,32},{64,48},{80,64},{96,80},{112,96},{17,1},{33... | collective-permute-start | bytes 3932168 | tf_op jit(solution)/shard_map/ppermute | solution.py:135
  217.6 36.2 %collective-permute-start.7 = (f32[4,5,128,128]{3,2,1,0:T(8,128)S(1)}, f32[4,5,128,128]{3,2,1,0:T(8,128)}, u32[]{:S(2)}, u32[]{:S(2)}) collective-permute-start(f32[4,5,128,128]{3,2,1,0:T(8,128)S(1)} %get-tuple-element.78), channel_id=1, source_target_pairs={{0,16},{16,32},{32,48},{48,64},{64,80},{80,96},{96,112},{1,17},{17... | collective-permute-start | bytes 3932168 | tf_op jit(solution)/shard_map/ppermute | solution.py:134
  228.2 33.4 %collective-permute-start.9 = (f32[4,14,64,128]{3,2,1,0:T(8,128)}, f32[4,14,64,128]{3,2,1,0:T(8,128)S(1)}, u32[]{:S(2)}, u32[]{:S(2)}) collective-permute-start(f32[4,14,64,128]{3,2,1,0:T(8,128)} %get-tuple-element.56), channel_id=1, source_target_pairs={{0,1},{1,0},{2,3},{3,2},{4,5},{5,4},{6,7},{7,6},{8,9},{9,8},{10,11... | collective-permute-start | bytes 5505032 | tf_op jit(solution)/shard_map/ppermute | solution.py:240
  261.5 3.3 collective-permute-start.10
  261.6 3.2 copy-start.9
  264.8 1.1 copy-start.11
  280.3 6.1 %copy-start.6 = (f32[8,16,64,128]{3,2,1,0:T(8,128)S(1)}, f32[8,16,64,128]{3,2,1,0:T(8,128)}, u32[]{:S(2)}) copy-start(f32[8,16,64,128]{3,2,1,0:T(8,128)} %shard_map.73) | copy-start | bytes 12582916
  282.1 4.2 %collective-permute-start.11 = (f32[4,16,8,8,128]{4,3,2,1,0:T(8,128)S(1)}, f32[4,16,8,8,128]{4,3,2,1,0:T(8,128)S(1)}, u32[]{:S(2)}, u32[]{:S(2)}) collective-permute-start(f32[4,16,8,8,128]{4,3,2,1,0:T(8,128)S(1)} %slice_bitcast_fusion), channel_id=1, source_target_pairs={{0,1},{1,0},{2,3},{3,2},{4,5},{5,4},{6,7},{7,6},{8,9},{9,8},{10,11... | collective-permute-start | bytes 6291464 | tf_op jit(solution)/shard_map/ppermute | solution.py:247
  287.2 2.2 copy-start.3
  290.6 2.0 copy-start.5
  292.7 10.2 %collective-permute-start.13 = (f32[4,1,128,128]{3,2,1,0:T(8,128)S(1)}, f32[4,1,128,128]{3,2,1,0:T(8,128)S(1)}, u32[]{:S(2)}, u32[]{:S(2)}) collective-permute-start(f32[4,1,128,128]{3,2,1,0:T(8,128)S(1)} %get-tuple-element.75), channel_id=1, source_target_pairs={{16,0},{32,16},{48,32},{64,48},{80,64},{96,80},{112,96},{17,1},{33... | collective-permute-start | bytes 786440 | tf_op jit(solution)/shard_map/ppermute | solution.py:135
  294.6 13.9 %collective-permute-start.12 = (f32[4,1,128,128]{3,2,1,0:T(8,128)S(1)}, f32[4,1,128,128]{3,2,1,0:T(8,128)S(1)}, u32[]{:S(2)}, u32[]{:S(2)}) collective-permute-start(f32[4,1,128,128]{3,2,1,0:T(8,128)S(1)} %get-tuple-element.76), channel_id=1, source_target_pairs={{0,16},{16,32},{32,48},{48,64},{64,80},{80,96},{96,112},{1,17},{17... | collective-permute-start | bytes 786440 | tf_op jit(solution)/shard_map/ppermute | solution.py:134
  302.9 5.5 %copy-start.12 = (f32[4,1,128,128]{3,2,1,0:T(8,128)}, f32[4,1,128,128]{3,2,1,0:T(8,128)S(1)}, u32[]{:S(2)}) copy-start(f32[4,1,128,128]{3,2,1,0:T(8,128)S(1)} %collective-permute-done.13.refs_2_) | copy-start | bytes 786436
  308.5 0.7 copy-start.13
  309.2 28.8 %copy-start.1 = (s32[64,2]{0,1:T(2,128)S(1)}, s32[64,2]{0,1:T(2,128)}, u32[]{:S(2)}) copy-start(s32[64,2]{0,1:T(2,128)} %param.8) | copy-start | bytes 1540
Sparse Core Ops, SparseCore 0:
  9.6 169.2 all-gather.1

commit v6 on v5

--- a/solution.py
+++ b/solution.py
@@ -16,13 +16,13 @@
 GRP = ("xl", "y", "core")
 
 
-def make_stencil_kernel(planes, has_rim, mode):
+def make_stencil_kernel(planes, has_rim, mode, n_after):
     def kernel(core_ref, *refs):
         n_in = 3 if has_rim else 1
         v_ref = refs[0]
         lo_ref, hi_ref = (refs[1], refs[2]) if has_rim else (None, None)
         st_ref, cc_ref, fxp_ref, fxm_ref, fyp_ref, fym_ref, fzp_ref, fzm_ref = refs[n_in : n_in + 8]
-        outs = refs[n_in + 8 :]
+        outs = refs[n_in + 8 + n_after :]
         width = v_ref.shape[1]
         ny, nz = v_ref.shape[2], v_ref.shape[3]
         core = core_ref[0]
@@ -62,7 +62,7 @@
     return kernel
 
 
-def stencil_call(planes, core, v, rims, st, coefs, mode):
+def stencil_call(planes, core, v, rims, st, coefs, mode, after=()):
     n_src, width, ny, nz = v.shape
     n_out = len(planes)
     own_block = pl.BlockSpec((1, width, ny, nz), lambda s: (s, 0, 0, 0))
@@ -77,25 +77,27 @@
         out_specs = [half, half]
         out_shape = [jax.ShapeDtypeStruct((n_src, n_out, ny // 2, nz), jnp.float32)] * 2
     return pl.pallas_call(
-        make_stencil_kernel(tuple(planes), len(rims) > 0, mode),
+        make_stencil_kernel(tuple(planes), len(rims) > 0, mode, len(after)),
         grid=(n_src,),
-        in_specs=[pl.BlockSpec(memory_space=pltpu.SMEM), own_block] + rim_specs + [st_block] + [coef_block] * 7,
+        in_specs=[pl.BlockSpec(memory_space=pltpu.SMEM), own_block] + rim_specs + [st_block] + [coef_block] * 7
+        + [pl.BlockSpec(memory_space=pl.ANY)] * len(after),
         out_specs=out_specs,
         out_shape=out_shape,
         interpret=INTERPRET,
-    )(core, v, *rims, st, *coefs)
-
-
-def make_correction_kernel(columns):
+    )(core, v, *rims, st, *coefs, *after)
+
+
+def make_correction_kernel(columns, has_partial):
     def kernel(mask_ref, inv_ref, *refs):
         out_ref = refs[-1]
-        pieces = refs[:-1]
+        partial_ref = refs[-2] if has_partial else None
+        pieces = refs[: len(refs) - (2 if has_partial else 1)]
         n_out = inv_ref.shape[0]
         halves = len(pieces) // 2
 
         def row(i, carry):
             accs = None
-            for j, (piece, plane) in enumerate(columns):
+            for j, piece, plane in columns:
                 w = inv_ref[i, j] * mask_ref[j]
                 terms = []
                 for half in range(2):
@@ -104,6 +106,8 @@
                         terms.append(w * src_ref[s, plane])
                 accs = terms if accs is None else [a + t for a, t in zip(accs, terms)]
             for s, acc in enumerate(accs):
+                if has_partial:
+                    acc = partial_ref[s, i] + acc
                 out_ref[s, i] = acc
             return carry
 
@@ -112,19 +116,21 @@
     return kernel
 
 
-def correction_call(mask, inv, own_pieces, got_pieces, columns, rows=8):
+def correction_call(mask, inv, own_pieces, got_pieces, columns, partial=None, rows=8):
     n_out, n_col, ny, nz = inv.shape
-    n_src = sum(p.shape[0] for p in own_pieces[:1]) * 2
+    n_src = own_pieces[0].shape[0] * 2
     specs = [pl.BlockSpec((p.shape[0], p.shape[1], rows, nz), lambda b: (0, 0, b, 0)) for p in own_pieces + got_pieces]
+    out_spec = pl.BlockSpec((n_src, n_out, rows, nz), lambda b: (0, 0, b, 0))
+    extra = [] if partial is None else [partial]
     return pl.pallas_call(
-        make_correction_kernel(tuple(columns)),
+        make_correction_kernel(tuple(columns), partial is not None),
         grid=(ny // rows,),
         in_specs=[pl.BlockSpec(memory_space=pltpu.SMEM),
-                  pl.BlockSpec((n_out, n_col, rows, nz), lambda b: (0, 0, b, 0))] + specs,
-        out_specs=pl.BlockSpec((n_src, n_out, rows, nz), lambda b: (0, 0, b, 0)),
+                  pl.BlockSpec((n_out, n_col, rows, nz), lambda b: (0, 0, b, 0))] + specs + [out_spec] * len(extra),
+        out_specs=out_spec,
         out_shape=jax.ShapeDtypeStruct((n_src, n_out, ny, nz), jnp.float32),
         interpret=INTERPRET,
-    )(mask, inv, *own_pieces, *got_pieces)
+    )(mask, inv, *own_pieces, *got_pieces, *extra)
 
 
 def rims_of(cells, depth_x, dim):
@@ -210,48 +216,48 @@
 
     mid_planes = list(range(1, width_x - 1))
     bnd_planes = list(range(-margin, 1)) + list(range(width_x - 1, width_x + margin))
-    own_planes = list(range(width_x))
 
     mid_coefs = [c[1 + margin : width_x - 1 + margin] for c in coefs]
     bnd_coefs = [jnp.concatenate([c[: margin + 1], c[width_x - 1 + margin :]], axis=0) for c in coefs]
-    own_coefs = [c[margin : margin + width_x] for c in coefs]
+    edge_planes = [0, width_x - 1]
+    edge_coefs = [jnp.concatenate([c[margin : margin + 1], c[margin + width_x - 1 : margin + width_x]], axis=0) for c in coefs]
+    edge_st = jnp.concatenate(
+        [source_term[:, margin : margin + 1], source_term[:, margin + width_x - 1 : margin + width_x]], axis=1)
     mid_st = source_term[:, 1 + margin : width_x - 1 + margin]
     bnd_st = jnp.concatenate([source_term[:, : margin + 1], source_term[:, width_x - 1 + margin :]], axis=1)
-    own_st = source_term[:, margin : margin + width_x]
-    mid_coefs, bnd_coefs, own_coefs, mid_st, bnd_st, own_st = lax.optimization_barrier(
-        (mid_coefs, bnd_coefs, own_coefs, mid_st, bnd_st, own_st)
+    mid_coefs, bnd_coefs, edge_coefs, mid_st, bnd_st, edge_st = lax.optimization_barrier(
+        (mid_coefs, bnd_coefs, edge_coefs, mid_st, bnd_st, edge_st)
     )
     core_vec = jnp.reshape(core, (1,)).astype(jnp.int32)
 
-    columns = []
-    for j in range(extended):
-        p = j - margin
-        if p in mid_planes:
-            columns.append((0, mid_planes.index(p)))
-        else:
-            columns.append((1, bnd_planes.index(p)))
+    mid_columns = [(j, 0, mid_planes.index(j - margin)) for j in range(extended) if j - margin in mid_planes]
+    bnd_columns = [(j, 0, bnd_planes.index(j - margin)) for j in range(extended) if j - margin in bnd_planes]
 
     swap = [(0, 1), (1, 0)]
 
     potential = potential_init
     for sweep in range(ITERS):
-        lo, hi = rims_of(potential, rim, 1)
-        mid_own, mid_other = stencil_call(mid_planes, core_vec, potential, [], mid_st, mid_coefs, "split")
-        mid_got = lax.ppermute(mid_other, CORE, swap)
-        bnd_own, bnd_other = stencil_call(bnd_planes, core_vec, potential, [lo, hi], bnd_st, bnd_coefs, "split")
-        bnd_got = lax.ppermute(bnd_other, CORE, swap)
-        correction = correction_call(
-            column_mask, inverse_mine, [mid_own, bnd_own], [mid_got, bnd_got], columns
-        ).reshape(2 * local_src, width_x, blocks, rows, depth)
-        mine = correction[:local_src]
-        back = lax.ppermute(correction[local_src:], CORE, swap)
-        first = jnp.where(core == 0, mine, back)
-        second = jnp.where(core == 0, back, mine)
-        update = jnp.stack([first, second], axis=3).reshape(potential.shape)
-        potential = potential + update
+      lo, hi = rims_of(potential, rim, 1)
+      mid_own, mid_other = stencil_call(mid_planes, core_vec, potential, [], mid_st, mid_coefs, "split")
+      mid_got = lax.ppermute(mid_other, CORE, swap)
+      inner = correction_call(column_mask, inverse_mine, [mid_own], [mid_got], mid_columns)
+      after = (inner,) if sweep > 0 else ()
+      bnd_own, bnd_other = stencil_call(
+          bnd_planes, core_vec, potential, [lo, hi], bnd_st, bnd_coefs, "split", after=after)
+      bnd_got = lax.ppermute(bnd_other, CORE, swap)
+      correction = correction_call(
+          column_mask, inverse_mine, [bnd_own], [bnd_got], bnd_columns, partial=inner
+      ).reshape(2 * local_src, width_x, blocks, rows, depth)
+      mine = correction[:local_src]
+      back = lax.ppermute(correction[local_src:], CORE, swap)
+      first = jnp.where(core == 0, mine, back)
+      second = jnp.where(core == 0, back, mine)
+      update = jnp.stack([first, second], axis=3).reshape(potential.shape)
+      potential = potential + update
     lo, hi = rims_of(potential, 1, 1)
-    squares = stencil_call(own_planes, core_vec, potential, [lo, hi], own_st, own_coefs, "norm")
-    totals = lax.psum(jnp.sum(squares, axis=(1, 2)), "sub")
+    inner_squares = stencil_call(mid_planes, core_vec, potential, [], mid_st, mid_coefs, "norm")
+    rim_squares = stencil_call(edge_planes, core_vec, potential, [lo, hi], edge_st, edge_coefs, "norm")
+    totals = lax.psum(jnp.sum(inner_squares + rim_squares, axis=(1, 2)), "sub")
     residual_norms = jnp.sqrt(totals / cell_count)
     return (potential, residual_norms)
 

time: 346 us -> 362 us (1.046)
  Pallas kernels: 70.4 us -> 92.2 us
  waiting for transfers between devices: 146 us -> 131 us
  other arithmetic: 20.2 us -> 27.2 us
  local copies, waits for them, and re-layouts: 38.2 us -> 33.7 us
    ppermute x4, waiting for transfers between devices: 32.7 us -> 1.96 us  [rims_of(): hi = lax.ppermute(head, 'sub', [(i + 1, i) for i in range(count - 1)])]
    pallas_call x7 -> x10, Pallas kernels: 70.4 us -> 92.2 us  [the longest x4 47.1 us: correction_call(): pl.pallas_call(make_correction_kernel(tuple(columns), partial is not None...]
    all_gather x1, waiting for transfers between devices: 79 us -> 89.6 us  [on_device(): inverse_mine = lax.all_gather(inverse_rows, CHIP_AXES, axis=2, tiled=True)]
    slice x8 -> x5, local copies, waits for them, and re-layouts: 9.77 us -> 0.1 us  [the longest x4 0.07 us: on_device(): c[margin:margin + 1]]
    ppermute x4, waiting for transfers between devices: 20.6 us -> 27.3 us  [rims_of(): lo = lax.ppermute(tail, 'sub', [(i, i + 1) for i in range(count - 1)])]
    concatenate x0 -> x8, other arithmetic: none -> 5.5 us  [the longest x7 4.67 us: on_device(): jnp.concatenate([c[margin:margin + 1], c[margin + width_x - 1:margin + wi...]
  transfers between devices with their start and end apart: 15 -> 15, of which waited for: 11 -> 8; matrix products, arithmetic and copies ran while one was open for 10% -> 10% of each run, Pallas kernels for 10% -> 13%
where the time goes in v6:
time: 362 us; the launch traced here: 361 us
  waiting for transfers between devices  131 us (36%)
  Pallas kernels  92.2 us (25%)
  starting transfers between devices  39.1 us (11%)
  local copies, waits for them, and re-layouts  33.7 us (9%)
  other arithmetic  27.2 us (8%)
  blocking collectives  22.5 us (6%)
  between operations  15.1 us (4%)
    all_gather x1, waiting for transfers between devices, on_device(): inverse_mine = lax.all_gather(inverse_rows, CHIP_AXES, axis=2, tiled=True)  89.6 us
    pallas_call x4, Pallas kernels, correction_call(): pl.pallas_call(make_correction_kernel(tuple(columns), partial is not None...  47.1 us
    pallas_call x6, Pallas kernels, stencil_call(): pl.pallas_call(make_stencil_kernel(tuple(planes), len(rims) > 0, mode, le...  45.1 us
    ppermute x4, starting transfers between devices, rims_of(): hi = lax.ppermute(head, 'sub', [(i + 1, i) for i in range(count - 1)])  29 us
    ppermute x4, waiting for transfers between devices, rims_of(): lo = lax.ppermute(tail, 'sub', [(i, i + 1) for i in range(count - 1)])  27.3 us
    psum x1, blocking collectives, on_device(): totals = lax.psum(jnp.sum(inner_squares + rim_squares, axis=(1, 2)), 'sub')  22.5 us
    unnamed x30, local copies, waits for them, and re-layouts  12 us
    ppermute x4, starting transfers between devices, rims_of(): lo = lax.ppermute(tail, 'sub', [(i, i + 1) for i in range(count - 1)])  9.55 us
  transfers between devices with their start and end apart: 15, of which 8 were waited for; matrix products, arithmetic and copies ran while one was open for 10% of the time, Pallas kernels for 13%

profile of v6, /device:TPU:6, one launch (start us, length us, event | category | flops | bytes accessed | tf_op | source)
XLA Modules:
  0.0 360.9 jit_solution(6570680438147384543)
XLA Ops:
  9.2 3.8 %collective-permute-start.2 = (f32[5,128,128]{2,1,0:T(8,128)}, f32[5,128,128]{2,1,0:T(8,128)}, u32[]{:S(2)}, u32[]{:S(2)}) collective-permute-start(f32[5,128,128]{2,1,0:T(8,128)} %get-tuple-element.121), channel_id=1, source_target_pairs={{0,16},{16,32},{32,48},{48,64},{64,80},{80,96},{96,112},{1,17},{17... | collective-permute-start | bytes 983048 | tf_op jit(solution)/shard_map/ppermute | solution.py:140
  13.0 5.6 %collective-permute-start.3 = (f32[5,128,128]{2,1,0:T(8,128)S(1)}, f32[5,128,128]{2,1,0:T(8,128)}, u32[]{:S(2)}, u32[]{:S(2)}) collective-permute-start(f32[5,128,128]{2,1,0:T(8,128)S(1)} %get-tuple-element.120), channel_id=1, source_target_pairs={{16,0},{32,16},{48,32},{64,48},{80,64},{96,80},{112,96},{17,1},{33... | collective-permute-start | bytes 983048 | tf_op jit(solution)/shard_map/ppermute | solution.py:141
  18.6 3.1 fusion.17
  21.7 1.9 collective-permute-start
  23.7 7.5 %collective-permute-start.1 = (f32[4,5,128,128]{3,2,1,0:T(8,128)S(1)}, f32[4,5,128,128]{3,2,1,0:T(8,128)}, u32[]{:S(2)}, u32[]{:S(2)}) collective-permute-start(f32[4,5,128,128]{3,2,1,0:T(8,128)S(1)} %get-tuple-element.81), channel_id=1, source_target_pairs={{16,0},{32,16},{48,32},{64,48},{80,64},{96,80},{112,96},{17,1},{33... | collective-permute-start | bytes 3932168 | tf_op jit(solution)/shard_map/ppermute | solution.py:141
  31.6 1.1 select_subtract_fusion
  33.8 2.0 slice.301.refs_1_
  35.8 1.8 pad_maximum_fusion.2.refs_3_
  39.6 2.3 broadcast_select_fusion
  50.6 1.0 slice.267.refs_3_
  51.6 1.0 slice.268.refs_4_
  53.7 1.0 slice.270.refs_6_
  54.7 1.0 slice.271.refs_7_
  55.7 1.0 slice.272.refs_8_
  60.4 8.8 %shard_map.69 = (f32[4,14,64,128]{3,2,1,0:T(8,128)}, f32[4,14,64,128]{3,2,1,0:T(8,128)}) custom-call(s32[1]{0:T(128)} %bitcast.2.core_ref, f32[4,16,128,128]{3,2,1,0:T(8,128)} %refs_0_.3, f32[4,14,128,128]{3,2,1,0:T(8,128)} %slice.301.refs_1_, f32[14,128,128]{2,1,0:T(8,128)} %slice.266.refs_2_, f32[14,128,128]{2,1,0:T(8,128)} %slice.267.refs_3_, ...), custom_call_target="tpu_custom_call" | custom-call | tf_op jit(solution)/shard_map/pallas_call | solution.py:79
  69.2 13.0 %collective-permute-done.refs_1_ = f32[4,5,128,128]{3,2,1,0:T(8,128)} collective-permute-done((f32[4,5,128,128]{3,2,1,0:T(8,128)}, f32[4,5,128,128]{3,2,1,0:T(8,128)}, u32[]{:S(2)}, u32[]{:S(2)}) %collective-permute-start) | collective-permute-done | bytes 1310752 | tf_op jit(solution)/shard_map/ppermute | solution.py:140
  82.2 1.1 collective-permute-done.1.refs_2_
  83.3 7.8 %shard_map.68 = (f32[4,10,64,128]{3,2,1,0:T(8,128)}, f32[4,10,64,128]{3,2,1,0:T(8,128)}) custom-call(s32[1]{0:T(128)} %bitcast.2.core_ref, f32[4,16,128,128]{3,2,1,0:T(8,128)} %refs_0_.3, f32[4,5,128,128]{3,2,1,0:T(8,128)} %collective-permute-done.refs_1_, f32[4,5,128,128]{3,2,1,0:T(8,128)} %collective-permute-done.1.refs_2_, ...), custom_call_target="tpu_custom_call" | custom-call | tf_op jit(solution)/shard_map/pallas_call | solution.py:79
  92.3 89.6 %all-gather.2.cloned.1.call-done.inv_ref = f32[16,24,64,128]{3,2,1,0:T(8,128)} async-done(((f32[16,24,8,128]{3,2,1,0:T(8,128)}), f32[16,24,64,128]{3,2,1,0:T(8,128)}) %all-gather.2.cloned.1.call-update) | async-done | bytes 12582928 | tf_op jit(solution)/shard_map/all_gather | solution.py:198
  182.0 11.7 %shard_map.70.refs_2_ = f32[8,16,64,128]{3,2,1,0:T(8,128)} custom-call(f32[24]{0:T(128)} %and_convert_fusion.mask_ref, f32[16,24,64,128]{3,2,1,0:T(8,128)} %all-gather.2.cloned.1.call-done.inv_ref, f32[4,14,64,128]{3,2,1,0:T(8,128)} %get-tuple-element.52.refs_0_, f32[4,14,64,128]{3,2,1,0:T(8,128)} %copy-done.7), custom_call_target="tpu_custom_call" | custom-call | tf_op jit(solution)/shard_map/pallas_call | solution.py:125
  193.7 1.1 copy-done.9
  194.7 11.9 %shard_map.71 = f32[8,16,64,128]{3,2,1,0:T(8,128)} custom-call(f32[24]{0:T(128)} %and_convert_fusion.mask_ref, f32[16,24,64,128]{3,2,1,0:T(8,128)} %all-gather.2.cloned.1.call-done.inv_ref, f32[4,10,64,128]{3,2,1,0:T(8,128)} %get-tuple-element.42.refs_0_, f32[4,10,64,128]{3,2,1,0:T(8,128)} %copy-done.9, f32[8,16,64,128]{3,2,1,0:T(8,128)} %shard_map.70.refs_2_), custom_call_target="tpu_custom_call" | custom-call | tf_op jit(solution)/shard_map/pallas_call | solution.py:125
  206.6 1.7 slice_bitcast_fusion.2
  208.4 4.3 %collective-permute-done.6 = f32[4,16,8,8,128]{4,3,2,1,0:T(8,128)} collective-permute-done((f32[4,16,8,8,128]{4,3,2,1,0:T(8,128)S(1)}, f32[4,16,8,8,128]{4,3,2,1,0:T(8,128)}, u32[]{:S(2)}, u32[]{:S(2)}) %collective-permute-start.6) | collective-permute-done | bytes 2097184 | tf_op jit(solution)/shard_map/ppermute | solution.py:252
  212.7 2.7 select_bitcast_fusion.3
  216.1 1.8 copy-done.3
  217.9 2.8 bitcast_add_fusion.1.refs_0_
  220.7 8.6 %shard_map.72 = (f32[4,14,64,128]{3,2,1,0:T(8,128)}, f32[4,14,64,128]{3,2,1,0:T(8,128)}) custom-call(s32[1]{0:T(128)} %bitcast.2.core_ref, f32[4,16,128,128]{3,2,1,0:T(8,128)} %bitcast_add_fusion.1.refs_0_, f32[4,14,128,128]{3,2,1,0:T(8,128)} %slice.301.refs_1_, f32[14,128,128]{2,1,0:T(8,128)} %slice.266.refs_2_, f32[14,128,128]{2,1,0:T(8,128)} %slice.267.refs_3_, ...), custom_call_target="tpu_custom_call" | custom-call | tf_op jit(solution)/shard_map/pallas_call | solution.py:79
  229.5 3.1 fusion.16
  232.5 1.9 collective-permute-start.7
  234.5 7.7 %collective-permute-start.8 = (f32[4,5,128,128]{3,2,1,0:T(8,128)S(1)}, f32[4,5,128,128]{3,2,1,0:T(8,128)}, u32[]{:S(2)}, u32[]{:S(2)}) collective-permute-start(f32[4,5,128,128]{3,2,1,0:T(8,128)S(1)} %get-tuple-element.79), channel_id=1, source_target_pairs={{16,0},{32,16},{48,32},{64,48},{80,64},{96,80},{112,96},{17,1},{33... | collective-permute-start | bytes 3932168 | tf_op jit(solution)/shard_map/ppermute | solution.py:141
  242.2 1.2 copy-done.8
  243.4 11.7 %shard_map.73.refs_11_.refs_2_ = f32[8,16,64,128]{3,2,1,0:T(8,128)} custom-call(f32[24]{0:T(128)} %and_convert_fusion.mask_ref, f32[16,24,64,128]{3,2,1,0:T(8,128)} %all-gather.2.cloned.1.call-done.inv_ref, f32[4,14,64,128]{3,2,1,0:T(8,128)} %get-tuple-element.54.refs_0_, f32[4,14,64,128]{3,2,1,0:T(8,128)} %copy-done.8), custom_call_target="tpu_custom_call" | custom-call | tf_op jit(solution)/shard_map/pallas_call | solution.py:125
  255.2 14.2 %collective-permute-done.7.refs_1_ = f32[4,5,128,128]{3,2,1,0:T(8,128)} collective-permute-done((f32[4,5,128,128]{3,2,1,0:T(8,128)}, f32[4,5,128,128]{3,2,1,0:T(8,128)}, u32[]{:S(2)}, u32[]{:S(2)}) %collective-permute-start.7) | collective-permute-done | bytes 1310752 | tf_op jit(solution)/shard_map/ppermute | solution.py:140
  270.3 7.8 %shard_map.74 = (f32[4,10,64,128]{3,2,1,0:T(8,128)}, f32[4,10,64,128]{3,2,1,0:T(8,128)}) custom-call(s32[1]{0:T(128)} %bitcast.2.core_ref, f32[4,16,128,128]{3,2,1,0:T(8,128)} %bitcast_add_fusion.1.refs_0_, f32[4,5,128,128]{3,2,1,0:T(8,128)} %collective-permute-done.7.refs_1_, f32[4,5,128,128]{3,2,1,0:T(8,128)} %collective-permute-done.8.refs_2_, ...), custom_call_target="tpu_custom_call" | custom-call | tf_op jit(solution)/shard_map/pallas_call | solution.py:79
  278.1 3.2 collective-permute-done.10.refs_1_
  281.3 1.1 copy-done.10
  282.4 11.9 %shard_map.75 = f32[8,16,64,128]{3,2,1,0:T(8,128)} custom-call(f32[24]{0:T(128)} %and_convert_fusion.mask_ref, f32[16,24,64,128]{3,2,1,0:T(8,128)} %all-gather.2.cloned.1.call-done.inv_ref, f32[4,10,64,128]{3,2,1,0:T(8,128)} %get-tuple-element.56.refs_0_, f32[4,10,64,128]{3,2,1,0:T(8,128)} %copy-done.10, f32[8,16,64,128]{3,2,1,0:T(8,128)} %shard_map.73.refs_11_.refs_2_), custom_call_target="tpu_custom_call" | custom-call | tf_op jit(solution)/shard_map/pallas_call | solution.py:125
  294.3 1.9 slice_bitcast_fusion
  296.4 4.0 %collective-permute-done.11 = f32[4,16,8,8,128]{4,3,2,1,0:T(8,128)S(1)} collective-permute-done((f32[4,16,8,8,128]{4,3,2,1,0:T(8,128)S(1)}, f32[4,16,8,8,128]{4,3,2,1,0:T(8,128)S(1)}, u32[]{:S(2)}, u32[]{:S(2)}) %collective-permute-start.11) | collective-permute-done | bytes 2097184 | tf_op jit(solution)/shard_map/ppermute | solution.py:252
  301.6 1.8 copy-done.2
  303.4 1.2 bitcast_add_fusion.refs_0_
  304.6 2.0 copy-done.4
  306.7 1.9 collective-permute-start.12
  308.6 8.1 %collective-permute-start.13 = (f32[4,1,128,128]{3,2,1,0:T(8,128)S(1)}, f32[4,1,128,128]{3,2,1,0:T(8,128)S(1)}, u32[]{:S(2)}, u32[]{:S(2)}) collective-permute-start(f32[4,1,128,128]{3,2,1,0:T(8,128)S(1)} %get-tuple-element.77), channel_id=1, source_target_pairs={{16,0},{32,16},{48,32},{64,48},{80,64},{96,80},{112,96},{17,1},{33... | collective-permute-start | bytes 786440 | tf_op jit(solution)/shard_map/ppermute | solution.py:141
  316.7 7.7 %shard_map.76 = f32[4,8,128]{2,1,0:T(8,128)} custom-call(s32[1]{0:T(128)} %bitcast.2.core_ref, f32[4,16,128,128]{3,2,1,0:T(8,128)} %copy-done.4, f32[4,14,128,128]{3,2,1,0:T(8,128)} %slice.301.refs_1_, f32[14,128,128]{2,1,0:T(8,128)} %slice.266.refs_2_, f32[14,128,128]{2,1,0:T(8,128)} %slice.267.refs_3_, f32[14,128,128]{2,1,0:T(8,128)} %slice.268.refs_4_, ...), custom_call_target="tpu_custom_call" | custom-call | tf_op jit(solution)/shard_map/pallas_call | solution.py:79
  325.8 4.4 %shard_map.77 = f32[4,8,128]{2,1,0:T(8,128)} custom-call(s32[1]{0:T(128)} %bitcast.2.core_ref, f32[4,16,128,128]{3,2,1,0:T(8,128)} %copy-done.4, f32[4,1,128,128]{3,2,1,0:T(8,128)} %copy-done.11, f32[4,1,128,128]{3,2,1,0:T(8,128)} %copy-done.12, f32[4,2,128,128]{3,2,1,0:T(8,128)} %pad_maximum_fusion.10.refs_3_, f32[2,128,128]{2,1,0:T(8,128)} %pad_maximum_fusion.11.refs_4_, ...), custom_call_target="tpu_custom_call" | custom-call | tf_op jit(solution)/shard_map/pallas_call | solution.py:79
  331.1 22.5 %psum.7 = f32[4]{0:T(128)S(1)} all-reduce(f32[4]{0:T(128)S(1)} %add_reduce_fusion), channel_id=1, replica_groups=mesh['sub'=8,'xl'=2,'y'=4,'core'=2] {'sub'}, use_global_device_ids=true, to_apply=%region_1.2 | all-reduce | flops 4 | bytes 32 | tf_op jit(solution)/shard_map/psum | solution.py:260
  (83 shorter events, 25.4 us)
Async XLA Ops:
  7.2 24.1 %copy-start = (s32[64,2]{0,1:T(2,128)S(1)}, s32[64,2]{0,1:T(2,128)}, u32[]{:S(2)}) copy-start(s32[64,2]{0,1:T(2,128)} %param.8) | copy-start | bytes 1540
  7.2 1.2 copy-start.6
  7.2 174.8 %all-gather.2.cloned.1.call-start = ((), (), s32[]{:S(2)}) async-start(), calls=%async_computation | async-start | bytes 14155776 | tf_op jit(solution)/shard_map/all_gather | solution.py:198
  9.2 28.4 %collective-permute-start.2 = (f32[5,128,128]{2,1,0:T(8,128)}, f32[5,128,128]{2,1,0:T(8,128)}, u32[]{:S(2)}, u32[]{:S(2)}) collective-permute-start(f32[5,128,128]{2,1,0:T(8,128)} %get-tuple-element.121), channel_id=1, source_target_pairs={{0,16},{16,32},{32,48},{48,64},{64,80},{80,96},{96,112},{1,17},{17... | collective-permute-start | bytes 983048 | tf_op jit(solution)/shard_map/ppermute | solution.py:140
  13.0 25.6 %collective-permute-start.3 = (f32[5,128,128]{2,1,0:T(8,128)S(1)}, f32[5,128,128]{2,1,0:T(8,128)}, u32[]{:S(2)}, u32[]{:S(2)}) collective-permute-start(f32[5,128,128]{2,1,0:T(8,128)S(1)} %get-tuple-element.120), channel_id=1, source_target_pairs={{16,0},{32,16},{48,32},{64,48},{80,64},{96,80},{112,96},{17,1},{33... | collective-permute-start | bytes 983048 | tf_op jit(solution)/shard_map/ppermute | solution.py:141
  21.7 60.5 %collective-permute-start = (f32[4,5,128,128]{3,2,1,0:T(8,128)}, f32[4,5,128,128]{3,2,1,0:T(8,128)}, u32[]{:S(2)}, u32[]{:S(2)}) collective-permute-start(f32[4,5,128,128]{3,2,1,0:T(8,128)} %get-tuple-element.82), channel_id=1, source_target_pairs={{0,16},{16,32},{32,48},{48,64},{64,80},{80,96},{96,112},{1,17},{17... | collective-permute-start | bytes 3932168 | tf_op jit(solution)/shard_map/ppermute | solution.py:140
  23.7 59.7 %collective-permute-start.1 = (f32[4,5,128,128]{3,2,1,0:T(8,128)S(1)}, f32[4,5,128,128]{3,2,1,0:T(8,128)}, u32[]{:S(2)}, u32[]{:S(2)}) collective-permute-start(f32[4,5,128,128]{3,2,1,0:T(8,128)S(1)} %get-tuple-element.81), channel_id=1, source_target_pairs={{16,0},{32,16},{48,32},{64,48},{80,64},{96,80},{112,96},{17,1},{33... | collective-permute-start | bytes 3932168 | tf_op jit(solution)/shard_map/ppermute | solution.py:141
  69.2 23.1 %collective-permute-start.5 = (f32[4,14,64,128]{3,2,1,0:T(8,128)}, f32[4,14,64,128]{3,2,1,0:T(8,128)S(1)}, u32[]{:S(2)}, u32[]{:S(2)}) collective-permute-start(f32[4,14,64,128]{3,2,1,0:T(8,128)} %get-tuple-element.53), channel_id=1, source_target_pairs={{0,1},{1,0},{2,3},{3,2},{4,5},{5,4},{6,7},{7,6},{8,9},{9,8},{10,11... | collective-permute-start | bytes 5505032 | tf_op jit(solution)/shard_map/ppermute | solution.py:242
  91.1 102.5 %collective-permute-start.4 = (f32[4,10,64,128]{3,2,1,0:T(8,128)}, f32[4,10,64,128]{3,2,1,0:T(8,128)S(1)}, u32[]{:S(2)}, u32[]{:S(2)}) collective-permute-start(f32[4,10,64,128]{3,2,1,0:T(8,128)} %get-tuple-element.43), channel_id=1, source_target_pairs={{0,1},{1,0},{2,3},{3,2},{4,5},{5,4},{6,7},{7,6},{8,9},{9,8},{10,11... | collective-permute-start | bytes 3932168 | tf_op jit(solution)/shard_map/ppermute | solution.py:247
  92.3 89.7 %copy-start.7 = (f32[4,14,64,128]{3,2,1,0:T(8,128)}, f32[4,14,64,128]{3,2,1,0:T(8,128)S(1)}, u32[]{:S(2)}) copy-start(f32[4,14,64,128]{3,2,1,0:T(8,128)S(1)} %collective-permute-done.5.refs_1_) | copy-start | bytes 5505028
  193.6 1.1 copy-start.9
  208.3 4.4 %collective-permute-start.6 = (f32[4,16,8,8,128]{4,3,2,1,0:T(8,128)S(1)}, f32[4,16,8,8,128]{4,3,2,1,0:T(8,128)}, u32[]{:S(2)}, u32[]{:S(2)}) collective-permute-start(f32[4,16,8,8,128]{4,3,2,1,0:T(8,128)S(1)} %slice_bitcast_fusion.2), channel_id=1, source_target_pairs={{0,1},{1,0},{2,3},{3,2},{4,5},{5,4},{6,7},{7,6},{8,9},{9,8},{10,11... | collective-permute-start | bytes 6291464 | tf_op jit(solution)/shard_map/ppermute | solution.py:252
  215.7 2.2 copy-start.3
  229.3 12.8 %collective-permute-start.9 = (f32[4,14,64,128]{3,2,1,0:T(8,128)}, f32[4,14,64,128]{3,2,1,0:T(8,128)S(1)}, u32[]{:S(2)}, u32[]{:S(2)}) collective-permute-start(f32[4,14,64,128]{3,2,1,0:T(8,128)} %get-tuple-element.55), channel_id=1, source_target_pairs={{0,1},{1,0},{2,3},{3,2},{4,5},{5,4},{6,7},{7,6},{8,9},{9,8},{10,11... | collective-permute-start | bytes 5505032 | tf_op jit(solution)/shard_map/ppermute | solution.py:242
  232.5 36.9 %collective-permute-start.7 = (f32[4,5,128,128]{3,2,1,0:T(8,128)}, f32[4,5,128,128]{3,2,1,0:T(8,128)}, u32[]{:S(2)}, u32[]{:S(2)}) collective-permute-start(f32[4,5,128,128]{3,2,1,0:T(8,128)} %get-tuple-element.80), channel_id=1, source_target_pairs={{0,16},{16,32},{32,48},{48,64},{64,80},{80,96},{96,112},{1,17},{17... | collective-permute-start | bytes 3932168 | tf_op jit(solution)/shard_map/ppermute | solution.py:140
  234.5 35.8 %collective-permute-start.8 = (f32[4,5,128,128]{3,2,1,0:T(8,128)S(1)}, f32[4,5,128,128]{3,2,1,0:T(8,128)}, u32[]{:S(2)}, u32[]{:S(2)}) collective-permute-start(f32[4,5,128,128]{3,2,1,0:T(8,128)S(1)} %get-tuple-element.79), channel_id=1, source_target_pairs={{16,0},{32,16},{48,32},{64,48},{80,64},{96,80},{112,96},{17,1},{33... | collective-permute-start | bytes 3932168 | tf_op jit(solution)/shard_map/ppermute | solution.py:141
  242.2 1.2 copy-start.8
  278.1 3.3 collective-permute-start.10
  281.3 1.1 copy-start.10
  294.3 6.1 %copy-start.5 = (f32[8,16,64,128]{3,2,1,0:T(8,128)S(1)}, f32[8,16,64,128]{3,2,1,0:T(8,128)}, u32[]{:S(2)}) copy-start(f32[8,16,64,128]{3,2,1,0:T(8,128)} %shard_map.75) | copy-start | bytes 12582916
  296.1 4.2 %collective-permute-start.11 = (f32[4,16,8,8,128]{4,3,2,1,0:T(8,128)S(1)}, f32[4,16,8,8,128]{4,3,2,1,0:T(8,128)S(1)}, u32[]{:S(2)}, u32[]{:S(2)}) collective-permute-start(f32[4,16,8,8,128]{4,3,2,1,0:T(8,128)S(1)} %slice_bitcast_fusion), channel_id=1, source_target_pairs={{0,1},{1,0},{2,3},{3,2},{4,5},{5,4},{6,7},{7,6},{8,9},{9,8},{10,11... | collective-permute-start | bytes 6291464 | tf_op jit(solution)/shard_map/ppermute | solution.py:252
  301.2 2.2 copy-start.2
  304.6 2.0 copy-start.4
  306.7 17.8 %collective-permute-start.12 = (f32[4,1,128,128]{3,2,1,0:T(8,128)S(1)}, f32[4,1,128,128]{3,2,1,0:T(8,128)S(1)}, u32[]{:S(2)}, u32[]{:S(2)}) collective-permute-start(f32[4,1,128,128]{3,2,1,0:T(8,128)S(1)} %get-tuple-element.78), channel_id=1, source_target_pairs={{0,16},{16,32},{32,48},{48,64},{64,80},{80,96},{96,112},{1,17},{17... | collective-permute-start | bytes 786440 | tf_op jit(solution)/shard_map/ppermute | solution.py:140
  308.6 15.8 %collective-permute-start.13 = (f32[4,1,128,128]{3,2,1,0:T(8,128)S(1)}, f32[4,1,128,128]{3,2,1,0:T(8,128)S(1)}, u32[]{:S(2)}, u32[]{:S(2)}) collective-permute-start(f32[4,1,128,128]{3,2,1,0:T(8,128)S(1)} %get-tuple-element.77), channel_id=1, source_target_pairs={{16,0},{32,16},{48,32},{64,48},{80,64},{96,80},{112,96},{17,1},{33... | collective-permute-start | bytes 786440 | tf_op jit(solution)/shard_map/ppermute | solution.py:141
  316.7 37.4 %copy-start.1 = (s32[64,2]{0,1:T(2,128)S(1)}, s32[64,2]{0,1:T(2,128)}, u32[]{:S(2)}) copy-start(s32[64,2]{0,1:T(2,128)} %param.8) | copy-start | bytes 1540
  324.4 5.8 %copy-start.13 = (f32[4,8,128]{2,1,0:T(8,128)S(1)}, f32[4,8,128]{2,1,0:T(8,128)}, u32[]{:S(2)}) copy-start(f32[4,8,128]{2,1,0:T(8,128)} %shard_map.76) | copy-start | bytes 49156
  324.4 0.7 copy-start.11
  325.1 0.7 copy-start.12
Sparse Core Ops, SparseCore 0:
  9.6 172.3 all-gather.1

commit v7 on v6

--- a/solution.py
+++ b/solution.py
@@ -97,8 +97,8 @@
 
         def row(i, carry):
             accs = None
-            for j, piece, plane in columns:
-                w = inv_ref[i, j] * mask_ref[j]
+            for j, col, piece, plane in columns:
+                w = inv_ref[i, col] * mask_ref[j]
                 terms = []
                 for half in range(2):
                     src_ref = pieces[half * halves + piece]
@@ -195,7 +195,13 @@
         & (column_x >= 0)
         & (column_x < width_x * n_sub)
     ).astype(jnp.float32)
-    inverse_mine = lax.all_gather(inverse_rows, CHIP_AXES, axis=2, tiled=True)
+    inner_cols = list(range(margin + 1, margin + width_x - 1))
+    rim_cols = list(range(0, margin + 1)) + list(range(margin + width_x - 1, extended))
+    inverse_inner = lax.all_gather(
+        inverse_rows[:, inner_cols[0] : inner_cols[-1] + 1], CHIP_AXES, axis=2, tiled=True)
+    inverse_rim = lax.all_gather(
+        jnp.concatenate([inverse_rows[:, : margin + 1], inverse_rows[:, margin + width_x - 1 :]], axis=1),
+        CHIP_AXES, axis=2, tiled=True)
 
     c_lo, c_hi = rims_of(conductivity, rim, 0)
     conduct_pad = jnp.pad(jnp.concatenate([c_lo, conductivity, c_hi], axis=0), ((0, 0), (1, 1), (1, 1)))
@@ -230,8 +236,8 @@
     )
     core_vec = jnp.reshape(core, (1,)).astype(jnp.int32)
 
-    mid_columns = [(j, 0, mid_planes.index(j - margin)) for j in range(extended) if j - margin in mid_planes]
-    bnd_columns = [(j, 0, bnd_planes.index(j - margin)) for j in range(extended) if j - margin in bnd_planes]
+    mid_columns = [(j, inner_cols.index(j), 0, mid_planes.index(j - margin)) for j in inner_cols]
+    bnd_columns = [(j, rim_cols.index(j), 0, bnd_planes.index(j - margin)) for j in rim_cols]
 
     swap = [(0, 1), (1, 0)]
 
@@ -240,13 +246,13 @@
       lo, hi = rims_of(potential, rim, 1)
       mid_own, mid_other = stencil_call(mid_planes, core_vec, potential, [], mid_st, mid_coefs, "split")
       mid_got = lax.ppermute(mid_other, CORE, swap)
-      inner = correction_call(column_mask, inverse_mine, [mid_own], [mid_got], mid_columns)
+      inner = correction_call(column_mask, inverse_inner, [mid_own], [mid_got], mid_columns)
       after = (inner,) if sweep > 0 else ()
       bnd_own, bnd_other = stencil_call(
           bnd_planes, core_vec, potential, [lo, hi], bnd_st, bnd_coefs, "split", after=after)
       bnd_got = lax.ppermute(bnd_other, CORE, swap)
       correction = correction_call(
-          column_mask, inverse_mine, [bnd_own], [bnd_got], bnd_columns, partial=inner
+          column_mask, inverse_rim, [bnd_own], [bnd_got], bnd_columns, partial=inner
       ).reshape(2 * local_src, width_x, blocks, rows, depth)
       mine = correction[:local_src]
       back = lax.ppermute(correction[local_src:], CORE, swap)

time: 362 us -> 364 us (level)
  Pallas kernels: 92.2 us -> 86.8 us
  waiting for transfers between devices: 131 us -> 135 us
    pallas_call x4, Pallas kernels: 47.1 us -> 41.7 us  [correction_call(): pl.pallas_call(make_correction_kernel(tuple(columns), partial is not None...]
    all_gather x1 -> x2, waiting for transfers between devices: 89.6 us -> 91.1 us  [the longest x1 57.5 us: on_device(): lax.all_gather(jnp.concatenate([inverse_rows[:, :margin + 1], inverse_row...]
  transfers between devices with their start and end apart: 15 -> 16, of which waited for: 8 -> 9; matrix products, arithmetic and copies ran while one was open for 10% -> 11% of each run, Pallas kernels for 13% -> 13%
where the time goes in v7:
time: 364 us; the launch traced here: 362 us
  waiting for transfers between devices  135 us (37%)
  Pallas kernels  86.8 us (24%)
  starting transfers between devices  39.1 us (11%)
  local copies, waits for them, and re-layouts  35.7 us (10%)
  other arithmetic  28.1 us (8%)
  blocking collectives  22.5 us (6%)
  between operations  15.1 us (4%)
    all_gather x1, waiting for transfers between devices, on_device(): lax.all_gather(jnp.concatenate([inverse_rows[:, :margin + 1], inverse_row...  57.5 us
    pallas_call x6, Pallas kernels, stencil_call(): pl.pallas_call(make_stencil_kernel(tuple(planes), len(rims) > 0, mode, le...  45.1 us
    pallas_call x4, Pallas kernels, correction_call(): pl.pallas_call(make_correction_kernel(tuple(columns), partial is not None...  41.7 us
    all_gather x1, waiting for transfers between devices, on_device(): lax.all_gather(inverse_rows[:, inner_cols[0]:inner_cols[-1] + 1], CHIP_AX...  33.7 us
    ppermute x4, waiting for transfers between devices, rims_of(): lo = lax.ppermute(tail, 'sub', [(i, i + 1) for i in range(count - 1)])  27.5 us
    ppermute x4, starting transfers between devices, rims_of(): hi = lax.ppermute(head, 'sub', [(i + 1, i) for i in range(count - 1)])  27.4 us
    psum x1, blocking collectives, on_device(): totals = lax.psum(jnp.sum(inner_squares + rim_squares, axis=(1, 2)), 'sub')  22.5 us
    ppermute x4, starting transfers between devices, rims_of(): lo = lax.ppermute(tail, 'sub', [(i, i + 1) for i in range(count - 1)])  11.2 us
  transfers between devices with their start and end apart: 16, of which 9 were waited for; matrix products, arithmetic and copies ran while one was open for 11% of the time, Pallas kernels for 13%

profile of v7, /device:TPU:6, one launch (start us, length us, event | category | flops | bytes accessed | tf_op | source)
XLA Modules:
  0.0 362.1 jit_solution(807246849366730760)
XLA Ops:
  7.2 2.2 slice.262
  9.5 1.2 fusion.32
  12.4 3.8 %collective-permute-start.2 = (f32[5,128,128]{2,1,0:T(8,128)}, f32[5,128,128]{2,1,0:T(8,128)}, u32[]{:S(2)}, u32[]{:S(2)}) collective-permute-start(f32[5,128,128]{2,1,0:T(8,128)} %get-tuple-element.123), channel_id=1, source_target_pairs={{0,16},{16,32},{32,48},{48,64},{64,80},{80,96},{96,112},{1,17},{17... | collective-permute-start | bytes 983048 | tf_op jit(solution)/shard_map/ppermute | solution.py:140
  16.2 5.6 %collective-permute-start.3 = (f32[5,128,128]{2,1,0:T(8,128)S(1)}, f32[5,128,128]{2,1,0:T(8,128)}, u32[]{:S(2)}, u32[]{:S(2)}) collective-permute-start(f32[5,128,128]{2,1,0:T(8,128)S(1)} %get-tuple-element.122), channel_id=1, source_target_pairs={{16,0},{32,16},{48,32},{64,48},{80,64},{96,80},{112,96},{17,1},{33... | collective-permute-start | bytes 983048 | tf_op jit(solution)/shard_map/ppermute | solution.py:141
  21.8 3.1 fusion.17
  25.0 1.9 collective-permute-start
  26.9 7.5 %collective-permute-start.1 = (f32[4,5,128,128]{3,2,1,0:T(8,128)S(1)}, f32[4,5,128,128]{3,2,1,0:T(8,128)}, u32[]{:S(2)}, u32[]{:S(2)}) collective-permute-start(f32[4,5,128,128]{3,2,1,0:T(8,128)S(1)} %get-tuple-element.81), channel_id=1, source_target_pairs={{16,0},{32,16},{48,32},{64,48},{80,64},{96,80},{112,96},{17,1},{33... | collective-permute-start | bytes 3932168 | tf_op jit(solution)/shard_map/ppermute | solution.py:141
  34.8 1.1 select_subtract_fusion
  37.0 2.0 slice.313.refs_1_
  39.0 1.7 pad_maximum_fusion.2.refs_3_
  42.9 2.3 broadcast_select_fusion
  53.9 1.0 slice.279.refs_3_
  54.9 1.0 slice.280.refs_4_
  59.0 1.0 slice.284.refs_8_
  63.7 8.8 %shard_map.69 = (f32[4,14,64,128]{3,2,1,0:T(8,128)}, f32[4,14,64,128]{3,2,1,0:T(8,128)}) custom-call(s32[1]{0:T(128)} %bitcast.2.core_ref, f32[4,16,128,128]{3,2,1,0:T(8,128)} %refs_0_.3, f32[4,14,128,128]{3,2,1,0:T(8,128)} %slice.313.refs_1_, f32[14,128,128]{2,1,0:T(8,128)} %slice.278.refs_2_, f32[14,128,128]{2,1,0:T(8,128)} %slice.279.refs_3_, ...), custom_call_target="tpu_custom_call" | custom-call | tf_op jit(solution)/shard_map/pallas_call | solution.py:79
  72.5 12.1 %collective-permute-done.refs_1_ = f32[4,5,128,128]{3,2,1,0:T(8,128)} collective-permute-done((f32[4,5,128,128]{3,2,1,0:T(8,128)}, f32[4,5,128,128]{3,2,1,0:T(8,128)}, u32[]{:S(2)}, u32[]{:S(2)}) %collective-permute-start) | collective-permute-done | bytes 1310752 | tf_op jit(solution)/shard_map/ppermute | solution.py:140
  84.6 3.8 %collective-permute-done.1.refs_2_ = f32[4,5,128,128]{3,2,1,0:T(8,128)} collective-permute-done((f32[4,5,128,128]{3,2,1,0:T(8,128)S(1)}, f32[4,5,128,128]{3,2,1,0:T(8,128)}, u32[]{:S(2)}, u32[]{:S(2)}) %collective-permute-start.1) | collective-permute-done | bytes 1310752 | tf_op jit(solution)/shard_map/ppermute | solution.py:141
  88.3 7.8 %shard_map.68 = (f32[4,10,64,128]{3,2,1,0:T(8,128)}, f32[4,10,64,128]{3,2,1,0:T(8,128)}) custom-call(s32[1]{0:T(128)} %bitcast.2.core_ref, f32[4,16,128,128]{3,2,1,0:T(8,128)} %refs_0_.3, f32[4,5,128,128]{3,2,1,0:T(8,128)} %collective-permute-done.refs_1_, f32[4,5,128,128]{3,2,1,0:T(8,128)} %collective-permute-done.1.refs_2_, ...), custom_call_target="tpu_custom_call" | custom-call | tf_op jit(solution)/shard_map/pallas_call | solution.py:79
  97.4 33.7 %all-gather.5.cloned.1.call-done.inv_ref = f32[16,14,64,128]{3,2,1,0:T(8,128)} async-done(((f32[16,14,8,128]{3,2,1,0:T(8,128)}), f32[16,14,64,128]{3,2,1,0:T(8,128)}) %all-gather.5.cloned.1.call-update) | async-done | bytes 7340048 | tf_op jit(solution)/shard_map/all_gather | solution.py:200
  131.1 10.6 %shard_map.70.refs_2_ = f32[8,16,64,128]{3,2,1,0:T(8,128)} custom-call(f32[24]{0:T(128)} %and_convert_fusion.mask_ref, f32[16,14,64,128]{3,2,1,0:T(8,128)} %all-gather.5.cloned.1.call-done.inv_ref, f32[4,14,64,128]{3,2,1,0:T(8,128)} %get-tuple-element.52.refs_0_, f32[4,14,64,128]{3,2,1,0:T(8,128)} %copy-done.7), custom_call_target="tpu_custom_call" | custom-call | tf_op jit(solution)/shard_map/pallas_call | solution.py:125
  141.6 57.5 %all-gather.3.cloned.1.call-done.inv_ref = f32[16,10,64,128]{3,2,1,0:T(8,128)} async-done(((f32[16,10,8,128]{3,2,1,0:T(8,128)}), f32[16,10,64,128]{3,2,1,0:T(8,128)}) %all-gather.3.cloned.1.call-update) | async-done | bytes 5242896 | tf_op jit(solution)/shard_map/all_gather | solution.py:202
  199.1 10.3 %shard_map.71 = f32[8,16,64,128]{3,2,1,0:T(8,128)} custom-call(f32[24]{0:T(128)} %and_convert_fusion.mask_ref, f32[16,10,64,128]{3,2,1,0:T(8,128)} %all-gather.3.cloned.1.call-done.inv_ref, f32[4,10,64,128]{3,2,1,0:T(8,128)} %get-tuple-element.42.refs_0_, f32[4,10,64,128]{3,2,1,0:T(8,128)} %copy-done.9, f32[8,16,64,128]{3,2,1,0:T(8,128)} %shard_map.70.refs_2_), custom_call_target="tpu_custom_call" | custom-call | tf_op jit(solution)/shard_map/pallas_call | solution.py:125
  209.4 1.7 slice_bitcast_fusion.2
  211.2 4.3 %collective-permute-done.6 = f32[4,16,8,8,128]{4,3,2,1,0:T(8,128)} collective-permute-done((f32[4,16,8,8,128]{4,3,2,1,0:T(8,128)S(1)}, f32[4,16,8,8,128]{4,3,2,1,0:T(8,128)}, u32[]{:S(2)}, u32[]{:S(2)}) %collective-permute-start.6) | collective-permute-done | bytes 2097184 | tf_op jit(solution)/shard_map/ppermute | solution.py:258
  215.5 2.7 select_bitcast_fusion.3
  218.9 1.8 copy-done.3
  220.7 2.8 bitcast_add_fusion.1.refs_0_
  223.5 8.7 %shard_map.72 = (f32[4,14,64,128]{3,2,1,0:T(8,128)}, f32[4,14,64,128]{3,2,1,0:T(8,128)}) custom-call(s32[1]{0:T(128)} %bitcast.2.core_ref, f32[4,16,128,128]{3,2,1,0:T(8,128)} %bitcast_add_fusion.1.refs_0_, f32[4,14,128,128]{3,2,1,0:T(8,128)} %slice.313.refs_1_, f32[14,128,128]{2,1,0:T(8,128)} %slice.278.refs_2_, f32[14,128,128]{2,1,0:T(8,128)} %slice.279.refs_3_, ...), custom_call_target="tpu_custom_call" | custom-call | tf_op jit(solution)/shard_map/pallas_call | solution.py:79
  232.3 3.0 fusion.16
  235.3 3.5 collective-permute-start.7
  238.8 6.2 %collective-permute-start.8 = (f32[4,5,128,128]{3,2,1,0:T(8,128)S(1)}, f32[4,5,128,128]{3,2,1,0:T(8,128)}, u32[]{:S(2)}, u32[]{:S(2)}) collective-permute-start(f32[4,5,128,128]{3,2,1,0:T(8,128)S(1)} %get-tuple-element.79), channel_id=1, source_target_pairs={{16,0},{32,16},{48,32},{64,48},{80,64},{96,80},{112,96},{17,1},{33... | collective-permute-start | bytes 3932168 | tf_op jit(solution)/shard_map/ppermute | solution.py:141
  245.0 1.3 copy-done.8
  246.2 10.6 %shard_map.73.refs_11_.refs_2_ = f32[8,16,64,128]{3,2,1,0:T(8,128)} custom-call(f32[24]{0:T(128)} %and_convert_fusion.mask_ref, f32[16,14,64,128]{3,2,1,0:T(8,128)} %all-gather.5.cloned.1.call-done.inv_ref, f32[4,14,64,128]{3,2,1,0:T(8,128)} %get-tuple-element.54.refs_0_, f32[4,14,64,128]{3,2,1,0:T(8,128)} %copy-done.8), custom_call_target="tpu_custom_call" | custom-call | tf_op jit(solution)/shard_map/pallas_call | solution.py:125
  256.8 15.4 %collective-permute-done.7.refs_1_ = f32[4,5,128,128]{3,2,1,0:T(8,128)} collective-permute-done((f32[4,5,128,128]{3,2,1,0:T(8,128)}, f32[4,5,128,128]{3,2,1,0:T(8,128)}, u32[]{:S(2)}, u32[]{:S(2)}) %collective-permute-start.7) | collective-permute-done | bytes 1310752 | tf_op jit(solution)/shard_map/ppermute | solution.py:140
  273.0 7.8 %shard_map.74 = (f32[4,10,64,128]{3,2,1,0:T(8,128)}, f32[4,10,64,128]{3,2,1,0:T(8,128)}) custom-call(s32[1]{0:T(128)} %bitcast.2.core_ref, f32[4,16,128,128]{3,2,1,0:T(8,128)} %bitcast_add_fusion.1.refs_0_, f32[4,5,128,128]{3,2,1,0:T(8,128)} %collective-permute-done.7.refs_1_, f32[4,5,128,128]{3,2,1,0:T(8,128)} %collective-permute-done.8.refs_2_, ...), custom_call_target="tpu_custom_call" | custom-call | tf_op jit(solution)/shard_map/pallas_call | solution.py:79
  280.8 3.2 collective-permute-done.10.refs_1_
  284.1 1.1 copy-done.10
  285.2 10.3 %shard_map.75 = f32[8,16,64,128]{3,2,1,0:T(8,128)} custom-call(f32[24]{0:T(128)} %and_convert_fusion.mask_ref, f32[16,10,64,128]{3,2,1,0:T(8,128)} %all-gather.3.cloned.1.call-done.inv_ref, f32[4,10,64,128]{3,2,1,0:T(8,128)} %get-tuple-element.56.refs_0_, f32[4,10,64,128]{3,2,1,0:T(8,128)} %copy-done.10, f32[8,16,64,128]{3,2,1,0:T(8,128)} %shard_map.73.refs_11_.refs_2_), custom_call_target="tpu_custom_call" | custom-call | tf_op jit(solution)/shard_map/pallas_call | solution.py:125
  295.4 1.9 slice_bitcast_fusion
  297.5 4.0 %collective-permute-done.11 = f32[4,16,8,8,128]{4,3,2,1,0:T(8,128)S(1)} collective-permute-done((f32[4,16,8,8,128]{4,3,2,1,0:T(8,128)S(1)}, f32[4,16,8,8,128]{4,3,2,1,0:T(8,128)S(1)}, u32[]{:S(2)}, u32[]{:S(2)}) %collective-permute-start.11) | collective-permute-done | bytes 2097184 | tf_op jit(solution)/shard_map/ppermute | solution.py:258
  302.8 1.8 copy-done.2
  304.6 1.2 bitcast_add_fusion.refs_0_
  305.8 2.0 copy-done.4
  307.8 2.0 collective-permute-start.12
  309.8 8.1 %collective-permute-start.13 = (f32[4,1,128,128]{3,2,1,0:T(8,128)S(1)}, f32[4,1,128,128]{3,2,1,0:T(8,128)S(1)}, u32[]{:S(2)}, u32[]{:S(2)}) collective-permute-start(f32[4,1,128,128]{3,2,1,0:T(8,128)S(1)} %get-tuple-element.77), channel_id=1, source_target_pairs={{16,0},{32,16},{48,32},{64,48},{80,64},{96,80},{112,96},{17,1},{33... | collective-permute-start | bytes 786440 | tf_op jit(solution)/shard_map/ppermute | solution.py:141
  317.9 7.7 %shard_map.76 = f32[4,8,128]{2,1,0:T(8,128)} custom-call(s32[1]{0:T(128)} %bitcast.2.core_ref, f32[4,16,128,128]{3,2,1,0:T(8,128)} %copy-done.4, f32[4,14,128,128]{3,2,1,0:T(8,128)} %slice.313.refs_1_, f32[14,128,128]{2,1,0:T(8,128)} %slice.278.refs_2_, f32[14,128,128]{2,1,0:T(8,128)} %slice.279.refs_3_, f32[14,128,128]{2,1,0:T(8,128)} %slice.280.refs_4_, ...), custom_call_target="tpu_custom_call" | custom-call | tf_op jit(solution)/shard_map/pallas_call | solution.py:79
  327.0 4.4 %shard_map.77 = f32[4,8,128]{2,1,0:T(8,128)} custom-call(s32[1]{0:T(128)} %bitcast.2.core_ref, f32[4,16,128,128]{3,2,1,0:T(8,128)} %copy-done.4, f32[4,1,128,128]{3,2,1,0:T(8,128)} %copy-done.11, f32[4,1,128,128]{3,2,1,0:T(8,128)} %copy-done.12, f32[4,2,128,128]{3,2,1,0:T(8,128)} %pad_maximum_fusion.11.refs_3_, f32[2,128,128]{2,1,0:T(8,128)} %pad_maximum_fusion.12.refs_4_, ...), custom_call_target="tpu_custom_call" | custom-call | tf_op jit(solution)/shard_map/pallas_call | solution.py:79
  332.2 22.5 %psum.7 = f32[4]{0:T(128)S(1)} all-reduce(f32[4]{0:T(128)S(1)} %add_reduce_fusion), channel_id=1, replica_groups=mesh['sub'=8,'xl'=2,'y'=4,'core'=2] {'sub'}, use_global_device_ids=true, to_apply=%region_1.2 | all-reduce | flops 4 | bytes 32 | tf_op jit(solution)/shard_map/psum | solution.py:266
  (89 shorter events, 27.3 us)
Async XLA Ops:
  7.2 27.3 %copy-start = (s32[64,2]{0,1:T(2,128)S(1)}, s32[64,2]{0,1:T(2,128)}, u32[]{:S(2)}) copy-start(s32[64,2]{0,1:T(2,128)} %param.8) | copy-start | bytes 1540
  7.2 123.9 %all-gather.5.cloned.1.call-start = ((), (), s32[]{:S(2)}) async-start(), calls=%async_computation.1 | async-start | bytes 8257536 | tf_op jit(solution)/shard_map/all_gather | solution.py:200
  9.4 2.2 copy-start.6
  9.4 189.7 %all-gather.3.cloned.1.call-start = ((), (), s32[]{:S(2)}) async-start(), calls=%async_computation | async-start | bytes 5898240 | tf_op jit(solution)/shard_map/all_gather | solution.py:202
  12.4 28.4 %collective-permute-start.2 = (f32[5,128,128]{2,1,0:T(8,128)}, f32[5,128,128]{2,1,0:T(8,128)}, u32[]{:S(2)}, u32[]{:S(2)}) collective-permute-start(f32[5,128,128]{2,1,0:T(8,128)} %get-tuple-element.123), channel_id=1, source_target_pairs={{0,16},{16,32},{32,48},{48,64},{64,80},{80,96},{96,112},{1,17},{17... | collective-permute-start | bytes 983048 | tf_op jit(solution)/shard_map/ppermute | solution.py:140
  16.2 25.6 %collective-permute-start.3 = (f32[5,128,128]{2,1,0:T(8,128)S(1)}, f32[5,128,128]{2,1,0:T(8,128)}, u32[]{:S(2)}, u32[]{:S(2)}) collective-permute-start(f32[5,128,128]{2,1,0:T(8,128)S(1)} %get-tuple-element.122), channel_id=1, source_target_pairs={{16,0},{32,16},{48,32},{64,48},{80,64},{96,80},{112,96},{17,1},{33... | collective-permute-start | bytes 983048 | tf_op jit(solution)/shard_map/ppermute | solution.py:141
  25.0 59.6 %collective-permute-start = (f32[4,5,128,128]{3,2,1,0:T(8,128)}, f32[4,5,128,128]{3,2,1,0:T(8,128)}, u32[]{:S(2)}, u32[]{:S(2)}) collective-permute-start(f32[4,5,128,128]{3,2,1,0:T(8,128)} %get-tuple-element.82), channel_id=1, source_target_pairs={{0,16},{16,32},{32,48},{48,64},{64,80},{80,96},{96,112},{1,17},{17... | collective-permute-start | bytes 3932168 | tf_op jit(solution)/shard_map/ppermute | solution.py:140
  26.9 61.4 %collective-permute-start.1 = (f32[4,5,128,128]{3,2,1,0:T(8,128)S(1)}, f32[4,5,128,128]{3,2,1,0:T(8,128)}, u32[]{:S(2)}, u32[]{:S(2)}) collective-permute-start(f32[4,5,128,128]{3,2,1,0:T(8,128)S(1)} %get-tuple-element.81), channel_id=1, source_target_pairs={{16,0},{32,16},{48,32},{64,48},{80,64},{96,80},{112,96},{17,1},{33... | collective-permute-start | bytes 3932168 | tf_op jit(solution)/shard_map/ppermute | solution.py:141
  72.4 25.0 %collective-permute-start.5 = (f32[4,14,64,128]{3,2,1,0:T(8,128)}, f32[4,14,64,128]{3,2,1,0:T(8,128)S(1)}, u32[]{:S(2)}, u32[]{:S(2)}) collective-permute-start(f32[4,14,64,128]{3,2,1,0:T(8,128)} %get-tuple-element.53), channel_id=1, source_target_pairs={{0,1},{1,0},{2,3},{3,2},{4,5},{5,4},{6,7},{7,6},{8,9},{9,8},{10,11... | collective-permute-start | bytes 5505032 | tf_op jit(solution)/shard_map/ppermute | solution.py:248
  96.2 45.5 %collective-permute-start.4 = (f32[4,10,64,128]{3,2,1,0:T(8,128)}, f32[4,10,64,128]{3,2,1,0:T(8,128)S(1)}, u32[]{:S(2)}, u32[]{:S(2)}) collective-permute-start(f32[4,10,64,128]{3,2,1,0:T(8,128)} %get-tuple-element.43), channel_id=1, source_target_pairs={{0,1},{1,0},{2,3},{3,2},{4,5},{5,4},{6,7},{7,6},{8,9},{9,8},{10,11... | collective-permute-start | bytes 3932168 | tf_op jit(solution)/shard_map/ppermute | solution.py:253
  97.4 33.7 %copy-start.7 = (f32[4,14,64,128]{3,2,1,0:T(8,128)}, f32[4,14,64,128]{3,2,1,0:T(8,128)S(1)}, u32[]{:S(2)}) copy-start(f32[4,14,64,128]{3,2,1,0:T(8,128)S(1)} %collective-permute-done.5.refs_1_) | copy-start | bytes 5505028
  141.6 57.5 %copy-start.9 = (f32[4,10,64,128]{3,2,1,0:T(8,128)}, f32[4,10,64,128]{3,2,1,0:T(8,128)S(1)}, u32[]{:S(2)}) copy-start(f32[4,10,64,128]{3,2,1,0:T(8,128)S(1)} %collective-permute-done.4.refs_1_) | copy-start | bytes 3932164
  211.1 4.4 %collective-permute-start.6 = (f32[4,16,8,8,128]{4,3,2,1,0:T(8,128)S(1)}, f32[4,16,8,8,128]{4,3,2,1,0:T(8,128)}, u32[]{:S(2)}, u32[]{:S(2)}) collective-permute-start(f32[4,16,8,8,128]{4,3,2,1,0:T(8,128)S(1)} %slice_bitcast_fusion.2), channel_id=1, source_target_pairs={{0,1},{1,0},{2,3},{3,2},{4,5},{5,4},{6,7},{7,6},{8,9},{9,8},{10,11... | collective-permute-start | bytes 6291464 | tf_op jit(solution)/shard_map/ppermute | solution.py:258
  218.5 2.2 copy-start.3
  232.2 12.8 %collective-permute-start.9 = (f32[4,14,64,128]{3,2,1,0:T(8,128)}, f32[4,14,64,128]{3,2,1,0:T(8,128)S(1)}, u32[]{:S(2)}, u32[]{:S(2)}) collective-permute-start(f32[4,14,64,128]{3,2,1,0:T(8,128)} %get-tuple-element.55), channel_id=1, source_target_pairs={{0,1},{1,0},{2,3},{3,2},{4,5},{5,4},{6,7},{7,6},{8,9},{9,8},{10,11... | collective-permute-start | bytes 5505032 | tf_op jit(solution)/shard_map/ppermute | solution.py:248
  235.3 36.9 %collective-permute-start.7 = (f32[4,5,128,128]{3,2,1,0:T(8,128)}, f32[4,5,128,128]{3,2,1,0:T(8,128)}, u32[]{:S(2)}, u32[]{:S(2)}) collective-permute-start(f32[4,5,128,128]{3,2,1,0:T(8,128)} %get-tuple-element.80), channel_id=1, source_target_pairs={{0,16},{16,32},{32,48},{48,64},{64,80},{80,96},{96,112},{1,17},{17... | collective-permute-start | bytes 3932168 | tf_op jit(solution)/shard_map/ppermute | solution.py:140
  238.8 34.3 %collective-permute-start.8 = (f32[4,5,128,128]{3,2,1,0:T(8,128)S(1)}, f32[4,5,128,128]{3,2,1,0:T(8,128)}, u32[]{:S(2)}, u32[]{:S(2)}) collective-permute-start(f32[4,5,128,128]{3,2,1,0:T(8,128)S(1)} %get-tuple-element.79), channel_id=1, source_target_pairs={{16,0},{32,16},{48,32},{64,48},{80,64},{96,80},{112,96},{17,1},{33... | collective-permute-start | bytes 3932168 | tf_op jit(solution)/shard_map/ppermute | solution.py:141
  244.9 1.3 copy-start.8
  280.8 3.3 collective-permute-start.10
  284.1 1.1 copy-start.10
  295.4 6.1 %copy-start.5 = (f32[8,16,64,128]{3,2,1,0:T(8,128)S(1)}, f32[8,16,64,128]{3,2,1,0:T(8,128)}, u32[]{:S(2)}) copy-start(f32[8,16,64,128]{3,2,1,0:T(8,128)} %shard_map.75) | copy-start | bytes 12582916
  297.3 4.2 %collective-permute-start.11 = (f32[4,16,8,8,128]{4,3,2,1,0:T(8,128)S(1)}, f32[4,16,8,8,128]{4,3,2,1,0:T(8,128)S(1)}, u32[]{:S(2)}, u32[]{:S(2)}) collective-permute-start(f32[4,16,8,8,128]{4,3,2,1,0:T(8,128)S(1)} %slice_bitcast_fusion), channel_id=1, source_target_pairs={{0,1},{1,0},{2,3},{3,2},{4,5},{5,4},{6,7},{7,6},{8,9},{9,8},{10,11... | collective-permute-start | bytes 6291464 | tf_op jit(solution)/shard_map/ppermute | solution.py:258
  302.4 2.2 copy-start.2
  305.8 2.0 copy-start.4
  307.8 17.8 %collective-permute-start.12 = (f32[4,1,128,128]{3,2,1,0:T(8,128)S(1)}, f32[4,1,128,128]{3,2,1,0:T(8,128)S(1)}, u32[]{:S(2)}, u32[]{:S(2)}) collective-permute-start(f32[4,1,128,128]{3,2,1,0:T(8,128)S(1)} %get-tuple-element.78), channel_id=1, source_target_pairs={{0,16},{16,32},{32,48},{48,64},{64,80},{80,96},{96,112},{1,17},{17... | collective-permute-start | bytes 786440 | tf_op jit(solution)/shard_map/ppermute | solution.py:140
  309.8 15.8 %collective-permute-start.13 = (f32[4,1,128,128]{3,2,1,0:T(8,128)S(1)}, f32[4,1,128,128]{3,2,1,0:T(8,128)S(1)}, u32[]{:S(2)}, u32[]{:S(2)}) collective-permute-start(f32[4,1,128,128]{3,2,1,0:T(8,128)S(1)} %get-tuple-element.77), channel_id=1, source_target_pairs={{16,0},{32,16},{48,32},{64,48},{80,64},{96,80},{112,96},{17,1},{33... | collective-permute-start | bytes 786440 | tf_op jit(solution)/shard_map/ppermute | solution.py:141
  317.9 37.3 %copy-start.1 = (s32[64,2]{0,1:T(2,128)S(1)}, s32[64,2]{0,1:T(2,128)}, u32[]{:S(2)}) copy-start(s32[64,2]{0,1:T(2,128)} %param.8) | copy-start | bytes 1540
  325.6 5.8 %copy-start.13 = (f32[4,8,128]{2,1,0:T(8,128)S(1)}, f32[4,8,128]{2,1,0:T(8,128)}, u32[]{:S(2)}) copy-start(f32[4,8,128]{2,1,0:T(8,128)} %shard_map.76) | copy-start | bytes 49156
  325.6 0.7 copy-start.11
  326.3 0.7 copy-start.12
Sparse Core Ops, SparseCore 0:
  9.6 121.4 all-gather.4
  132.6 66.4 all-gather.2

commit v8 on v5

--- a/solution.py
+++ b/solution.py
@@ -189,9 +189,11 @@
         & (column_x >= 0)
         & (column_x < width_x * n_sub)
     ).astype(jnp.float32)
+    c_lo, c_hi = rims_of(conductivity, rim, 0)
+    first_lo, first_hi = rims_of(potential_init, rim, 1)
+    inverse_rows, c_lo, c_hi, first_lo, first_hi = lax.optimization_barrier(
+        (inverse_rows, c_lo, c_hi, first_lo, first_hi))
     inverse_mine = lax.all_gather(inverse_rows, CHIP_AXES, axis=2, tiled=True)
-
-    c_lo, c_hi = rims_of(conductivity, rim, 0)
     conduct_pad = jnp.pad(jnp.concatenate([c_lo, conductivity, c_hi], axis=0), ((0, 0), (1, 1), (1, 1)))
     center_coef, face_coefs = face_terms(conduct_pad)
     y_ids = lax.broadcasted_iota(jnp.int32, center_coef.shape, 1)
@@ -235,7 +237,7 @@
 
     potential = potential_init
     for sweep in range(ITERS):
-        lo, hi = rims_of(potential, rim, 1)
+        lo, hi = (first_lo, first_hi) if sweep == 0 else rims_of(potential, rim, 1)
         mid_own, mid_other = stencil_call(mid_planes, core_vec, potential, [], mid_st, mid_coefs, "split")
         mid_got = lax.ppermute(mid_other, CORE, swap)
         bnd_own, bnd_other = stencil_call(bnd_planes, core_vec, potential, [lo, hi], bnd_st, bnd_coefs, "split")

time: 346 us -> 358 us (1.035)
  waiting for transfers between devices: 146 us -> 162 us
    ppermute x4, waiting for transfers between devices: 32.7 us -> 46 us  [rims_of(): hi = lax.ppermute(head, 'sub', [(i + 1, i) for i in range(count - 1)])]
    unnamed x30 -> x36, local copies, waits for them, and re-layouts: 9.9 us -> 9.97 us
  transfers between devices with their start and end apart: 15 -> 15, of which waited for: 11 -> 11; matrix products, arithmetic and copies ran while one was open for 10% -> 9% of each run, Pallas kernels for 10% -> 9%
where the time goes in v8:
time: 358 us; the launch traced here: 356 us
  waiting for transfers between devices  162 us (45%)
  Pallas kernels  70.3 us (20%)
  local copies, waits for them, and re-layouts  37 us (10%)
  starting transfers between devices  32.6 us (9%)
  other arithmetic  20.6 us (6%)
  blocking collectives  19 us (5%)
  between operations  15.1 us (4%)
    all_gather x1, waiting for transfers between devices, on_device(): inverse_mine = lax.all_gather(inverse_rows, CHIP_AXES, axis=2, tiled=True)  81.9 us
    ppermute x4, waiting for transfers between devices, rims_of(): hi = lax.ppermute(head, 'sub', [(i + 1, i) for i in range(count - 1)])  46 us
    pallas_call x5, Pallas kernels, stencil_call(): pl.pallas_call(make_stencil_kernel(tuple(planes), len(rims) > 0, mode), g...  41.6 us
    pallas_call x2, Pallas kernels, correction_call(): pl.pallas_call(make_correction_kernel(tuple(columns)), grid=(ny // rows,)...  28.7 us
    ppermute x4, starting transfers between devices, rims_of(): hi = lax.ppermute(head, 'sub', [(i + 1, i) for i in range(count - 1)])  22 us
    ppermute x4, waiting for transfers between devices, rims_of(): lo = lax.ppermute(tail, 'sub', [(i, i + 1) for i in range(count - 1)])  20.8 us
    psum x1, blocking collectives, on_device(): totals = lax.psum(jnp.sum(squares, axis=(1, 2)), 'sub')  19 us
    unnamed x36, local copies, waits for them, and re-layouts  9.97 us
  transfers between devices with their start and end apart: 15, of which 11 were waited for; matrix products, arithmetic and copies ran while one was open for 9% of the time, Pallas kernels for 9%

profile of v8, /device:TPU:6, one launch (start us, length us, event | category | flops | bytes accessed | tf_op | source)
XLA Modules:
  0.0 356.4 jit_solution(648924787660302608)
XLA Ops:
  7.2 2.0 fusion.16
  9.2 6.8 %collective-permute-start.3 = (f32[4,5,128,128]{3,2,1,0:T(8,128)S(1)}, f32[4,5,128,128]{3,2,1,0:T(8,128)S(1)}, u32[]{:S(2)}, u32[]{:S(2)}) collective-permute-start(f32[4,5,128,128]{3,2,1,0:T(8,128)S(1)} %get-tuple-element.89), channel_id=1, source_target_pairs={{16,0},{32,16},{48,32},{64,48},{80,64},{96,80},{112,96},{17,1},{33... | collective-permute-start | bytes 3932168 | tf_op jit(solution)/shard_map/ppermute | solution.py:135
  16.0 1.9 collective-permute-start.2
  18.0 7.5 %collective-permute-start.1 = (f32[5,128,128]{2,1,0:T(8,128)S(1)}, f32[5,128,128]{2,1,0:T(8,128)S(1)}, u32[]{:S(2)}, u32[]{:S(2)}) collective-permute-start(f32[5,128,128]{2,1,0:T(8,128)S(1)} %get-tuple-element.114), channel_id=1, source_target_pairs={{16,0},{32,16},{48,32},{64,48},{80,64},{96,80},{112,96},{17,1},{33... | collective-permute-start | bytes 983048 | tf_op jit(solution)/shard_map/ppermute | solution.py:135
  25.5 1.9 collective-permute-start
  27.5 23.6 %collective-permute-done.1 = f32[5,128,128]{2,1,0:T(8,128)S(1)} collective-permute-done((f32[5,128,128]{2,1,0:T(8,128)S(1)}, f32[5,128,128]{2,1,0:T(8,128)S(1)}, u32[]{:S(2)}, u32[]{:S(2)}) %collective-permute-start.1) | collective-permute-done | bytes 327712 | tf_op jit(solution)/shard_map/ppermute | solution.py:135
  51.0 7.7 %collective-permute-done = f32[5,128,128]{2,1,0:T(8,128)S(1)} collective-permute-done((f32[5,128,128]{2,1,0:T(8,128)S(1)}, f32[5,128,128]{2,1,0:T(8,128)S(1)}, u32[]{:S(2)}, u32[]{:S(2)}) %collective-permute-start) | collective-permute-done | bytes 327712 | tf_op jit(solution)/shard_map/ppermute | solution.py:134
  60.6 1.1 select_subtract_fusion
  61.6 2.0 slice.262.refs_1_
  63.7 2.2 slice.265.refs_3_
  66.2 1.7 pad_maximum_fusion.2.refs_3_
  68.0 2.6 broadcast_select_fusion
  73.7 1.1 slice.261.refs_10_
  75.8 1.1 slice.260.refs_9_
  77.9 1.1 slice.259.refs_8_
  80.1 1.1 slice.258.refs_7_
  82.2 1.1 slice.257.refs_6_
  91.9 8.8 %shard_map.68 = (f32[4,14,64,128]{3,2,1,0:T(8,128)}, f32[4,14,64,128]{3,2,1,0:T(8,128)}) custom-call(s32[1]{0:T(128)} %bitcast.2.core_ref, f32[4,16,128,128]{3,2,1,0:T(8,128)} %refs_0_.3, f32[4,14,128,128]{3,2,1,0:T(8,128)} %slice.262.refs_1_, f32[14,128,128]{2,1,0:T(8,128)} %slice.234.refs_2_, f32[14,128,128]{2,1,0:T(8,128)} %slice.235.refs_3_, ...), custom_call_target="tpu_custom_call" | custom-call | tf_op jit(solution)/shard_map/pallas_call | solution.py:79
  100.7 7.8 %shard_map.69 = (f32[4,10,64,128]{3,2,1,0:T(8,128)}, f32[4,10,64,128]{3,2,1,0:T(8,128)}) custom-call(s32[1]{0:T(128)} %bitcast.2.core_ref, f32[4,16,128,128]{3,2,1,0:T(8,128)} %refs_0_.3, f32[4,5,128,128]{3,2,1,0:T(8,128)} %collective-permute-done.2.refs_1_, f32[4,5,128,128]{3,2,1,0:T(8,128)} %copy-done.12, f32[4,10,128,128]{3,2,1,0:T(8,128)} %pad_maximum_fusion.2.refs_3_, ...), custom_call_target="tpu_custom_call" | custom-call | tf_op jit(solution)/shard_map/pallas_call | solution.py:79
  110.4 1.6 collective-permute-done.5.refs_3_
  112.0 81.9 %all-gather.2.cloned.1.call-done.inv_ref = f32[16,24,64,128]{3,2,1,0:T(8,128)} async-done(((f32[16,24,8,128]{3,2,1,0:T(8,128)}), f32[16,24,64,128]{3,2,1,0:T(8,128)}) %all-gather.2.cloned.1.call-update) | async-done | bytes 12582928 | tf_op jit(solution)/shard_map/all_gather | solution.py:196
  193.9 14.3 %shard_map.70 = f32[8,16,64,128]{3,2,1,0:T(8,128)} custom-call(f32[24]{0:T(128)} %and_convert_fusion.mask_ref, f32[16,24,64,128]{3,2,1,0:T(8,128)} %all-gather.2.cloned.1.call-done.inv_ref, f32[4,14,64,128]{3,2,1,0:T(8,128)} %get-tuple-element.50.refs_0_, f32[4,10,64,128]{3,2,1,0:T(8,128)} %get-tuple-element.61.refs_1_, f32[4,14,64,128]{3,2,1,0:T(8,128)} %copy-done.9, ...), custom_call_target="tpu_custom_call" | custom-call | tf_op jit(solution)/shard_map/pallas_call | solution.py:119
  208.2 1.7 slice_bitcast_fusion.2
  210.1 4.3 %collective-permute-done.6 = f32[4,16,8,8,128]{4,3,2,1,0:T(8,128)} collective-permute-done((f32[4,16,8,8,128]{4,3,2,1,0:T(8,128)S(1)}, f32[4,16,8,8,128]{4,3,2,1,0:T(8,128)}, u32[]{:S(2)}, u32[]{:S(2)}) %collective-permute-start.6) | collective-permute-done | bytes 2097184 | tf_op jit(solution)/shard_map/ppermute | solution.py:249
  214.3 2.7 select_bitcast_fusion.3
  218.0 1.8 copy-done.4
  219.8 1.2 bitcast_add_fusion.1.refs_0_
  221.0 1.4 fusion.15
  223.4 5.7 %collective-permute-start.8 = (f32[4,5,128,128]{3,2,1,0:T(8,128)}, f32[4,5,128,128]{3,2,1,0:T(8,128)}, u32[]{:S(2)}, u32[]{:S(2)}) collective-permute-start(f32[4,5,128,128]{3,2,1,0:T(8,128)} %get-tuple-element.87), channel_id=1, source_target_pairs={{16,0},{32,16},{48,32},{64,48},{80,64},{96,80},{112,96},{17,1},{33... | collective-permute-start | bytes 3932168 | tf_op jit(solution)/shard_map/ppermute | solution.py:135
  229.1 1.9 collective-permute-start.7
  231.1 8.7 %shard_map.71 = (f32[4,14,64,128]{3,2,1,0:T(8,128)}, f32[4,14,64,128]{3,2,1,0:T(8,128)}) custom-call(s32[1]{0:T(128)} %bitcast.2.core_ref, f32[4,16,128,128]{3,2,1,0:T(8,128)} %copy-done.2, f32[4,14,128,128]{3,2,1,0:T(8,128)} %slice.262.refs_1_, f32[14,128,128]{2,1,0:T(8,128)} %slice.234.refs_2_, f32[14,128,128]{2,1,0:T(8,128)} %slice.235.refs_3_, ...), custom_call_target="tpu_custom_call" | custom-call | tf_op jit(solution)/shard_map/pallas_call | solution.py:79
  239.8 18.0 %collective-permute-done.8.refs_2_ = f32[4,5,128,128]{3,2,1,0:T(8,128)} collective-permute-done((f32[4,5,128,128]{3,2,1,0:T(8,128)}, f32[4,5,128,128]{3,2,1,0:T(8,128)}, u32[]{:S(2)}, u32[]{:S(2)}) %collective-permute-start.8) | collective-permute-done | bytes 1310752 | tf_op jit(solution)/shard_map/ppermute | solution.py:135
  257.8 7.5 %collective-permute-done.7.refs_1_ = f32[4,5,128,128]{3,2,1,0:T(8,128)} collective-permute-done((f32[4,5,128,128]{3,2,1,0:T(8,128)S(1)}, f32[4,5,128,128]{3,2,1,0:T(8,128)}, u32[]{:S(2)}, u32[]{:S(2)}) %collective-permute-start.7) | collective-permute-done | bytes 1310752 | tf_op jit(solution)/shard_map/ppermute | solution.py:134
  265.3 7.8 %shard_map.72 = (f32[4,10,64,128]{3,2,1,0:T(8,128)}, f32[4,10,64,128]{3,2,1,0:T(8,128)}) custom-call(s32[1]{0:T(128)} %bitcast.2.core_ref, f32[4,16,128,128]{3,2,1,0:T(8,128)} %copy-done.2, f32[4,5,128,128]{3,2,1,0:T(8,128)} %collective-permute-done.7.refs_1_, f32[4,5,128,128]{3,2,1,0:T(8,128)} %collective-permute-done.8.refs_2_, ...), custom_call_target="tpu_custom_call" | custom-call | tf_op jit(solution)/shard_map/pallas_call | solution.py:79
  273.2 3.2 collective-permute-done.10.refs_3_
  276.4 1.1 copy-done.11
  277.5 14.4 %shard_map.73 = f32[8,16,64,128]{3,2,1,0:T(8,128)} custom-call(f32[24]{0:T(128)} %and_convert_fusion.mask_ref, f32[16,24,64,128]{3,2,1,0:T(8,128)} %all-gather.2.cloned.1.call-done.inv_ref, f32[4,14,64,128]{3,2,1,0:T(8,128)} %get-tuple-element.64.refs_0_, f32[4,10,64,128]{3,2,1,0:T(8,128)} %get-tuple-element.65.refs_1_, f32[4,14,64,128]{3,2,1,0:T(8,128)} %copy-done.8, ...), custom_call_target="tpu_custom_call" | custom-call | tf_op jit(solution)/shard_map/pallas_call | solution.py:119
  291.8 1.9 slice_bitcast_fusion
  293.9 4.0 %collective-permute-done.11 = f32[4,16,8,8,128]{4,3,2,1,0:T(8,128)S(1)} collective-permute-done((f32[4,16,8,8,128]{4,3,2,1,0:T(8,128)S(1)}, f32[4,16,8,8,128]{4,3,2,1,0:T(8,128)S(1)}, u32[]{:S(2)}, u32[]{:S(2)}) %collective-permute-start.11) | collective-permute-done | bytes 2097184 | tf_op jit(solution)/shard_map/ppermute | solution.py:249
  299.2 1.8 copy-done.3
  301.0 1.2 bitcast_add_fusion.refs_0_
  302.2 2.0 copy-done.5
  304.2 1.9 collective-permute-start.13
  306.2 3.9 %collective-permute-start.12 = (f32[4,1,128,128]{3,2,1,0:T(8,128)S(1)}, f32[4,1,128,128]{3,2,1,0:T(8,128)S(1)}, u32[]{:S(2)}, u32[]{:S(2)}) collective-permute-start(f32[4,1,128,128]{3,2,1,0:T(8,128)S(1)} %get-tuple-element.86), channel_id=1, source_target_pairs={{0,16},{16,32},{32,48},{48,64},{64,80},{80,96},{96,112},{1,17},{17... | collective-permute-start | bytes 786440 | tf_op jit(solution)/shard_map/ppermute | solution.py:134
  310.1 4.4 %collective-permute-done.13.refs_2_ = f32[4,1,128,128]{3,2,1,0:T(8,128)S(1)} collective-permute-done((f32[4,1,128,128]{3,2,1,0:T(8,128)S(1)}, f32[4,1,128,128]{3,2,1,0:T(8,128)S(1)}, u32[]{:S(2)}, u32[]{:S(2)}) %collective-permute-start.13) | collective-permute-done | bytes 262176 | tf_op jit(solution)/shard_map/ppermute | solution.py:135
  314.5 5.5 %collective-permute-done.12.refs_1_ = f32[4,1,128,128]{3,2,1,0:T(8,128)S(1)} collective-permute-done((f32[4,1,128,128]{3,2,1,0:T(8,128)S(1)}, f32[4,1,128,128]{3,2,1,0:T(8,128)S(1)}, u32[]{:S(2)}, u32[]{:S(2)}) %collective-permute-start.12) | collective-permute-done | bytes 262176 | tf_op jit(solution)/shard_map/ppermute | solution.py:134
  320.7 8.5 %shard_map.74 = f32[4,8,128]{2,1,0:T(8,128)} custom-call(s32[1]{0:T(128)} %bitcast.2.core_ref, f32[4,16,128,128]{3,2,1,0:T(8,128)} %copy-done.5, f32[4,1,128,128]{3,2,1,0:T(8,128)} %copy-done.16, f32[4,1,128,128]{3,2,1,0:T(8,128)} %copy-done.15, f32[4,16,128,128]{3,2,1,0:T(8,128)} %slice.265.refs_3_, f32[16,128,128]{2,1,0:T(8,128)} %slice.255.refs_4_, ...), custom_call_target="tpu_custom_call" | custom-call | tf_op jit(solution)/shard_map/pallas_call | solution.py:79
  330.0 19.0 %psum.7 = f32[4]{0:T(128)S(1)} all-reduce(f32[4]{0:T(128)S(1)} %reduce_sum.9), channel_id=1, replica_groups=mesh['sub'=8,'xl'=2,'y'=4,'core'=2] {'sub'}, use_global_device_ids=true, to_apply=%region_1.2 | all-reduce | flops 4 | bytes 32 | tf_op jit(solution)/shard_map/psum | solution.py:256
  (81 shorter events, 24.9 us)
Async XLA Ops:
  7.2 52.4 %copy-start = (s32[64,2]{0,1:T(2,128)S(1)}, s32[64,2]{0,1:T(2,128)}, u32[]{:S(2)}) copy-start(s32[64,2]{0,1:T(2,128)} %param.8) | copy-start | bytes 1540
  7.2 10.8 %copy-start.7 = (f32[16,128,128]{2,1,0:T(8,128)S(1)}, f32[16,128,128]{2,1,0:T(8,128)}, u32[]{:S(2)}) copy-start(f32[16,128,128]{2,1,0:T(8,128)} %param.6) | copy-start | bytes 3145732
  7.2 186.7 %all-gather.2.cloned.1.call-start = ((), (), s32[]{:S(2)}) async-start(), calls=%async_computation | async-start | bytes 14155776 | tf_op jit(solution)/shard_map/all_gather | solution.py:196
  9.2 49.6 %collective-permute-start.3 = (f32[4,5,128,128]{3,2,1,0:T(8,128)S(1)}, f32[4,5,128,128]{3,2,1,0:T(8,128)S(1)}, u32[]{:S(2)}, u32[]{:S(2)}) collective-permute-start(f32[4,5,128,128]{3,2,1,0:T(8,128)S(1)} %get-tuple-element.89), channel_id=1, source_target_pairs={{16,0},{32,16},{48,32},{64,48},{80,64},{96,80},{112,96},{17,1},{33... | collective-permute-start | bytes 3932168 | tf_op jit(solution)/shard_map/ppermute | solution.py:135
  16.0 43.5 %collective-permute-start.2 = (f32[4,5,128,128]{3,2,1,0:T(8,128)S(1)}, f32[4,5,128,128]{3,2,1,0:T(8,128)}, u32[]{:S(2)}, u32[]{:S(2)}) collective-permute-start(f32[4,5,128,128]{3,2,1,0:T(8,128)S(1)} %get-tuple-element.90), channel_id=1, source_target_pairs={{0,16},{16,32},{32,48},{48,64},{64,80},{80,96},{96,112},{1,17},{17... | collective-permute-start | bytes 3932168 | tf_op jit(solution)/shard_map/ppermute | solution.py:134
  18.0 33.0 %collective-permute-start.1 = (f32[5,128,128]{2,1,0:T(8,128)S(1)}, f32[5,128,128]{2,1,0:T(8,128)S(1)}, u32[]{:S(2)}, u32[]{:S(2)}) collective-permute-start(f32[5,128,128]{2,1,0:T(8,128)S(1)} %get-tuple-element.114), channel_id=1, source_target_pairs={{16,0},{32,16},{48,32},{64,48},{80,64},{96,80},{112,96},{17,1},{33... | collective-permute-start | bytes 983048 | tf_op jit(solution)/shard_map/ppermute | solution.py:135
  25.5 33.2 %collective-permute-start = (f32[5,128,128]{2,1,0:T(8,128)S(1)}, f32[5,128,128]{2,1,0:T(8,128)S(1)}, u32[]{:S(2)}, u32[]{:S(2)}) collective-permute-start(f32[5,128,128]{2,1,0:T(8,128)S(1)} %get-tuple-element.115), channel_id=1, source_target_pairs={{0,16},{16,32},{32,48},{48,64},{64,80},{80,96},{96,112},{1,17},{17... | collective-permute-start | bytes 983048 | tf_op jit(solution)/shard_map/ppermute | solution.py:134
  58.8 0.7 copy-start.13
  59.5 1.1 copy-start.12
  66.2 1.7 copy-start.14
  100.7 11.3 %collective-permute-start.4 = (f32[4,14,64,128]{3,2,1,0:T(8,128)}, f32[4,14,64,128]{3,2,1,0:T(8,128)S(1)}, u32[]{:S(2)}, u32[]{:S(2)}) collective-permute-start(f32[4,14,64,128]{3,2,1,0:T(8,128)} %get-tuple-element.62), channel_id=1, source_target_pairs={{0,1},{1,0},{2,3},{3,2},{4,5},{5,4},{6,7},{7,6},{8,9},{9,8},{10,11... | collective-permute-start | bytes 5505032 | tf_op jit(solution)/shard_map/ppermute | solution.py:242
  108.6 3.4 collective-permute-start.5
  112.0 81.9 %copy-start.10 = (f32[4,10,64,128]{3,2,1,0:T(8,128)}, f32[4,10,64,128]{3,2,1,0:T(8,128)S(1)}, u32[]{:S(2)}) copy-start(f32[4,10,64,128]{3,2,1,0:T(8,128)S(1)} %collective-permute-done.5.refs_3_) | copy-start | bytes 3932164
  112.0 81.9 %copy-start.9 = (f32[4,14,64,128]{3,2,1,0:T(8,128)}, f32[4,14,64,128]{3,2,1,0:T(8,128)S(1)}, u32[]{:S(2)}) copy-start(f32[4,14,64,128]{3,2,1,0:T(8,128)S(1)} %collective-permute-done.4.refs_2_) | copy-start | bytes 5505028
  210.0 4.4 %collective-permute-start.6 = (f32[4,16,8,8,128]{4,3,2,1,0:T(8,128)S(1)}, f32[4,16,8,8,128]{4,3,2,1,0:T(8,128)}, u32[]{:S(2)}, u32[]{:S(2)}) collective-permute-start(f32[4,16,8,8,128]{4,3,2,1,0:T(8,128)S(1)} %slice_bitcast_fusion.2), channel_id=1, source_target_pairs={{0,1},{1,0},{2,3},{3,2},{4,5},{5,4},{6,7},{7,6},{8,9},{9,8},{10,11... | collective-permute-start | bytes 6291464 | tf_op jit(solution)/shard_map/ppermute | solution.py:249
  217.6 2.2 copy-start.4
  221.0 2.4 copy-start.2
  223.4 34.4 %collective-permute-start.8 = (f32[4,5,128,128]{3,2,1,0:T(8,128)}, f32[4,5,128,128]{3,2,1,0:T(8,128)}, u32[]{:S(2)}, u32[]{:S(2)}) collective-permute-start(f32[4,5,128,128]{3,2,1,0:T(8,128)} %get-tuple-element.87), channel_id=1, source_target_pairs={{16,0},{32,16},{48,32},{64,48},{80,64},{96,80},{112,96},{17,1},{33... | collective-permute-start | bytes 3932168 | tf_op jit(solution)/shard_map/ppermute | solution.py:135
  229.1 36.2 %collective-permute-start.7 = (f32[4,5,128,128]{3,2,1,0:T(8,128)S(1)}, f32[4,5,128,128]{3,2,1,0:T(8,128)}, u32[]{:S(2)}, u32[]{:S(2)}) collective-permute-start(f32[4,5,128,128]{3,2,1,0:T(8,128)S(1)} %get-tuple-element.88), channel_id=1, source_target_pairs={{0,16},{16,32},{32,48},{48,64},{64,80},{80,96},{96,112},{1,17},{17... | collective-permute-start | bytes 3932168 | tf_op jit(solution)/shard_map/ppermute | solution.py:134
  239.7 33.4 %collective-permute-start.9 = (f32[4,14,64,128]{3,2,1,0:T(8,128)}, f32[4,14,64,128]{3,2,1,0:T(8,128)S(1)}, u32[]{:S(2)}, u32[]{:S(2)}) collective-permute-start(f32[4,14,64,128]{3,2,1,0:T(8,128)} %get-tuple-element.66), channel_id=1, source_target_pairs={{0,1},{1,0},{2,3},{3,2},{4,5},{5,4},{6,7},{7,6},{8,9},{9,8},{10,11... | collective-permute-start | bytes 5505032 | tf_op jit(solution)/shard_map/ppermute | solution.py:242
  273.1 3.3 collective-permute-start.10
  273.2 3.2 copy-start.8
  276.4 1.1 copy-start.11
  291.8 6.1 %copy-start.6 = (f32[8,16,64,128]{3,2,1,0:T(8,128)S(1)}, f32[8,16,64,128]{3,2,1,0:T(8,128)}, u32[]{:S(2)}) copy-start(f32[8,16,64,128]{3,2,1,0:T(8,128)} %shard_map.73) | copy-start | bytes 12582916
  293.7 4.2 %collective-permute-start.11 = (f32[4,16,8,8,128]{4,3,2,1,0:T(8,128)S(1)}, f32[4,16,8,8,128]{4,3,2,1,0:T(8,128)S(1)}, u32[]{:S(2)}, u32[]{:S(2)}) collective-permute-start(f32[4,16,8,8,128]{4,3,2,1,0:T(8,128)S(1)} %slice_bitcast_fusion), channel_id=1, source_target_pairs={{0,1},{1,0},{2,3},{3,2},{4,5},{5,4},{6,7},{7,6},{8,9},{9,8},{10,11... | collective-permute-start | bytes 6291464 | tf_op jit(solution)/shard_map/ppermute | solution.py:249
  298.8 2.2 copy-start.3
  302.2 2.0 copy-start.5
  304.2 10.2 %collective-permute-start.13 = (f32[4,1,128,128]{3,2,1,0:T(8,128)S(1)}, f32[4,1,128,128]{3,2,1,0:T(8,128)S(1)}, u32[]{:S(2)}, u32[]{:S(2)}) collective-permute-start(f32[4,1,128,128]{3,2,1,0:T(8,128)S(1)} %get-tuple-element.85), channel_id=1, source_target_pairs={{16,0},{32,16},{48,32},{64,48},{80,64},{96,80},{112,96},{17,1},{33... | collective-permute-start | bytes 786440 | tf_op jit(solution)/shard_map/ppermute | solution.py:135
  306.2 13.9 %collective-permute-start.12 = (f32[4,1,128,128]{3,2,1,0:T(8,128)S(1)}, f32[4,1,128,128]{3,2,1,0:T(8,128)S(1)}, u32[]{:S(2)}, u32[]{:S(2)}) collective-permute-start(f32[4,1,128,128]{3,2,1,0:T(8,128)S(1)} %get-tuple-element.86), channel_id=1, source_target_pairs={{0,16},{16,32},{32,48},{48,64},{64,80},{80,96},{96,112},{1,17},{17... | collective-permute-start | bytes 786440 | tf_op jit(solution)/shard_map/ppermute | solution.py:134
  314.5 5.5 %copy-start.15 = (f32[4,1,128,128]{3,2,1,0:T(8,128)}, f32[4,1,128,128]{3,2,1,0:T(8,128)S(1)}, u32[]{:S(2)}) copy-start(f32[4,1,128,128]{3,2,1,0:T(8,128)S(1)} %collective-permute-done.13.refs_2_) | copy-start | bytes 786436
  320.0 0.7 copy-start.16
  320.7 28.8 %copy-start.1 = (s32[64,2]{0,1:T(2,128)S(1)}, s32[64,2]{0,1:T(2,128)}, u32[]{:S(2)}) copy-start(s32[64,2]{0,1:T(2,128)} %param.8) | copy-start | bytes 1540
Sparse Core Ops, SparseCore 0:
  59.7 134.2 all-gather.1

commit v9 on v5

--- a/solution.py
+++ b/solution.py
@@ -251,7 +251,11 @@
         potential = potential + update
     lo, hi = rims_of(potential, 1, 1)
     squares = stencil_call(own_planes, core_vec, potential, [lo, hi], own_st, own_coefs, "norm")
-    totals = lax.psum(jnp.sum(squares, axis=(1, 2)), "sub")
+    totals = jnp.sum(squares, axis=(1, 2))
+    step_size = 1
+    while step_size < n_sub:
+        totals = totals + lax.ppermute(totals, "sub", [(i, i ^ step_size) for i in range(n_sub)])
+        step_size *= 2
     residual_norms = jnp.sqrt(totals / cell_count)
     return (potential, residual_norms)
 

time: 346 us -> 341 us (0.986)
  blocking collectives: 19 us -> 0 us
  waiting for transfers between devices: 146 us -> 160 us
    psum x1 -> x0, blocking collectives: 19 us -> none  [on_device(): totals = lax.psum(jnp.sum(squares, axis=(1, 2)), 'sub')]
    ppermute x0 -> x3, waiting for transfers between devices: none -> 13.7 us  [on_device(): lax.ppermute(totals, 'sub', [(i, i ^ step_size) for i in range(n_sub)])]
  transfers between devices with their start and end apart: 15 -> 18, of which waited for: 11 -> 14; matrix products, arithmetic and copies ran while one was open for 10% -> 11% of each run, Pallas kernels for 10% -> 10%
where the time goes in v9:
time: 341 us; the launch traced here: 340 us
  waiting for transfers between devices  160 us (47%)
  Pallas kernels  70.4 us (21%)
  local copies, waits for them, and re-layouts  38.3 us (11%)
  starting transfers between devices  35.5 us (10%)
  other arithmetic  20.3 us (6%)
  between operations  15.1 us (4%)
    all_gather x1, waiting for transfers between devices, on_device(): inverse_mine = lax.all_gather(inverse_rows, CHIP_AXES, axis=2, tiled=True)  79 us
    pallas_call x5, Pallas kernels, stencil_call(): pl.pallas_call(make_stencil_kernel(tuple(planes), len(rims) > 0, mode), g...  41.7 us
    ppermute x4, waiting for transfers between devices, rims_of(): hi = lax.ppermute(head, 'sub', [(i + 1, i) for i in range(count - 1)])  32.5 us
    pallas_call x2, Pallas kernels, correction_call(): pl.pallas_call(make_correction_kernel(tuple(columns)), grid=(ny // rows,)...  28.7 us
    ppermute x4, starting transfers between devices, rims_of(): hi = lax.ppermute(head, 'sub', [(i + 1, i) for i in range(count - 1)])  25.4 us
    ppermute x4, waiting for transfers between devices, rims_of(): lo = lax.ppermute(tail, 'sub', [(i, i + 1) for i in range(count - 1)])  20.6 us
    ppermute x3, waiting for transfers between devices, on_device(): lax.ppermute(totals, 'sub', [(i, i ^ step_size) for i in range(n_sub)])  13.7 us
    unnamed x30, local copies, waits for them, and re-layouts  10 us
  transfers between devices with their start and end apart: 18, of which 14 were waited for; matrix products, arithmetic and copies ran while one was open for 11% of the time, Pallas kernels for 10%

profile of v9, /device:TPU:6, one launch (start us, length us, event | category | flops | bytes accessed | tf_op | source)
XLA Modules:
  0.0 339.6 jit_solution(4346744464794727375)
XLA Ops:
  8.5 6.8 %collective-permute-start.1 = (f32[5,128,128]{2,1,0:T(8,128)S(1)}, f32[5,128,128]{2,1,0:T(8,128)S(1)}, u32[]{:S(2)}, u32[]{:S(2)}) collective-permute-start(f32[5,128,128]{2,1,0:T(8,128)S(1)} %get-tuple-element.104), channel_id=1, source_target_pairs={{16,0},{32,16},{48,32},{64,48},{80,64},{96,80},{112,96},{17,1},{33... | collective-permute-start | bytes 983048 | tf_op jit(solution)/shard_map/ppermute | solution.py:135
  15.3 1.9 collective-permute-start
  17.2 3.0 fusion.16
  20.2 7.5 %collective-permute-start.3 = (f32[4,5,128,128]{3,2,1,0:T(8,128)}, f32[4,5,128,128]{3,2,1,0:T(8,128)}, u32[]{:S(2)}, u32[]{:S(2)}) collective-permute-start(f32[4,5,128,128]{3,2,1,0:T(8,128)} %get-tuple-element.79), channel_id=1, source_target_pairs={{16,0},{32,16},{48,32},{64,48},{80,64},{96,80},{112,96},{17,1},{33... | collective-permute-start | bytes 3932168 | tf_op jit(solution)/shard_map/ppermute | solution.py:135
  27.8 1.9 collective-permute-start.2
  31.4 2.0 slice.262.refs_1_
  33.5 2.2 slice.265.refs_3_
  35.7 1.7 pad_maximum_fusion.2.refs_3_
  38.5 2.3 broadcast_select_fusion
  41.8 1.1 slice.255.refs_4_
  44.0 1.1 slice.261.refs_10_
  48.2 1.1 slice.259.refs_8_
  52.4 1.1 slice.257.refs_6_
  62.3 8.6 %shard_map.68 = (f32[4,14,64,128]{3,2,1,0:T(8,128)}, f32[4,14,64,128]{3,2,1,0:T(8,128)}) custom-call(s32[1]{0:T(128)} %bitcast.2.core_ref, f32[4,16,128,128]{3,2,1,0:T(8,128)} %refs_0_.3, f32[4,14,128,128]{3,2,1,0:T(8,128)} %slice.262.refs_1_, f32[14,128,128]{2,1,0:T(8,128)} %slice.234.refs_2_, f32[14,128,128]{2,1,0:T(8,128)} %slice.235.refs_3_, ...), custom_call_target="tpu_custom_call" | custom-call | tf_op jit(solution)/shard_map/pallas_call | solution.py:79
  70.9 10.1 %collective-permute-done.3.refs_2_ = f32[4,5,128,128]{3,2,1,0:T(8,128)} collective-permute-done((f32[4,5,128,128]{3,2,1,0:T(8,128)}, f32[4,5,128,128]{3,2,1,0:T(8,128)}, u32[]{:S(2)}, u32[]{:S(2)}) %collective-permute-start.3) | collective-permute-done | bytes 1310752 | tf_op jit(solution)/shard_map/ppermute | solution.py:135
  81.0 7.6 %collective-permute-done.2.refs_1_ = f32[4,5,128,128]{3,2,1,0:T(8,128)} collective-permute-done((f32[4,5,128,128]{3,2,1,0:T(8,128)S(1)}, f32[4,5,128,128]{3,2,1,0:T(8,128)}, u32[]{:S(2)}, u32[]{:S(2)}) %collective-permute-start.2) | collective-permute-done | bytes 1310752 | tf_op jit(solution)/shard_map/ppermute | solution.py:134
  88.6 8.1 %shard_map.69 = (f32[4,10,64,128]{3,2,1,0:T(8,128)}, f32[4,10,64,128]{3,2,1,0:T(8,128)}) custom-call(s32[1]{0:T(128)} %bitcast.2.core_ref, f32[4,16,128,128]{3,2,1,0:T(8,128)} %refs_0_.3, f32[4,5,128,128]{3,2,1,0:T(8,128)} %collective-permute-done.2.refs_1_, f32[4,5,128,128]{3,2,1,0:T(8,128)} %collective-permute-done.3.refs_2_, ...), custom_call_target="tpu_custom_call" | custom-call | tf_op jit(solution)/shard_map/pallas_call | solution.py:79
  97.9 2.0 collective-permute-done.5.refs_3_
  99.9 79.0 %all-gather.2.cloned.1.call-done.inv_ref = f32[16,24,64,128]{3,2,1,0:T(8,128)} async-done(((f32[16,24,8,128]{3,2,1,0:T(8,128)}), f32[16,24,64,128]{3,2,1,0:T(8,128)}) %all-gather.2.cloned.1.call-update) | async-done | bytes 12582928 | tf_op jit(solution)/shard_map/all_gather | solution.py:192
  178.9 14.3 %shard_map.70 = f32[8,16,64,128]{3,2,1,0:T(8,128)} custom-call(f32[24]{0:T(128)} %and_convert_fusion.mask_ref, f32[16,24,64,128]{3,2,1,0:T(8,128)} %all-gather.2.cloned.1.call-done.inv_ref, f32[4,14,64,128]{3,2,1,0:T(8,128)} %get-tuple-element.42.refs_0_, f32[4,10,64,128]{3,2,1,0:T(8,128)} %get-tuple-element.51.refs_1_, f32[4,14,64,128]{3,2,1,0:T(8,128)} %copy-done.8, ...), custom_call_target="tpu_custom_call" | custom-call | tf_op jit(solution)/shard_map/pallas_call | solution.py:119
  193.2 1.7 slice_bitcast_fusion.2
  195.0 4.3 %collective-permute-done.6 = f32[4,16,8,8,128]{4,3,2,1,0:T(8,128)} collective-permute-done((f32[4,16,8,8,128]{4,3,2,1,0:T(8,128)S(1)}, f32[4,16,8,8,128]{4,3,2,1,0:T(8,128)}, u32[]{:S(2)}, u32[]{:S(2)}) %collective-permute-start.6) | collective-permute-done | bytes 2097184 | tf_op jit(solution)/shard_map/ppermute | solution.py:247
  199.3 2.7 select_bitcast_fusion.3
  203.0 1.8 copy-done.4
  204.8 1.2 bitcast_add_fusion.1.refs_0_
  206.0 1.4 fusion.15
  208.4 9.2 %collective-permute-start.8 = (f32[4,5,128,128]{3,2,1,0:T(8,128)}, f32[4,5,128,128]{3,2,1,0:T(8,128)}, u32[]{:S(2)}, u32[]{:S(2)}) collective-permute-start(f32[4,5,128,128]{3,2,1,0:T(8,128)} %get-tuple-element.77), channel_id=1, source_target_pairs={{16,0},{32,16},{48,32},{64,48},{80,64},{96,80},{112,96},{17,1},{33... | collective-permute-start | bytes 3932168 | tf_op jit(solution)/shard_map/ppermute | solution.py:135
  217.6 1.9 collective-permute-start.7
  219.5 8.7 %shard_map.71 = (f32[4,14,64,128]{3,2,1,0:T(8,128)}, f32[4,14,64,128]{3,2,1,0:T(8,128)}) custom-call(s32[1]{0:T(128)} %bitcast.2.core_ref, f32[4,16,128,128]{3,2,1,0:T(8,128)} %copy-done.2, f32[4,14,128,128]{3,2,1,0:T(8,128)} %slice.262.refs_1_, f32[14,128,128]{2,1,0:T(8,128)} %slice.234.refs_2_, f32[14,128,128]{2,1,0:T(8,128)} %slice.235.refs_3_, ...), custom_call_target="tpu_custom_call" | custom-call | tf_op jit(solution)/shard_map/pallas_call | solution.py:79
  228.2 18.0 %collective-permute-done.8.refs_2_ = f32[4,5,128,128]{3,2,1,0:T(8,128)} collective-permute-done((f32[4,5,128,128]{3,2,1,0:T(8,128)}, f32[4,5,128,128]{3,2,1,0:T(8,128)}, u32[]{:S(2)}, u32[]{:S(2)}) %collective-permute-start.8) | collective-permute-done | bytes 1310752 | tf_op jit(solution)/shard_map/ppermute | solution.py:135
  246.2 7.5 %collective-permute-done.7.refs_1_ = f32[4,5,128,128]{3,2,1,0:T(8,128)} collective-permute-done((f32[4,5,128,128]{3,2,1,0:T(8,128)S(1)}, f32[4,5,128,128]{3,2,1,0:T(8,128)}, u32[]{:S(2)}, u32[]{:S(2)}) %collective-permute-start.7) | collective-permute-done | bytes 1310752 | tf_op jit(solution)/shard_map/ppermute | solution.py:134
  253.7 7.8 %shard_map.72 = (f32[4,10,64,128]{3,2,1,0:T(8,128)}, f32[4,10,64,128]{3,2,1,0:T(8,128)}) custom-call(s32[1]{0:T(128)} %bitcast.2.core_ref, f32[4,16,128,128]{3,2,1,0:T(8,128)} %copy-done.2, f32[4,5,128,128]{3,2,1,0:T(8,128)} %collective-permute-done.7.refs_1_, f32[4,5,128,128]{3,2,1,0:T(8,128)} %collective-permute-done.8.refs_2_, ...), custom_call_target="tpu_custom_call" | custom-call | tf_op jit(solution)/shard_map/pallas_call | solution.py:79
  261.6 3.2 collective-permute-done.10.refs_3_
  264.8 1.1 copy-done.11
  265.9 14.4 %shard_map.73 = f32[8,16,64,128]{3,2,1,0:T(8,128)} custom-call(f32[24]{0:T(128)} %and_convert_fusion.mask_ref, f32[16,24,64,128]{3,2,1,0:T(8,128)} %all-gather.2.cloned.1.call-done.inv_ref, f32[4,14,64,128]{3,2,1,0:T(8,128)} %get-tuple-element.54.refs_0_, f32[4,10,64,128]{3,2,1,0:T(8,128)} %get-tuple-element.55.refs_1_, f32[4,14,64,128]{3,2,1,0:T(8,128)} %copy-done.9, ...), custom_call_target="tpu_custom_call" | custom-call | tf_op jit(solution)/shard_map/pallas_call | solution.py:119
  280.3 1.9 slice_bitcast_fusion
  282.4 4.0 %collective-permute-done.11 = f32[4,16,8,8,128]{4,3,2,1,0:T(8,128)S(1)} collective-permute-done((f32[4,16,8,8,128]{4,3,2,1,0:T(8,128)S(1)}, f32[4,16,8,8,128]{4,3,2,1,0:T(8,128)S(1)}, u32[]{:S(2)}, u32[]{:S(2)}) %collective-permute-start.11) | collective-permute-done | bytes 2097184 | tf_op jit(solution)/shard_map/ppermute | solution.py:247
  287.7 1.8 copy-done.3
  289.4 1.2 bitcast_add_fusion.refs_0_
  290.6 2.0 copy-done.5
  292.7 1.9 collective-permute-start.13
  294.6 3.9 %collective-permute-start.12 = (f32[4,1,128,128]{3,2,1,0:T(8,128)S(1)}, f32[4,1,128,128]{3,2,1,0:T(8,128)S(1)}, u32[]{:S(2)}, u32[]{:S(2)}) collective-permute-start(f32[4,1,128,128]{3,2,1,0:T(8,128)S(1)} %get-tuple-element.76), channel_id=1, source_target_pairs={{0,16},{16,32},{32,48},{48,64},{64,80},{80,96},{96,112},{1,17},{17... | collective-permute-start | bytes 786440 | tf_op jit(solution)/shard_map/ppermute | solution.py:134
  298.5 4.4 %collective-permute-done.13.refs_2_ = f32[4,1,128,128]{3,2,1,0:T(8,128)S(1)} collective-permute-done((f32[4,1,128,128]{3,2,1,0:T(8,128)S(1)}, f32[4,1,128,128]{3,2,1,0:T(8,128)S(1)}, u32[]{:S(2)}, u32[]{:S(2)}) %collective-permute-start.13) | collective-permute-done | bytes 262176 | tf_op jit(solution)/shard_map/ppermute | solution.py:135
  302.9 5.5 %collective-permute-done.12.refs_1_ = f32[4,1,128,128]{3,2,1,0:T(8,128)S(1)} collective-permute-done((f32[4,1,128,128]{3,2,1,0:T(8,128)S(1)}, f32[4,1,128,128]{3,2,1,0:T(8,128)S(1)}, u32[]{:S(2)}, u32[]{:S(2)}) %collective-permute-start.12) | collective-permute-done | bytes 262176 | tf_op jit(solution)/shard_map/ppermute | solution.py:134
  309.2 8.5 %shard_map.74 = f32[4,8,128]{2,1,0:T(8,128)} custom-call(s32[1]{0:T(128)} %bitcast.2.core_ref, f32[4,16,128,128]{3,2,1,0:T(8,128)} %copy-done.5, f32[4,1,128,128]{3,2,1,0:T(8,128)} %copy-done.13, f32[4,1,128,128]{3,2,1,0:T(8,128)} %copy-done.12, f32[4,16,128,128]{3,2,1,0:T(8,128)} %slice.265.refs_3_, f32[16,128,128]{2,1,0:T(8,128)} %slice.255.refs_4_, ...), custom_call_target="tpu_custom_call" | custom-call | tf_op jit(solution)/shard_map/pallas_call | solution.py:79
  318.6 3.6 %collective-permute-done.14 = f32[4]{0:T(128)S(1)} collective-permute-done((f32[4]{0:T(128)S(1)}, f32[4]{0:T(128)S(1)}, u32[]{:S(2)}, u32[]{:S(2)}) %collective-permute-start.14) | collective-permute-done | bytes 48 | tf_op jit(solution)/shard_map/ppermute | solution.py:257
  322.1 5.1 %collective-permute-done.15 = f32[4]{0:T(128)S(1)} collective-permute-done((f32[4]{0:T(128)S(1)}, f32[4]{0:T(128)S(1)}, u32[]{:S(2)}, u32[]{:S(2)}) %collective-permute-start.15) | collective-permute-done | bytes 48 | tf_op jit(solution)/shard_map/ppermute | solution.py:257
  327.2 5.1 %collective-permute-done.16 = f32[4]{0:T(128)S(1)} collective-permute-done((f32[4]{0:T(128)S(1)}, f32[4]{0:T(128)S(1)}, u32[]{:S(2)}, u32[]{:S(2)}) %collective-permute-start.16) | collective-permute-done | bytes 48 | tf_op jit(solution)/shard_map/ppermute | solution.py:257
  (82 shorter events, 27.4 us)
Async XLA Ops:
  7.2 22.6 %copy-start = (s32[64,2]{0,1:T(2,128)S(1)}, s32[64,2]{0,1:T(2,128)}, u32[]{:S(2)}) copy-start(s32[64,2]{0,1:T(2,128)} %param.8) | copy-start | bytes 1540
  7.2 1.2 copy-start.7
  7.2 171.7 %all-gather.2.cloned.1.call-start = ((), (), s32[]{:S(2)}) async-start(), calls=%async_computation | async-start | bytes 14155776 | tf_op jit(solution)/shard_map/all_gather | solution.py:192
  8.5 30.0 %collective-permute-start.1 = (f32[5,128,128]{2,1,0:T(8,128)S(1)}, f32[5,128,128]{2,1,0:T(8,128)S(1)}, u32[]{:S(2)}, u32[]{:S(2)}) collective-permute-start(f32[5,128,128]{2,1,0:T(8,128)S(1)} %get-tuple-element.104), channel_id=1, source_target_pairs={{16,0},{32,16},{48,32},{64,48},{80,64},{96,80},{112,96},{17,1},{33... | collective-permute-start | bytes 983048 | tf_op jit(solution)/shard_map/ppermute | solution.py:135
  15.3 22.2 %collective-permute-start = (f32[5,128,128]{2,1,0:T(8,128)S(1)}, f32[5,128,128]{2,1,0:T(8,128)}, u32[]{:S(2)}, u32[]{:S(2)}) collective-permute-start(f32[5,128,128]{2,1,0:T(8,128)S(1)} %get-tuple-element.105), channel_id=1, source_target_pairs={{0,16},{16,32},{32,48},{48,64},{64,80},{80,96},{96,112},{1,17},{17... | collective-permute-start | bytes 983048 | tf_op jit(solution)/shard_map/ppermute | solution.py:134
  20.2 60.8 %collective-permute-start.3 = (f32[4,5,128,128]{3,2,1,0:T(8,128)}, f32[4,5,128,128]{3,2,1,0:T(8,128)}, u32[]{:S(2)}, u32[]{:S(2)}) collective-permute-start(f32[4,5,128,128]{3,2,1,0:T(8,128)} %get-tuple-element.79), channel_id=1, source_target_pairs={{16,0},{32,16},{48,32},{64,48},{80,64},{96,80},{112,96},{17,1},{33... | collective-permute-start | bytes 3932168 | tf_op jit(solution)/shard_map/ppermute | solution.py:135
  27.8 60.8 %collective-permute-start.2 = (f32[4,5,128,128]{3,2,1,0:T(8,128)S(1)}, f32[4,5,128,128]{3,2,1,0:T(8,128)}, u32[]{:S(2)}, u32[]{:S(2)}) collective-permute-start(f32[4,5,128,128]{3,2,1,0:T(8,128)S(1)} %get-tuple-element.80), channel_id=1, source_target_pairs={{0,16},{16,32},{32,48},{48,64},{64,80},{80,96},{96,112},{1,17},{17... | collective-permute-start | bytes 3932168 | tf_op jit(solution)/shard_map/ppermute | solution.py:134
  70.9 27.0 %collective-permute-start.4 = (f32[4,14,64,128]{3,2,1,0:T(8,128)}, f32[4,14,64,128]{3,2,1,0:T(8,128)S(1)}, u32[]{:S(2)}, u32[]{:S(2)}) collective-permute-start(f32[4,14,64,128]{3,2,1,0:T(8,128)} %get-tuple-element.52), channel_id=1, source_target_pairs={{0,1},{1,0},{2,3},{3,2},{4,5},{5,4},{6,7},{7,6},{8,9},{9,8},{10,11... | collective-permute-start | bytes 5505032 | tf_op jit(solution)/shard_map/ppermute | solution.py:240
  96.6 3.2 collective-permute-start.5
  97.9 81.0 %copy-start.8 = (f32[4,14,64,128]{3,2,1,0:T(8,128)}, f32[4,14,64,128]{3,2,1,0:T(8,128)S(1)}, u32[]{:S(2)}) copy-start(f32[4,14,64,128]{3,2,1,0:T(8,128)S(1)} %collective-permute-done.4.refs_2_) | copy-start | bytes 5505028
  99.9 79.0 %copy-start.10 = (f32[4,10,64,128]{3,2,1,0:T(8,128)}, f32[4,10,64,128]{3,2,1,0:T(8,128)S(1)}, u32[]{:S(2)}) copy-start(f32[4,10,64,128]{3,2,1,0:T(8,128)S(1)} %collective-permute-done.5.refs_3_) | copy-start | bytes 3932164
  194.9 4.4 %collective-permute-start.6 = (f32[4,16,8,8,128]{4,3,2,1,0:T(8,128)S(1)}, f32[4,16,8,8,128]{4,3,2,1,0:T(8,128)}, u32[]{:S(2)}, u32[]{:S(2)}) collective-permute-start(f32[4,16,8,8,128]{4,3,2,1,0:T(8,128)S(1)} %slice_bitcast_fusion.2), channel_id=1, source_target_pairs={{0,1},{1,0},{2,3},{3,2},{4,5},{5,4},{6,7},{7,6},{8,9},{9,8},{10,11... | collective-permute-start | bytes 6291464 | tf_op jit(solution)/shard_map/ppermute | solution.py:247
  202.6 2.2 copy-start.4
  206.0 2.4 copy-start.2
  208.4 37.8 %collective-permute-start.8 = (f32[4,5,128,128]{3,2,1,0:T(8,128)}, f32[4,5,128,128]{3,2,1,0:T(8,128)}, u32[]{:S(2)}, u32[]{:S(2)}) collective-permute-start(f32[4,5,128,128]{3,2,1,0:T(8,128)} %get-tuple-element.77), channel_id=1, source_target_pairs={{16,0},{32,16},{48,32},{64,48},{80,64},{96,80},{112,96},{17,1},{33... | collective-permute-start | bytes 3932168 | tf_op jit(solution)/shard_map/ppermute | solution.py:135
  217.6 36.2 %collective-permute-start.7 = (f32[4,5,128,128]{3,2,1,0:T(8,128)S(1)}, f32[4,5,128,128]{3,2,1,0:T(8,128)}, u32[]{:S(2)}, u32[]{:S(2)}) collective-permute-start(f32[4,5,128,128]{3,2,1,0:T(8,128)S(1)} %get-tuple-element.78), channel_id=1, source_target_pairs={{0,16},{16,32},{32,48},{48,64},{64,80},{80,96},{96,112},{1,17},{17... | collective-permute-start | bytes 3932168 | tf_op jit(solution)/shard_map/ppermute | solution.py:134
  228.2 33.4 %collective-permute-start.9 = (f32[4,14,64,128]{3,2,1,0:T(8,128)}, f32[4,14,64,128]{3,2,1,0:T(8,128)S(1)}, u32[]{:S(2)}, u32[]{:S(2)}) collective-permute-start(f32[4,14,64,128]{3,2,1,0:T(8,128)} %get-tuple-element.56), channel_id=1, source_target_pairs={{0,1},{1,0},{2,3},{3,2},{4,5},{5,4},{6,7},{7,6},{8,9},{9,8},{10,11... | collective-permute-start | bytes 5505032 | tf_op jit(solution)/shard_map/ppermute | solution.py:240
  261.6 3.2 collective-permute-start.10
  261.6 3.2 copy-start.9
  264.8 1.1 copy-start.11
  280.3 6.1 %copy-start.6 = (f32[8,16,64,128]{3,2,1,0:T(8,128)S(1)}, f32[8,16,64,128]{3,2,1,0:T(8,128)}, u32[]{:S(2)}) copy-start(f32[8,16,64,128]{3,2,1,0:T(8,128)} %shard_map.73) | copy-start | bytes 12582916
  282.2 4.2 %collective-permute-start.11 = (f32[4,16,8,8,128]{4,3,2,1,0:T(8,128)S(1)}, f32[4,16,8,8,128]{4,3,2,1,0:T(8,128)S(1)}, u32[]{:S(2)}, u32[]{:S(2)}) collective-permute-start(f32[4,16,8,8,128]{4,3,2,1,0:T(8,128)S(1)} %slice_bitcast_fusion), channel_id=1, source_target_pairs={{0,1},{1,0},{2,3},{3,2},{4,5},{5,4},{6,7},{7,6},{8,9},{9,8},{10,11... | collective-permute-start | bytes 6291464 | tf_op jit(solution)/shard_map/ppermute | solution.py:247
  287.2 2.2 copy-start.3
  290.6 2.0 copy-start.5
  292.7 10.2 %collective-permute-start.13 = (f32[4,1,128,128]{3,2,1,0:T(8,128)S(1)}, f32[4,1,128,128]{3,2,1,0:T(8,128)S(1)}, u32[]{:S(2)}, u32[]{:S(2)}) collective-permute-start(f32[4,1,128,128]{3,2,1,0:T(8,128)S(1)} %get-tuple-element.75), channel_id=1, source_target_pairs={{16,0},{32,16},{48,32},{64,48},{80,64},{96,80},{112,96},{17,1},{33... | collective-permute-start | bytes 786440 | tf_op jit(solution)/shard_map/ppermute | solution.py:135
  294.6 13.9 %collective-permute-start.12 = (f32[4,1,128,128]{3,2,1,0:T(8,128)S(1)}, f32[4,1,128,128]{3,2,1,0:T(8,128)S(1)}, u32[]{:S(2)}, u32[]{:S(2)}) collective-permute-start(f32[4,1,128,128]{3,2,1,0:T(8,128)S(1)} %get-tuple-element.76), channel_id=1, source_target_pairs={{0,16},{16,32},{32,48},{48,64},{64,80},{80,96},{96,112},{1,17},{17... | collective-permute-start | bytes 786440 | tf_op jit(solution)/shard_map/ppermute | solution.py:134
  302.9 5.5 %copy-start.12 = (f32[4,1,128,128]{3,2,1,0:T(8,128)}, f32[4,1,128,128]{3,2,1,0:T(8,128)S(1)}, u32[]{:S(2)}) copy-start(f32[4,1,128,128]{3,2,1,0:T(8,128)S(1)} %collective-permute-done.13.refs_2_) | copy-start | bytes 786436
  308.5 0.7 copy-start.13
  309.2 23.6 %copy-start.1 = (s32[64,2]{0,1:T(2,128)S(1)}, s32[64,2]{0,1:T(2,128)}, u32[]{:S(2)}) copy-start(s32[64,2]{0,1:T(2,128)} %param.8) | copy-start | bytes 1540
  318.5 3.6 %collective-permute-start.14 = (f32[4]{0:T(128)S(1)}, f32[4]{0:T(128)S(1)}, u32[]{:S(2)}, u32[]{:S(2)}) collective-permute-start(f32[4]{0:T(128)S(1)} %reduce_sum.9), channel_id=1, source_target_pairs={{0,16},{16,0},{32,48},{48,32},{64,80},{80,64},{96,112},{112,96},{1... | collective-permute-start | bytes 56 | tf_op jit(solution)/shard_map/ppermute | solution.py:257
  322.1 5.1 %collective-permute-start.15 = (f32[4]{0:T(128)S(1)}, f32[4]{0:T(128)S(1)}, u32[]{:S(2)}, u32[]{:S(2)}) collective-permute-start(f32[4]{0:T(128)S(1)} %add.107), channel_id=1, source_target_pairs={{0,32},{16,48},{32,0},{48,16},{64,96},{80,112},{96,64},{112,80},{1... | collective-permute-start | bytes 56 | tf_op jit(solution)/shard_map/ppermute | solution.py:257
  327.2 5.1 %collective-permute-start.16 = (f32[4]{0:T(128)S(1)}, f32[4]{0:T(128)S(1)}, u32[]{:S(2)}, u32[]{:S(2)}) collective-permute-start(f32[4]{0:T(128)S(1)} %add.108), channel_id=1, source_target_pairs={{0,64},{16,80},{32,96},{48,112},{64,0},{80,16},{96,32},{112,48},{1... | collective-permute-start | bytes 56 | tf_op jit(solution)/shard_map/ppermute | solution.py:257
Sparse Core Ops, SparseCore 0:
  9.6 169.2 all-gather.1

commit v10 on v9

--- a/solution.py
+++ b/solution.py
@@ -86,28 +86,34 @@
     )(core, v, *rims, st, *coefs)
 
 
-def make_correction_kernel(columns):
+def make_correction_kernel(columns, chunk=4):
     def kernel(mask_ref, inv_ref, *refs):
         out_ref = refs[-1]
         pieces = refs[:-1]
         n_out = inv_ref.shape[0]
         halves = len(pieces) // 2
 
-        def row(i, carry):
+        def rows(c, carry):
+            base = c * chunk
             accs = None
             for j, (piece, plane) in enumerate(columns):
-                w = inv_ref[i, j] * mask_ref[j]
+                weights = [inv_ref[base + k, j] * mask_ref[j] for k in range(chunk)]
                 terms = []
                 for half in range(2):
                     src_ref = pieces[half * halves + piece]
                     for s in range(src_ref.shape[0]):
-                        terms.append(w * src_ref[s, plane])
-                accs = terms if accs is None else [a + t for a, t in zip(accs, terms)]
-            for s, acc in enumerate(accs):
-                out_ref[s, i] = acc
+                        value = src_ref[s, plane]
+                        terms.append([w * value for w in weights])
+                if accs is None:
+                    accs = terms
+                else:
+                    accs = [[a + t for a, t in zip(acc_s, term_s)] for acc_s, term_s in zip(accs, terms)]
+            for s, acc_s in enumerate(accs):
+                for k in range(chunk):
+                    out_ref[s, base + k] = acc_s[k]
             return carry
 
-        lax.fori_loop(0, n_out, row, 0)
+        lax.fori_loop(0, n_out // chunk, rows, 0)
 
     return kernel
 

time: 341 us -> 339 us (level)
  no operation moved by 1% of the time
where the time goes in v10:
time: 339 us; the launch traced here: 338 us
  waiting for transfers between devices  160 us (47%)
  Pallas kernels  68.4 us (20%)
  local copies, waits for them, and re-layouts  38.3 us (11%)
  starting transfers between devices  35.5 us (10%)
  other arithmetic  20.3 us (6%)
  between operations  15.1 us (4%)
    all_gather x1, waiting for transfers between devices, on_device(): inverse_mine = lax.all_gather(inverse_rows, CHIP_AXES, axis=2, tiled=True)  79 us
    pallas_call x5, Pallas kernels, stencil_call(): pl.pallas_call(make_stencil_kernel(tuple(planes), len(rims) > 0, mode), g...  41.7 us
    ppermute x4, waiting for transfers between devices, rims_of(): hi = lax.ppermute(head, 'sub', [(i + 1, i) for i in range(count - 1)])  32.5 us
    pallas_call x2, Pallas kernels, correction_call(): pl.pallas_call(make_correction_kernel(tuple(columns)), grid=(ny // rows,)...  26.7 us
    ppermute x4, starting transfers between devices, rims_of(): hi = lax.ppermute(head, 'sub', [(i + 1, i) for i in range(count - 1)])  25.4 us
    ppermute x4, waiting for transfers between devices, rims_of(): lo = lax.ppermute(tail, 'sub', [(i, i + 1) for i in range(count - 1)])  20.6 us
    ppermute x3, waiting for transfers between devices, on_device(): lax.ppermute(totals, 'sub', [(i, i ^ step_size) for i in range(n_sub)])  13.7 us
    unnamed x30, local copies, waits for them, and re-layouts  10 us
  transfers between devices with their start and end apart: 18, of which 14 were waited for; matrix products, arithmetic and copies ran while one was open for 11% of the time, Pallas kernels for 10%

profile of v10, /device:TPU:6, one launch (start us, length us, event | category | flops | bytes accessed | tf_op | source)
XLA Modules:
  0.0 337.6 jit_solution(15638775899807811992)
XLA Ops:
  8.5 6.8 %collective-permute-start.1 = (f32[5,128,128]{2,1,0:T(8,128)S(1)}, f32[5,128,128]{2,1,0:T(8,128)S(1)}, u32[]{:S(2)}, u32[]{:S(2)}) collective-permute-start(f32[5,128,128]{2,1,0:T(8,128)S(1)} %get-tuple-element.104), channel_id=1, source_target_pairs={{16,0},{32,16},{48,32},{64,48},{80,64},{96,80},{112,96},{17,1},{33... | collective-permute-start | bytes 983048 | tf_op jit(solution)/shard_map/ppermute | solution.py:141
  15.3 1.9 collective-permute-start
  17.2 3.0 fusion.16
  20.2 7.5 %collective-permute-start.3 = (f32[4,5,128,128]{3,2,1,0:T(8,128)}, f32[4,5,128,128]{3,2,1,0:T(8,128)}, u32[]{:S(2)}, u32[]{:S(2)}) collective-permute-start(f32[4,5,128,128]{3,2,1,0:T(8,128)} %get-tuple-element.79), channel_id=1, source_target_pairs={{16,0},{32,16},{48,32},{64,48},{80,64},{96,80},{112,96},{17,1},{33... | collective-permute-start | bytes 3932168 | tf_op jit(solution)/shard_map/ppermute | solution.py:141
  27.8 1.9 collective-permute-start.2
  31.4 2.0 slice.262.refs_1_
  33.5 2.2 slice.265.refs_3_
  35.7 1.7 pad_maximum_fusion.2.refs_3_
  38.5 2.3 broadcast_select_fusion
  41.8 1.1 slice.255.refs_4_
  44.0 1.1 slice.261.refs_10_
  48.2 1.1 slice.259.refs_8_
  52.4 1.1 slice.257.refs_6_
  62.3 8.6 %shard_map.68 = (f32[4,14,64,128]{3,2,1,0:T(8,128)}, f32[4,14,64,128]{3,2,1,0:T(8,128)}) custom-call(s32[1]{0:T(128)} %bitcast.2.core_ref, f32[4,16,128,128]{3,2,1,0:T(8,128)} %refs_0_.3, f32[4,14,128,128]{3,2,1,0:T(8,128)} %slice.262.refs_1_, f32[14,128,128]{2,1,0:T(8,128)} %slice.234.refs_2_, f32[14,128,128]{2,1,0:T(8,128)} %slice.235.refs_3_, ...), custom_call_target="tpu_custom_call" | custom-call | tf_op jit(solution)/shard_map/pallas_call | solution.py:79
  70.9 10.1 %collective-permute-done.3.refs_2_ = f32[4,5,128,128]{3,2,1,0:T(8,128)} collective-permute-done((f32[4,5,128,128]{3,2,1,0:T(8,128)}, f32[4,5,128,128]{3,2,1,0:T(8,128)}, u32[]{:S(2)}, u32[]{:S(2)}) %collective-permute-start.3) | collective-permute-done | bytes 1310752 | tf_op jit(solution)/shard_map/ppermute | solution.py:141
  81.0 7.6 %collective-permute-done.2.refs_1_ = f32[4,5,128,128]{3,2,1,0:T(8,128)} collective-permute-done((f32[4,5,128,128]{3,2,1,0:T(8,128)S(1)}, f32[4,5,128,128]{3,2,1,0:T(8,128)}, u32[]{:S(2)}, u32[]{:S(2)}) %collective-permute-start.2) | collective-permute-done | bytes 1310752 | tf_op jit(solution)/shard_map/ppermute | solution.py:140
  88.6 8.1 %shard_map.69 = (f32[4,10,64,128]{3,2,1,0:T(8,128)}, f32[4,10,64,128]{3,2,1,0:T(8,128)}) custom-call(s32[1]{0:T(128)} %bitcast.2.core_ref, f32[4,16,128,128]{3,2,1,0:T(8,128)} %refs_0_.3, f32[4,5,128,128]{3,2,1,0:T(8,128)} %collective-permute-done.2.refs_1_, f32[4,5,128,128]{3,2,1,0:T(8,128)} %collective-permute-done.3.refs_2_, ...), custom_call_target="tpu_custom_call" | custom-call | tf_op jit(solution)/shard_map/pallas_call | solution.py:79
  97.9 2.0 collective-permute-done.5.refs_3_
  99.9 79.0 %all-gather.2.cloned.1.call-done.inv_ref = f32[16,24,64,128]{3,2,1,0:T(8,128)} async-done(((f32[16,24,8,128]{3,2,1,0:T(8,128)}), f32[16,24,64,128]{3,2,1,0:T(8,128)}) %all-gather.2.cloned.1.call-update) | async-done | bytes 12582928 | tf_op jit(solution)/shard_map/all_gather | solution.py:198
  178.9 13.3 %shard_map.70 = f32[8,16,64,128]{3,2,1,0:T(8,128)} custom-call(f32[24]{0:T(128)} %and_convert_fusion.mask_ref, f32[16,24,64,128]{3,2,1,0:T(8,128)} %all-gather.2.cloned.1.call-done.inv_ref, f32[4,14,64,128]{3,2,1,0:T(8,128)} %get-tuple-element.42.refs_0_, f32[4,10,64,128]{3,2,1,0:T(8,128)} %get-tuple-element.51.refs_1_, f32[4,14,64,128]{3,2,1,0:T(8,128)} %copy-done.8, ...), custom_call_target="tpu_custom_call" | custom-call | tf_op jit(solution)/shard_map/pallas_call | solution.py:125
  192.2 1.7 slice_bitcast_fusion.2
  194.0 4.3 %collective-permute-done.6 = f32[4,16,8,8,128]{4,3,2,1,0:T(8,128)} collective-permute-done((f32[4,16,8,8,128]{4,3,2,1,0:T(8,128)S(1)}, f32[4,16,8,8,128]{4,3,2,1,0:T(8,128)}, u32[]{:S(2)}, u32[]{:S(2)}) %collective-permute-start.6) | collective-permute-done | bytes 2097184 | tf_op jit(solution)/shard_map/ppermute | solution.py:253
  198.3 2.7 select_bitcast_fusion.3
  202.0 1.8 copy-done.4
  203.8 1.2 bitcast_add_fusion.1.refs_0_
  205.0 1.4 fusion.15
  207.4 9.2 %collective-permute-start.8 = (f32[4,5,128,128]{3,2,1,0:T(8,128)}, f32[4,5,128,128]{3,2,1,0:T(8,128)}, u32[]{:S(2)}, u32[]{:S(2)}) collective-permute-start(f32[4,5,128,128]{3,2,1,0:T(8,128)} %get-tuple-element.77), channel_id=1, source_target_pairs={{16,0},{32,16},{48,32},{64,48},{80,64},{96,80},{112,96},{17,1},{33... | collective-permute-start | bytes 3932168 | tf_op jit(solution)/shard_map/ppermute | solution.py:141
  216.6 1.9 collective-permute-start.7
  218.5 8.7 %shard_map.71 = (f32[4,14,64,128]{3,2,1,0:T(8,128)}, f32[4,14,64,128]{3,2,1,0:T(8,128)}) custom-call(s32[1]{0:T(128)} %bitcast.2.core_ref, f32[4,16,128,128]{3,2,1,0:T(8,128)} %copy-done.2, f32[4,14,128,128]{3,2,1,0:T(8,128)} %slice.262.refs_1_, f32[14,128,128]{2,1,0:T(8,128)} %slice.234.refs_2_, f32[14,128,128]{2,1,0:T(8,128)} %slice.235.refs_3_, ...), custom_call_target="tpu_custom_call" | custom-call | tf_op jit(solution)/shard_map/pallas_call | solution.py:79
  227.2 18.0 %collective-permute-done.8.refs_2_ = f32[4,5,128,128]{3,2,1,0:T(8,128)} collective-permute-done((f32[4,5,128,128]{3,2,1,0:T(8,128)}, f32[4,5,128,128]{3,2,1,0:T(8,128)}, u32[]{:S(2)}, u32[]{:S(2)}) %collective-permute-start.8) | collective-permute-done | bytes 1310752 | tf_op jit(solution)/shard_map/ppermute | solution.py:141
  245.2 7.5 %collective-permute-done.7.refs_1_ = f32[4,5,128,128]{3,2,1,0:T(8,128)} collective-permute-done((f32[4,5,128,128]{3,2,1,0:T(8,128)S(1)}, f32[4,5,128,128]{3,2,1,0:T(8,128)}, u32[]{:S(2)}, u32[]{:S(2)}) %collective-permute-start.7) | collective-permute-done | bytes 1310752 | tf_op jit(solution)/shard_map/ppermute | solution.py:140
  252.7 7.8 %shard_map.72 = (f32[4,10,64,128]{3,2,1,0:T(8,128)}, f32[4,10,64,128]{3,2,1,0:T(8,128)}) custom-call(s32[1]{0:T(128)} %bitcast.2.core_ref, f32[4,16,128,128]{3,2,1,0:T(8,128)} %copy-done.2, f32[4,5,128,128]{3,2,1,0:T(8,128)} %collective-permute-done.7.refs_1_, f32[4,5,128,128]{3,2,1,0:T(8,128)} %collective-permute-done.8.refs_2_, ...), custom_call_target="tpu_custom_call" | custom-call | tf_op jit(solution)/shard_map/pallas_call | solution.py:79
  260.6 3.2 collective-permute-done.10.refs_3_
  263.8 1.1 copy-done.11
  264.9 13.4 %shard_map.73 = f32[8,16,64,128]{3,2,1,0:T(8,128)} custom-call(f32[24]{0:T(128)} %and_convert_fusion.mask_ref, f32[16,24,64,128]{3,2,1,0:T(8,128)} %all-gather.2.cloned.1.call-done.inv_ref, f32[4,14,64,128]{3,2,1,0:T(8,128)} %get-tuple-element.54.refs_0_, f32[4,10,64,128]{3,2,1,0:T(8,128)} %get-tuple-element.55.refs_1_, f32[4,14,64,128]{3,2,1,0:T(8,128)} %copy-done.9, ...), custom_call_target="tpu_custom_call" | custom-call | tf_op jit(solution)/shard_map/pallas_call | solution.py:125
  278.3 1.9 slice_bitcast_fusion
  280.4 4.0 %collective-permute-done.11 = f32[4,16,8,8,128]{4,3,2,1,0:T(8,128)S(1)} collective-permute-done((f32[4,16,8,8,128]{4,3,2,1,0:T(8,128)S(1)}, f32[4,16,8,8,128]{4,3,2,1,0:T(8,128)S(1)}, u32[]{:S(2)}, u32[]{:S(2)}) %collective-permute-start.11) | collective-permute-done | bytes 2097184 | tf_op jit(solution)/shard_map/ppermute | solution.py:253
  285.7 1.8 copy-done.3
  287.4 1.2 bitcast_add_fusion.refs_0_
  288.6 2.0 copy-done.5
  290.7 1.9 collective-permute-start.13
  292.6 3.9 %collective-permute-start.12 = (f32[4,1,128,128]{3,2,1,0:T(8,128)S(1)}, f32[4,1,128,128]{3,2,1,0:T(8,128)S(1)}, u32[]{:S(2)}, u32[]{:S(2)}) collective-permute-start(f32[4,1,128,128]{3,2,1,0:T(8,128)S(1)} %get-tuple-element.76), channel_id=1, source_target_pairs={{0,16},{16,32},{32,48},{48,64},{64,80},{80,96},{96,112},{1,17},{17... | collective-permute-start | bytes 786440 | tf_op jit(solution)/shard_map/ppermute | solution.py:140
  296.5 4.4 %collective-permute-done.13.refs_2_ = f32[4,1,128,128]{3,2,1,0:T(8,128)S(1)} collective-permute-done((f32[4,1,128,128]{3,2,1,0:T(8,128)S(1)}, f32[4,1,128,128]{3,2,1,0:T(8,128)S(1)}, u32[]{:S(2)}, u32[]{:S(2)}) %collective-permute-start.13) | collective-permute-done | bytes 262176 | tf_op jit(solution)/shard_map/ppermute | solution.py:141
  300.9 5.5 %collective-permute-done.12.refs_1_ = f32[4,1,128,128]{3,2,1,0:T(8,128)S(1)} collective-permute-done((f32[4,1,128,128]{3,2,1,0:T(8,128)S(1)}, f32[4,1,128,128]{3,2,1,0:T(8,128)S(1)}, u32[]{:S(2)}, u32[]{:S(2)}) %collective-permute-start.12) | collective-permute-done | bytes 262176 | tf_op jit(solution)/shard_map/ppermute | solution.py:140
  307.2 8.5 %shard_map.74 = f32[4,8,128]{2,1,0:T(8,128)} custom-call(s32[1]{0:T(128)} %bitcast.2.core_ref, f32[4,16,128,128]{3,2,1,0:T(8,128)} %copy-done.5, f32[4,1,128,128]{3,2,1,0:T(8,128)} %copy-done.13, f32[4,1,128,128]{3,2,1,0:T(8,128)} %copy-done.12, f32[4,16,128,128]{3,2,1,0:T(8,128)} %slice.265.refs_3_, f32[16,128,128]{2,1,0:T(8,128)} %slice.255.refs_4_, ...), custom_call_target="tpu_custom_call" | custom-call | tf_op jit(solution)/shard_map/pallas_call | solution.py:79
  316.5 3.6 %collective-permute-done.14 = f32[4]{0:T(128)S(1)} collective-permute-done((f32[4]{0:T(128)S(1)}, f32[4]{0:T(128)S(1)}, u32[]{:S(2)}, u32[]{:S(2)}) %collective-permute-start.14) | collective-permute-done | bytes 48 | tf_op jit(solution)/shard_map/ppermute | solution.py:263
  320.1 5.1 %collective-permute-done.15 = f32[4]{0:T(128)S(1)} collective-permute-done((f32[4]{0:T(128)S(1)}, f32[4]{0:T(128)S(1)}, u32[]{:S(2)}, u32[]{:S(2)}) %collective-permute-start.15) | collective-permute-done | bytes 48 | tf_op jit(solution)/shard_map/ppermute | solution.py:263
  325.2 5.1 %collective-permute-done.16 = f32[4]{0:T(128)S(1)} collective-permute-done((f32[4]{0:T(128)S(1)}, f32[4]{0:T(128)S(1)}, u32[]{:S(2)}, u32[]{:S(2)}) %collective-permute-start.16) | collective-permute-done | bytes 48 | tf_op jit(solution)/shard_map/ppermute | solution.py:263
  (82 shorter events, 27.4 us)
Async XLA Ops:
  7.2 22.6 %copy-start = (s32[64,2]{0,1:T(2,128)S(1)}, s32[64,2]{0,1:T(2,128)}, u32[]{:S(2)}) copy-start(s32[64,2]{0,1:T(2,128)} %param.8) | copy-start | bytes 1540
  7.2 1.2 copy-start.7
  7.2 171.7 %all-gather.2.cloned.1.call-start = ((), (), s32[]{:S(2)}) async-start(), calls=%async_computation | async-start | bytes 14155776 | tf_op jit(solution)/shard_map/all_gather | solution.py:198
  8.5 30.0 %collective-permute-start.1 = (f32[5,128,128]{2,1,0:T(8,128)S(1)}, f32[5,128,128]{2,1,0:T(8,128)S(1)}, u32[]{:S(2)}, u32[]{:S(2)}) collective-permute-start(f32[5,128,128]{2,1,0:T(8,128)S(1)} %get-tuple-element.104), channel_id=1, source_target_pairs={{16,0},{32,16},{48,32},{64,48},{80,64},{96,80},{112,96},{17,1},{33... | collective-permute-start | bytes 983048 | tf_op jit(solution)/shard_map/ppermute | solution.py:141
  15.3 22.2 %collective-permute-start = (f32[5,128,128]{2,1,0:T(8,128)S(1)}, f32[5,128,128]{2,1,0:T(8,128)}, u32[]{:S(2)}, u32[]{:S(2)}) collective-permute-start(f32[5,128,128]{2,1,0:T(8,128)S(1)} %get-tuple-element.105), channel_id=1, source_target_pairs={{0,16},{16,32},{32,48},{48,64},{64,80},{80,96},{96,112},{1,17},{17... | collective-permute-start | bytes 983048 | tf_op jit(solution)/shard_map/ppermute | solution.py:140
  20.2 60.8 %collective-permute-start.3 = (f32[4,5,128,128]{3,2,1,0:T(8,128)}, f32[4,5,128,128]{3,2,1,0:T(8,128)}, u32[]{:S(2)}, u32[]{:S(2)}) collective-permute-start(f32[4,5,128,128]{3,2,1,0:T(8,128)} %get-tuple-element.79), channel_id=1, source_target_pairs={{16,0},{32,16},{48,32},{64,48},{80,64},{96,80},{112,96},{17,1},{33... | collective-permute-start | bytes 3932168 | tf_op jit(solution)/shard_map/ppermute | solution.py:141
  27.8 60.8 %collective-permute-start.2 = (f32[4,5,128,128]{3,2,1,0:T(8,128)S(1)}, f32[4,5,128,128]{3,2,1,0:T(8,128)}, u32[]{:S(2)}, u32[]{:S(2)}) collective-permute-start(f32[4,5,128,128]{3,2,1,0:T(8,128)S(1)} %get-tuple-element.80), channel_id=1, source_target_pairs={{0,16},{16,32},{32,48},{48,64},{64,80},{80,96},{96,112},{1,17},{17... | collective-permute-start | bytes 3932168 | tf_op jit(solution)/shard_map/ppermute | solution.py:140
  70.9 27.0 %collective-permute-start.4 = (f32[4,14,64,128]{3,2,1,0:T(8,128)}, f32[4,14,64,128]{3,2,1,0:T(8,128)S(1)}, u32[]{:S(2)}, u32[]{:S(2)}) collective-permute-start(f32[4,14,64,128]{3,2,1,0:T(8,128)} %get-tuple-element.52), channel_id=1, source_target_pairs={{0,1},{1,0},{2,3},{3,2},{4,5},{5,4},{6,7},{7,6},{8,9},{9,8},{10,11... | collective-permute-start | bytes 5505032 | tf_op jit(solution)/shard_map/ppermute | solution.py:246
  96.6 3.2 collective-permute-start.5
  97.9 81.0 %copy-start.8 = (f32[4,14,64,128]{3,2,1,0:T(8,128)}, f32[4,14,64,128]{3,2,1,0:T(8,128)S(1)}, u32[]{:S(2)}) copy-start(f32[4,14,64,128]{3,2,1,0:T(8,128)S(1)} %collective-permute-done.4.refs_2_) | copy-start | bytes 5505028
  99.9 79.0 %copy-start.10 = (f32[4,10,64,128]{3,2,1,0:T(8,128)}, f32[4,10,64,128]{3,2,1,0:T(8,128)S(1)}, u32[]{:S(2)}) copy-start(f32[4,10,64,128]{3,2,1,0:T(8,128)S(1)} %collective-permute-done.5.refs_3_) | copy-start | bytes 3932164
  193.9 4.4 %collective-permute-start.6 = (f32[4,16,8,8,128]{4,3,2,1,0:T(8,128)S(1)}, f32[4,16,8,8,128]{4,3,2,1,0:T(8,128)}, u32[]{:S(2)}, u32[]{:S(2)}) collective-permute-start(f32[4,16,8,8,128]{4,3,2,1,0:T(8,128)S(1)} %slice_bitcast_fusion.2), channel_id=1, source_target_pairs={{0,1},{1,0},{2,3},{3,2},{4,5},{5,4},{6,7},{7,6},{8,9},{9,8},{10,11... | collective-permute-start | bytes 6291464 | tf_op jit(solution)/shard_map/ppermute | solution.py:253
  201.6 2.2 copy-start.4
  205.0 2.4 copy-start.2
  207.4 37.8 %collective-permute-start.8 = (f32[4,5,128,128]{3,2,1,0:T(8,128)}, f32[4,5,128,128]{3,2,1,0:T(8,128)}, u32[]{:S(2)}, u32[]{:S(2)}) collective-permute-start(f32[4,5,128,128]{3,2,1,0:T(8,128)} %get-tuple-element.77), channel_id=1, source_target_pairs={{16,0},{32,16},{48,32},{64,48},{80,64},{96,80},{112,96},{17,1},{33... | collective-permute-start | bytes 3932168 | tf_op jit(solution)/shard_map/ppermute | solution.py:141
  216.6 36.2 %collective-permute-start.7 = (f32[4,5,128,128]{3,2,1,0:T(8,128)S(1)}, f32[4,5,128,128]{3,2,1,0:T(8,128)}, u32[]{:S(2)}, u32[]{:S(2)}) collective-permute-start(f32[4,5,128,128]{3,2,1,0:T(8,128)S(1)} %get-tuple-element.78), channel_id=1, source_target_pairs={{0,16},{16,32},{32,48},{48,64},{64,80},{80,96},{96,112},{1,17},{17... | collective-permute-start | bytes 3932168 | tf_op jit(solution)/shard_map/ppermute | solution.py:140
  227.2 33.4 %collective-permute-start.9 = (f32[4,14,64,128]{3,2,1,0:T(8,128)}, f32[4,14,64,128]{3,2,1,0:T(8,128)S(1)}, u32[]{:S(2)}, u32[]{:S(2)}) collective-permute-start(f32[4,14,64,128]{3,2,1,0:T(8,128)} %get-tuple-element.56), channel_id=1, source_target_pairs={{0,1},{1,0},{2,3},{3,2},{4,5},{5,4},{6,7},{7,6},{8,9},{9,8},{10,11... | collective-permute-start | bytes 5505032 | tf_op jit(solution)/shard_map/ppermute | solution.py:246
  260.6 3.2 collective-permute-start.10
  260.6 3.2 copy-start.9
  263.8 1.1 copy-start.11
  278.3 6.1 %copy-start.6 = (f32[8,16,64,128]{3,2,1,0:T(8,128)S(1)}, f32[8,16,64,128]{3,2,1,0:T(8,128)}, u32[]{:S(2)}) copy-start(f32[8,16,64,128]{3,2,1,0:T(8,128)} %shard_map.73) | copy-start | bytes 12582916
  280.2 4.2 %collective-permute-start.11 = (f32[4,16,8,8,128]{4,3,2,1,0:T(8,128)S(1)}, f32[4,16,8,8,128]{4,3,2,1,0:T(8,128)S(1)}, u32[]{:S(2)}, u32[]{:S(2)}) collective-permute-start(f32[4,16,8,8,128]{4,3,2,1,0:T(8,128)S(1)} %slice_bitcast_fusion), channel_id=1, source_target_pairs={{0,1},{1,0},{2,3},{3,2},{4,5},{5,4},{6,7},{7,6},{8,9},{9,8},{10,11... | collective-permute-start | bytes 6291464 | tf_op jit(solution)/shard_map/ppermute | solution.py:253
  285.2 2.2 copy-start.3
  288.6 2.0 copy-start.5
  290.7 10.2 %collective-permute-start.13 = (f32[4,1,128,128]{3,2,1,0:T(8,128)S(1)}, f32[4,1,128,128]{3,2,1,0:T(8,128)S(1)}, u32[]{:S(2)}, u32[]{:S(2)}) collective-permute-start(f32[4,1,128,128]{3,2,1,0:T(8,128)S(1)} %get-tuple-element.75), channel_id=1, source_target_pairs={{16,0},{32,16},{48,32},{64,48},{80,64},{96,80},{112,96},{17,1},{33... | collective-permute-start | bytes 786440 | tf_op jit(solution)/shard_map/ppermute | solution.py:141
  292.6 13.9 %collective-permute-start.12 = (f32[4,1,128,128]{3,2,1,0:T(8,128)S(1)}, f32[4,1,128,128]{3,2,1,0:T(8,128)S(1)}, u32[]{:S(2)}, u32[]{:S(2)}) collective-permute-start(f32[4,1,128,128]{3,2,1,0:T(8,128)S(1)} %get-tuple-element.76), channel_id=1, source_target_pairs={{0,16},{16,32},{32,48},{48,64},{64,80},{80,96},{96,112},{1,17},{17... | collective-permute-start | bytes 786440 | tf_op jit(solution)/shard_map/ppermute | solution.py:140
  300.9 5.5 %copy-start.12 = (f32[4,1,128,128]{3,2,1,0:T(8,128)}, f32[4,1,128,128]{3,2,1,0:T(8,128)S(1)}, u32[]{:S(2)}) copy-start(f32[4,1,128,128]{3,2,1,0:T(8,128)S(1)} %collective-permute-done.13.refs_2_) | copy-start | bytes 786436
  306.5 0.7 copy-start.13
  307.2 23.6 %copy-start.1 = (s32[64,2]{0,1:T(2,128)S(1)}, s32[64,2]{0,1:T(2,128)}, u32[]{:S(2)}) copy-start(s32[64,2]{0,1:T(2,128)} %param.8) | copy-start | bytes 1540
  316.5 3.6 %collective-permute-start.14 = (f32[4]{0:T(128)S(1)}, f32[4]{0:T(128)S(1)}, u32[]{:S(2)}, u32[]{:S(2)}) collective-permute-start(f32[4]{0:T(128)S(1)} %reduce_sum.9), channel_id=1, source_target_pairs={{0,16},{16,0},{32,48},{48,32},{64,80},{80,64},{96,112},{112,96},{1... | collective-permute-start | bytes 56 | tf_op jit(solution)/shard_map/ppermute | solution.py:263
  320.1 5.1 %collective-permute-start.15 = (f32[4]{0:T(128)S(1)}, f32[4]{0:T(128)S(1)}, u32[]{:S(2)}, u32[]{:S(2)}) collective-permute-start(f32[4]{0:T(128)S(1)} %add.107), channel_id=1, source_target_pairs={{0,32},{16,48},{32,0},{48,16},{64,96},{80,112},{96,64},{112,80},{1... | collective-permute-start | bytes 56 | tf_op jit(solution)/shard_map/ppermute | solution.py:263
  325.2 5.1 %collective-permute-start.16 = (f32[4]{0:T(128)S(1)}, f32[4]{0:T(128)S(1)}, u32[]{:S(2)}, u32[]{:S(2)}) collective-permute-start(f32[4]{0:T(128)S(1)} %add.108), channel_id=1, source_target_pairs={{0,64},{16,80},{32,96},{48,112},{64,0},{80,16},{96,32},{112,48},{1... | collective-permute-start | bytes 56 | tf_op jit(solution)/shard_map/ppermute | solution.py:263
Sparse Core Ops, SparseCore 0:
  9.6 169.2 all-gather.1

commit v11 on v10

--- a/solution.py
+++ b/solution.py
@@ -86,7 +86,7 @@
     )(core, v, *rims, st, *coefs)
 
 
-def make_correction_kernel(columns, chunk=4):
+def make_correction_kernel(columns, chunk=2):
     def kernel(mask_ref, inv_ref, *refs):
         out_ref = refs[-1]
         pieces = refs[:-1]
@@ -118,7 +118,7 @@
     return kernel
 
 
-def correction_call(mask, inv, own_pieces, got_pieces, columns, rows=8):
+def correction_call(mask, inv, own_pieces, got_pieces, columns, rows=16):
     n_out, n_col, ny, nz = inv.shape
     n_src = sum(p.shape[0] for p in own_pieces[:1]) * 2
     specs = [pl.BlockSpec((p.shape[0], p.shape[1], rows, nz), lambda b: (0, 0, b, 0)) for p in own_pieces + got_pieces]

time: 339 us -> 336 us (level)
  no operation moved by 1% of the time
where the time goes in v11:
time: 336 us
  waiting for transfers between devices  160 us (48%)
  Pallas kernels  66.5 us (20%)
  local copies, waits for them, and re-layouts  38.3 us (11%)
  starting transfers between devices  35.5 us (11%)
  other arithmetic  20.3 us (6%)
  between operations  15.1 us (4%)
    all_gather x1, waiting for transfers between devices, on_device(): inverse_mine = lax.all_gather(inverse_rows, CHIP_AXES, axis=2, tiled=True)  79 us
    pallas_call x5, Pallas kernels, stencil_call(): pl.pallas_call(make_stencil_kernel(tuple(planes), len(rims) > 0, mode), g...  41.7 us
    ppermute x4, waiting for transfers between devices, rims_of(): hi = lax.ppermute(head, 'sub', [(i + 1, i) for i in range(count - 1)])  32.5 us
    ppermute x4, starting transfers between devices, rims_of(): hi = lax.ppermute(head, 'sub', [(i + 1, i) for i in range(count - 1)])  25.4 us
    pallas_call x2, Pallas kernels, correction_call(): pl.pallas_call(make_correction_kernel(tuple(columns)), grid=(ny // rows,)...  24.8 us
    ppermute x4, waiting for transfers between devices, rims_of(): lo = lax.ppermute(tail, 'sub', [(i, i + 1) for i in range(count - 1)])  20.6 us
    ppermute x3, waiting for transfers between devices, on_device(): lax.ppermute(totals, 'sub', [(i, i ^ step_size) for i in range(n_sub)])  13.7 us
    unnamed x30, local copies, waits for them, and re-layouts  10 us
  transfers between devices with their start and end apart: 18, of which 14 were waited for; matrix products, arithmetic and copies ran while one was open for 11% of the time, Pallas kernels for 10%

profile of v11, /device:TPU:6, one launch (start us, length us, event | category | flops | bytes accessed | tf_op | source)
XLA Modules:
  0.0 335.7 jit_solution(17189660925250447958)
XLA Ops:
  8.5 6.8 %collective-permute-start.1 = (f32[5,128,128]{2,1,0:T(8,128)S(1)}, f32[5,128,128]{2,1,0:T(8,128)S(1)}, u32[]{:S(2)}, u32[]{:S(2)}) collective-permute-start(f32[5,128,128]{2,1,0:T(8,128)S(1)} %get-tuple-element.104), channel_id=1, source_target_pairs={{16,0},{32,16},{48,32},{64,48},{80,64},{96,80},{112,96},{17,1},{33... | collective-permute-start | bytes 983048 | tf_op jit(solution)/shard_map/ppermute | solution.py:141
  15.3 1.9 collective-permute-start
  17.2 3.0 fusion.16
  20.2 7.5 %collective-permute-start.3 = (f32[4,5,128,128]{3,2,1,0:T(8,128)}, f32[4,5,128,128]{3,2,1,0:T(8,128)}, u32[]{:S(2)}, u32[]{:S(2)}) collective-permute-start(f32[4,5,128,128]{3,2,1,0:T(8,128)} %get-tuple-element.79), channel_id=1, source_target_pairs={{16,0},{32,16},{48,32},{64,48},{80,64},{96,80},{112,96},{17,1},{33... | collective-permute-start | bytes 3932168 | tf_op jit(solution)/shard_map/ppermute | solution.py:141
  27.8 1.9 collective-permute-start.2
  31.4 2.0 slice.262.refs_1_
  33.5 2.2 slice.265.refs_3_
  35.7 1.7 pad_maximum_fusion.2.refs_3_
  38.5 2.3 broadcast_select_fusion
  41.8 1.1 slice.255.refs_4_
  44.0 1.1 slice.261.refs_10_
  48.2 1.1 slice.259.refs_8_
  52.4 1.1 slice.257.refs_6_
  62.3 8.6 %shard_map.68 = (f32[4,14,64,128]{3,2,1,0:T(8,128)}, f32[4,14,64,128]{3,2,1,0:T(8,128)}) custom-call(s32[1]{0:T(128)} %bitcast.2.core_ref, f32[4,16,128,128]{3,2,1,0:T(8,128)} %refs_0_.3, f32[4,14,128,128]{3,2,1,0:T(8,128)} %slice.262.refs_1_, f32[14,128,128]{2,1,0:T(8,128)} %slice.234.refs_2_, f32[14,128,128]{2,1,0:T(8,128)} %slice.235.refs_3_, ...), custom_call_target="tpu_custom_call" | custom-call | tf_op jit(solution)/shard_map/pallas_call | solution.py:79
  70.9 10.1 %collective-permute-done.3.refs_2_ = f32[4,5,128,128]{3,2,1,0:T(8,128)} collective-permute-done((f32[4,5,128,128]{3,2,1,0:T(8,128)}, f32[4,5,128,128]{3,2,1,0:T(8,128)}, u32[]{:S(2)}, u32[]{:S(2)}) %collective-permute-start.3) | collective-permute-done | bytes 1310752 | tf_op jit(solution)/shard_map/ppermute | solution.py:141
  81.0 7.6 %collective-permute-done.2.refs_1_ = f32[4,5,128,128]{3,2,1,0:T(8,128)} collective-permute-done((f32[4,5,128,128]{3,2,1,0:T(8,128)S(1)}, f32[4,5,128,128]{3,2,1,0:T(8,128)}, u32[]{:S(2)}, u32[]{:S(2)}) %collective-permute-start.2) | collective-permute-done | bytes 1310752 | tf_op jit(solution)/shard_map/ppermute | solution.py:140
  88.6 8.1 %shard_map.69 = (f32[4,10,64,128]{3,2,1,0:T(8,128)}, f32[4,10,64,128]{3,2,1,0:T(8,128)}) custom-call(s32[1]{0:T(128)} %bitcast.2.core_ref, f32[4,16,128,128]{3,2,1,0:T(8,128)} %refs_0_.3, f32[4,5,128,128]{3,2,1,0:T(8,128)} %collective-permute-done.2.refs_1_, f32[4,5,128,128]{3,2,1,0:T(8,128)} %collective-permute-done.3.refs_2_, ...), custom_call_target="tpu_custom_call" | custom-call | tf_op jit(solution)/shard_map/pallas_call | solution.py:79
  97.9 2.0 collective-permute-done.5.refs_3_
  99.9 79.0 %all-gather.2.cloned.1.call-done.inv_ref = f32[16,24,64,128]{3,2,1,0:T(8,128)} async-done(((f32[16,24,8,128]{3,2,1,0:T(8,128)}), f32[16,24,64,128]{3,2,1,0:T(8,128)}) %all-gather.2.cloned.1.call-update) | async-done | bytes 12582928 | tf_op jit(solution)/shard_map/all_gather | solution.py:198
  178.9 12.4 %shard_map.70 = f32[8,16,64,128]{3,2,1,0:T(8,128)} custom-call(f32[24]{0:T(128)} %and_convert_fusion.mask_ref, f32[16,24,64,128]{3,2,1,0:T(8,128)} %all-gather.2.cloned.1.call-done.inv_ref, f32[4,14,64,128]{3,2,1,0:T(8,128)} %get-tuple-element.42.refs_0_, f32[4,10,64,128]{3,2,1,0:T(8,128)} %get-tuple-element.51.refs_1_, f32[4,14,64,128]{3,2,1,0:T(8,128)} %copy-done.8, ...), custom_call_target="tpu_custom_call" | custom-call | tf_op jit(solution)/shard_map/pallas_call | solution.py:125
  191.3 1.7 slice_bitcast_fusion.2
  193.1 4.3 %collective-permute-done.6 = f32[4,16,8,8,128]{4,3,2,1,0:T(8,128)} collective-permute-done((f32[4,16,8,8,128]{4,3,2,1,0:T(8,128)S(1)}, f32[4,16,8,8,128]{4,3,2,1,0:T(8,128)}, u32[]{:S(2)}, u32[]{:S(2)}) %collective-permute-start.6) | collective-permute-done | bytes 2097184 | tf_op jit(solution)/shard_map/ppermute | solution.py:253
  197.4 2.7 select_bitcast_fusion.3
  201.0 1.8 copy-done.4
  202.8 1.2 bitcast_add_fusion.1.refs_0_
  204.0 1.4 fusion.15
  206.4 9.2 %collective-permute-start.8 = (f32[4,5,128,128]{3,2,1,0:T(8,128)}, f32[4,5,128,128]{3,2,1,0:T(8,128)}, u32[]{:S(2)}, u32[]{:S(2)}) collective-permute-start(f32[4,5,128,128]{3,2,1,0:T(8,128)} %get-tuple-element.77), channel_id=1, source_target_pairs={{16,0},{32,16},{48,32},{64,48},{80,64},{96,80},{112,96},{17,1},{33... | collective-permute-start | bytes 3932168 | tf_op jit(solution)/shard_map/ppermute | solution.py:141
  215.6 1.9 collective-permute-start.7
  217.5 8.7 %shard_map.71 = (f32[4,14,64,128]{3,2,1,0:T(8,128)}, f32[4,14,64,128]{3,2,1,0:T(8,128)}) custom-call(s32[1]{0:T(128)} %bitcast.2.core_ref, f32[4,16,128,128]{3,2,1,0:T(8,128)} %copy-done.2, f32[4,14,128,128]{3,2,1,0:T(8,128)} %slice.262.refs_1_, f32[14,128,128]{2,1,0:T(8,128)} %slice.234.refs_2_, f32[14,128,128]{2,1,0:T(8,128)} %slice.235.refs_3_, ...), custom_call_target="tpu_custom_call" | custom-call | tf_op jit(solution)/shard_map/pallas_call | solution.py:79
  226.2 18.0 %collective-permute-done.8.refs_2_ = f32[4,5,128,128]{3,2,1,0:T(8,128)} collective-permute-done((f32[4,5,128,128]{3,2,1,0:T(8,128)}, f32[4,5,128,128]{3,2,1,0:T(8,128)}, u32[]{:S(2)}, u32[]{:S(2)}) %collective-permute-start.8) | collective-permute-done | bytes 1310752 | tf_op jit(solution)/shard_map/ppermute | solution.py:141
  244.2 7.5 %collective-permute-done.7.refs_1_ = f32[4,5,128,128]{3,2,1,0:T(8,128)} collective-permute-done((f32[4,5,128,128]{3,2,1,0:T(8,128)S(1)}, f32[4,5,128,128]{3,2,1,0:T(8,128)}, u32[]{:S(2)}, u32[]{:S(2)}) %collective-permute-start.7) | collective-permute-done | bytes 1310752 | tf_op jit(solution)/shard_map/ppermute | solution.py:140
  251.7 7.8 %shard_map.72 = (f32[4,10,64,128]{3,2,1,0:T(8,128)}, f32[4,10,64,128]{3,2,1,0:T(8,128)}) custom-call(s32[1]{0:T(128)} %bitcast.2.core_ref, f32[4,16,128,128]{3,2,1,0:T(8,128)} %copy-done.2, f32[4,5,128,128]{3,2,1,0:T(8,128)} %collective-permute-done.7.refs_1_, f32[4,5,128,128]{3,2,1,0:T(8,128)} %collective-permute-done.8.refs_2_, ...), custom_call_target="tpu_custom_call" | custom-call | tf_op jit(solution)/shard_map/pallas_call | solution.py:79
  259.6 3.2 collective-permute-done.10.refs_3_
  262.8 1.1 copy-done.11
  263.9 12.4 %shard_map.73 = f32[8,16,64,128]{3,2,1,0:T(8,128)} custom-call(f32[24]{0:T(128)} %and_convert_fusion.mask_ref, f32[16,24,64,128]{3,2,1,0:T(8,128)} %all-gather.2.cloned.1.call-done.inv_ref, f32[4,14,64,128]{3,2,1,0:T(8,128)} %get-tuple-element.54.refs_0_, f32[4,10,64,128]{3,2,1,0:T(8,128)} %get-tuple-element.55.refs_1_, f32[4,14,64,128]{3,2,1,0:T(8,128)} %copy-done.9, ...), custom_call_target="tpu_custom_call" | custom-call | tf_op jit(solution)/shard_map/pallas_call | solution.py:125
  276.4 1.9 slice_bitcast_fusion
  278.5 4.0 %collective-permute-done.11 = f32[4,16,8,8,128]{4,3,2,1,0:T(8,128)S(1)} collective-permute-done((f32[4,16,8,8,128]{4,3,2,1,0:T(8,128)S(1)}, f32[4,16,8,8,128]{4,3,2,1,0:T(8,128)S(1)}, u32[]{:S(2)}, u32[]{:S(2)}) %collective-permute-start.11) | collective-permute-done | bytes 2097184 | tf_op jit(solution)/shard_map/ppermute | solution.py:253
  283.7 1.8 copy-done.3
  285.5 1.2 bitcast_add_fusion.refs_0_
  286.7 2.0 copy-done.5
  288.8 1.9 collective-permute-start.13
  290.7 3.9 %collective-permute-start.12 = (f32[4,1,128,128]{3,2,1,0:T(8,128)S(1)}, f32[4,1,128,128]{3,2,1,0:T(8,128)S(1)}, u32[]{:S(2)}, u32[]{:S(2)}) collective-permute-start(f32[4,1,128,128]{3,2,1,0:T(8,128)S(1)} %get-tuple-element.76), channel_id=1, source_target_pairs={{0,16},{16,32},{32,48},{48,64},{64,80},{80,96},{96,112},{1,17},{17... | collective-permute-start | bytes 786440 | tf_op jit(solution)/shard_map/ppermute | solution.py:140
  294.6 4.4 %collective-permute-done.13.refs_2_ = f32[4,1,128,128]{3,2,1,0:T(8,128)S(1)} collective-permute-done((f32[4,1,128,128]{3,2,1,0:T(8,128)S(1)}, f32[4,1,128,128]{3,2,1,0:T(8,128)S(1)}, u32[]{:S(2)}, u32[]{:S(2)}) %collective-permute-start.13) | collective-permute-done | bytes 262176 | tf_op jit(solution)/shard_map/ppermute | solution.py:141
  299.0 5.5 %collective-permute-done.12.refs_1_ = f32[4,1,128,128]{3,2,1,0:T(8,128)S(1)} collective-permute-done((f32[4,1,128,128]{3,2,1,0:T(8,128)S(1)}, f32[4,1,128,128]{3,2,1,0:T(8,128)S(1)}, u32[]{:S(2)}, u32[]{:S(2)}) %collective-permute-start.12) | collective-permute-done | bytes 262176 | tf_op jit(solution)/shard_map/ppermute | solution.py:140
  305.3 8.5 %shard_map.74 = f32[4,8,128]{2,1,0:T(8,128)} custom-call(s32[1]{0:T(128)} %bitcast.2.core_ref, f32[4,16,128,128]{3,2,1,0:T(8,128)} %copy-done.5, f32[4,1,128,128]{3,2,1,0:T(8,128)} %copy-done.13, f32[4,1,128,128]{3,2,1,0:T(8,128)} %copy-done.12, f32[4,16,128,128]{3,2,1,0:T(8,128)} %slice.265.refs_3_, f32[16,128,128]{2,1,0:T(8,128)} %slice.255.refs_4_, ...), custom_call_target="tpu_custom_call" | custom-call | tf_op jit(solution)/shard_map/pallas_call | solution.py:79
  314.6 3.6 %collective-permute-done.14 = f32[4]{0:T(128)S(1)} collective-permute-done((f32[4]{0:T(128)S(1)}, f32[4]{0:T(128)S(1)}, u32[]{:S(2)}, u32[]{:S(2)}) %collective-permute-start.14) | collective-permute-done | bytes 48 | tf_op jit(solution)/shard_map/ppermute | solution.py:263
  318.2 5.1 %collective-permute-done.15 = f32[4]{0:T(128)S(1)} collective-permute-done((f32[4]{0:T(128)S(1)}, f32[4]{0:T(128)S(1)}, u32[]{:S(2)}, u32[]{:S(2)}) %collective-permute-start.15) | collective-permute-done | bytes 48 | tf_op jit(solution)/shard_map/ppermute | solution.py:263
  323.3 5.1 %collective-permute-done.16 = f32[4]{0:T(128)S(1)} collective-permute-done((f32[4]{0:T(128)S(1)}, f32[4]{0:T(128)S(1)}, u32[]{:S(2)}, u32[]{:S(2)}) %collective-permute-start.16) | collective-permute-done | bytes 48 | tf_op jit(solution)/shard_map/ppermute | solution.py:263
  (82 shorter events, 27.4 us)
Async XLA Ops:
  7.2 22.6 %copy-start = (s32[64,2]{0,1:T(2,128)S(1)}, s32[64,2]{0,1:T(2,128)}, u32[]{:S(2)}) copy-start(s32[64,2]{0,1:T(2,128)} %param.8) | copy-start | bytes 1540
  7.2 1.2 copy-start.7
  7.2 171.7 %all-gather.2.cloned.1.call-start = ((), (), s32[]{:S(2)}) async-start(), calls=%async_computation | async-start | bytes 14155776 | tf_op jit(solution)/shard_map/all_gather | solution.py:198
  8.5 30.0 %collective-permute-start.1 = (f32[5,128,128]{2,1,0:T(8,128)S(1)}, f32[5,128,128]{2,1,0:T(8,128)S(1)}, u32[]{:S(2)}, u32[]{:S(2)}) collective-permute-start(f32[5,128,128]{2,1,0:T(8,128)S(1)} %get-tuple-element.104), channel_id=1, source_target_pairs={{16,0},{32,16},{48,32},{64,48},{80,64},{96,80},{112,96},{17,1},{33... | collective-permute-start | bytes 983048 | tf_op jit(solution)/shard_map/ppermute | solution.py:141
  15.3 22.2 %collective-permute-start = (f32[5,128,128]{2,1,0:T(8,128)S(1)}, f32[5,128,128]{2,1,0:T(8,128)}, u32[]{:S(2)}, u32[]{:S(2)}) collective-permute-start(f32[5,128,128]{2,1,0:T(8,128)S(1)} %get-tuple-element.105), channel_id=1, source_target_pairs={{0,16},{16,32},{32,48},{48,64},{64,80},{80,96},{96,112},{1,17},{17... | collective-permute-start | bytes 983048 | tf_op jit(solution)/shard_map/ppermute | solution.py:140
  20.2 60.8 %collective-permute-start.3 = (f32[4,5,128,128]{3,2,1,0:T(8,128)}, f32[4,5,128,128]{3,2,1,0:T(8,128)}, u32[]{:S(2)}, u32[]{:S(2)}) collective-permute-start(f32[4,5,128,128]{3,2,1,0:T(8,128)} %get-tuple-element.79), channel_id=1, source_target_pairs={{16,0},{32,16},{48,32},{64,48},{80,64},{96,80},{112,96},{17,1},{33... | collective-permute-start | bytes 3932168 | tf_op jit(solution)/shard_map/ppermute | solution.py:141
  27.8 60.8 %collective-permute-start.2 = (f32[4,5,128,128]{3,2,1,0:T(8,128)S(1)}, f32[4,5,128,128]{3,2,1,0:T(8,128)}, u32[]{:S(2)}, u32[]{:S(2)}) collective-permute-start(f32[4,5,128,128]{3,2,1,0:T(8,128)S(1)} %get-tuple-element.80), channel_id=1, source_target_pairs={{0,16},{16,32},{32,48},{48,64},{64,80},{80,96},{96,112},{1,17},{17... | collective-permute-start | bytes 3932168 | tf_op jit(solution)/shard_map/ppermute | solution.py:140
  70.9 27.0 %collective-permute-start.4 = (f32[4,14,64,128]{3,2,1,0:T(8,128)}, f32[4,14,64,128]{3,2,1,0:T(8,128)S(1)}, u32[]{:S(2)}, u32[]{:S(2)}) collective-permute-start(f32[4,14,64,128]{3,2,1,0:T(8,128)} %get-tuple-element.52), channel_id=1, source_target_pairs={{0,1},{1,0},{2,3},{3,2},{4,5},{5,4},{6,7},{7,6},{8,9},{9,8},{10,11... | collective-permute-start | bytes 5505032 | tf_op jit(solution)/shard_map/ppermute | solution.py:246
  96.6 3.2 collective-permute-start.5
  97.9 81.0 %copy-start.8 = (f32[4,14,64,128]{3,2,1,0:T(8,128)}, f32[4,14,64,128]{3,2,1,0:T(8,128)S(1)}, u32[]{:S(2)}) copy-start(f32[4,14,64,128]{3,2,1,0:T(8,128)S(1)} %collective-permute-done.4.refs_2_) | copy-start | bytes 5505028
  99.9 79.0 %copy-start.10 = (f32[4,10,64,128]{3,2,1,0:T(8,128)}, f32[4,10,64,128]{3,2,1,0:T(8,128)S(1)}, u32[]{:S(2)}) copy-start(f32[4,10,64,128]{3,2,1,0:T(8,128)S(1)} %collective-permute-done.5.refs_3_) | copy-start | bytes 3932164
  193.0 4.4 %collective-permute-start.6 = (f32[4,16,8,8,128]{4,3,2,1,0:T(8,128)S(1)}, f32[4,16,8,8,128]{4,3,2,1,0:T(8,128)}, u32[]{:S(2)}, u32[]{:S(2)}) collective-permute-start(f32[4,16,8,8,128]{4,3,2,1,0:T(8,128)S(1)} %slice_bitcast_fusion.2), channel_id=1, source_target_pairs={{0,1},{1,0},{2,3},{3,2},{4,5},{5,4},{6,7},{7,6},{8,9},{9,8},{10,11... | collective-permute-start | bytes 6291464 | tf_op jit(solution)/shard_map/ppermute | solution.py:253
  200.6 2.2 copy-start.4
  204.0 2.4 copy-start.2
  206.4 37.8 %collective-permute-start.8 = (f32[4,5,128,128]{3,2,1,0:T(8,128)}, f32[4,5,128,128]{3,2,1,0:T(8,128)}, u32[]{:S(2)}, u32[]{:S(2)}) collective-permute-start(f32[4,5,128,128]{3,2,1,0:T(8,128)} %get-tuple-element.77), channel_id=1, source_target_pairs={{16,0},{32,16},{48,32},{64,48},{80,64},{96,80},{112,96},{17,1},{33... | collective-permute-start | bytes 3932168 | tf_op jit(solution)/shard_map/ppermute | solution.py:141
  215.6 36.2 %collective-permute-start.7 = (f32[4,5,128,128]{3,2,1,0:T(8,128)S(1)}, f32[4,5,128,128]{3,2,1,0:T(8,128)}, u32[]{:S(2)}, u32[]{:S(2)}) collective-permute-start(f32[4,5,128,128]{3,2,1,0:T(8,128)S(1)} %get-tuple-element.78), channel_id=1, source_target_pairs={{0,16},{16,32},{32,48},{48,64},{64,80},{80,96},{96,112},{1,17},{17... | collective-permute-start | bytes 3932168 | tf_op jit(solution)/shard_map/ppermute | solution.py:140
  226.2 33.4 %collective-permute-start.9 = (f32[4,14,64,128]{3,2,1,0:T(8,128)}, f32[4,14,64,128]{3,2,1,0:T(8,128)S(1)}, u32[]{:S(2)}, u32[]{:S(2)}) collective-permute-start(f32[4,14,64,128]{3,2,1,0:T(8,128)} %get-tuple-element.56), channel_id=1, source_target_pairs={{0,1},{1,0},{2,3},{3,2},{4,5},{5,4},{6,7},{7,6},{8,9},{9,8},{10,11... | collective-permute-start | bytes 5505032 | tf_op jit(solution)/shard_map/ppermute | solution.py:246
  259.6 3.2 collective-permute-start.10
  259.6 3.2 copy-start.9
  262.8 1.1 copy-start.11
  276.4 6.1 %copy-start.6 = (f32[8,16,64,128]{3,2,1,0:T(8,128)S(1)}, f32[8,16,64,128]{3,2,1,0:T(8,128)}, u32[]{:S(2)}) copy-start(f32[8,16,64,128]{3,2,1,0:T(8,128)} %shard_map.73) | copy-start | bytes 12582916
  278.2 4.2 %collective-permute-start.11 = (f32[4,16,8,8,128]{4,3,2,1,0:T(8,128)S(1)}, f32[4,16,8,8,128]{4,3,2,1,0:T(8,128)S(1)}, u32[]{:S(2)}, u32[]{:S(2)}) collective-permute-start(f32[4,16,8,8,128]{4,3,2,1,0:T(8,128)S(1)} %slice_bitcast_fusion), channel_id=1, source_target_pairs={{0,1},{1,0},{2,3},{3,2},{4,5},{5,4},{6,7},{7,6},{8,9},{9,8},{10,11... | collective-permute-start | bytes 6291464 | tf_op jit(solution)/shard_map/ppermute | solution.py:253
  283.3 2.2 copy-start.3
  286.7 2.0 copy-start.5
  288.8 10.2 %collective-permute-start.13 = (f32[4,1,128,128]{3,2,1,0:T(8,128)S(1)}, f32[4,1,128,128]{3,2,1,0:T(8,128)S(1)}, u32[]{:S(2)}, u32[]{:S(2)}) collective-permute-start(f32[4,1,128,128]{3,2,1,0:T(8,128)S(1)} %get-tuple-element.75), channel_id=1, source_target_pairs={{16,0},{32,16},{48,32},{64,48},{80,64},{96,80},{112,96},{17,1},{33... | collective-permute-start | bytes 786440 | tf_op jit(solution)/shard_map/ppermute | solution.py:141
  290.7 13.9 %collective-permute-start.12 = (f32[4,1,128,128]{3,2,1,0:T(8,128)S(1)}, f32[4,1,128,128]{3,2,1,0:T(8,128)S(1)}, u32[]{:S(2)}, u32[]{:S(2)}) collective-permute-start(f32[4,1,128,128]{3,2,1,0:T(8,128)S(1)} %get-tuple-element.76), channel_id=1, source_target_pairs={{0,16},{16,32},{32,48},{48,64},{64,80},{80,96},{96,112},{1,17},{17... | collective-permute-start | bytes 786440 | tf_op jit(solution)/shard_map/ppermute | solution.py:140
  299.0 5.5 %copy-start.12 = (f32[4,1,128,128]{3,2,1,0:T(8,128)}, f32[4,1,128,128]{3,2,1,0:T(8,128)S(1)}, u32[]{:S(2)}) copy-start(f32[4,1,128,128]{3,2,1,0:T(8,128)S(1)} %collective-permute-done.13.refs_2_) | copy-start | bytes 786436
  304.6 0.7 copy-start.13
  305.3 23.6 %copy-start.1 = (s32[64,2]{0,1:T(2,128)S(1)}, s32[64,2]{0,1:T(2,128)}, u32[]{:S(2)}) copy-start(s32[64,2]{0,1:T(2,128)} %param.8) | copy-start | bytes 1540
  314.6 3.6 %collective-permute-start.14 = (f32[4]{0:T(128)S(1)}, f32[4]{0:T(128)S(1)}, u32[]{:S(2)}, u32[]{:S(2)}) collective-permute-start(f32[4]{0:T(128)S(1)} %reduce_sum.9), channel_id=1, source_target_pairs={{0,16},{16,0},{32,48},{48,32},{64,80},{80,64},{96,112},{112,96},{1... | collective-permute-start | bytes 56 | tf_op jit(solution)/shard_map/ppermute | solution.py:263
  318.2 5.1 %collective-permute-start.15 = (f32[4]{0:T(128)S(1)}, f32[4]{0:T(128)S(1)}, u32[]{:S(2)}, u32[]{:S(2)}) collective-permute-start(f32[4]{0:T(128)S(1)} %add.107), channel_id=1, source_target_pairs={{0,32},{16,48},{32,0},{48,16},{64,96},{80,112},{96,64},{112,80},{1... | collective-permute-start | bytes 56 | tf_op jit(solution)/shard_map/ppermute | solution.py:263
  323.3 5.1 %collective-permute-start.16 = (f32[4]{0:T(128)S(1)}, f32[4]{0:T(128)S(1)}, u32[]{:S(2)}, u32[]{:S(2)}) collective-permute-start(f32[4]{0:T(128)S(1)} %add.108), channel_id=1, source_target_pairs={{0,64},{16,80},{32,96},{48,112},{64,0},{80,16},{96,32},{112,48},{1... | collective-permute-start | bytes 56 | tf_op jit(solution)/shard_map/ppermute | solution.py:263
Sparse Core Ops, SparseCore 0:
  9.6 169.2 all-gather.1

commit v12 on v11

--- a/solution.py
+++ b/solution.py
@@ -16,15 +16,15 @@
 GRP = ("xl", "y", "core")
 
 
-def make_stencil_kernel(planes, has_rim, mode):
+def make_stencil_kernel(planes, has_rim, mode, width, edges):
     def kernel(core_ref, *refs):
-        n_in = 3 if has_rim else 1
-        v_ref = refs[0]
-        lo_ref, hi_ref = (refs[1], refs[2]) if has_rim else (None, None)
+        n_v = 2 if edges else 1
+        n_in = n_v + (2 if has_rim else 0)
+        v_refs = refs[:n_v]
+        lo_ref, hi_ref = (refs[n_v], refs[n_v + 1]) if has_rim else (None, None)
         st_ref, cc_ref, fxp_ref, fxm_ref, fyp_ref, fym_ref, fzp_ref, fzm_ref = refs[n_in : n_in + 8]
         outs = refs[n_in + 8 :]
-        width = v_ref.shape[1]
-        ny, nz = v_ref.shape[2], v_ref.shape[3]
+        ny, nz = v_refs[0].shape[2], v_refs[0].shape[3]
         core = core_ref[0]
 
         def load(q):
@@ -32,7 +32,11 @@
                 return lo_ref[0, lo_ref.shape[1] + q]
             if q >= width:
                 return hi_ref[0, q - width]
-            return v_ref[0, q]
+            if not edges:
+                return v_refs[0][0, q]
+            if q < EDGE:
+                return v_refs[0][0, q]
+            return v_refs[1][0, q - (width - EDGE)]
 
         total = None
         for o, p in enumerate(planes):
@@ -62,10 +66,21 @@
     return kernel
 
 
+EDGE = 2
+
+
 def stencil_call(planes, core, v, rims, st, coefs, mode):
     n_src, width, ny, nz = v.shape
     n_out = len(planes)
-    own_block = pl.BlockSpec((1, width, ny, nz), lambda s: (s, 0, 0, 0))
+    reads = {q for p in planes for q in (p - 1, p, p + 1) if 0 <= q < width}
+    edges = width % EDGE == 0 and width >= 2 * EDGE and all(q < EDGE or q >= width - EDGE for q in reads)
+    if edges:
+        own_specs = [pl.BlockSpec((1, EDGE, ny, nz), lambda s: (s, 0, 0, 0)),
+                     pl.BlockSpec((1, EDGE, ny, nz), lambda s: (s, width // EDGE - 1, 0, 0))]
+        own_args = [v, v]
+    else:
+        own_specs = [pl.BlockSpec((1, width, ny, nz), lambda s: (s, 0, 0, 0))]
+        own_args = [v]
     st_block = pl.BlockSpec((1, n_out, ny, nz), lambda s: (s, 0, 0, 0))
     coef_block = pl.BlockSpec((n_out, ny, nz), lambda s: (0, 0, 0))
     rim_specs = [pl.BlockSpec((1, r.shape[1], ny, nz), lambda s: (s, 0, 0, 0)) for r in rims]
@@ -77,13 +92,13 @@
         out_specs = [half, half]
         out_shape = [jax.ShapeDtypeStruct((n_src, n_out, ny // 2, nz), jnp.float32)] * 2
     return pl.pallas_call(
-        make_stencil_kernel(tuple(planes), len(rims) > 0, mode),
+        make_stencil_kernel(tuple(planes), len(rims) > 0, mode, width, edges),
         grid=(n_src,),
-        in_specs=[pl.BlockSpec(memory_space=pltpu.SMEM), own_block] + rim_specs + [st_block] + [coef_block] * 7,
+        in_specs=[pl.BlockSpec(memory_space=pltpu.SMEM)] + own_specs + rim_specs + [st_block] + [coef_block] * 7,
         out_specs=out_specs,
         out_shape=out_shape,
         interpret=INTERPRET,
-    )(core, v, *rims, st, *coefs)
+    )(core, *own_args, *rims, st, *coefs)
 
 
 def make_correction_kernel(columns, chunk=2):
@@ -216,16 +231,17 @@
 
     mid_planes = list(range(1, width_x - 1))
     bnd_planes = list(range(-margin, 1)) + list(range(width_x - 1, width_x + margin))
-    own_planes = list(range(width_x))
 
     mid_coefs = [c[1 + margin : width_x - 1 + margin] for c in coefs]
     bnd_coefs = [jnp.concatenate([c[: margin + 1], c[width_x - 1 + margin :]], axis=0) for c in coefs]
-    own_coefs = [c[margin : margin + width_x] for c in coefs]
+    edge_planes = [0, width_x - 1]
+    edge_coefs = [jnp.concatenate([c[margin : margin + 1], c[margin + width_x - 1 : margin + width_x]], axis=0) for c in coefs]
+    edge_st = jnp.concatenate(
+        [source_term[:, margin : margin + 1], source_term[:, margin + width_x - 1 : margin + width_x]], axis=1)
     mid_st = source_term[:, 1 + margin : width_x - 1 + margin]
     bnd_st = jnp.concatenate([source_term[:, : margin + 1], source_term[:, width_x - 1 + margin :]], axis=1)
-    own_st = source_term[:, margin : margin + width_x]
-    mid_coefs, bnd_coefs, own_coefs, mid_st, bnd_st, own_st = lax.optimization_barrier(
-        (mid_coefs, bnd_coefs, own_coefs, mid_st, bnd_st, own_st)
+    mid_coefs, bnd_coefs, edge_coefs, mid_st, bnd_st, edge_st = lax.optimization_barrier(
+        (mid_coefs, bnd_coefs, edge_coefs, mid_st, bnd_st, edge_st)
     )
     core_vec = jnp.reshape(core, (1,)).astype(jnp.int32)
 
@@ -256,8 +272,9 @@
         update = jnp.stack([first, second], axis=3).reshape(potential.shape)
         potential = potential + update
     lo, hi = rims_of(potential, 1, 1)
-    squares = stencil_call(own_planes, core_vec, potential, [lo, hi], own_st, own_coefs, "norm")
-    totals = jnp.sum(squares, axis=(1, 2))
+    inner_squares = stencil_call(mid_planes, core_vec, potential, [], mid_st, mid_coefs, "norm")
+    rim_squares = stencil_call(edge_planes, core_vec, potential, [lo, hi], edge_st, edge_coefs, "norm")
+    totals = jnp.sum(inner_squares + rim_squares, axis=(1, 2))
     step_size = 1
     while step_size < n_sub:
         totals = totals + lax.ppermute(totals, "sub", [(i, i ^ step_size) for i in range(n_sub)])

time: 336 us -> 332 us (0.988)
  local copies, waits for them, and re-layouts: 38.3 us -> 30.1 us
  other arithmetic: 20.3 us -> 25.8 us
  waiting for transfers between devices: 160 us -> 156 us
    slice x8 -> x5, local copies, waits for them, and re-layouts: 9.82 us -> 0.1 us  [the longest x4 0.06 us: on_device(): c[margin:margin + 1]]
    concatenate x0 -> x8, other arithmetic: none -> 5.44 us  [the longest x7 4.61 us: on_device(): jnp.concatenate([c[margin:margin + 1], c[margin + width_x - 1:margin + wi...]
    pallas_call x5 -> x6, Pallas kernels: 41.7 us -> 43.7 us  [stencil_call(): pl.pallas_call(make_stencil_kernel(tuple(planes), len(rims) > 0, mode, wi...]
    unnamed x30 -> x32, local copies, waits for them, and re-layouts: 10 us -> 10 us
  transfers between devices with their start and end apart: 18 -> 18, of which waited for: 14 -> 14; matrix products, arithmetic and copies ran while one was open for 11% -> 10% of each run, Pallas kernels for 10% -> 12%
where the time goes in v12:
time: 332 us; the launch traced here: 331 us
  waiting for transfers between devices  156 us (47%)
  Pallas kernels  68.5 us (21%)
  starting transfers between devices  35.2 us (11%)
  local copies, waits for them, and re-layouts  30.1 us (9%)
  other arithmetic  25.8 us (8%)
  between operations  15.1 us (5%)
    all_gather x1, waiting for transfers between devices, on_device(): inverse_mine = lax.all_gather(inverse_rows, CHIP_AXES, axis=2, tiled=True)  78.8 us
    pallas_call x6, Pallas kernels, stencil_call(): pl.pallas_call(make_stencil_kernel(tuple(planes), len(rims) > 0, mode, wi...  43.7 us
    ppermute x4, waiting for transfers between devices, rims_of(): hi = lax.ppermute(head, 'sub', [(i + 1, i) for i in range(count - 1)])  29.4 us
    ppermute x4, starting transfers between devices, rims_of(): hi = lax.ppermute(head, 'sub', [(i + 1, i) for i in range(count - 1)])  25.1 us
    pallas_call x2, Pallas kernels, correction_call(): pl.pallas_call(make_correction_kernel(tuple(columns)), grid=(ny // rows,)...  24.8 us
    ppermute x4, waiting for transfers between devices, rims_of(): lo = lax.ppermute(tail, 'sub', [(i, i + 1) for i in range(count - 1)])  20.2 us
    ppermute x3, waiting for transfers between devices, on_device(): lax.ppermute(totals, 'sub', [(i, i ^ step_size) for i in range(n_sub)])  13.7 us
    unnamed x32, local copies, waits for them, and re-layouts  10 us
  transfers between devices with their start and end apart: 18, of which 14 were waited for; matrix products, arithmetic and copies ran while one was open for 10% of the time, Pallas kernels for 12%

profile of v12, /device:TPU:6, one launch (start us, length us, event | category | flops | bytes accessed | tf_op | source)
XLA Modules:
  0.0 331.0 jit_solution(10695004748693907613)
XLA Ops:
  9.2 6.8 %collective-permute-start.1 = (f32[5,128,128]{2,1,0:T(8,128)S(1)}, f32[5,128,128]{2,1,0:T(8,128)}, u32[]{:S(2)}, u32[]{:S(2)}) collective-permute-start(f32[5,128,128]{2,1,0:T(8,128)S(1)} %get-tuple-element.120), channel_id=1, source_target_pairs={{16,0},{32,16},{48,32},{64,48},{80,64},{96,80},{112,96},{17,1},{33... | collective-permute-start | bytes 983048 | tf_op jit(solution)/shard_map/ppermute | solution.py:156
  16.0 1.9 collective-permute-start
  17.9 3.0 fusion.17
  20.9 7.6 %collective-permute-start.3 = (f32[4,5,128,128]{3,2,1,0:T(8,128)}, f32[4,5,128,128]{3,2,1,0:T(8,128)}, u32[]{:S(2)}, u32[]{:S(2)}) collective-permute-start(f32[4,5,128,128]{3,2,1,0:T(8,128)} %get-tuple-element.81), channel_id=1, source_target_pairs={{16,0},{32,16},{48,32},{64,48},{80,64},{96,80},{112,96},{17,1},{33... | collective-permute-start | bytes 3932168 | tf_op jit(solution)/shard_map/ppermute | solution.py:156
  28.5 1.9 collective-permute-start.2
  30.8 1.1 select_subtract_fusion
  33.0 2.1 slice.301.refs_1_
  35.0 1.8 pad_maximum_fusion.2.refs_4_
  36.8 2.1 collective-permute-done
  41.0 2.3 broadcast_select_fusion
  45.3 1.0 slice.271.refs_7_
  46.3 1.0 slice.270.refs_6_
  61.7 8.7 %shard_map.68 = (f32[4,14,64,128]{3,2,1,0:T(8,128)}, f32[4,14,64,128]{3,2,1,0:T(8,128)}) custom-call(s32[1]{0:T(128)} %bitcast.2.core_ref, f32[4,16,128,128]{3,2,1,0:T(8,128)} %refs_1_.1, f32[4,14,128,128]{3,2,1,0:T(8,128)} %slice.301.refs_1_, f32[14,128,128]{2,1,0:T(8,128)} %slice.266.refs_2_, f32[14,128,128]{2,1,0:T(8,128)} %slice.267.refs_3_, ...), custom_call_target="tpu_custom_call" | custom-call | tf_op jit(solution)/shard_map/pallas_call | solution.py:94
  70.4 11.3 %collective-permute-done.3.refs_3_ = f32[4,5,128,128]{3,2,1,0:T(8,128)} collective-permute-done((f32[4,5,128,128]{3,2,1,0:T(8,128)}, f32[4,5,128,128]{3,2,1,0:T(8,128)}, u32[]{:S(2)}, u32[]{:S(2)}) %collective-permute-start.3) | collective-permute-done | bytes 1310752 | tf_op jit(solution)/shard_map/ppermute | solution.py:156
  81.7 8.3 %collective-permute-done.2.refs_2_ = f32[4,5,128,128]{3,2,1,0:T(8,128)} collective-permute-done((f32[4,5,128,128]{3,2,1,0:T(8,128)S(1)}, f32[4,5,128,128]{3,2,1,0:T(8,128)}, u32[]{:S(2)}, u32[]{:S(2)}) %collective-permute-start.2) | collective-permute-done | bytes 1310752 | tf_op jit(solution)/shard_map/ppermute | solution.py:155
  90.1 7.4 %shard_map.69 = (f32[4,10,64,128]{3,2,1,0:T(8,128)}, f32[4,10,64,128]{3,2,1,0:T(8,128)}) custom-call(s32[1]{0:T(128)} %bitcast.2.core_ref, f32[4,16,128,128]{3,2,1,0:T(8,128)} %refs_1_.1, f32[4,16,128,128]{3,2,1,0:T(8,128)} %refs_1_.1, f32[4,5,128,128]{3,2,1,0:T(8,128)} %collective-permute-done.2.refs_2_, f32[4,5,128,128]{3,2,1,0:T(8,128)} %collective-permute-done.3.refs_3_, ...), custom_call_target="tpu_custom_call" | custom-call | tf_op jit(solution)/shard_map/pallas_call | solution.py:94
  98.7 2.0 collective-permute-done.5.refs_3_
  100.8 78.8 %all-gather.2.cloned.1.call-done.inv_ref = f32[16,24,64,128]{3,2,1,0:T(8,128)} async-done(((f32[16,24,8,128]{3,2,1,0:T(8,128)}), f32[16,24,64,128]{3,2,1,0:T(8,128)}) %all-gather.2.cloned.1.call-update) | async-done | bytes 12582928 | tf_op jit(solution)/shard_map/all_gather | solution.py:213
  179.6 12.4 %shard_map.70 = f32[8,16,64,128]{3,2,1,0:T(8,128)} custom-call(f32[24]{0:T(128)} %and_convert_fusion.mask_ref, f32[16,24,64,128]{3,2,1,0:T(8,128)} %all-gather.2.cloned.1.call-done.inv_ref, f32[4,14,64,128]{3,2,1,0:T(8,128)} %get-tuple-element.42.refs_0_, f32[4,10,64,128]{3,2,1,0:T(8,128)} %get-tuple-element.51.refs_1_, f32[4,14,64,128]{3,2,1,0:T(8,128)} %copy-done.8, ...), custom_call_target="tpu_custom_call" | custom-call | tf_op jit(solution)/shard_map/pallas_call | solution.py:140
  192.0 1.7 slice_bitcast_fusion.2
  193.8 4.3 %collective-permute-done.6 = f32[4,16,8,8,128]{4,3,2,1,0:T(8,128)} collective-permute-done((f32[4,16,8,8,128]{4,3,2,1,0:T(8,128)S(1)}, f32[4,16,8,8,128]{4,3,2,1,0:T(8,128)}, u32[]{:S(2)}, u32[]{:S(2)}) %collective-permute-start.6) | collective-permute-done | bytes 2097184 | tf_op jit(solution)/shard_map/ppermute | solution.py:269
  198.1 2.7 select_bitcast_fusion.3
  201.7 1.8 copy-done.4
  203.5 1.2 bitcast_add_fusion.1.refs_0_.refs_1_
  204.7 1.4 fusion.16
  206.1 1.0 copy-done.2
  207.1 8.8 %collective-permute-start.8 = (f32[4,5,128,128]{3,2,1,0:T(8,128)}, f32[4,5,128,128]{3,2,1,0:T(8,128)}, u32[]{:S(2)}, u32[]{:S(2)}) collective-permute-start(f32[4,5,128,128]{3,2,1,0:T(8,128)} %get-tuple-element.79), channel_id=1, source_target_pairs={{16,0},{32,16},{48,32},{64,48},{80,64},{96,80},{112,96},{17,1},{33... | collective-permute-start | bytes 3932168 | tf_op jit(solution)/shard_map/ppermute | solution.py:156
  215.9 1.9 collective-permute-start.7
  217.9 8.7 %shard_map.71 = (f32[4,14,64,128]{3,2,1,0:T(8,128)}, f32[4,14,64,128]{3,2,1,0:T(8,128)}) custom-call(s32[1]{0:T(128)} %bitcast.2.core_ref, f32[4,16,128,128]{3,2,1,0:T(8,128)} %copy-done.2, f32[4,14,128,128]{3,2,1,0:T(8,128)} %slice.301.refs_1_, f32[14,128,128]{2,1,0:T(8,128)} %slice.266.refs_2_, f32[14,128,128]{2,1,0:T(8,128)} %slice.267.refs_3_, ...), custom_call_target="tpu_custom_call" | custom-call | tf_op jit(solution)/shard_map/pallas_call | solution.py:94
  226.5 18.0 %collective-permute-done.8.refs_3_ = f32[4,5,128,128]{3,2,1,0:T(8,128)} collective-permute-done((f32[4,5,128,128]{3,2,1,0:T(8,128)}, f32[4,5,128,128]{3,2,1,0:T(8,128)}, u32[]{:S(2)}, u32[]{:S(2)}) %collective-permute-start.8) | collective-permute-done | bytes 1310752 | tf_op jit(solution)/shard_map/ppermute | solution.py:156
  244.6 7.5 %collective-permute-done.7.refs_2_ = f32[4,5,128,128]{3,2,1,0:T(8,128)} collective-permute-done((f32[4,5,128,128]{3,2,1,0:T(8,128)S(1)}, f32[4,5,128,128]{3,2,1,0:T(8,128)}, u32[]{:S(2)}, u32[]{:S(2)}) %collective-permute-start.7) | collective-permute-done | bytes 1310752 | tf_op jit(solution)/shard_map/ppermute | solution.py:155
  252.1 7.2 %shard_map.72 = (f32[4,10,64,128]{3,2,1,0:T(8,128)}, f32[4,10,64,128]{3,2,1,0:T(8,128)}) custom-call(s32[1]{0:T(128)} %bitcast.2.core_ref, f32[4,16,128,128]{3,2,1,0:T(8,128)} %copy-done.2, f32[4,16,128,128]{3,2,1,0:T(8,128)} %copy-done.2, f32[4,5,128,128]{3,2,1,0:T(8,128)} %collective-permute-done.7.refs_2_, ...), custom_call_target="tpu_custom_call" | custom-call | tf_op jit(solution)/shard_map/pallas_call | solution.py:94
  259.4 3.2 collective-permute-done.10.refs_3_
  262.6 1.1 copy-done.11
  263.6 12.4 %shard_map.73 = f32[8,16,64,128]{3,2,1,0:T(8,128)} custom-call(f32[24]{0:T(128)} %and_convert_fusion.mask_ref, f32[16,24,64,128]{3,2,1,0:T(8,128)} %all-gather.2.cloned.1.call-done.inv_ref, f32[4,14,64,128]{3,2,1,0:T(8,128)} %get-tuple-element.54.refs_0_, f32[4,10,64,128]{3,2,1,0:T(8,128)} %get-tuple-element.55.refs_1_, f32[4,14,64,128]{3,2,1,0:T(8,128)} %copy-done.9, ...), custom_call_target="tpu_custom_call" | custom-call | tf_op jit(solution)/shard_map/pallas_call | solution.py:140
  276.1 1.9 slice_bitcast_fusion
  278.1 4.0 %collective-permute-done.11 = f32[4,16,8,8,128]{4,3,2,1,0:T(8,128)S(1)} collective-permute-done((f32[4,16,8,8,128]{4,3,2,1,0:T(8,128)S(1)}, f32[4,16,8,8,128]{4,3,2,1,0:T(8,128)S(1)}, u32[]{:S(2)}, u32[]{:S(2)}) %collective-permute-start.11) | collective-permute-done | bytes 2097184 | tf_op jit(solution)/shard_map/ppermute | solution.py:269
  283.4 1.8 copy-done.3
  285.2 1.2 bitcast_add_fusion.refs_0_.refs_1_
  286.4 2.0 copy-done.5
  288.5 1.9 collective-permute-start.13
  290.4 3.9 %collective-permute-start.12 = (f32[4,1,128,128]{3,2,1,0:T(8,128)S(1)}, f32[4,1,128,128]{3,2,1,0:T(8,128)S(1)}, u32[]{:S(2)}, u32[]{:S(2)}) collective-permute-start(f32[4,1,128,128]{3,2,1,0:T(8,128)S(1)} %get-tuple-element.78), channel_id=1, source_target_pairs={{0,16},{16,32},{32,48},{48,64},{64,80},{80,96},{96,112},{1,17},{17... | collective-permute-start | bytes 786440 | tf_op jit(solution)/shard_map/ppermute | solution.py:155
  294.3 7.7 %shard_map.74 = f32[4,8,128]{2,1,0:T(8,128)} custom-call(s32[1]{0:T(128)} %bitcast.2.core_ref, f32[4,16,128,128]{3,2,1,0:T(8,128)} %copy-done.5, f32[4,14,128,128]{3,2,1,0:T(8,128)} %slice.301.refs_1_, f32[14,128,128]{2,1,0:T(8,128)} %slice.266.refs_2_, f32[14,128,128]{2,1,0:T(8,128)} %slice.267.refs_3_, f32[14,128,128]{2,1,0:T(8,128)} %slice.268.refs_4_, ...), custom_call_target="tpu_custom_call" | custom-call | tf_op jit(solution)/shard_map/pallas_call | solution.py:94
  302.0 2.2 collective-permute-done.12.refs_2_
  305.0 4.0 %shard_map.75 = f32[4,8,128]{2,1,0:T(8,128)} custom-call(s32[1]{0:T(128)} %bitcast.2.core_ref, f32[4,16,128,128]{3,2,1,0:T(8,128)} %copy-done.5, f32[4,16,128,128]{3,2,1,0:T(8,128)} %copy-done.5, f32[4,1,128,128]{3,2,1,0:T(8,128)} %copy-done.13, f32[4,1,128,128]{3,2,1,0:T(8,128)} %copy-done.12, f32[4,2,128,128]{3,2,1,0:T(8,128)} %pad_maximum_fusion.10.refs_4_, ...), custom_call_target="tpu_custom_call" | custom-call | tf_op jit(solution)/shard_map/pallas_call | solution.py:94
  309.9 3.6 %collective-permute-done.14 = f32[4]{0:T(128)S(1)} collective-permute-done((f32[4]{0:T(128)S(1)}, f32[4]{0:T(128)S(1)}, u32[]{:S(2)}, u32[]{:S(2)}) %collective-permute-start.14) | collective-permute-done | bytes 48 | tf_op jit(solution)/shard_map/ppermute | solution.py:280
  313.5 5.1 %collective-permute-done.15 = f32[4]{0:T(128)S(1)} collective-permute-done((f32[4]{0:T(128)S(1)}, f32[4]{0:T(128)S(1)}, u32[]{:S(2)}, u32[]{:S(2)}) %collective-permute-start.15) | collective-permute-done | bytes 48 | tf_op jit(solution)/shard_map/ppermute | solution.py:280
  318.5 5.1 %collective-permute-done.16 = f32[4]{0:T(128)S(1)} collective-permute-done((f32[4]{0:T(128)S(1)}, f32[4]{0:T(128)S(1)}, u32[]{:S(2)}, u32[]{:S(2)}) %collective-permute-start.16) | collective-permute-done | bytes 48 | tf_op jit(solution)/shard_map/ppermute | solution.py:280
  (90 shorter events, 27.1 us)
Async XLA Ops:
  7.2 23.3 %copy-start = (s32[64,2]{0,1:T(2,128)S(1)}, s32[64,2]{0,1:T(2,128)}, u32[]{:S(2)}) copy-start(s32[64,2]{0,1:T(2,128)} %param.8) | copy-start | bytes 1540
  7.2 1.2 copy-start.7
  7.2 172.4 %all-gather.2.cloned.1.call-start = ((), (), s32[]{:S(2)}) async-start(), calls=%async_computation | async-start | bytes 14155776 | tf_op jit(solution)/shard_map/all_gather | solution.py:213
  9.2 30.8 %collective-permute-start.1 = (f32[5,128,128]{2,1,0:T(8,128)S(1)}, f32[5,128,128]{2,1,0:T(8,128)}, u32[]{:S(2)}, u32[]{:S(2)}) collective-permute-start(f32[5,128,128]{2,1,0:T(8,128)S(1)} %get-tuple-element.120), channel_id=1, source_target_pairs={{16,0},{32,16},{48,32},{64,48},{80,64},{96,80},{112,96},{17,1},{33... | collective-permute-start | bytes 983048 | tf_op jit(solution)/shard_map/ppermute | solution.py:156
  16.0 23.0 %collective-permute-start = (f32[5,128,128]{2,1,0:T(8,128)}, f32[5,128,128]{2,1,0:T(8,128)}, u32[]{:S(2)}, u32[]{:S(2)}) collective-permute-start(f32[5,128,128]{2,1,0:T(8,128)} %get-tuple-element.121), channel_id=1, source_target_pairs={{0,16},{16,32},{32,48},{48,64},{64,80},{80,96},{96,112},{1,17},{17... | collective-permute-start | bytes 983048 | tf_op jit(solution)/shard_map/ppermute | solution.py:155
  20.9 60.8 %collective-permute-start.3 = (f32[4,5,128,128]{3,2,1,0:T(8,128)}, f32[4,5,128,128]{3,2,1,0:T(8,128)}, u32[]{:S(2)}, u32[]{:S(2)}) collective-permute-start(f32[4,5,128,128]{3,2,1,0:T(8,128)} %get-tuple-element.81), channel_id=1, source_target_pairs={{16,0},{32,16},{48,32},{64,48},{80,64},{96,80},{112,96},{17,1},{33... | collective-permute-start | bytes 3932168 | tf_op jit(solution)/shard_map/ppermute | solution.py:156
  28.5 61.6 %collective-permute-start.2 = (f32[4,5,128,128]{3,2,1,0:T(8,128)S(1)}, f32[4,5,128,128]{3,2,1,0:T(8,128)}, u32[]{:S(2)}, u32[]{:S(2)}) collective-permute-start(f32[4,5,128,128]{3,2,1,0:T(8,128)S(1)} %get-tuple-element.82), channel_id=1, source_target_pairs={{0,16},{16,32},{32,48},{48,64},{64,80},{80,96},{96,112},{1,17},{17... | collective-permute-start | bytes 3932168 | tf_op jit(solution)/shard_map/ppermute | solution.py:155
  70.4 28.3 %collective-permute-start.4 = (f32[4,14,64,128]{3,2,1,0:T(8,128)}, f32[4,14,64,128]{3,2,1,0:T(8,128)S(1)}, u32[]{:S(2)}, u32[]{:S(2)}) collective-permute-start(f32[4,14,64,128]{3,2,1,0:T(8,128)} %get-tuple-element.52), channel_id=1, source_target_pairs={{0,1},{1,0},{2,3},{3,2},{4,5},{5,4},{6,7},{7,6},{8,9},{9,8},{10,11... | collective-permute-start | bytes 5505032 | tf_op jit(solution)/shard_map/ppermute | solution.py:262
  97.5 3.3 collective-permute-start.5
  98.7 80.9 %copy-start.8 = (f32[4,14,64,128]{3,2,1,0:T(8,128)}, f32[4,14,64,128]{3,2,1,0:T(8,128)S(1)}, u32[]{:S(2)}) copy-start(f32[4,14,64,128]{3,2,1,0:T(8,128)S(1)} %collective-permute-done.4.refs_2_) | copy-start | bytes 5505028
  100.8 78.8 %copy-start.10 = (f32[4,10,64,128]{3,2,1,0:T(8,128)}, f32[4,10,64,128]{3,2,1,0:T(8,128)S(1)}, u32[]{:S(2)}) copy-start(f32[4,10,64,128]{3,2,1,0:T(8,128)S(1)} %collective-permute-done.5.refs_3_) | copy-start | bytes 3932164
  193.7 4.4 %collective-permute-start.6 = (f32[4,16,8,8,128]{4,3,2,1,0:T(8,128)S(1)}, f32[4,16,8,8,128]{4,3,2,1,0:T(8,128)}, u32[]{:S(2)}, u32[]{:S(2)}) collective-permute-start(f32[4,16,8,8,128]{4,3,2,1,0:T(8,128)S(1)} %slice_bitcast_fusion.2), channel_id=1, source_target_pairs={{0,1},{1,0},{2,3},{3,2},{4,5},{5,4},{6,7},{7,6},{8,9},{9,8},{10,11... | collective-permute-start | bytes 6291464 | tf_op jit(solution)/shard_map/ppermute | solution.py:269
  201.3 2.2 copy-start.4
  204.7 2.4 copy-start.2
  207.1 37.4 %collective-permute-start.8 = (f32[4,5,128,128]{3,2,1,0:T(8,128)}, f32[4,5,128,128]{3,2,1,0:T(8,128)}, u32[]{:S(2)}, u32[]{:S(2)}) collective-permute-start(f32[4,5,128,128]{3,2,1,0:T(8,128)} %get-tuple-element.79), channel_id=1, source_target_pairs={{16,0},{32,16},{48,32},{64,48},{80,64},{96,80},{112,96},{17,1},{33... | collective-permute-start | bytes 3932168 | tf_op jit(solution)/shard_map/ppermute | solution.py:156
  215.9 36.2 %collective-permute-start.7 = (f32[4,5,128,128]{3,2,1,0:T(8,128)S(1)}, f32[4,5,128,128]{3,2,1,0:T(8,128)}, u32[]{:S(2)}, u32[]{:S(2)}) collective-permute-start(f32[4,5,128,128]{3,2,1,0:T(8,128)S(1)} %get-tuple-element.80), channel_id=1, source_target_pairs={{0,16},{16,32},{32,48},{48,64},{64,80},{80,96},{96,112},{1,17},{17... | collective-permute-start | bytes 3932168 | tf_op jit(solution)/shard_map/ppermute | solution.py:155
  226.5 32.8 %collective-permute-start.9 = (f32[4,14,64,128]{3,2,1,0:T(8,128)}, f32[4,14,64,128]{3,2,1,0:T(8,128)S(1)}, u32[]{:S(2)}, u32[]{:S(2)}) collective-permute-start(f32[4,14,64,128]{3,2,1,0:T(8,128)} %get-tuple-element.56), channel_id=1, source_target_pairs={{0,1},{1,0},{2,3},{3,2},{4,5},{5,4},{6,7},{7,6},{8,9},{9,8},{10,11... | collective-permute-start | bytes 5505032 | tf_op jit(solution)/shard_map/ppermute | solution.py:262
  259.3 3.3 collective-permute-start.10
  259.4 3.2 copy-start.9
  262.6 1.1 copy-start.11
  276.1 6.1 %copy-start.6 = (f32[8,16,64,128]{3,2,1,0:T(8,128)S(1)}, f32[8,16,64,128]{3,2,1,0:T(8,128)}, u32[]{:S(2)}) copy-start(f32[8,16,64,128]{3,2,1,0:T(8,128)} %shard_map.73) | copy-start | bytes 12582916
  277.9 4.2 %collective-permute-start.11 = (f32[4,16,8,8,128]{4,3,2,1,0:T(8,128)S(1)}, f32[4,16,8,8,128]{4,3,2,1,0:T(8,128)S(1)}, u32[]{:S(2)}, u32[]{:S(2)}) collective-permute-start(f32[4,16,8,8,128]{4,3,2,1,0:T(8,128)S(1)} %slice_bitcast_fusion), channel_id=1, source_target_pairs={{0,1},{1,0},{2,3},{3,2},{4,5},{5,4},{6,7},{7,6},{8,9},{9,8},{10,11... | collective-permute-start | bytes 6291464 | tf_op jit(solution)/shard_map/ppermute | solution.py:269
  283.0 2.2 copy-start.3
  286.4 2.0 copy-start.5
  288.5 13.5 %collective-permute-start.13 = (f32[4,1,128,128]{3,2,1,0:T(8,128)S(1)}, f32[4,1,128,128]{3,2,1,0:T(8,128)S(1)}, u32[]{:S(2)}, u32[]{:S(2)}) collective-permute-start(f32[4,1,128,128]{3,2,1,0:T(8,128)S(1)} %get-tuple-element.77), channel_id=1, source_target_pairs={{16,0},{32,16},{48,32},{64,48},{80,64},{96,80},{112,96},{17,1},{33... | collective-permute-start | bytes 786440 | tf_op jit(solution)/shard_map/ppermute | solution.py:156
  290.4 13.9 %collective-permute-start.12 = (f32[4,1,128,128]{3,2,1,0:T(8,128)S(1)}, f32[4,1,128,128]{3,2,1,0:T(8,128)S(1)}, u32[]{:S(2)}, u32[]{:S(2)}) collective-permute-start(f32[4,1,128,128]{3,2,1,0:T(8,128)S(1)} %get-tuple-element.78), channel_id=1, source_target_pairs={{0,16},{16,32},{32,48},{48,64},{64,80},{80,96},{96,112},{1,17},{17... | collective-permute-start | bytes 786440 | tf_op jit(solution)/shard_map/ppermute | solution.py:155
  302.0 7.0 %copy-start.14 = (f32[4,8,128]{2,1,0:T(8,128)S(1)}, f32[4,8,128]{2,1,0:T(8,128)}, u32[]{:S(2)}) copy-start(f32[4,8,128]{2,1,0:T(8,128)} %shard_map.74) | copy-start | bytes 49156
  302.0 2.2 copy-start.12
  304.2 0.7 copy-start.13
  305.0 19.2 %copy-start.1 = (s32[64,2]{0,1:T(2,128)S(1)}, s32[64,2]{0,1:T(2,128)}, u32[]{:S(2)}) copy-start(s32[64,2]{0,1:T(2,128)} %param.8) | copy-start | bytes 1540
  309.8 3.6 %collective-permute-start.14 = (f32[4]{0:T(128)S(1)}, f32[4]{0:T(128)S(1)}, u32[]{:S(2)}, u32[]{:S(2)}) collective-permute-start(f32[4]{0:T(128)S(1)} %add_reduce_fusion), channel_id=1, source_target_pairs={{0,16},{16,0},{32,48},{48,32},{64,80},{80,64},{96,112},{112,96},{1... | collective-permute-start | bytes 56 | tf_op jit(solution)/shard_map/ppermute | solution.py:280
  313.5 5.1 %collective-permute-start.15 = (f32[4]{0:T(128)S(1)}, f32[4]{0:T(128)S(1)}, u32[]{:S(2)}, u32[]{:S(2)}) collective-permute-start(f32[4]{0:T(128)S(1)} %add.111), channel_id=1, source_target_pairs={{0,32},{16,48},{32,0},{48,16},{64,96},{80,112},{96,64},{112,80},{1... | collective-permute-start | bytes 56 | tf_op jit(solution)/shard_map/ppermute | solution.py:280
  318.5 5.1 %collective-permute-start.16 = (f32[4]{0:T(128)S(1)}, f32[4]{0:T(128)S(1)}, u32[]{:S(2)}, u32[]{:S(2)}) collective-permute-start(f32[4]{0:T(128)S(1)} %add.112), channel_id=1, source_target_pairs={{0,64},{16,80},{32,96},{48,112},{64,0},{80,16},{96,32},{112,48},{1... | collective-permute-start | bytes 56 | tf_op jit(solution)/shard_map/ppermute | solution.py:280
Sparse Core Ops, SparseCore 0:
  9.6 169.9 all-gather.1

commit v13 on v12

--- a/solution.py
+++ b/solution.py
@@ -103,8 +103,8 @@
 
 def make_correction_kernel(columns, chunk=2):
     def kernel(mask_ref, inv_ref, *refs):
-        out_ref = refs[-1]
-        pieces = refs[:-1]
+        mine_ref, theirs_ref = refs[-2:]
+        pieces = refs[:-2]
         n_out = inv_ref.shape[0]
         halves = len(pieces) // 2
 
@@ -123,9 +123,11 @@
                     accs = terms
                 else:
                     accs = [[a + t for a, t in zip(acc_s, term_s)] for acc_s, term_s in zip(accs, terms)]
+            n_half = len(accs) // 2
             for s, acc_s in enumerate(accs):
+                dest, slot = (mine_ref, s) if s < n_half else (theirs_ref, s - n_half)
                 for k in range(chunk):
-                    out_ref[s, base + k] = acc_s[k]
+                    dest[slot, base + k] = acc_s[k]
             return carry
 
         lax.fori_loop(0, n_out // chunk, rows, 0)
@@ -142,8 +144,8 @@
         grid=(ny // rows,),
         in_specs=[pl.BlockSpec(memory_space=pltpu.SMEM),
                   pl.BlockSpec((n_out, n_col, rows, nz), lambda b: (0, 0, b, 0))] + specs,
-        out_specs=pl.BlockSpec((n_src, n_out, rows, nz), lambda b: (0, 0, b, 0)),
-        out_shape=jax.ShapeDtypeStruct((n_src, n_out, ny, nz), jnp.float32),
+        out_specs=[pl.BlockSpec((n_src // 2, n_out, rows, nz), lambda b: (0, 0, b, 0))] * 2,
+        out_shape=[jax.ShapeDtypeStruct((n_src // 2, n_out, ny, nz), jnp.float32)] * 2,
         interpret=INTERPRET,
     )(mask, inv, *own_pieces, *got_pieces)
 
@@ -262,11 +264,10 @@
         mid_got = lax.ppermute(mid_other, CORE, swap)
         bnd_own, bnd_other = stencil_call(bnd_planes, core_vec, potential, [lo, hi], bnd_st, bnd_coefs, "split")
         bnd_got = lax.ppermute(bnd_other, CORE, swap)
-        correction = correction_call(
-            column_mask, inverse_mine, [mid_own, bnd_own], [mid_got, bnd_got], columns
-        ).reshape(2 * local_src, width_x, blocks, rows, depth)
-        mine = correction[:local_src]
-        back = lax.ppermute(correction[local_src:], CORE, swap)
+        mine, theirs = correction_call(
+            column_mask, inverse_mine, [mid_own, bnd_own], [mid_got, bnd_got], columns)
+        mine = mine.reshape(local_src, width_x, blocks, rows, depth)
+        back = lax.ppermute(theirs, CORE, swap).reshape(local_src, width_x, blocks, rows, depth)
         first = jnp.where(core == 0, mine, back)
         second = jnp.where(core == 0, back, mine)
         update = jnp.stack([first, second], axis=3).reshape(potential.shape)

time: 332 us -> 327 us (0.985)
  waiting for transfers between devices: 156 us -> 150 us
  starting transfers between devices: 35.2 us -> 38.9 us
    ppermute x4, waiting for transfers between devices: 29.4 us -> 1.94 us  [rims_of(): hi = lax.ppermute(head, 'sub', [(i + 1, i) for i in range(count - 1)])]
    ppermute x4, waiting for transfers between devices: 20.2 us -> 31.6 us  [rims_of(): lo = lax.ppermute(tail, 'sub', [(i, i + 1) for i in range(count - 1)])]
    all_gather x1, waiting for transfers between devices: 78.8 us -> 88.2 us  [on_device(): inverse_mine = lax.all_gather(inverse_rows, CHIP_AXES, axis=2, tiled=True)]
    select_n x0 -> x2, other arithmetic: none -> 4.68 us  [on_device(): first = jnp.where(core == 0, mine, back)]
    ppermute x4, starting transfers between devices: 25.1 us -> 28.8 us  [rims_of(): hi = lax.ppermute(head, 'sub', [(i + 1, i) for i in range(count - 1)])]
    another operation x4 -> x2, other arithmetic: 4.46 us -> 0.72 us  [on_device(): update = jnp.stack([first, second], axis=3).reshape(potential.shape)]
    slice x2 -> x0, local copies, waits for them, and re-layouts: 3.6 us -> none  [on_device(): back = lax.ppermute(correction[local_src:], CORE, swap)]
    unnamed x32 -> x30, local copies, waits for them, and re-layouts: 10 us -> 10.6 us
  transfers between devices with their start and end apart: 18 -> 18, of which waited for: 14 -> 12; matrix products, arithmetic and copies ran while one was open for 10% -> 10% of each run, Pallas kernels for 12% -> 12%
where the time goes in v13:
time: 327 us; the launch traced here: 326 us
  waiting for transfers between devices  150 us (46%)
  Pallas kernels  68.5 us (21%)
  starting transfers between devices  38.9 us (12%)
  local copies, waits for them, and re-layouts  26.9 us (8%)
  other arithmetic  26.7 us (8%)
  between operations  15.1 us (5%)
    all_gather x1, waiting for transfers between devices, on_device(): inverse_mine = lax.all_gather(inverse_rows, CHIP_AXES, axis=2, tiled=True)  88.2 us
    pallas_call x6, Pallas kernels, stencil_call(): pl.pallas_call(make_stencil_kernel(tuple(planes), len(rims) > 0, mode, wi...  43.6 us
    ppermute x4, waiting for transfers between devices, rims_of(): lo = lax.ppermute(tail, 'sub', [(i, i + 1) for i in range(count - 1)])  31.6 us
    ppermute x4, starting transfers between devices, rims_of(): hi = lax.ppermute(head, 'sub', [(i + 1, i) for i in range(count - 1)])  28.8 us
    pallas_call x2, Pallas kernels, correction_call(): pl.pallas_call(make_correction_kernel(tuple(columns)), grid=(ny // rows,)...  24.9 us
    ppermute x3, waiting for transfers between devices, on_device(): lax.ppermute(totals, 'sub', [(i, i ^ step_size) for i in range(n_sub)])  13.7 us
    unnamed x30, local copies, waits for them, and re-layouts  10.6 us
    ppermute x4, starting transfers between devices, rims_of(): lo = lax.ppermute(tail, 'sub', [(i, i + 1) for i in range(count - 1)])  9.55 us
  transfers between devices with their start and end apart: 18, of which 12 were waited for; matrix products, arithmetic and copies ran while one was open for 10% of the time, Pallas kernels for 12%

profile of v13, /device:TPU:6, one launch (start us, length us, event | category | flops | bytes accessed | tf_op | source)
XLA Modules:
  0.0 326.0 jit_solution(15323204298524343904)
XLA Ops:
  9.2 3.8 %collective-permute-start = (f32[5,128,128]{2,1,0:T(8,128)}, f32[5,128,128]{2,1,0:T(8,128)}, u32[]{:S(2)}, u32[]{:S(2)}) collective-permute-start(f32[5,128,128]{2,1,0:T(8,128)} %get-tuple-element.129), channel_id=1, source_target_pairs={{0,16},{16,32},{32,48},{48,64},{64,80},{80,96},{96,112},{1,17},{17... | collective-permute-start | bytes 983048 | tf_op jit(solution)/shard_map/ppermute | solution.py:157
  13.0 5.6 %collective-permute-start.1 = (f32[5,128,128]{2,1,0:T(8,128)S(1)}, f32[5,128,128]{2,1,0:T(8,128)}, u32[]{:S(2)}, u32[]{:S(2)}) collective-permute-start(f32[5,128,128]{2,1,0:T(8,128)S(1)} %get-tuple-element.128), channel_id=1, source_target_pairs={{16,0},{32,16},{48,32},{64,48},{80,64},{96,80},{112,96},{17,1},{33... | collective-permute-start | bytes 983048 | tf_op jit(solution)/shard_map/ppermute | solution.py:158
  18.6 3.1 fusion.17
  21.8 1.9 collective-permute-start.2
  23.7 7.5 %collective-permute-start.3 = (f32[4,5,128,128]{3,2,1,0:T(8,128)S(1)}, f32[4,5,128,128]{3,2,1,0:T(8,128)}, u32[]{:S(2)}, u32[]{:S(2)}) collective-permute-start(f32[4,5,128,128]{3,2,1,0:T(8,128)S(1)} %get-tuple-element.89), channel_id=1, source_target_pairs={{16,0},{32,16},{48,32},{64,48},{80,64},{96,80},{112,96},{17,1},{33... | collective-permute-start | bytes 3932168 | tf_op jit(solution)/shard_map/ppermute | solution.py:158
  31.6 1.1 select_subtract_fusion
  33.8 2.0 slice.269.refs_1_
  35.8 1.7 pad_maximum_fusion.2.refs_4_
  38.6 1.0 constant_dynamic-update-slice_fusion
  39.6 2.3 broadcast_select_fusion
  49.6 1.0 slice.234.refs_2_
  50.7 1.0 slice.235.refs_3_
  52.7 1.0 slice.237.refs_5_
  53.7 1.0 slice.238.refs_6_
  54.7 1.0 slice.239.refs_7_
  55.7 1.0 slice.240.refs_8_
  60.3 8.8 %shard_map.68 = (f32[4,14,64,128]{3,2,1,0:T(8,128)}, f32[4,14,64,128]{3,2,1,0:T(8,128)}) custom-call(s32[1]{0:T(128)} %bitcast.2.core_ref, f32[4,16,128,128]{3,2,1,0:T(8,128)} %refs_1_.1, f32[4,14,128,128]{3,2,1,0:T(8,128)} %slice.269.refs_1_, f32[14,128,128]{2,1,0:T(8,128)} %slice.234.refs_2_, f32[14,128,128]{2,1,0:T(8,128)} %slice.235.refs_3_, ...), custom_call_target="tpu_custom_call" | custom-call | tf_op jit(solution)/shard_map/pallas_call | solution.py:94
  69.1 13.1 %collective-permute-done.2.refs_2_ = f32[4,5,128,128]{3,2,1,0:T(8,128)} collective-permute-done((f32[4,5,128,128]{3,2,1,0:T(8,128)}, f32[4,5,128,128]{3,2,1,0:T(8,128)}, u32[]{:S(2)}, u32[]{:S(2)}) %collective-permute-start.2) | collective-permute-done | bytes 1310752 | tf_op jit(solution)/shard_map/ppermute | solution.py:157
  82.3 1.1 collective-permute-done.3.refs_3_
  83.3 7.2 %shard_map.69 = (f32[4,10,64,128]{3,2,1,0:T(8,128)}, f32[4,10,64,128]{3,2,1,0:T(8,128)}) custom-call(s32[1]{0:T(128)} %bitcast.2.core_ref, f32[4,16,128,128]{3,2,1,0:T(8,128)} %refs_1_.1, f32[4,16,128,128]{3,2,1,0:T(8,128)} %refs_1_.1, f32[4,5,128,128]{3,2,1,0:T(8,128)} %collective-permute-done.2.refs_2_, f32[4,5,128,128]{3,2,1,0:T(8,128)} %collective-permute-done.3.refs_3_, ...), custom_call_target="tpu_custom_call" | custom-call | tf_op jit(solution)/shard_map/pallas_call | solution.py:94
  91.8 2.0 collective-permute-done.5.refs_3_
  93.8 88.2 %all-gather.2.cloned.1.call-done.inv_ref = f32[16,24,64,128]{3,2,1,0:T(8,128)} async-done(((f32[16,24,8,128]{3,2,1,0:T(8,128)}), f32[16,24,64,128]{3,2,1,0:T(8,128)}) %all-gather.2.cloned.1.call-update) | async-done | bytes 12582928 | tf_op jit(solution)/shard_map/all_gather | solution.py:215
  182.0 12.5 %shard_map.70 = (f32[4,16,64,128]{3,2,1,0:T(8,128)}, f32[4,16,64,128]{3,2,1,0:T(8,128)}) custom-call(f32[24]{0:T(128)} %and_convert_fusion.mask_ref, f32[16,24,64,128]{3,2,1,0:T(8,128)} %all-gather.2.cloned.1.call-done.inv_ref, f32[4,14,64,128]{3,2,1,0:T(8,128)} %get-tuple-element.46.refs_0_, f32[4,10,64,128]{3,2,1,0:T(8,128)} %get-tuple-element.55.refs_1_, ...), custom_call_target="tpu_custom_call" | custom-call | tf_op jit(solution)/shard_map/pallas_call | solution.py:142
  194.5 4.4 %collective-permute-done.6 = f32[4,16,64,128]{3,2,1,0:T(8,128)S(1)} collective-permute-done((f32[4,16,64,128]{3,2,1,0:T(8,128)}, f32[4,16,64,128]{3,2,1,0:T(8,128)S(1)}, u32[]{:S(2)}, u32[]{:S(2)}) %collective-permute-start.6) | collective-permute-done | bytes 2097184 | tf_op jit(solution)/shard_map/ppermute | solution.py:270
  198.8 2.3 select_bitcast_fusion.3
  201.5 1.8 copy-done.4
  203.4 1.2 bitcast_add_fusion.1.refs_0_.refs_1_
  204.6 1.5 fusion.16
  207.0 1.9 collective-permute-start.7
  208.9 7.5 %collective-permute-start.8 = (f32[4,5,128,128]{3,2,1,0:T(8,128)S(1)}, f32[4,5,128,128]{3,2,1,0:T(8,128)}, u32[]{:S(2)}, u32[]{:S(2)}) collective-permute-start(f32[4,5,128,128]{3,2,1,0:T(8,128)S(1)} %get-tuple-element.85), channel_id=1, source_target_pairs={{16,0},{32,16},{48,32},{64,48},{80,64},{96,80},{112,96},{17,1},{33... | collective-permute-start | bytes 3932168 | tf_op jit(solution)/shard_map/ppermute | solution.py:158
  216.4 8.7 %shard_map.71 = (f32[4,14,64,128]{3,2,1,0:T(8,128)}, f32[4,14,64,128]{3,2,1,0:T(8,128)}) custom-call(s32[1]{0:T(128)} %bitcast.2.core_ref, f32[4,16,128,128]{3,2,1,0:T(8,128)} %copy-done.2, f32[4,14,128,128]{3,2,1,0:T(8,128)} %slice.269.refs_1_, f32[14,128,128]{2,1,0:T(8,128)} %slice.234.refs_2_, f32[14,128,128]{2,1,0:T(8,128)} %slice.235.refs_3_, ...), custom_call_target="tpu_custom_call" | custom-call | tf_op jit(solution)/shard_map/pallas_call | solution.py:94
  225.1 18.5 %collective-permute-done.7.refs_2_ = f32[4,5,128,128]{3,2,1,0:T(8,128)} collective-permute-done((f32[4,5,128,128]{3,2,1,0:T(8,128)}, f32[4,5,128,128]{3,2,1,0:T(8,128)}, u32[]{:S(2)}, u32[]{:S(2)}) %collective-permute-start.7) | collective-permute-done | bytes 1310752 | tf_op jit(solution)/shard_map/ppermute | solution.py:157
  244.5 7.2 %shard_map.72 = (f32[4,10,64,128]{3,2,1,0:T(8,128)}, f32[4,10,64,128]{3,2,1,0:T(8,128)}) custom-call(s32[1]{0:T(128)} %bitcast.2.core_ref, f32[4,16,128,128]{3,2,1,0:T(8,128)} %copy-done.2, f32[4,16,128,128]{3,2,1,0:T(8,128)} %copy-done.2, f32[4,5,128,128]{3,2,1,0:T(8,128)} %collective-permute-done.7.refs_2_, ...), custom_call_target="tpu_custom_call" | custom-call | tf_op jit(solution)/shard_map/pallas_call | solution.py:94
  251.9 3.2 collective-permute-done.10.refs_3_
  255.2 1.1 copy-done.10
  256.2 12.4 %shard_map.73 = (f32[4,16,64,128]{3,2,1,0:T(8,128)}, f32[4,16,64,128]{3,2,1,0:T(8,128)}) custom-call(f32[24]{0:T(128)} %and_convert_fusion.mask_ref, f32[16,24,64,128]{3,2,1,0:T(8,128)} %all-gather.2.cloned.1.call-done.inv_ref, f32[4,14,64,128]{3,2,1,0:T(8,128)} %get-tuple-element.60.refs_0_, f32[4,10,64,128]{3,2,1,0:T(8,128)} %get-tuple-element.61.refs_1_, ...), custom_call_target="tpu_custom_call" | custom-call | tf_op jit(solution)/shard_map/pallas_call | solution.py:142
  268.8 4.2 %collective-permute-done.11 = f32[4,16,64,128]{3,2,1,0:T(8,128)S(1)} collective-permute-done((f32[4,16,64,128]{3,2,1,0:T(8,128)}, f32[4,16,64,128]{3,2,1,0:T(8,128)S(1)}, u32[]{:S(2)}, u32[]{:S(2)}) %collective-permute-start.11) | collective-permute-done | bytes 2097184 | tf_op jit(solution)/shard_map/ppermute | solution.py:270
  273.0 2.3 select_bitcast_fusion.1
  275.8 1.8 copy-done.3
  277.6 1.2 bitcast_add_fusion.refs_0_.refs_1_
  278.8 2.0 copy-done.5
  280.8 1.9 collective-permute-start.12
  282.8 8.1 %collective-permute-start.13 = (f32[4,1,128,128]{3,2,1,0:T(8,128)S(1)}, f32[4,1,128,128]{3,2,1,0:T(8,128)S(1)}, u32[]{:S(2)}, u32[]{:S(2)}) collective-permute-start(f32[4,1,128,128]{3,2,1,0:T(8,128)S(1)} %get-tuple-element.81), channel_id=1, source_target_pairs={{16,0},{32,16},{48,32},{64,48},{80,64},{96,80},{112,96},{17,1},{33... | collective-permute-start | bytes 786440 | tf_op jit(solution)/shard_map/ppermute | solution.py:158
  290.9 7.7 %shard_map.74 = f32[4,8,128]{2,1,0:T(8,128)} custom-call(s32[1]{0:T(128)} %bitcast.2.core_ref, f32[4,16,128,128]{3,2,1,0:T(8,128)} %copy-done.5, f32[4,14,128,128]{3,2,1,0:T(8,128)} %slice.269.refs_1_, f32[14,128,128]{2,1,0:T(8,128)} %slice.234.refs_2_, f32[14,128,128]{2,1,0:T(8,128)} %slice.235.refs_3_, f32[14,128,128]{2,1,0:T(8,128)} %slice.236.refs_4_, ...), custom_call_target="tpu_custom_call" | custom-call | tf_op jit(solution)/shard_map/pallas_call | solution.py:94
  300.0 4.0 %shard_map.75 = f32[4,8,128]{2,1,0:T(8,128)} custom-call(s32[1]{0:T(128)} %bitcast.2.core_ref, f32[4,16,128,128]{3,2,1,0:T(8,128)} %copy-done.5, f32[4,16,128,128]{3,2,1,0:T(8,128)} %copy-done.5, f32[4,1,128,128]{3,2,1,0:T(8,128)} %copy-done.11, f32[4,1,128,128]{3,2,1,0:T(8,128)} %copy-done.12, f32[4,2,128,128]{3,2,1,0:T(8,128)} %pad_maximum_fusion.10.refs_4_, ...), custom_call_target="tpu_custom_call" | custom-call | tf_op jit(solution)/shard_map/pallas_call | solution.py:94
  304.9 3.6 %collective-permute-done.14 = f32[4]{0:T(128)S(1)} collective-permute-done((f32[4]{0:T(128)S(1)}, f32[4]{0:T(128)S(1)}, u32[]{:S(2)}, u32[]{:S(2)}) %collective-permute-start.14) | collective-permute-done | bytes 48 | tf_op jit(solution)/shard_map/ppermute | solution.py:281
  308.5 5.1 %collective-permute-done.15 = f32[4]{0:T(128)S(1)} collective-permute-done((f32[4]{0:T(128)S(1)}, f32[4]{0:T(128)S(1)}, u32[]{:S(2)}, u32[]{:S(2)}) %collective-permute-start.15) | collective-permute-done | bytes 48 | tf_op jit(solution)/shard_map/ppermute | solution.py:281
  313.6 5.0 %collective-permute-done.16 = f32[4]{0:T(128)S(1)} collective-permute-done((f32[4]{0:T(128)S(1)}, f32[4]{0:T(128)S(1)}, u32[]{:S(2)}, u32[]{:S(2)}) %collective-permute-start.16) | collective-permute-done | bytes 48 | tf_op jit(solution)/shard_map/ppermute | solution.py:281
  (85 shorter events, 23.2 us)
Async XLA Ops:
  7.2 24.1 %copy-start = (s32[64,2]{0,1:T(2,128)S(1)}, s32[64,2]{0,1:T(2,128)}, u32[]{:S(2)}) copy-start(s32[64,2]{0,1:T(2,128)} %param.8) | copy-start | bytes 1540
  7.2 1.2 copy-start.6
  7.2 174.8 %all-gather.2.cloned.1.call-start = ((), (), s32[]{:S(2)}) async-start(), calls=%async_computation | async-start | bytes 14155776 | tf_op jit(solution)/shard_map/all_gather | solution.py:215
  9.2 28.4 %collective-permute-start = (f32[5,128,128]{2,1,0:T(8,128)}, f32[5,128,128]{2,1,0:T(8,128)}, u32[]{:S(2)}, u32[]{:S(2)}) collective-permute-start(f32[5,128,128]{2,1,0:T(8,128)} %get-tuple-element.129), channel_id=1, source_target_pairs={{0,16},{16,32},{32,48},{48,64},{64,80},{80,96},{96,112},{1,17},{17... | collective-permute-start | bytes 983048 | tf_op jit(solution)/shard_map/ppermute | solution.py:157
  13.0 25.6 %collective-permute-start.1 = (f32[5,128,128]{2,1,0:T(8,128)S(1)}, f32[5,128,128]{2,1,0:T(8,128)}, u32[]{:S(2)}, u32[]{:S(2)}) collective-permute-start(f32[5,128,128]{2,1,0:T(8,128)S(1)} %get-tuple-element.128), channel_id=1, source_target_pairs={{16,0},{32,16},{48,32},{64,48},{80,64},{96,80},{112,96},{17,1},{33... | collective-permute-start | bytes 983048 | tf_op jit(solution)/shard_map/ppermute | solution.py:158
  21.8 60.5 %collective-permute-start.2 = (f32[4,5,128,128]{3,2,1,0:T(8,128)}, f32[4,5,128,128]{3,2,1,0:T(8,128)}, u32[]{:S(2)}, u32[]{:S(2)}) collective-permute-start(f32[4,5,128,128]{3,2,1,0:T(8,128)} %get-tuple-element.90), channel_id=1, source_target_pairs={{0,16},{16,32},{32,48},{48,64},{64,80},{80,96},{96,112},{1,17},{17... | collective-permute-start | bytes 3932168 | tf_op jit(solution)/shard_map/ppermute | solution.py:157
  23.7 59.7 %collective-permute-start.3 = (f32[4,5,128,128]{3,2,1,0:T(8,128)S(1)}, f32[4,5,128,128]{3,2,1,0:T(8,128)}, u32[]{:S(2)}, u32[]{:S(2)}) collective-permute-start(f32[4,5,128,128]{3,2,1,0:T(8,128)S(1)} %get-tuple-element.89), channel_id=1, source_target_pairs={{16,0},{32,16},{48,32},{64,48},{80,64},{96,80},{112,96},{17,1},{33... | collective-permute-start | bytes 3932168 | tf_op jit(solution)/shard_map/ppermute | solution.py:158
  69.1 22.7 %collective-permute-start.4 = (f32[4,14,64,128]{3,2,1,0:T(8,128)}, f32[4,14,64,128]{3,2,1,0:T(8,128)S(1)}, u32[]{:S(2)}, u32[]{:S(2)}) collective-permute-start(f32[4,14,64,128]{3,2,1,0:T(8,128)} %get-tuple-element.56), channel_id=1, source_target_pairs={{0,1},{1,0},{2,3},{3,2},{4,5},{5,4},{6,7},{7,6},{8,9},{9,8},{10,11... | collective-permute-start | bytes 5505032 | tf_op jit(solution)/shard_map/ppermute | solution.py:264
  90.5 3.3 collective-permute-start.5
  91.8 90.2 %copy-start.7 = (f32[4,14,64,128]{3,2,1,0:T(8,128)}, f32[4,14,64,128]{3,2,1,0:T(8,128)S(1)}, u32[]{:S(2)}) copy-start(f32[4,14,64,128]{3,2,1,0:T(8,128)S(1)} %collective-permute-done.4.refs_2_) | copy-start | bytes 5505028
  93.8 88.2 %copy-start.9 = (f32[4,10,64,128]{3,2,1,0:T(8,128)}, f32[4,10,64,128]{3,2,1,0:T(8,128)S(1)}, u32[]{:S(2)}) copy-start(f32[4,10,64,128]{3,2,1,0:T(8,128)S(1)} %collective-permute-done.5.refs_3_) | copy-start | bytes 3932164
  194.4 4.4 %collective-permute-start.6 = (f32[4,16,64,128]{3,2,1,0:T(8,128)}, f32[4,16,64,128]{3,2,1,0:T(8,128)S(1)}, u32[]{:S(2)}, u32[]{:S(2)}) collective-permute-start(f32[4,16,64,128]{3,2,1,0:T(8,128)} %get-tuple-element.59), channel_id=1, source_target_pairs={{0,1},{1,0},{2,3},{3,2},{4,5},{5,4},{6,7},{7,6},{8,9},{9,8},{10,11... | collective-permute-start | bytes 6291464 | tf_op jit(solution)/shard_map/ppermute | solution.py:270
  201.2 2.2 copy-start.4
  204.6 2.4 copy-start.2
  207.0 36.6 %collective-permute-start.7 = (f32[4,5,128,128]{3,2,1,0:T(8,128)}, f32[4,5,128,128]{3,2,1,0:T(8,128)}, u32[]{:S(2)}, u32[]{:S(2)}) collective-permute-start(f32[4,5,128,128]{3,2,1,0:T(8,128)} %get-tuple-element.86), channel_id=1, source_target_pairs={{0,16},{16,32},{32,48},{48,64},{64,80},{80,96},{96,112},{1,17},{17... | collective-permute-start | bytes 3932168 | tf_op jit(solution)/shard_map/ppermute | solution.py:157
  208.9 35.6 %collective-permute-start.8 = (f32[4,5,128,128]{3,2,1,0:T(8,128)S(1)}, f32[4,5,128,128]{3,2,1,0:T(8,128)}, u32[]{:S(2)}, u32[]{:S(2)}) collective-permute-start(f32[4,5,128,128]{3,2,1,0:T(8,128)S(1)} %get-tuple-element.85), channel_id=1, source_target_pairs={{16,0},{32,16},{48,32},{64,48},{80,64},{96,80},{112,96},{17,1},{33... | collective-permute-start | bytes 3932168 | tf_op jit(solution)/shard_map/ppermute | solution.py:158
  225.1 26.8 %collective-permute-start.9 = (f32[4,14,64,128]{3,2,1,0:T(8,128)}, f32[4,14,64,128]{3,2,1,0:T(8,128)S(1)}, u32[]{:S(2)}, u32[]{:S(2)}) collective-permute-start(f32[4,14,64,128]{3,2,1,0:T(8,128)} %get-tuple-element.62), channel_id=1, source_target_pairs={{0,1},{1,0},{2,3},{3,2},{4,5},{5,4},{6,7},{7,6},{8,9},{9,8},{10,11... | collective-permute-start | bytes 5505032 | tf_op jit(solution)/shard_map/ppermute | solution.py:264
  251.7 3.5 %collective-permute-start.10 = (f32[4,10,64,128]{3,2,1,0:T(8,128)}, f32[4,10,64,128]{3,2,1,0:T(8,128)S(1)}, u32[]{:S(2)}, u32[]{:S(2)}) collective-permute-start(f32[4,10,64,128]{3,2,1,0:T(8,128)} %get-tuple-element.63), channel_id=1, source_target_pairs={{0,1},{1,0},{2,3},{3,2},{4,5},{5,4},{6,7},{7,6},{8,9},{9,8},{10,11... | collective-permute-start | bytes 3932168 | tf_op jit(solution)/shard_map/ppermute | solution.py:266
  251.9 3.2 copy-start.8
  255.2 1.1 copy-start.10
  268.7 4.4 %collective-permute-start.11 = (f32[4,16,64,128]{3,2,1,0:T(8,128)}, f32[4,16,64,128]{3,2,1,0:T(8,128)S(1)}, u32[]{:S(2)}, u32[]{:S(2)}) collective-permute-start(f32[4,16,64,128]{3,2,1,0:T(8,128)} %get-tuple-element.65), channel_id=1, source_target_pairs={{0,1},{1,0},{2,3},{3,2},{4,5},{5,4},{6,7},{7,6},{8,9},{9,8},{10,11... | collective-permute-start | bytes 6291464 | tf_op jit(solution)/shard_map/ppermute | solution.py:270
  275.4 2.2 copy-start.3
  278.8 2.0 copy-start.5
  280.8 17.7 %collective-permute-start.12 = (f32[4,1,128,128]{3,2,1,0:T(8,128)S(1)}, f32[4,1,128,128]{3,2,1,0:T(8,128)S(1)}, u32[]{:S(2)}, u32[]{:S(2)}) collective-permute-start(f32[4,1,128,128]{3,2,1,0:T(8,128)S(1)} %get-tuple-element.82), channel_id=1, source_target_pairs={{0,16},{16,32},{32,48},{48,64},{64,80},{80,96},{96,112},{1,17},{17... | collective-permute-start | bytes 786440 | tf_op jit(solution)/shard_map/ppermute | solution.py:157
  282.8 15.8 %collective-permute-start.13 = (f32[4,1,128,128]{3,2,1,0:T(8,128)S(1)}, f32[4,1,128,128]{3,2,1,0:T(8,128)S(1)}, u32[]{:S(2)}, u32[]{:S(2)}) collective-permute-start(f32[4,1,128,128]{3,2,1,0:T(8,128)S(1)} %get-tuple-element.81), channel_id=1, source_target_pairs={{16,0},{32,16},{48,32},{64,48},{80,64},{96,80},{112,96},{17,1},{33... | collective-permute-start | bytes 786440 | tf_op jit(solution)/shard_map/ppermute | solution.py:158
  298.6 5.4 %copy-start.13 = (f32[4,8,128]{2,1,0:T(8,128)S(1)}, f32[4,8,128]{2,1,0:T(8,128)}, u32[]{:S(2)}) copy-start(f32[4,8,128]{2,1,0:T(8,128)} %shard_map.74) | copy-start | bytes 49156
  298.6 0.7 copy-start.11
  299.3 0.7 copy-start.12
  300.0 19.2 %copy-start.1 = (s32[64,2]{0,1:T(2,128)S(1)}, s32[64,2]{0,1:T(2,128)}, u32[]{:S(2)}) copy-start(s32[64,2]{0,1:T(2,128)} %param.8) | copy-start | bytes 1540
  304.8 3.6 %collective-permute-start.14 = (f32[4]{0:T(128)S(1)}, f32[4]{0:T(128)S(1)}, u32[]{:S(2)}, u32[]{:S(2)}) collective-permute-start(f32[4]{0:T(128)S(1)} %add_reduce_fusion), channel_id=1, source_target_pairs={{0,16},{16,0},{32,48},{48,32},{64,80},{80,64},{96,112},{112,96},{1... | collective-permute-start | bytes 56 | tf_op jit(solution)/shard_map/ppermute | solution.py:281
  308.5 5.1 %collective-permute-start.15 = (f32[4]{0:T(128)S(1)}, f32[4]{0:T(128)S(1)}, u32[]{:S(2)}, u32[]{:S(2)}) collective-permute-start(f32[4]{0:T(128)S(1)} %add.111), channel_id=1, source_target_pairs={{0,32},{16,48},{32,0},{48,16},{64,96},{80,112},{96,64},{112,80},{1... | collective-permute-start | bytes 56 | tf_op jit(solution)/shard_map/ppermute | solution.py:281
  313.6 5.1 %collective-permute-start.16 = (f32[4]{0:T(128)S(1)}, f32[4]{0:T(128)S(1)}, u32[]{:S(2)}, u32[]{:S(2)}) collective-permute-start(f32[4]{0:T(128)S(1)} %add.112), channel_id=1, source_target_pairs={{0,64},{16,80},{32,96},{48,112},{64,0},{80,16},{96,32},{112,48},{1... | collective-permute-start | bytes 56 | tf_op jit(solution)/shard_map/ppermute | solution.py:281
Sparse Core Ops, SparseCore 0:
  9.6 172.3 all-gather.1

commit v14 on v13

--- a/solution.py
+++ b/solution.py
@@ -101,7 +101,7 @@
     )(core, *own_args, *rims, st, *coefs)
 
 
-def make_correction_kernel(columns, chunk=2):
+def make_correction_kernel(columns, chunk=1):
     def kernel(mask_ref, inv_ref, *refs):
         mine_ref, theirs_ref = refs[-2:]
         pieces = refs[:-2]
@@ -135,7 +135,7 @@
     return kernel
 
 
-def correction_call(mask, inv, own_pieces, got_pieces, columns, rows=16):
+def correction_call(mask, inv, own_pieces, got_pieces, columns, rows=32):
     n_out, n_col, ny, nz = inv.shape
     n_src = sum(p.shape[0] for p in own_pieces[:1]) * 2
     specs = [pl.BlockSpec((p.shape[0], p.shape[1], rows, nz), lambda b: (0, 0, b, 0)) for p in own_pieces + got_pieces]

time: 327 us -> 331 us (1.012)
  Pallas kernels: 68.5 us -> 72.4 us
    pallas_call x2, Pallas kernels: 24.9 us -> 28.8 us  [correction_call(): pl.pallas_call(make_correction_kernel(tuple(columns)), grid=(ny // rows,)...]
where the time goes in v14:
time: 331 us; the launch traced here: 330 us
  waiting for transfers between devices  150 us (45%)
  Pallas kernels  72.4 us (22%)
  starting transfers between devices  38.9 us (12%)
  local copies, waits for them, and re-layouts  26.9 us (8%)
  other arithmetic  26.7 us (8%)
  between operations  15.1 us (5%)
    all_gather x1, waiting for transfers between devices, on_device(): inverse_mine = lax.all_gather(inverse_rows, CHIP_AXES, axis=2, tiled=True)  88.2 us
    pallas_call x6, Pallas kernels, stencil_call(): pl.pallas_call(make_stencil_kernel(tuple(planes), len(rims) > 0, mode, wi...  43.6 us
    ppermute x4, waiting for transfers between devices, rims_of(): lo = lax.ppermute(tail, 'sub', [(i, i + 1) for i in range(count - 1)])  31.6 us
    ppermute x4, starting transfers between devices, rims_of(): hi = lax.ppermute(head, 'sub', [(i + 1, i) for i in range(count - 1)])  28.8 us
    pallas_call x2, Pallas kernels, correction_call(): pl.pallas_call(make_correction_kernel(tuple(columns)), grid=(ny // rows,)...  28.8 us
    ppermute x3, waiting for transfers between devices, on_device(): lax.ppermute(totals, 'sub', [(i, i ^ step_size) for i in range(n_sub)])  13.7 us
    unnamed x30, local copies, waits for them, and re-layouts  10.6 us
    ppermute x4, starting transfers between devices, rims_of(): lo = lax.ppermute(tail, 'sub', [(i, i + 1) for i in range(count - 1)])  9.55 us
  transfers between devices with their start and end apart: 18, of which 12 were waited for; matrix products, arithmetic and copies ran while one was open for 10% of the time, Pallas kernels for 12%

profile of v14, /device:TPU:6, one launch (start us, length us, event | category | flops | bytes accessed | tf_op | source)
XLA Modules:
  0.0 329.9 jit_solution(12926006528313940498)
XLA Ops:
  9.2 3.8 %collective-permute-start = (f32[5,128,128]{2,1,0:T(8,128)}, f32[5,128,128]{2,1,0:T(8,128)}, u32[]{:S(2)}, u32[]{:S(2)}) collective-permute-start(f32[5,128,128]{2,1,0:T(8,128)} %get-tuple-element.129), channel_id=1, source_target_pairs={{0,16},{16,32},{32,48},{48,64},{64,80},{80,96},{96,112},{1,17},{17... | collective-permute-start | bytes 983048 | tf_op jit(solution)/shard_map/ppermute | solution.py:157
  13.0 5.6 %collective-permute-start.1 = (f32[5,128,128]{2,1,0:T(8,128)S(1)}, f32[5,128,128]{2,1,0:T(8,128)}, u32[]{:S(2)}, u32[]{:S(2)}) collective-permute-start(f32[5,128,128]{2,1,0:T(8,128)S(1)} %get-tuple-element.128), channel_id=1, source_target_pairs={{16,0},{32,16},{48,32},{64,48},{80,64},{96,80},{112,96},{17,1},{33... | collective-permute-start | bytes 983048 | tf_op jit(solution)/shard_map/ppermute | solution.py:158
  18.6 3.1 fusion.17
  21.8 1.9 collective-permute-start.2
  23.7 7.5 %collective-permute-start.3 = (f32[4,5,128,128]{3,2,1,0:T(8,128)S(1)}, f32[4,5,128,128]{3,2,1,0:T(8,128)}, u32[]{:S(2)}, u32[]{:S(2)}) collective-permute-start(f32[4,5,128,128]{3,2,1,0:T(8,128)S(1)} %get-tuple-element.89), channel_id=1, source_target_pairs={{16,0},{32,16},{48,32},{64,48},{80,64},{96,80},{112,96},{17,1},{33... | collective-permute-start | bytes 3932168 | tf_op jit(solution)/shard_map/ppermute | solution.py:158
  31.6 1.1 select_subtract_fusion
  33.8 2.0 slice.269.refs_1_
  35.8 1.7 pad_maximum_fusion.2.refs_4_
  38.6 1.0 constant_dynamic-update-slice_fusion
  39.6 2.3 broadcast_select_fusion
  49.6 1.0 slice.234.refs_2_
  50.7 1.0 slice.235.refs_3_
  52.7 1.0 slice.237.refs_5_
  53.7 1.0 slice.238.refs_6_
  54.7 1.0 slice.239.refs_7_
  55.7 1.0 slice.240.refs_8_
  60.3 8.8 %shard_map.68 = (f32[4,14,64,128]{3,2,1,0:T(8,128)}, f32[4,14,64,128]{3,2,1,0:T(8,128)}) custom-call(s32[1]{0:T(128)} %bitcast.2.core_ref, f32[4,16,128,128]{3,2,1,0:T(8,128)} %refs_1_.1, f32[4,14,128,128]{3,2,1,0:T(8,128)} %slice.269.refs_1_, f32[14,128,128]{2,1,0:T(8,128)} %slice.234.refs_2_, f32[14,128,128]{2,1,0:T(8,128)} %slice.235.refs_3_, ...), custom_call_target="tpu_custom_call" | custom-call | tf_op jit(solution)/shard_map/pallas_call | solution.py:94
  69.1 13.1 %collective-permute-done.2.refs_2_ = f32[4,5,128,128]{3,2,1,0:T(8,128)} collective-permute-done((f32[4,5,128,128]{3,2,1,0:T(8,128)}, f32[4,5,128,128]{3,2,1,0:T(8,128)}, u32[]{:S(2)}, u32[]{:S(2)}) %collective-permute-start.2) | collective-permute-done | bytes 1310752 | tf_op jit(solution)/shard_map/ppermute | solution.py:157
  82.3 1.1 collective-permute-done.3.refs_3_
  83.3 7.2 %shard_map.69 = (f32[4,10,64,128]{3,2,1,0:T(8,128)}, f32[4,10,64,128]{3,2,1,0:T(8,128)}) custom-call(s32[1]{0:T(128)} %bitcast.2.core_ref, f32[4,16,128,128]{3,2,1,0:T(8,128)} %refs_1_.1, f32[4,16,128,128]{3,2,1,0:T(8,128)} %refs_1_.1, f32[4,5,128,128]{3,2,1,0:T(8,128)} %collective-permute-done.2.refs_2_, f32[4,5,128,128]{3,2,1,0:T(8,128)} %collective-permute-done.3.refs_3_, ...), custom_call_target="tpu_custom_call" | custom-call | tf_op jit(solution)/shard_map/pallas_call | solution.py:94
  91.8 2.0 collective-permute-done.5.refs_3_
  93.8 88.2 %all-gather.2.cloned.1.call-done.inv_ref = f32[16,24,64,128]{3,2,1,0:T(8,128)} async-done(((f32[16,24,8,128]{3,2,1,0:T(8,128)}), f32[16,24,64,128]{3,2,1,0:T(8,128)}) %all-gather.2.cloned.1.call-update) | async-done | bytes 12582928 | tf_op jit(solution)/shard_map/all_gather | solution.py:215
  182.0 14.4 %shard_map.70 = (f32[4,16,64,128]{3,2,1,0:T(8,128)}, f32[4,16,64,128]{3,2,1,0:T(8,128)}) custom-call(f32[24]{0:T(128)} %and_convert_fusion.mask_ref, f32[16,24,64,128]{3,2,1,0:T(8,128)} %all-gather.2.cloned.1.call-done.inv_ref, f32[4,14,64,128]{3,2,1,0:T(8,128)} %get-tuple-element.46.refs_0_, f32[4,10,64,128]{3,2,1,0:T(8,128)} %get-tuple-element.55.refs_1_, ...), custom_call_target="tpu_custom_call" | custom-call | tf_op jit(solution)/shard_map/pallas_call | solution.py:142
  196.4 4.4 %collective-permute-done.6 = f32[4,16,64,128]{3,2,1,0:T(8,128)S(1)} collective-permute-done((f32[4,16,64,128]{3,2,1,0:T(8,128)}, f32[4,16,64,128]{3,2,1,0:T(8,128)S(1)}, u32[]{:S(2)}, u32[]{:S(2)}) %collective-permute-start.6) | collective-permute-done | bytes 2097184 | tf_op jit(solution)/shard_map/ppermute | solution.py:270
  200.8 2.3 select_bitcast_fusion.3
  203.5 1.8 copy-done.4
  205.3 1.2 bitcast_add_fusion.1.refs_0_.refs_1_
  206.5 1.5 fusion.16
  208.9 1.9 collective-permute-start.7
  210.8 7.5 %collective-permute-start.8 = (f32[4,5,128,128]{3,2,1,0:T(8,128)S(1)}, f32[4,5,128,128]{3,2,1,0:T(8,128)}, u32[]{:S(2)}, u32[]{:S(2)}) collective-permute-start(f32[4,5,128,128]{3,2,1,0:T(8,128)S(1)} %get-tuple-element.85), channel_id=1, source_target_pairs={{16,0},{32,16},{48,32},{64,48},{80,64},{96,80},{112,96},{17,1},{33... | collective-permute-start | bytes 3932168 | tf_op jit(solution)/shard_map/ppermute | solution.py:158
  218.4 8.7 %shard_map.71 = (f32[4,14,64,128]{3,2,1,0:T(8,128)}, f32[4,14,64,128]{3,2,1,0:T(8,128)}) custom-call(s32[1]{0:T(128)} %bitcast.2.core_ref, f32[4,16,128,128]{3,2,1,0:T(8,128)} %copy-done.2, f32[4,14,128,128]{3,2,1,0:T(8,128)} %slice.269.refs_1_, f32[14,128,128]{2,1,0:T(8,128)} %slice.234.refs_2_, f32[14,128,128]{2,1,0:T(8,128)} %slice.235.refs_3_, ...), custom_call_target="tpu_custom_call" | custom-call | tf_op jit(solution)/shard_map/pallas_call | solution.py:94
  227.1 18.5 %collective-permute-done.7.refs_2_ = f32[4,5,128,128]{3,2,1,0:T(8,128)} collective-permute-done((f32[4,5,128,128]{3,2,1,0:T(8,128)}, f32[4,5,128,128]{3,2,1,0:T(8,128)}, u32[]{:S(2)}, u32[]{:S(2)}) %collective-permute-start.7) | collective-permute-done | bytes 1310752 | tf_op jit(solution)/shard_map/ppermute | solution.py:157
  246.4 7.2 %shard_map.72 = (f32[4,10,64,128]{3,2,1,0:T(8,128)}, f32[4,10,64,128]{3,2,1,0:T(8,128)}) custom-call(s32[1]{0:T(128)} %bitcast.2.core_ref, f32[4,16,128,128]{3,2,1,0:T(8,128)} %copy-done.2, f32[4,16,128,128]{3,2,1,0:T(8,128)} %copy-done.2, f32[4,5,128,128]{3,2,1,0:T(8,128)} %collective-permute-done.7.refs_2_, ...), custom_call_target="tpu_custom_call" | custom-call | tf_op jit(solution)/shard_map/pallas_call | solution.py:94
  253.9 3.2 collective-permute-done.10.refs_3_
  257.1 1.1 copy-done.10
  258.2 14.4 %shard_map.73 = (f32[4,16,64,128]{3,2,1,0:T(8,128)}, f32[4,16,64,128]{3,2,1,0:T(8,128)}) custom-call(f32[24]{0:T(128)} %and_convert_fusion.mask_ref, f32[16,24,64,128]{3,2,1,0:T(8,128)} %all-gather.2.cloned.1.call-done.inv_ref, f32[4,14,64,128]{3,2,1,0:T(8,128)} %get-tuple-element.60.refs_0_, f32[4,10,64,128]{3,2,1,0:T(8,128)} %get-tuple-element.61.refs_1_, ...), custom_call_target="tpu_custom_call" | custom-call | tf_op jit(solution)/shard_map/pallas_call | solution.py:142
  272.7 4.2 %collective-permute-done.11 = f32[4,16,64,128]{3,2,1,0:T(8,128)S(1)} collective-permute-done((f32[4,16,64,128]{3,2,1,0:T(8,128)}, f32[4,16,64,128]{3,2,1,0:T(8,128)S(1)}, u32[]{:S(2)}, u32[]{:S(2)}) %collective-permute-start.11) | collective-permute-done | bytes 2097184 | tf_op jit(solution)/shard_map/ppermute | solution.py:270
  277.0 2.3 select_bitcast_fusion.1
  279.7 1.8 copy-done.3
  281.5 1.2 bitcast_add_fusion.refs_0_.refs_1_
  282.7 2.0 copy-done.5
  284.8 1.9 collective-permute-start.12
  286.7 8.1 %collective-permute-start.13 = (f32[4,1,128,128]{3,2,1,0:T(8,128)S(1)}, f32[4,1,128,128]{3,2,1,0:T(8,128)S(1)}, u32[]{:S(2)}, u32[]{:S(2)}) collective-permute-start(f32[4,1,128,128]{3,2,1,0:T(8,128)S(1)} %get-tuple-element.81), channel_id=1, source_target_pairs={{16,0},{32,16},{48,32},{64,48},{80,64},{96,80},{112,96},{17,1},{33... | collective-permute-start | bytes 786440 | tf_op jit(solution)/shard_map/ppermute | solution.py:158
  294.8 7.7 %shard_map.74 = f32[4,8,128]{2,1,0:T(8,128)} custom-call(s32[1]{0:T(128)} %bitcast.2.core_ref, f32[4,16,128,128]{3,2,1,0:T(8,128)} %copy-done.5, f32[4,14,128,128]{3,2,1,0:T(8,128)} %slice.269.refs_1_, f32[14,128,128]{2,1,0:T(8,128)} %slice.234.refs_2_, f32[14,128,128]{2,1,0:T(8,128)} %slice.235.refs_3_, f32[14,128,128]{2,1,0:T(8,128)} %slice.236.refs_4_, ...), custom_call_target="tpu_custom_call" | custom-call | tf_op jit(solution)/shard_map/pallas_call | solution.py:94
  303.9 4.0 %shard_map.75 = f32[4,8,128]{2,1,0:T(8,128)} custom-call(s32[1]{0:T(128)} %bitcast.2.core_ref, f32[4,16,128,128]{3,2,1,0:T(8,128)} %copy-done.5, f32[4,16,128,128]{3,2,1,0:T(8,128)} %copy-done.5, f32[4,1,128,128]{3,2,1,0:T(8,128)} %copy-done.11, f32[4,1,128,128]{3,2,1,0:T(8,128)} %copy-done.12, f32[4,2,128,128]{3,2,1,0:T(8,128)} %pad_maximum_fusion.10.refs_4_, ...), custom_call_target="tpu_custom_call" | custom-call | tf_op jit(solution)/shard_map/pallas_call | solution.py:94
  308.8 3.6 %collective-permute-done.14 = f32[4]{0:T(128)S(1)} collective-permute-done((f32[4]{0:T(128)S(1)}, f32[4]{0:T(128)S(1)}, u32[]{:S(2)}, u32[]{:S(2)}) %collective-permute-start.14) | collective-permute-done | bytes 48 | tf_op jit(solution)/shard_map/ppermute | solution.py:281
  312.4 5.1 %collective-permute-done.15 = f32[4]{0:T(128)S(1)} collective-permute-done((f32[4]{0:T(128)S(1)}, f32[4]{0:T(128)S(1)}, u32[]{:S(2)}, u32[]{:S(2)}) %collective-permute-start.15) | collective-permute-done | bytes 48 | tf_op jit(solution)/shard_map/ppermute | solution.py:281
  317.5 5.0 %collective-permute-done.16 = f32[4]{0:T(128)S(1)} collective-permute-done((f32[4]{0:T(128)S(1)}, f32[4]{0:T(128)S(1)}, u32[]{:S(2)}, u32[]{:S(2)}) %collective-permute-start.16) | collective-permute-done | bytes 48 | tf_op jit(solution)/shard_map/ppermute | solution.py:281
  (85 shorter events, 23.2 us)
Async XLA Ops:
  7.2 24.1 %copy-start = (s32[64,2]{0,1:T(2,128)S(1)}, s32[64,2]{0,1:T(2,128)}, u32[]{:S(2)}) copy-start(s32[64,2]{0,1:T(2,128)} %param.8) | copy-start | bytes 1540
  7.2 1.2 copy-start.6
  7.2 174.8 %all-gather.2.cloned.1.call-start = ((), (), s32[]{:S(2)}) async-start(), calls=%async_computation | async-start | bytes 14155776 | tf_op jit(solution)/shard_map/all_gather | solution.py:215
  9.2 28.4 %collective-permute-start = (f32[5,128,128]{2,1,0:T(8,128)}, f32[5,128,128]{2,1,0:T(8,128)}, u32[]{:S(2)}, u32[]{:S(2)}) collective-permute-start(f32[5,128,128]{2,1,0:T(8,128)} %get-tuple-element.129), channel_id=1, source_target_pairs={{0,16},{16,32},{32,48},{48,64},{64,80},{80,96},{96,112},{1,17},{17... | collective-permute-start | bytes 983048 | tf_op jit(solution)/shard_map/ppermute | solution.py:157
  13.0 25.6 %collective-permute-start.1 = (f32[5,128,128]{2,1,0:T(8,128)S(1)}, f32[5,128,128]{2,1,0:T(8,128)}, u32[]{:S(2)}, u32[]{:S(2)}) collective-permute-start(f32[5,128,128]{2,1,0:T(8,128)S(1)} %get-tuple-element.128), channel_id=1, source_target_pairs={{16,0},{32,16},{48,32},{64,48},{80,64},{96,80},{112,96},{17,1},{33... | collective-permute-start | bytes 983048 | tf_op jit(solution)/shard_map/ppermute | solution.py:158
  21.8 60.5 %collective-permute-start.2 = (f32[4,5,128,128]{3,2,1,0:T(8,128)}, f32[4,5,128,128]{3,2,1,0:T(8,128)}, u32[]{:S(2)}, u32[]{:S(2)}) collective-permute-start(f32[4,5,128,128]{3,2,1,0:T(8,128)} %get-tuple-element.90), channel_id=1, source_target_pairs={{0,16},{16,32},{32,48},{48,64},{64,80},{80,96},{96,112},{1,17},{17... | collective-permute-start | bytes 3932168 | tf_op jit(solution)/shard_map/ppermute | solution.py:157
  23.7 59.7 %collective-permute-start.3 = (f32[4,5,128,128]{3,2,1,0:T(8,128)S(1)}, f32[4,5,128,128]{3,2,1,0:T(8,128)}, u32[]{:S(2)}, u32[]{:S(2)}) collective-permute-start(f32[4,5,128,128]{3,2,1,0:T(8,128)S(1)} %get-tuple-element.89), channel_id=1, source_target_pairs={{16,0},{32,16},{48,32},{64,48},{80,64},{96,80},{112,96},{17,1},{33... | collective-permute-start | bytes 3932168 | tf_op jit(solution)/shard_map/ppermute | solution.py:158
  69.1 22.7 %collective-permute-start.4 = (f32[4,14,64,128]{3,2,1,0:T(8,128)}, f32[4,14,64,128]{3,2,1,0:T(8,128)S(1)}, u32[]{:S(2)}, u32[]{:S(2)}) collective-permute-start(f32[4,14,64,128]{3,2,1,0:T(8,128)} %get-tuple-element.56), channel_id=1, source_target_pairs={{0,1},{1,0},{2,3},{3,2},{4,5},{5,4},{6,7},{7,6},{8,9},{9,8},{10,11... | collective-permute-start | bytes 5505032 | tf_op jit(solution)/shard_map/ppermute | solution.py:264
  90.5 3.3 collective-permute-start.5
  91.8 90.2 %copy-start.7 = (f32[4,14,64,128]{3,2,1,0:T(8,128)}, f32[4,14,64,128]{3,2,1,0:T(8,128)S(1)}, u32[]{:S(2)}) copy-start(f32[4,14,64,128]{3,2,1,0:T(8,128)S(1)} %collective-permute-done.4.refs_2_) | copy-start | bytes 5505028
  93.8 88.2 %copy-start.9 = (f32[4,10,64,128]{3,2,1,0:T(8,128)}, f32[4,10,64,128]{3,2,1,0:T(8,128)S(1)}, u32[]{:S(2)}) copy-start(f32[4,10,64,128]{3,2,1,0:T(8,128)S(1)} %collective-permute-done.5.refs_3_) | copy-start | bytes 3932164
  196.4 4.4 %collective-permute-start.6 = (f32[4,16,64,128]{3,2,1,0:T(8,128)}, f32[4,16,64,128]{3,2,1,0:T(8,128)S(1)}, u32[]{:S(2)}, u32[]{:S(2)}) collective-permute-start(f32[4,16,64,128]{3,2,1,0:T(8,128)} %get-tuple-element.59), channel_id=1, source_target_pairs={{0,1},{1,0},{2,3},{3,2},{4,5},{5,4},{6,7},{7,6},{8,9},{9,8},{10,11... | collective-permute-start | bytes 6291464 | tf_op jit(solution)/shard_map/ppermute | solution.py:270
  203.1 2.2 copy-start.4
  206.5 2.4 copy-start.2
  208.9 36.6 %collective-permute-start.7 = (f32[4,5,128,128]{3,2,1,0:T(8,128)}, f32[4,5,128,128]{3,2,1,0:T(8,128)}, u32[]{:S(2)}, u32[]{:S(2)}) collective-permute-start(f32[4,5,128,128]{3,2,1,0:T(8,128)} %get-tuple-element.86), channel_id=1, source_target_pairs={{0,16},{16,32},{32,48},{48,64},{64,80},{80,96},{96,112},{1,17},{17... | collective-permute-start | bytes 3932168 | tf_op jit(solution)/shard_map/ppermute | solution.py:157
  210.8 35.6 %collective-permute-start.8 = (f32[4,5,128,128]{3,2,1,0:T(8,128)S(1)}, f32[4,5,128,128]{3,2,1,0:T(8,128)}, u32[]{:S(2)}, u32[]{:S(2)}) collective-permute-start(f32[4,5,128,128]{3,2,1,0:T(8,128)S(1)} %get-tuple-element.85), channel_id=1, source_target_pairs={{16,0},{32,16},{48,32},{64,48},{80,64},{96,80},{112,96},{17,1},{33... | collective-permute-start | bytes 3932168 | tf_op jit(solution)/shard_map/ppermute | solution.py:158
  227.1 26.8 %collective-permute-start.9 = (f32[4,14,64,128]{3,2,1,0:T(8,128)}, f32[4,14,64,128]{3,2,1,0:T(8,128)S(1)}, u32[]{:S(2)}, u32[]{:S(2)}) collective-permute-start(f32[4,14,64,128]{3,2,1,0:T(8,128)} %get-tuple-element.62), channel_id=1, source_target_pairs={{0,1},{1,0},{2,3},{3,2},{4,5},{5,4},{6,7},{7,6},{8,9},{9,8},{10,11... | collective-permute-start | bytes 5505032 | tf_op jit(solution)/shard_map/ppermute | solution.py:264
  253.7 3.5 %collective-permute-start.10 = (f32[4,10,64,128]{3,2,1,0:T(8,128)}, f32[4,10,64,128]{3,2,1,0:T(8,128)S(1)}, u32[]{:S(2)}, u32[]{:S(2)}) collective-permute-start(f32[4,10,64,128]{3,2,1,0:T(8,128)} %get-tuple-element.63), channel_id=1, source_target_pairs={{0,1},{1,0},{2,3},{3,2},{4,5},{5,4},{6,7},{7,6},{8,9},{9,8},{10,11... | collective-permute-start | bytes 3932168 | tf_op jit(solution)/shard_map/ppermute | solution.py:266
  253.9 3.2 copy-start.8
  257.1 1.1 copy-start.10
  272.6 4.4 %collective-permute-start.11 = (f32[4,16,64,128]{3,2,1,0:T(8,128)}, f32[4,16,64,128]{3,2,1,0:T(8,128)S(1)}, u32[]{:S(2)}, u32[]{:S(2)}) collective-permute-start(f32[4,16,64,128]{3,2,1,0:T(8,128)} %get-tuple-element.65), channel_id=1, source_target_pairs={{0,1},{1,0},{2,3},{3,2},{4,5},{5,4},{6,7},{7,6},{8,9},{9,8},{10,11... | collective-permute-start | bytes 6291464 | tf_op jit(solution)/shard_map/ppermute | solution.py:270
  279.3 2.2 copy-start.3
  282.7 2.0 copy-start.5
  284.8 17.7 %collective-permute-start.12 = (f32[4,1,128,128]{3,2,1,0:T(8,128)S(1)}, f32[4,1,128,128]{3,2,1,0:T(8,128)S(1)}, u32[]{:S(2)}, u32[]{:S(2)}) collective-permute-start(f32[4,1,128,128]{3,2,1,0:T(8,128)S(1)} %get-tuple-element.82), channel_id=1, source_target_pairs={{0,16},{16,32},{32,48},{48,64},{64,80},{80,96},{96,112},{1,17},{17... | collective-permute-start | bytes 786440 | tf_op jit(solution)/shard_map/ppermute | solution.py:157
  286.7 15.8 %collective-permute-start.13 = (f32[4,1,128,128]{3,2,1,0:T(8,128)S(1)}, f32[4,1,128,128]{3,2,1,0:T(8,128)S(1)}, u32[]{:S(2)}, u32[]{:S(2)}) collective-permute-start(f32[4,1,128,128]{3,2,1,0:T(8,128)S(1)} %get-tuple-element.81), channel_id=1, source_target_pairs={{16,0},{32,16},{48,32},{64,48},{80,64},{96,80},{112,96},{17,1},{33... | collective-permute-start | bytes 786440 | tf_op jit(solution)/shard_map/ppermute | solution.py:158
  302.5 5.4 %copy-start.13 = (f32[4,8,128]{2,1,0:T(8,128)S(1)}, f32[4,8,128]{2,1,0:T(8,128)}, u32[]{:S(2)}) copy-start(f32[4,8,128]{2,1,0:T(8,128)} %shard_map.74) | copy-start | bytes 49156
  302.5 0.7 copy-start.11
  303.2 0.7 copy-start.12
  303.9 19.2 %copy-start.1 = (s32[64,2]{0,1:T(2,128)S(1)}, s32[64,2]{0,1:T(2,128)}, u32[]{:S(2)}) copy-start(s32[64,2]{0,1:T(2,128)} %param.8) | copy-start | bytes 1540
  308.8 3.6 %collective-permute-start.14 = (f32[4]{0:T(128)S(1)}, f32[4]{0:T(128)S(1)}, u32[]{:S(2)}, u32[]{:S(2)}) collective-permute-start(f32[4]{0:T(128)S(1)} %add_reduce_fusion), channel_id=1, source_target_pairs={{0,16},{16,0},{32,48},{48,32},{64,80},{80,64},{96,112},{112,96},{1... | collective-permute-start | bytes 56 | tf_op jit(solution)/shard_map/ppermute | solution.py:281
  312.4 5.1 %collective-permute-start.15 = (f32[4]{0:T(128)S(1)}, f32[4]{0:T(128)S(1)}, u32[]{:S(2)}, u32[]{:S(2)}) collective-permute-start(f32[4]{0:T(128)S(1)} %add.111), channel_id=1, source_target_pairs={{0,32},{16,48},{32,0},{48,16},{64,96},{80,112},{96,64},{112,80},{1... | collective-permute-start | bytes 56 | tf_op jit(solution)/shard_map/ppermute | solution.py:281
  317.5 5.1 %collective-permute-start.16 = (f32[4]{0:T(128)S(1)}, f32[4]{0:T(128)S(1)}, u32[]{:S(2)}, u32[]{:S(2)}) collective-permute-start(f32[4]{0:T(128)S(1)} %add.112), channel_id=1, source_target_pairs={{0,64},{16,80},{32,96},{48,112},{64,0},{80,16},{96,32},{112,48},{1... | collective-permute-start | bytes 56 | tf_op jit(solution)/shard_map/ppermute | solution.py:281
Sparse Core Ops, SparseCore 0:
  9.6 172.3 all-gather.1
